TPU v7x, 128 devices: a whole 4x4x4 slice. The times are simulated.
128 devices in a mesh: ctx: 32 (over y, x, core), head: 4 (over z).
Axes of the slice: x: 4, y: 4, z: 4, core: 2. Of those that a mesh axis runs over, the one named last changes fastest.
Arguments:
- queries: bfloat16 [8192, 4, 8, 128], P('ctx', 'head'), may hold values from -6 to 6
- keys: bfloat16 [8192, 8, 128], P('ctx'), may hold values from -6 to 6
- values: bfloat16 [8192, 8, 128], P('ctx'), may hold values from -6 to 6
- dout: bfloat16 [8192, 4, 8, 128], P('ctx', 'head'), may hold values from -24 to 24
- signs: int32 [2, 128, 32], replicated, may hold values from 0 to 1
Outputs:
- dq: bfloat16 [8192, 4, 8, 128], P('ctx', 'head')
- dk: bfloat16 [8192, 8, 128], P('ctx', 'head')
- dv: bfloat16 [8192, 8, 128], P('ctx', 'head')
All inputs are finite; a program needn't handle non-finite values.
Results may differ from a plain program's by a relative error of at most 0.0075.
Values may be sent and summed in bfloat16 or wider, within the bound.
No kernel may reach another device: no remote copies, remote signals or barrier semaphores. Data moves between devices by JAX's collectives and lax.ppermute only.
A program may use at most 128 MiB of HBM per device.

v0:
```python
import jax
import jax.numpy as jnp
from jax import lax
from jax.sharding import PartitionSpec as P

highest = lax.Precision.HIGHEST


def prefix(part, axis, combine, identity, reverse):
    count = lax.axis_size(axis)
    place = lax.axis_index(axis)
    ahead = count - 1 - place if reverse else place
    gathered = jax.tree.map(lambda a: lax.all_gather(a, axis), part)
    state = jax.tree.map(lambda a, e: jnp.zeros_like(a) + jnp.asarray(e, a.dtype), part, identity)

    def one(step, state):
        source = count - 1 - step if reverse else step
        return combine(
            state, jax.tree.map(lambda a: lax.dynamic_index_in_dim(a, source, 0, False), gathered)
        )

    return lax.fori_loop(0, ahead, one, state)


def sketch_parts(tokens, projector, pattern):
    inverse = tokens.shape[-1] ** (-0.5)
    sketch_one = (
        jnp.einsum(pattern, tokens, projector[0], preferred_element_type=jnp.float32) * inverse
    )
    sketch_two = (
        jnp.einsum(pattern, tokens, projector[1], preferred_element_type=jnp.float32) * inverse
    )
    return (sketch_one, sketch_two)


def features(sketch_one, sketch_two):
    width = sketch_one.shape[-1]
    sketch = sketch_one * sketch_two
    outer = sketch[..., :, None] * sketch[..., None, :] * (1.0 / width)
    return outer.reshape(sketch.shape[:-1] + (width * width,)).astype(jnp.bfloat16)


def feature_back(cotangent, sketch_one, sketch_two, proj_wide):
    width = sketch_one.shape[-1]
    sketch = sketch_one * sketch_two
    square = cotangent.reshape(cotangent.shape[:-1] + (width, width))
    dsketch = (
        jnp.einsum("...ab,...b->...a", square, sketch, precision=highest)
        + jnp.einsum("...ab,...a->...b", square, sketch, precision=highest)
    ) * (1.0 / width)
    back_one = jnp.einsum("...f,df->...d", dsketch * sketch_two, proj_wide[0], precision=highest)
    back_two = jnp.einsum("...f,df->...d", dsketch * sketch_one, proj_wide[1], precision=highest)
    return (back_one + back_two) * proj_wide.shape[1] ** (-0.5)


def head_step(inputs):
    key_feat, value_head, state_in, total_in, query_feat, grad_out = inputs
    length = key_feat.shape[0]
    causal = lax.broadcasted_iota(jnp.int32, (length, length), 0) >= lax.broadcasted_iota(
        jnp.int32, (length, length), 1
    )

    def member(query_one, grad_one):
        scores = jnp.where(
            causal,
            jnp.einsum("if,jf->ij", query_one, key_feat, preferred_element_type=jnp.float32),
            0.0,
        )
        weights = scores.astype(jnp.bfloat16)
        query_wide = query_one.astype(jnp.float32)
        numerator = jnp.dot(weights, value_head, preferred_element_type=jnp.float32) + jnp.dot(
            query_wide, state_in, precision=highest
        )
        denominator = 1.0 + jnp.sum(scores, 1) + jnp.dot(query_wide, total_in, precision=highest)
        output_rows = numerator / denominator[:, None]
        grad_rows = grad_one.astype(jnp.float32) / denominator[:, None]
        grad_low = grad_rows.astype(jnp.bfloat16)
        correction = -jnp.sum(grad_rows * output_rows, 1)
        dscores = jnp.where(
            causal,
            jnp.einsum("id,jd->ij", grad_low, value_head, preferred_element_type=jnp.float32)
            + correction[:, None],
            0.0,
        ).astype(jnp.bfloat16)
        grad_qfeat = (
            jnp.dot(dscores, key_feat, preferred_element_type=jnp.float32)
            + jnp.dot(grad_rows, state_in.T, precision=highest)
            + correction[:, None] * total_in[None, :]
        )
        grad_kfeat = jnp.einsum("ij,if->jf", dscores, query_one, preferred_element_type=jnp.float32)
        grad_value = jnp.einsum("ij,id->jd", weights, grad_low, preferred_element_type=jnp.float32)
        suffix_part = jnp.einsum(
            "if,id->fd", query_one, grad_low, preferred_element_type=jnp.float32
        )
        suffix_sum = jnp.dot(correction, query_wide, precision=highest)
        return (grad_qfeat, grad_kfeat, grad_value, suffix_part, suffix_sum)

    results = jax.vmap(member)(query_feat, grad_out)
    return (
        results[0],
        jnp.sum(results[1], 0),
        jnp.sum(results[2], 0),
        jnp.sum(results[3], 0),
        jnp.sum(results[4], 0),
    )


def add_states(earlier, later):
    return (earlier[0] + later[0], earlier[1] + later[1])


def prefix_scan(state, total):
    return prefix(
        (state, total), "ctx", add_states, (jnp.zeros_like(state), jnp.zeros_like(total)), False
    )


def suffix_scan(state, total):
    return prefix(
        (state, total), "ctx", add_states, (jnp.zeros_like(state), jnp.zeros_like(total)), True
    )


def later_terms(key_feat, value_heads, merged_state, merged_total):
    kfeat_extra = (
        jnp.einsum("htd,hfd->htf", value_heads.astype(jnp.float32), merged_state, precision=highest)
        + merged_total[:, None, :]
    )
    value_extra = jnp.einsum(
        "htf,hfd->htd", key_feat.astype(jnp.float32), merged_state, precision=highest
    )
    return (kfeat_extra, value_extra)


def body(queries, keys, values, dout, signs):
    projector = (2 * signs - 1).astype(jnp.bfloat16)
    proj_wide = projector.astype(jnp.float32)
    heads_all = keys.shape[1]
    owned = heads_all // lax.axis_size("head")
    offset = lax.axis_index("head") * owned
    key_part = lax.dynamic_slice_in_dim(keys, offset, owned, 1)
    value_part = lax.dynamic_slice_in_dim(values, offset, owned, 1)
    query_part, grad_part = (
        lax.all_to_all(queries, "head", split_axis=2, concat_axis=1, tiled=True),
        lax.all_to_all(dout, "head", split_axis=2, concat_axis=1, tiled=True),
    )
    key_one, key_two = sketch_parts(key_part, projector, "thd,df->htf")
    key_feat = features(key_one, key_two)
    query_one, query_two = sketch_parts(query_part, projector, "tmhd,df->hmtf")
    query_feat = features(query_one, query_two)
    value_heads = value_part.transpose(1, 0, 2)
    grad_heads = grad_part.transpose(2, 1, 0, 3)
    block_state = jnp.einsum(
        "htf,htd->hfd", key_feat, value_heads, preferred_element_type=jnp.float32
    )
    block_total = jnp.sum(key_feat, 1, dtype=jnp.float32)
    state_in, total_in = prefix_scan(block_state, block_total)
    grad_qfeat, grad_kfeat, grad_value, suffix_part, suffix_sum = lax.map(
        head_step, (key_feat, value_heads, state_in, total_in, query_feat, grad_heads)
    )
    query_grad = feature_back(grad_qfeat, query_one, query_two, proj_wide)
    query_low = query_grad.transpose(2, 1, 0, 3).astype(jnp.bfloat16)
    query_out = lax.all_to_all(query_low, "head", split_axis=1, concat_axis=2, tiled=True)
    merged_state, merged_total = suffix_scan(suffix_part, suffix_sum)
    kfeat_extra, value_extra = later_terms(key_feat, value_heads, merged_state, merged_total)
    key_sum = feature_back(grad_kfeat + kfeat_extra, key_one, key_two, proj_wide)
    value_sum = grad_value + value_extra
    key_out = key_sum.transpose(1, 0, 2).astype(jnp.bfloat16)
    value_out = value_sum.transpose(1, 0, 2).astype(jnp.bfloat16)
    return (query_out, key_out, value_out)


def solution(mesh):
    in_specs = (
        P("ctx", "head", None, None),
        P("ctx", None, None),
        P("ctx", None, None),
        P("ctx", "head", None, None),
        P(),
    )
    out_specs = (P("ctx", "head", None, None), P("ctx", "head", None), P("ctx", "head", None))
    return jax.shard_map(body, mesh=mesh, in_specs=in_specs, out_specs=out_specs, check_vma=False)
```

profile of v0, /device:TPU:1, one launch (start us, length us, event | category | flops | bytes accessed | tf_op | source)
XLA Modules:
  0.0 446.2 jit_solution(8889384571155527893)
XLA Ops:
  10.9 1.4 fusion.130
  13.2 5.9 %all-to-all-start.1 = ((bf16[256,1,8,128]{3,0,1,2:T(8,128)(2,1)}), bf16[256,1,8,128]{3,0,1,2:T(8,128)(2,1)S(1)}, u32[]{:S(2)}, u32[]{:S(2)}) async-start(bf16[256,1,8,128]{3,0,1,2:T(8,128)(2,1)} %copy.129), calls=%async_computation.1 | async-start | bytes 1048576 | tf_op jit(solution)/shard_map/all_to_all | solution.py:144
  20.8 28.1 %all_gather.27 = f32[32,2,1024]{2,1,0:T(2,128)} all-gather(f32[1,2,1024]{2,1,0:T(2,128)S(1)} %all_gather.26), channel_id=1, replica_groups=mesh['ctx'=32,'head'=4] {'ctx'}, dimensions={0}, use_global_device_ids=true | all-gather | bytes 270336 | tf_op jit(solution)/shard_map/all_gather | solution.py:13
  48.8 4.5 %all-to-all-start = ((bf16[256,1,8,128]{3,0,1,2:T(8,128)(2,1)}), bf16[256,1,8,128]{3,0,1,2:T(8,128)(2,1)S(1)}, u32[]{:S(2)}, u32[]{:S(2)}) async-start(bf16[256,1,8,128]{3,0,1,2:T(8,128)(2,1)} %copy.128), calls=%async_computation | async-start | bytes 1048576 | tf_op jit(solution)/shard_map/all_to_all | solution.py:145
  54.6 4.2 multiply_convert_fusion
  58.9 71.5 %all-gather.7.cloned.1.call-done = f32[64,1024,128]{2,1,0:T(8,128)} async-done(((f32[2,1024,128]{2,1,0:T(8,128)}), f32[64,1024,128]{2,1,0:T(8,128)}) %all-gather.7.cloned.1.call-update) | async-done | bytes 33554448 | tf_op jit(solution)/shard_map/all_gather | solution.py:13
  130.4 2.4 while.44
  131.2 1.4 bitcast_add_fusion.10
  134.5 71.2 %while.45 = (s32[]{:T(128)}, f32[2,4,256,1024]{2,3,1,0:T(8,128)}, f32[2,256,1024]{2,1,0:T(8,128)}, f32[2,256,128]{2,1,0:T(8,128)}, f32[2,1024,128]{2,1,0:T(8,128...) while((s32[]{:T(128)}, f32[2,4,256,1024]{2,3,1,0:T(8,128)}, ...), condition=%wide.region_6.7_spmd, body=%wide.region_3.6_spmd.sunk | while | flops 5333779456 | bytes 86299912 | solution.py:158
  134.5 2.5 fusion.199
  138.4 2.5 fusion.197
  144.3 1.7 fusion.206
  148.6 3.1 fusion.205
  151.8 1.7 fusion.203
  154.3 5.8 %add_bitcast_fusion.2 = f32[1,4,256,1024]{3,2,1,0:T(8,128)} fusion(f32[4,256,1024]{2,1,0:T(8,128)S(1)} %fusion.202, f32[1024]{0:T(1024)S(1)} %bitcast.284, f32[4,256]{1,0:T(4,128)S(1)} %get-tuple-element.479, f32[2,1024,128]{2,1,0:T(8,128)S(1)} %get-tuple-element.553, s32[]{:T(128)S(6)} %copy.268, bf16[1,4,256,128]{2,3,1,0:T(8,128)(2,1)S(1)} %copy.246, ...), kind=kOutput, calls=%fused_computation.2.clone.1 | convolution fusion | flops 1614020608 | bytes 9187332 | tf_op jit(solution)/shard_map/while/body/eval_jaxpr/vmap()/dot_general | solution.py:87
  160.1 5.4 %copy.247 = f32[1,4,256,1024]{2,3,1,0:T(8,128)} copy(f32[1,4,256,1024]{3,2,1,0:T(8,128)} %add_bitcast_fusion.2) | data formatting | bytes 8388608 | tf_op jit(solution)/shard_map/while/body/jit(dynamic_update_index_in_dim)/dynamic_update_slice | solution.py:158
  165.5 4.6 %constant_dynamic-update-slice_fusion.2 = f32[2,4,256,1024]{2,3,1,0:T(8,128)} fusion(f32[2,4,256,1024]{2,3,1,0:T(8,128)} %get-tuple-element.529, f32[1,4,256,1024]{2,3,1,0:T(8,128)} %copy.247, s32[]{:T(128)S(6)} %copy.268), kind=kLoop, calls=%fused_computation.71.clone.1 | loop fusion | bytes 8388612 | tf_op jit(solution)/shard_map/while/body/jit(dynamic_update_index_in_dim)/dynamic_update_slice | solution.py:158
  170.1 2.5 fusion.199
  174.0 2.5 fusion.197
  179.9 1.7 fusion.206
  184.3 3.1 fusion.205
  187.4 1.7 fusion.203
  189.9 5.8 %add_bitcast_fusion.2 = f32[1,4,256,1024]{3,2,1,0:T(8,128)} fusion(f32[4,256,1024]{2,1,0:T(8,128)S(1)} %fusion.202, f32[1024]{0:T(1024)S(1)} %bitcast.284, f32[4,256]{1,0:T(4,128)S(1)} %get-tuple-element.479, f32[2,1024,128]{2,1,0:T(8,128)S(1)} %get-tuple-element.553, s32[]{:T(128)S(6)} %copy.268, bf16[1,4,256,128]{2,3,1,0:T(8,128)(2,1)S(1)} %copy.246, ...), kind=kOutput, calls=%fused_computation.2.clone.1 | convolution fusion | flops 1614020608 | bytes 9187332 | tf_op jit(solution)/shard_map/while/body/eval_jaxpr/vmap()/dot_general | solution.py:87
  195.8 5.4 %copy.247 = f32[1,4,256,1024]{2,3,1,0:T(8,128)} copy(f32[1,4,256,1024]{3,2,1,0:T(8,128)} %add_bitcast_fusion.2) | data formatting | bytes 8388608 | tf_op jit(solution)/shard_map/while/body/jit(dynamic_update_index_in_dim)/dynamic_update_slice | solution.py:158
  201.1 4.5 %constant_dynamic-update-slice_fusion.2 = f32[2,4,256,1024]{2,3,1,0:T(8,128)} fusion(f32[2,4,256,1024]{2,3,1,0:T(8,128)} %get-tuple-element.529, f32[1,4,256,1024]{2,3,1,0:T(8,128)} %copy.247, s32[]{:T(128)S(6)} %copy.268), kind=kLoop, calls=%fused_computation.71.clone.1 | loop fusion | bytes 8388612 | tf_op jit(solution)/shard_map/while/body/jit(dynamic_update_index_in_dim)/dynamic_update_slice | solution.py:158
  205.7 5.4 %multiply_reduce_fusion.1 = f32[2,4,256,32]{2,3,1,0:T(8,128)S(1)} fusion(f32[2,4,256,1024]{2,3,1,0:T(8,128)} %get-tuple-element.186, f32[2,4,256,32]{2,3,0,1:T(8,128)} %copy-done.5), kind=kLoop, calls=%fused_computation.82 | loop fusion | flops 4128768 | bytes 8912896
  211.6 1.4 multiply_reduce_fusion
  215.9 4.2 all-to-all-start.2
  220.0 87.2 %all-gather.3 = f32[32,2,1024]{2,1,0:T(2,128)S(1)} all-gather(f32[1,2,1024]{2,1,0:T(2,128)} %bitcast.58), channel_id=4, replica_groups=mesh['ctx'=32,'head'=4] {'ctx'}, dimensions={0}, use_global_device_ids=true | all-gather | bytes 270336 | tf_op jit(solution)/shard_map/all_gather | solution.py:13
  308.4 75.2 %all-gather.9.cloned.1.call-done = f32[64,1024,128]{2,1,0:T(8,128)} async-done(((f32[2,1024,128]{2,1,0:T(8,128)}), f32[64,1024,128]{2,1,0:T(8,128)}) %all-gather.9.cloned.1.call-update) | async-done | bytes 33554448 | tf_op jit(solution)/shard_map/all_gather | solution.py:13
  383.7 44.4 %while.46 = (s32[]{:T(128)}, f32[2,1024,128]{2,1,0:T(8,128)S(1)}, f32[2,1024]{1,0:T(2,128)S(1)}, s32[]{:T(128)}, f32[32,2,1024,128]{3,2,1,0:T(8,128)}, /*index=5...) while((s32[]{:T(128)}, f32[2,1024,128]{2,1,0:T(8,128)S(1)}, ...), condition=%wide.region_8.9_spmd, body=%wide.region_7.8_spmd.sunk | while | flops 264198 | bytes 3170467 | solution.py:22
  383.7 1.4 bitcast_add_fusion.13
  385.2 1.4 bitcast_add_fusion.13
  386.7 1.4 bitcast_add_fusion.13
  388.2 1.4 bitcast_add_fusion.13
  389.6 1.4 bitcast_add_fusion.13
  391.1 1.4 bitcast_add_fusion.13
  392.6 1.4 bitcast_add_fusion.13
  394.1 1.4 bitcast_add_fusion.13
  395.6 1.4 bitcast_add_fusion.13
  397.0 1.4 bitcast_add_fusion.13
  398.5 1.4 bitcast_add_fusion.13
  400.0 1.4 bitcast_add_fusion.13
  401.5 1.4 bitcast_add_fusion.13
  403.0 1.4 bitcast_add_fusion.13
  404.4 1.4 bitcast_add_fusion.13
  405.9 1.4 bitcast_add_fusion.13
  407.4 1.4 bitcast_add_fusion.13
  408.9 1.4 bitcast_add_fusion.13
  410.4 1.4 bitcast_add_fusion.13
  411.8 1.4 bitcast_add_fusion.13
  413.3 1.4 bitcast_add_fusion.13
  414.8 1.4 bitcast_add_fusion.13
  416.3 1.4 bitcast_add_fusion.13
  417.8 1.4 bitcast_add_fusion.13
  419.2 1.4 bitcast_add_fusion.13
  420.7 1.4 bitcast_add_fusion.13
  422.2 1.4 bitcast_add_fusion.13
  423.7 1.4 bitcast_add_fusion.13
  425.2 1.4 bitcast_add_fusion.13
  426.6 1.4 bitcast_add_fusion.13
  428.1 2.2 fusion.98
  430.3 4.1 add_add_fusion
  434.3 2.0 copy.189
  (140 shorter events, 34.3 us)
Async XLA Ops:
  7.2 1.1 copy-start
  7.2 5.1 %copy-start.14 = (bf16[256,1,8,128]{3,2,1,0:T(8,128)(2,1)S(1)}, bf16[256,1,8,128]{3,2,1,0:T(8,128)(2,1)}, u32[]{:S(2)}) copy-start(bf16[256,1,8,128]{3,2,1,0:T(8,128)(2,1)} %param.11) | copy-start | bytes 1572868
  7.2 12.5 %copy-start.15 = (bf16[256,1,8,128]{3,2,1,0:T(8,128)(2,1)S(1)}, bf16[256,1,8,128]{3,2,1,0:T(8,128)(2,1)}, u32[]{:S(2)}) copy-start(bf16[256,1,8,128]{3,2,1,0:T(8,128)(2,1)} %param.14) | copy-start | bytes 1572868
  7.2 123.2 %all-gather.7.cloned.1.call-start = ((), (), s32[]{:S(2)}) async-start(), calls=%async_computation.3 | async-start | bytes 34603008 | tf_op jit(solution)/shard_map/all_gather | solution.py:13
  8.1 45.5 %copy-start.17 = (bf16[2,128,32]{1,2,0:T(8,128)(2,1)}, bf16[2,128,32]{1,2,0:T(8,128)(2,1)S(1)}, u32[]{:S(2)}) copy-start(bf16[2,128,32]{1,2,0:T(8,128)(2,1)S(1)} %add_convert_fusion) | copy-start | bytes 49156
  9.7 3.5 copy-start.12
  10.5 2.7 copy-start.9
  13.2 35.6 %all-to-all-start.1 = ((bf16[256,1,8,128]{3,0,1,2:T(8,128)(2,1)}), bf16[256,1,8,128]{3,0,1,2:T(8,128)(2,1)S(1)}, u32[]{:S(2)}, u32[]{:S(2)}) async-start(bf16[256,1,8,128]{3,0,1,2:T(8,128)(2,1)} %copy.129), calls=%async_computation.1 | async-start | bytes 1048576 | tf_op jit(solution)/shard_map/all_to_all | solution.py:144
  48.8 84.0 %all-to-all-start = ((bf16[256,1,8,128]{3,0,1,2:T(8,128)(2,1)}), bf16[256,1,8,128]{3,0,1,2:T(8,128)(2,1)S(1)}, u32[]{:S(2)}, u32[]{:S(2)}) async-start(bf16[256,1,8,128]{3,0,1,2:T(8,128)(2,1)} %copy.128), calls=%async_computation | async-start | bytes 1048576 | tf_op jit(solution)/shard_map/all_to_all | solution.py:145
  53.3 330.3 %all-gather.9.cloned.1.call-start = ((), (), s32[]{:S(2)}) async-start(), calls=%async_computation.4 | async-start | bytes 34603008 | tf_op jit(solution)/shard_map/all_gather | solution.py:13
  53.6 1.0 copy-start.7
  54.6 75.8 %copy-start.5 = (f32[2,4,256,32]{2,3,0,1:T(8,128)}, f32[2,4,256,32]{2,3,0,1:T(8,128)S(1)}, u32[]{:S(2)}) copy-start(f32[2,4,256,32]{2,3,0,1:T(8,128)S(1)} %get-tuple-element.324) | copy-start | bytes 786436
  138.4 4.6 %copy-start.2 = (bf16[2,4,256,1024]{2,3,1,0:T(8,128)(2,1)S(1)}, bf16[2,4,256,1024]{2,3,1,0:T(8,128)(2,1)}, u32[]{:S(2)}) copy-start(bf16[2,4,256,1024]{2,3,1,0:T(8,128)(2,1)} %get-tuple-element.549) | copy-start | bytes 12582916 | tf_op jit(solution)/shard_map/while
  147.3 4.4 copy-start.3
  151.8 2.5 copy-start.16
  174.0 4.6 %copy-start.2 = (bf16[2,4,256,1024]{2,3,1,0:T(8,128)(2,1)S(1)}, bf16[2,4,256,1024]{2,3,1,0:T(8,128)(2,1)}, u32[]{:S(2)}) copy-start(bf16[2,4,256,1024]{2,3,1,0:T(8,128)(2,1)} %get-tuple-element.549) | copy-start | bytes 12582916 | tf_op jit(solution)/shard_map/while
  183.0 4.4 copy-start.3
  187.4 2.5 copy-start.16
  205.7 5.8 %copy-start.4 = (f32[2,4,256,1024]{2,3,1,0:T(8,128)S(1)}, f32[2,4,256,1024]{2,3,1,0:T(8,128)}, u32[]{:S(2)}) copy-start(f32[2,4,256,1024]{2,3,1,0:T(8,128)} %get-tuple-element.186) | copy-start | bytes 25165828
  205.7 5.8 %copy-start.6 = (f32[2,4,256,32]{2,3,0,1:T(8,128)S(1)}, f32[2,4,256,32]{2,3,0,1:T(8,128)}, u32[]{:S(2)}) copy-start(f32[2,4,256,32]{2,3,0,1:T(8,128)} %copy-done.5) | copy-start | bytes 786436
  211.5 1.4 copy-start.8
  211.5 1.4 copy-start.11
  211.5 1.5 copy-start.18
  215.9 91.4 %all-to-all-start.2 = ((bf16[256,4,2,128]{3,0,2,1:T(8,128)(2,1)}), bf16[256,4,2,128]{3,0,2,1:T(8,128)(2,1)S(1)}, u32[]{:S(2)}, u32[]{:S(2)}) async-start(bf16[256,4,2,128]{3,0,2,1:T(8,128)(2,1)} %copy.141), calls=%async_computation.2 | async-start | bytes 1048576 | tf_op jit(solution)/shard_map/all_to_all | solution.py:163
  430.2 6.8 %copy-start.10 = (f32[2,256,32]{1,2,0:T(8,128)S(1)}, f32[2,256,32]{1,2,0:T(8,128)}, u32[]{:S(2)}) copy-start(f32[2,256,32]{1,2,0:T(8,128)} %copy-done.9) | copy-start | bytes 196612
  430.3 9.1 %copy-start.1 = (bf16[256,8,128]{2,1,0:T(8,128)(2,1)S(1)}, bf16[256,8,128]{2,1,0:T(8,128)(2,1)}, u32[]{:S(2)}) copy-start(bf16[256,8,128]{2,1,0:T(8,128)(2,1)} %param.13) | copy-start | bytes 1572868
  434.3 3.4 copy-start.13
  434.3 3.8 copy-start.19
Sparse Core Ops, SparseCore 0:
  12.4 117.8 all-gather.6
  205.8 177.7 all-gather.8
where the time goes:
time: 450 us; the launch traced here: 446 us
  waiting for transfers between devices  147 us (33%)
  blocking collectives  115 us (26%)
  other arithmetic  59.9 us (13%)
  matrix products  58.2 us (13%)
  local copies, waits for them, and re-layouts  35.9 us (8%)
  starting transfers between devices  14.6 us (3%)
  between operations  14.3 us (3%)
    all_gather x2, waiting for transfers between devices, prefix(): gathered = jax.tree.map(lambda a: lax.all_gather(a, axis), part)  147 us
    all_gather x2, blocking collectives, prefix(): gathered = jax.tree.map(lambda a: lax.all_gather(a, axis), part)  115 us
    add x62, other arithmetic, add_states(): return (earlier[0] + later[0], earlier[1] + later[1])  45.7 us
    dynamic_update_slice x6, local copies, waits for them, and re-layouts, body(): lax.map(head_step, (key_feat, value_heads, state_in, total_in, query_feat...  22.6 us
    dot_general x2, matrix products, member(): jnp.dot(grad_rows, state_in.T, precision=highest)  11.6 us
  transfers between devices with their start and end apart: 5, of which 2 were waited for; matrix products, arithmetic and copies ran while one was open for 5% of the time, Pallas kernels for 0%

commit v1 on v0

v1 whole, which is shorter than its diff:
```python
import jax
import jax.numpy as jnp
from jax import lax
from jax.sharding import PartitionSpec as P

highest = lax.Precision.HIGHEST
f32 = jnp.float32
bf16 = jnp.bfloat16


def split2(x):
    hi = x.astype(bf16)
    lo = (x - hi.astype(f32)).astype(bf16)
    return hi, lo


def dot_split(pattern, exact, wide):
    hi, lo = split2(wide)
    return jnp.einsum(pattern, exact, hi, preferred_element_type=f32) + jnp.einsum(
        pattern, exact, lo, preferred_element_type=f32
    )


def dot_split3(pattern, first, second):
    fh, fl = split2(first)
    sh, sl = split2(second)
    return (
        jnp.einsum(pattern, fh, sh, preferred_element_type=f32)
        + jnp.einsum(pattern, fh, sl, preferred_element_type=f32)
        + jnp.einsum(pattern, fl, sh, preferred_element_type=f32)
    )


def ctx_scan(state, total, reverse):
    n = lax.axis_size("ctx")
    heads, feat, width = state.shape
    total_rows = feat // width
    rows = feat + total_rows
    per_head = n // heads
    unit = per_head * 8
    padded = -(-rows // unit) * unit
    comb = jnp.concatenate(
        [
            state,
            total.reshape(heads, total_rows, width),
            jnp.zeros((heads, padded - rows, width), f32),
        ],
        axis=1,
    )
    chunks = comb.reshape(n, padded // per_head, width)
    got = lax.all_to_all(chunks, "ctx", 0, 0, tiled=True)
    src = lax.broadcasted_iota(jnp.int32, (n, n), 1)
    dst = lax.broadcasted_iota(jnp.int32, (n, n), 0)
    mask = (src > dst if reverse else src < dst).astype(f32)
    summed = jnp.einsum("ij,jrc->irc", mask, got, precision=highest)
    back = lax.all_to_all(summed, "ctx", 0, 0, tiled=True)
    comb_out = back.reshape(heads, padded, width)
    return comb_out[:, :feat], comb_out[:, feat:rows].reshape(heads, feat)


def sketch_parts(tokens, projector, pattern):
    inverse = tokens.shape[-1] ** (-0.5)
    sketch_one = jnp.einsum(pattern, tokens, projector[0], preferred_element_type=f32) * inverse
    sketch_two = jnp.einsum(pattern, tokens, projector[1], preferred_element_type=f32) * inverse
    return (sketch_one, sketch_two)


def features(sketch_one, sketch_two):
    width = sketch_one.shape[-1]
    sketch = sketch_one * sketch_two
    outer = sketch[..., :, None] * sketch[..., None, :] * (1.0 / width)
    return outer.reshape(sketch.shape[:-1] + (width * width,)).astype(bf16)


def feature_back(cotangent, sketch_one, sketch_two, proj_wide):
    width = sketch_one.shape[-1]
    sketch = sketch_one * sketch_two
    square = cotangent.reshape(cotangent.shape[:-1] + (width, width))
    dsketch = (
        jnp.einsum("...ab,...b->...a", square, sketch, precision=highest)
        + jnp.einsum("...ab,...a->...b", square, sketch, precision=highest)
    ) * (1.0 / width)
    back_one = jnp.einsum("...f,df->...d", dsketch * sketch_two, proj_wide[0], precision=highest)
    back_two = jnp.einsum("...f,df->...d", dsketch * sketch_one, proj_wide[1], precision=highest)
    return (back_one + back_two) * proj_wide.shape[1] ** (-0.5)


def body(queries, keys, values, dout, signs):
    projector = (2 * signs - 1).astype(bf16)
    proj_wide = projector.astype(f32)
    heads_all = keys.shape[1]
    owned = heads_all // lax.axis_size("head")
    offset = lax.axis_index("head") * owned
    key_part = lax.dynamic_slice_in_dim(keys, offset, owned, 1)
    value_part = lax.dynamic_slice_in_dim(values, offset, owned, 1)
    query_part = lax.all_to_all(queries, "head", split_axis=2, concat_axis=1, tiled=True)
    grad_part = lax.all_to_all(dout, "head", split_axis=2, concat_axis=1, tiled=True)
    key_one, key_two = sketch_parts(key_part, projector, "thd,df->htf")
    key_feat = features(key_one, key_two)
    value_heads = value_part.transpose(1, 0, 2)
    block_state = jnp.einsum("htf,htd->hfd", key_feat, value_heads, preferred_element_type=f32)
    block_total = jnp.sum(key_feat, 1, dtype=f32)
    state_in, total_in = ctx_scan(block_state, block_total, False)

    query_one, query_two = sketch_parts(query_part, projector, "tmhd,df->hmtf")
    query_feat = features(query_one, query_two)
    grad_heads = grad_part.transpose(2, 1, 0, 3).astype(f32)
    length = key_feat.shape[1]
    causal = lax.broadcasted_iota(jnp.int32, (length, length), 0) >= lax.broadcasted_iota(
        jnp.int32, (length, length), 1
    )
    scores = jnp.where(
        causal, jnp.einsum("hmif,hjf->hmij", query_feat, key_feat, preferred_element_type=f32), 0.0
    )
    weights = scores.astype(bf16)
    numerator = jnp.einsum(
        "hmij,hjd->hmid", weights, value_heads, preferred_element_type=f32
    ) + dot_split("hmif,hfd->hmid", query_feat, state_in)
    denominator = 1.0 + jnp.sum(scores, -1) + dot_split("hmif,hf->hmi", query_feat, total_in)
    output_rows = numerator / denominator[..., None]
    grad_rows = grad_heads / denominator[..., None]
    grad_low = grad_rows.astype(bf16)
    correction = -jnp.sum(grad_rows * output_rows, -1)
    suffix_part = jnp.einsum("hmif,hmid->hfd", query_feat, grad_low, preferred_element_type=f32)
    suffix_sum = dot_split("hmif,hmi->hf", query_feat, correction)
    merged_state, merged_total = ctx_scan(suffix_part, suffix_sum, True)

    dscores = jnp.where(
        causal,
        jnp.einsum("hmid,hjd->hmij", grad_low, value_heads, preferred_element_type=f32)
        + correction[..., None],
        0.0,
    ).astype(bf16)
    grad_qfeat = (
        jnp.einsum("hmij,hjf->hmif", dscores, key_feat, preferred_element_type=f32)
        + dot_split3("hmid,hfd->hmif", grad_rows, state_in)
        + correction[..., None] * total_in[:, None, None, :]
    )
    query_grad = feature_back(grad_qfeat, query_one, query_two, proj_wide)
    query_low = query_grad.transpose(2, 1, 0, 3).astype(bf16)
    query_out = lax.all_to_all(query_low, "head", split_axis=1, concat_axis=2, tiled=True)

    grad_kfeat = jnp.einsum("hmij,hmif->hjf", dscores, query_feat, preferred_element_type=f32)
    grad_value = jnp.einsum("hmij,hmid->hjd", weights, grad_low, preferred_element_type=f32)
    kfeat_total = (
        grad_kfeat
        + dot_split("htd,hfd->htf", value_heads, merged_state)
        + merged_total[:, None, :]
    )
    value_total = grad_value + dot_split("htf,hfd->htd", key_feat, merged_state)
    key_sum = feature_back(kfeat_total, key_one, key_two, proj_wide)
    key_out = key_sum.transpose(1, 0, 2).astype(bf16)
    value_out = value_total.transpose(1, 0, 2).astype(bf16)
    return (query_out, key_out, value_out)


def solution(mesh):
    in_specs = (
        P("ctx", "head", None, None),
        P("ctx", None, None),
        P("ctx", None, None),
        P("ctx", "head", None, None),
        P(),
    )
    out_specs = (P("ctx", "head", None, None), P("ctx", "head", None), P("ctx", "head", None))
    return jax.shard_map(body, mesh=mesh, in_specs=in_specs, out_specs=out_specs, check_vma=False)
```

time: 450 us -> 191 us (0.42)
  blocking collectives: 115 us -> 0 us
  waiting for transfers between devices: 147 us -> 45.7 us
  other arithmetic: 59.9 us -> 12.6 us
  starting transfers between devices: 14.6 us -> 44.8 us
  between operations: 14.3 us -> 1.04 us
  matrix products: 58.2 us -> 53 us
    all_gather x2 -> x0, waiting for transfers between devices: 147 us -> none  [prefix(): gathered = jax.tree.map(lambda a: lax.all_gather(a, axis), part)]
    all_gather x2 -> x0, blocking collectives: 115 us -> none  [prefix(): gathered = jax.tree.map(lambda a: lax.all_gather(a, axis), part)]
    add x64 -> x1, other arithmetic: 45.7 us -> 0.01 us  [body(): 1.0 + jnp.sum(scores, -1) + dot_split('hmif,hf->hmi', query_feat, total_in)]
    all_to_all x0 -> x4, waiting for transfers between devices: none -> 32 us  [the longest x2 16.8 us: ctx_scan(): back = lax.all_to_all(summed, 'ctx', 0, 0, tiled=True)]
    all_to_all x0 -> x4, starting transfers between devices: none -> 30.7 us  [the longest x2 15.6 us: ctx_scan(): back = lax.all_to_all(summed, 'ctx', 0, 0, tiled=True)]
    dynamic_update_slice x6 -> x0, local copies, waits for them, and re-layouts: 22.6 us -> none  [body(): lax.map(head_step, (key_feat, value_heads, state_in, total_in, query_feat...]
    unnamed x41 -> x50, local copies, waits for them, and re-layouts: 7.77 us -> 23.2 us
    all_to_all x1, waiting for transfers between devices: 0.01 us -> 5.25 us  [body(): lax.all_to_all(query_low, 'head', split_axis=1, concat_axis=2, tiled=True)]
  transfers between devices with their start and end apart: 5 -> 7, of which waited for: 2 -> 6; matrix products, arithmetic and copies ran while one was open for 5% -> 32% of each run, Pallas kernels for 0% -> 0%
where the time goes in v1:
time: 191 us; the launch traced here: 190 us
  matrix products  53 us (28%)
  waiting for transfers between devices  45.7 us (24%)
  starting transfers between devices  44.8 us (23%)
  local copies, waits for them, and re-layouts  32.4 us (17%)
  other arithmetic  12.6 us (7%)
    unnamed x50, local copies, waits for them, and re-layouts  23.2 us
    all_to_all x2, waiting for transfers between devices, ctx_scan(): back = lax.all_to_all(summed, 'ctx', 0, 0, tiled=True)  16.8 us
    all_to_all x2, starting transfers between devices, ctx_scan(): back = lax.all_to_all(summed, 'ctx', 0, 0, tiled=True)  15.6 us
    all_to_all x2, waiting for transfers between devices, ctx_scan(): got = lax.all_to_all(chunks, 'ctx', 0, 0, tiled=True)  15.1 us
    all_to_all x2, starting transfers between devices, ctx_scan(): got = lax.all_to_all(chunks, 'ctx', 0, 0, tiled=True)  15.1 us
    dot_general x1, matrix products, dot_split3(): jnp.einsum(pattern, fl, sh, preferred_element_type=f32)  9.18 us
    dot_general x5, matrix products, dot_split(): jnp.einsum(pattern, exact, lo, preferred_element_type=f32)  7.45 us
    unnamed x3, other arithmetic  6.75 us
  transfers between devices with their start and end apart: 7, of which 6 were waited for; matrix products, arithmetic and copies ran while one was open for 32% of the time, Pallas kernels for 0%

profile of v1, /device:TPU:1, one launch (start us, length us, event | category | flops | bytes accessed | tf_op | source)
XLA Modules:
  0.0 189.6 jit_solution(6725487639584662659)
XLA Ops:
  0.6 1.9 %copy.167 = bf16[256,1,8,128]{3,0,1,2:T(8,128)(2,1)} copy(bf16[256,1,8,128]{3,2,1,0:T(8,128)(2,1)} %param.5) | data formatting | bytes 1048576 | tf_op args[0]
  2.5 5.9 %all-to-all-start.1 = ((bf16[256,1,8,128]{3,0,1,2:T(8,128)(2,1)}), bf16[256,1,8,128]{3,0,1,2:T(8,128)(2,1)S(1)}, u32[]{:S(2)}, u32[]{:S(2)}) async-start(bf16[256,1,8,128]{3,0,1,2:T(8,128)(2,1)} %copy.167), calls=%async_computation.1 | async-start | bytes 1048576 | tf_op jit(solution)/shard_map/all_to_all | solution.py:96
  8.4 1.5 constant_dynamic-slice_fusion
  10.0 0.8 fusion.97
  11.8 1.3 maximum_maximum_fusion
  13.1 3.6 %all-to-all-done.1 = bf16[256,1,8,128]{3,0,1,2:T(8,128)(2,1)S(1)} async-done(((bf16[256,1,8,128]{3,0,1,2:T(8,128)(2,1)}), bf16[256,1,8,128]{3,0,1,2:T(8,128)(2,1)S(1)}, u32[]{:S(2)}, u32[]{:S(2)}) %all-to-all-start.1) | async-done | bytes 524320 | tf_op jit(solution)/shard_map/all_to_all | solution.py:96
  16.7 9.2 %all-to-all-start.2 = ((f32[32,72,128]{2,1,0:T(8,128)}), f32[32,72,128]{2,1,0:T(8,128)S(1)}, u32[]{:S(2)}, u32[]{:S(2)}) async-start(f32[32,72,128]{2,1,0:T(8,128)} %bitcast.23), calls=%async_computation.2 | async-start | bytes 2359296 | tf_op jit(solution)/shard_map/all_to_all | solution.py:51
  25.9 1.9 %copy.164 = bf16[256,1,8,128]{3,0,1,2:T(8,128)(2,1)} copy(bf16[256,1,8,128]{3,2,1,0:T(8,128)(2,1)} %param.8) | data formatting | bytes 1048576 | tf_op args[3]
  27.8 0.7 iota_compare_fusion
  28.5 15.1 %all-to-all-done.2 = f32[32,72,128]{2,1,0:T(8,128)S(1)} async-done(((f32[32,72,128]{2,1,0:T(8,128)}), f32[32,72,128]{2,1,0:T(8,128)S(1)}, u32[]{:S(2)}, u32[]{:S(2)}) %all-to-all-start.2) | async-done | bytes 1179680 | tf_op jit(solution)/shard_map/all_to_all | solution.py:51
  43.6 4.1 %all-to-all-start = ((bf16[256,1,8,128]{3,0,1,2:T(8,128)(2,1)}), bf16[256,1,8,128]{3,0,1,2:T(8,128)(2,1)}, u32[]{:S(2)}, u32[]{:S(2)}) async-start(bf16[256,1,8,128]{3,0,1,2:T(8,128)(2,1)} %copy.164), calls=%async_computation | async-start | bytes 1048576 | tf_op jit(solution)/shard_map/all_to_all | solution.py:97
  48.0 0.8 fusion.10
  48.8 1.7 copy.175
  50.5 4.9 %all-to-all-done = bf16[256,1,8,128]{3,0,1,2:T(8,128)(2,1)} async-done(((bf16[256,1,8,128]{3,0,1,2:T(8,128)(2,1)}), bf16[256,1,8,128]{3,0,1,2:T(8,128)(2,1)}, u32[]{:S(2)}, u32[]{:S(2)}) %all-to-all-start) | async-done | bytes 524320 | tf_op jit(solution)/shard_map/all_to_all | solution.py:97
  55.5 6.9 %all-to-all-start.3 = ((f32[32,72,128]{2,1,0:T(8,128)}), f32[32,72,128]{2,1,0:T(8,128)S(1)}, u32[]{:S(2)}, u32[]{:S(2)}) async-start(f32[32,72,128]{2,1,0:T(8,128)} %copy.175), calls=%async_computation.3 | async-start | bytes 2359296 | tf_op jit(solution)/shard_map/all_to_all | solution.py:56
  62.4 1.0 fusion.96
  63.4 2.3 %copy.166 = f32[256,4,2,128]{0,3,1,2:T(8,128)} copy(bf16[256,4,2,128]{3,0,2,1:T(8,128)(2,1)} %bitcast.65) | data formatting | bytes 1572864 | tf_op jit(solution)/shard_map/convert_element_type | solution.py:107
  65.7 1.5 multiply_convert_fusion
  67.2 1.4 select_reduce_fusion
  68.6 0.6 copy-done
  69.1 1.0 copy-done.7
  70.1 1.4 fusion.28
  71.5 8.6 %all-to-all-done.3 = f32[32,72,128]{2,1,0:T(8,128)S(1)} async-done(((f32[32,72,128]{2,1,0:T(8,128)}), f32[32,72,128]{2,1,0:T(8,128)S(1)}, u32[]{:S(2)}, u32[]{:S(2)}) %all-to-all-start.3) | async-done | bytes 1179680 | tf_op jit(solution)/shard_map/all_to_all | solution.py:56
  80.1 1.0 slice.33
  81.2 1.6 copy.283
  82.7 3.0 %fusion.76 = f32[2,1,4,256]{3,1,2,0:T(1,128)S(1)} fusion(bf16[2,4,256,1024]{2,3,1,0:T(8,128)(2,1)} %bitcast.204, bf16[2,1024,1,1]{1,0,2,3:T(2,128)(2,1)S(1)} %fusion.88), kind=kOutput, calls=%fused_computation.114 | convolution fusion | flops 4194304 | bytes 4206592 | tf_op jit(solution)/shard_map/hmif,hf->hmi/dot_general | solution.py:19
  85.7 0.5 copy-done.1
  86.2 0.6 fusion.78
  86.8 0.7 fusion.26
  87.6 0.5 copy-done.3
  88.2 1.2 convolution_bitcast_fusion
  89.4 4.5 %fusion.36 = f32[2,4,256,1024]{3,2,1,0:T(8,128)} fusion(bf16[2,4,256,128]{2,3,1,0:T(8,128)(2,1)S(1)} %fusion.95, f32[2,1024,128]{1,2,0:T(8,128)S(1)} %copy.283), kind=kOutput, calls=%fused_computation.67 | convolution fusion | flops 537919488 | bytes 9961472 | tf_op jit(solution)/shard_map/hmid,hfd->hmif/dot_general | solution.py:29
  94.0 4.5 %fusion.24 = f32[2,4,256,1024]{3,2,1,0:T(8,128)} fusion(bf16[2,4,256,128]{2,3,1,0:T(8,128)(2,1)S(1)} %fusion.95, f32[2,1024,128]{1,2,0:T(8,128)S(1)} %copy.283), kind=kOutput, calls=%fused_computation.53 | convolution fusion | flops 537133056 | bytes 9961472 | tf_op jit(solution)/shard_map/hmid,hfd->hmif/dot_general | solution.py:28
  98.5 1.0 fusion.7
  99.5 1.2 fusion.74
  100.7 1.2 fusion.72
  101.9 1.5 select_convert_fusion
  103.4 1.3 maximum_maximum_fusion.1
  104.7 5.8 %all-to-all-start.5 = ((f32[32,72,128]{2,1,0:T(8,128)}), f32[32,72,128]{2,1,0:T(8,128)}, u32[]{:S(2)}, u32[]{:S(2)}) async-start(f32[32,72,128]{2,1,0:T(8,128)} %bitcast.224), calls=%async_computation.5 | async-start | bytes 2359296 | tf_op jit(solution)/shard_map/all_to_all | solution.py:51
  110.5 2.8 %fusion.98 = f32[2,4,256,1024]{3,2,1,0:T(8,128)S(1)} fusion(bf16[2,4,256,256]{2,3,1,0:T(8,128)(2,1)} %select_convert_fusion, bf16[2,256,1024,1]{1,2,3,0:T(8,128)(2,1)S(1)} %bitcast.215), kind=kOutput, calls=%fused_computation.142 | convolution fusion | flops 1073741824 | bytes 10485760 | tf_op jit(solution)/shard_map/hmij,hjf->hmif/dot_general | solution.py:135
  113.4 9.2 %multiply_add_fusion = f32[2,4,256,1024]{3,2,1,0:T(8,128)} fusion(f32[2,4,256,1024]{3,2,1,0:T(8,128)S(1)} %fusion.98, f32[2,4,256,1024]{3,2,1,0:T(8,128)} %fusion.24, f32[2,4,256,1024]{3,2,1,0:T(8,128)} %fusion.36, f32[2,1024]{1,0:T(2,128)S(1)} %bitcast.229, f32[2,4,256]{2,1,0:T(4,128)S(1)} %get-tuple-element.24, bf16[2,4,256,128]{2,3,1,0:T(8,128)(2,1)S(1)} %fusion.95, ...), kind=kOutput, calls=%fused_computation.2 | convolution fusion | flops 548667392 | bytes 36200448 | tf_op jit(solution)/shard_map/hmid,hfd->hmif/dot_general | solution.py:30
  122.5 8.7 %copy.279 = f32[2,4,256,1024]{2,3,1,0:T(8,128)} copy(f32[2,4,256,1024]{3,2,1,0:T(8,128)} %multiply_add_fusion) | data formatting | bytes 16777216
  131.3 5.4 %multiply_reduce_fusion.1 = f32[2,4,256,32]{2,3,1,0:T(8,128)S(1)} fusion(f32[2,4,256,1024]{2,3,1,0:T(8,128)} %copy.279, f32[2,4,256,32]{2,3,0,1:T(8,128)S(1)} %get-tuple-element.25), kind=kLoop, calls=%fused_computation.1 | loop fusion | flops 4128768 | bytes 8912896
  137.0 1.4 multiply_reduce_fusion
  138.5 1.0 fusion.31
  139.5 1.0 fusion.6
  140.5 0.8 copy.194
  141.3 4.2 %all-to-all-start.4 = ((bf16[256,4,2,128]{3,0,2,1:T(8,128)(2,1)}), bf16[256,4,2,128]{3,0,2,1:T(8,128)(2,1)}, u32[]{:S(2)}, u32[]{:S(2)}) async-start(bf16[256,4,2,128]{3,0,2,1:T(8,128)(2,1)} %copy.194), calls=%async_computation.4 | async-start | bytes 1048576 | tf_op jit(solution)/shard_map/all_to_all | solution.py:141
  145.5 2.0 %fusion.8 = f32[32,72,128]{2,0,1:T(8,128)S(1)} fusion(f32[32,72,128]{2,1,0:T(8,128)} %all-to-all-done.5), kind=kOutput, calls=%fused_computation.25 | convolution fusion | flops 113247232 | bytes 2359296 | tf_op jit(solution)/shard_map/ij,jrc->irc/dot_general | solution.py:55
  147.5 1.7 copy.198
  149.2 5.3 %all-to-all-done.4 = bf16[256,4,2,128]{3,0,2,1:T(8,128)(2,1)} async-done(((bf16[256,4,2,128]{3,0,2,1:T(8,128)(2,1)}), bf16[256,4,2,128]{3,0,2,1:T(8,128)(2,1)}, u32[]{:S(2)}, u32[]{:S(2)}) %all-to-all-start.4) | async-done | bytes 524320 | tf_op jit(solution)/shard_map/all_to_all | solution.py:141
  154.5 8.6 %all-to-all-start.6 = ((f32[32,72,128]{2,1,0:T(8,128)}), f32[32,72,128]{2,1,0:T(8,128)S(1)}, u32[]{:S(2)}, u32[]{:S(2)}) async-start(f32[32,72,128]{2,1,0:T(8,128)} %copy.198), calls=%async_computation.6 | async-start | bytes 2359296 | tf_op jit(solution)/shard_map/all_to_all | solution.py:56
  163.2 2.4 %convolution_bitcast_fusion.1 = f32[2,256,128]{2,1,0:T(8,128)} fusion(bf16[2,4,256,128]{2,3,1,0:T(8,128)(2,1)S(1)} %fusion.95, bf16[2,4,256,256]{2,3,1,0:T(8,128)(2,1)} %copy-done.7, pred[256,256]{0,1:T(8,128)(4,1)S(1)} %copy-done.12), kind=kOutput, calls=%fused_computation.37 | convolution fusion | flops 134742016 | bytes 1900544 | tf_op jit(solution)/shard_map/hmij,hmid->hjd/dot_general | solution.py:144
  165.6 4.8 %fusion.99 = f32[2,256,1024,1]{2,1,3,0:T(8,128)} fusion(bf16[2,4,256,256]{2,3,1,0:T(8,128)(2,1)S(1)} %copy-done.6, bf16[2,4,256,1024]{2,3,1,0:T(8,128)(2,1)} %bitcast.205), kind=kOutput, calls=%fused_computation.143 | convolution fusion | flops 1073741824 | bytes 7340032 | tf_op jit(solution)/shard_map/hmij,hmif->hjf/dot_general | solution.py:143
  170.4 2.2 %copy.203 = bf16[256,1,8,128]{3,2,1,0:T(8,128)(2,1)} copy(bf16[256,1,8,128]{3,0,2,1:T(8,128)(2,1)} %bitcast.46) | data formatting | bytes 1048576
  172.6 8.2 %all-to-all-done.6 = f32[32,72,128]{2,1,0:T(8,128)S(1)} async-done(((f32[32,72,128]{2,1,0:T(8,128)}), f32[32,72,128]{2,1,0:T(8,128)S(1)}, u32[]{:S(2)}, u32[]{:S(2)}) %all-to-all-start.6) | async-done | bytes 1179680 | tf_op jit(solution)/shard_map/all_to_all | solution.py:56
  180.8 0.5 fusion.94
  181.3 0.4 fusion.42
  181.8 0.5 copy-done.14
  182.3 0.5 fusion.19
  182.8 0.8 copy.205
  183.6 1.8 fusion
  185.4 1.9 %copy.280 = f32[2,256,1024]{1,2,0:T(8,128)S(1)} copy(f32[2,256,1024]{2,1,0:T(8,128)} %fusion) | data formatting | bytes 4194304
  188.8 0.8 copy.204
  (56 shorter events, 3.5 us)
Async XLA Ops:
  0.6 7.8 %copy-start.17 = (s32[2,128,32]{1,2,0:T(8,128)S(1)}, s32[2,128,32]{1,2,0:T(8,128)}, u32[]{:S(2)}) copy-start(s32[2,128,32]{1,2,0:T(8,128)} %param.9) | copy-start | bytes 98308
  2.5 14.1 %all-to-all-start.1 = ((bf16[256,1,8,128]{3,0,1,2:T(8,128)(2,1)}), bf16[256,1,8,128]{3,0,1,2:T(8,128)(2,1)S(1)}, u32[]{:S(2)}, u32[]{:S(2)}) async-start(bf16[256,1,8,128]{3,0,1,2:T(8,128)(2,1)} %copy.167), calls=%async_computation.1 | async-start | bytes 1048576 | tf_op jit(solution)/shard_map/all_to_all | solution.py:96
  11.4 1.7 copy-start.15
  16.7 26.9 %all-to-all-start.2 = ((f32[32,72,128]{2,1,0:T(8,128)}), f32[32,72,128]{2,1,0:T(8,128)S(1)}, u32[]{:S(2)}, u32[]{:S(2)}) async-start(f32[32,72,128]{2,1,0:T(8,128)} %bitcast.23), calls=%async_computation.2 | async-start | bytes 2359296 | tf_op jit(solution)/shard_map/all_to_all | solution.py:51
  43.6 11.8 %all-to-all-start = ((bf16[256,1,8,128]{3,0,1,2:T(8,128)(2,1)}), bf16[256,1,8,128]{3,0,1,2:T(8,128)(2,1)}, u32[]{:S(2)}, u32[]{:S(2)}) async-start(bf16[256,1,8,128]{3,0,1,2:T(8,128)(2,1)} %copy.164), calls=%async_computation | async-start | bytes 1048576 | tf_op jit(solution)/shard_map/all_to_all | solution.py:97
  55.5 24.6 %all-to-all-start.3 = ((f32[32,72,128]{2,1,0:T(8,128)}), f32[32,72,128]{2,1,0:T(8,128)S(1)}, u32[]{:S(2)}, u32[]{:S(2)}) async-start(f32[32,72,128]{2,1,0:T(8,128)} %copy.175), calls=%async_computation.3 | async-start | bytes 2359296 | tf_op jit(solution)/shard_map/all_to_all | solution.py:56
  65.7 1.5 copy-start.10
  67.2 2.0 %copy-start = (bf16[2,4,256,32,32]{2,4,3,1,0:T(8,128)(2,1)}, bf16[2,4,256,32,32]{2,4,3,1,0:T(8,128)(2,1)S(1)}, u32[]{:S(2)}) copy-start(bf16[2,4,256,32,32]{2,4,3,1,0:T(8,128)(2,1)S(1)} %multiply_convert_fusion) | copy-start | bytes 12582916
  69.1 1.0 copy-start.7
  82.7 3.5 %copy-start.1 = (bf16[2,4,256,32,32]{2,4,3,1,0:T(8,128)(2,1)S(1)}, bf16[2,4,256,32,32]{2,4,3,1,0:T(8,128)(2,1)}, u32[]{:S(2)}) copy-start(bf16[2,4,256,32,32]{2,4,3,1,0:T(8,128)(2,1)} %copy-done) | copy-start | bytes 12582916
  86.8 1.2 copy-start.3
  94.0 4.5 %copy-start.8 = (f32[2,4,256,128]{2,3,1,0:T(8,128)S(1)}, f32[2,4,256,128]{2,3,1,0:T(8,128)}, u32[]{:S(2)}) copy-start(f32[2,4,256,128]{2,3,1,0:T(8,128)} %fusion.28) | copy-start | bytes 3145732
  100.7 1.2 copy-start.11
  101.9 1.6 copy-start.16
  104.7 36.7 %all-to-all-start.5 = ((f32[32,72,128]{2,1,0:T(8,128)}), f32[32,72,128]{2,1,0:T(8,128)}, u32[]{:S(2)}, u32[]{:S(2)}) async-start(f32[32,72,128]{2,1,0:T(8,128)} %bitcast.224), calls=%async_computation.5 | async-start | bytes 2359296 | tf_op jit(solution)/shard_map/all_to_all | solution.py:51
  110.5 2.8 %copy-start.4 = (f32[256,4,2,128]{0,3,1,2:T(8,128)S(1)}, f32[256,4,2,128]{0,3,1,2:T(8,128)}, u32[]{:S(2)}) copy-start(f32[256,4,2,128]{0,3,1,2:T(8,128)} %copy.166) | copy-start | bytes 3145732
  131.3 5.8 %copy-start.2 = (f32[2,4,256,1024]{2,3,1,0:T(8,128)S(1)}, f32[2,4,256,1024]{2,3,1,0:T(8,128)}, u32[]{:S(2)}) copy-start(f32[2,4,256,1024]{2,3,1,0:T(8,128)} %copy.279) | copy-start | bytes 25165828
  137.0 1.4 copy-start.9
  141.3 13.2 %all-to-all-start.4 = ((bf16[256,4,2,128]{3,0,2,1:T(8,128)(2,1)}), bf16[256,4,2,128]{3,0,2,1:T(8,128)(2,1)}, u32[]{:S(2)}, u32[]{:S(2)}) async-start(bf16[256,4,2,128]{3,0,2,1:T(8,128)(2,1)} %copy.194), calls=%async_computation.4 | async-start | bytes 1048576 | tf_op jit(solution)/shard_map/all_to_all | solution.py:141
  147.5 15.6 %copy-start.12 = (pred[256,256]{0,1:T(8,128)(4,1)S(1)}, pred[256,256]{0,1:T(8,128)(4,1)}, u32[]{:S(2)}) copy-start(pred[256,256]{0,1:T(8,128)(4,1)} %iota_compare_fusion) | copy-start | bytes 196612
  154.5 26.3 %all-to-all-start.6 = ((f32[32,72,128]{2,1,0:T(8,128)}), f32[32,72,128]{2,1,0:T(8,128)S(1)}, u32[]{:S(2)}, u32[]{:S(2)}) async-start(f32[32,72,128]{2,1,0:T(8,128)} %copy.198), calls=%async_computation.6 | async-start | bytes 2359296 | tf_op jit(solution)/shard_map/all_to_all | solution.py:56
  163.1 2.5 %copy-start.6 = (bf16[2,4,256,256]{2,3,1,0:T(8,128)(2,1)S(1)}, bf16[2,4,256,256]{2,3,1,0:T(8,128)(2,1)}, u32[]{:S(2)}) copy-start(bf16[2,4,256,256]{2,3,1,0:T(8,128)(2,1)} %select_convert_fusion) | copy-start | bytes 3145732
  181.3 1.0 copy-start.14
  181.8 1.8 copy-start.5
  187.3 1.1 copy-start.13

commit v2 on v1

v2 whole, which is shorter than its diff:
```python
import jax
import jax.numpy as jnp
import numpy as np
from jax import lax
from jax.sharding import PartitionSpec as P

highest = lax.Precision.HIGHEST
f32 = jnp.float32
bf16 = jnp.bfloat16


def triangle(width):
    rows, cols = np.triu_indices(width)
    take_a = np.eye(width, dtype=np.float32)[:, rows]
    take_b = np.eye(width, dtype=np.float32)[:, cols]
    weight = np.where(rows == cols, 1.0, 2.0).astype(np.float32)
    off = (rows != cols).astype(np.float32)
    return take_a, take_b, weight, off


def split_parts(x, count):
    parts = []
    rest = x
    for _ in range(count - 1):
        hi = lax.reduce_precision(rest, exponent_bits=8, mantissa_bits=7)
        parts.append(hi.astype(bf16))
        rest = rest - hi
    parts.append(rest.astype(bf16))
    return parts


def dot_parts(pattern, wide, other, count, wide_first=True):
    total = None
    for part in split_parts(wide, count):
        args = (part, other) if wide_first else (other, part)
        term = jnp.einsum(pattern, *args, preferred_element_type=f32)
        total = term if total is None else total + term
    return total


def dot_split(pattern, exact, wide):
    return dot_parts(pattern, wide, exact, 2, wide_first=False)


def dot_split3(pattern, first, second):
    fh, fl = split_parts(first, 2)
    sh, sl = split_parts(second, 2)
    return (
        jnp.einsum(pattern, fh, sh, preferred_element_type=f32)
        + jnp.einsum(pattern, fh, sl, preferred_element_type=f32)
        + jnp.einsum(pattern, fl, sh, preferred_element_type=f32)
    )


def take_exact(x, select):
    return dot_parts("...a,ak->...k", x, select, 3)


def ctx_scan(state, total, reverse):
    n = lax.axis_size("ctx")
    heads, feat, width = state.shape
    total_rows = -(-feat // width)
    flat = jnp.concatenate(
        [
            state.reshape(heads * feat, width),
            jnp.pad(total, ((0, 0), (0, total_rows * width - feat))).reshape(
                heads * total_rows, width
            ),
        ],
        axis=0,
    )
    rows = flat.shape[0]
    per = -(-rows // (n * 8)) * 8
    flat = jnp.pad(flat, ((0, n * per - rows), (0, 0)))
    got = lax.all_to_all(flat.reshape(n, per, width), "ctx", 0, 0, tiled=True)
    src = lax.broadcasted_iota(jnp.int32, (n, n), 1)
    dst = lax.broadcasted_iota(jnp.int32, (n, n), 0)
    mask = (src > dst if reverse else src < dst).astype(f32)
    summed = jnp.einsum("ij,jrc->irc", mask, got, precision=highest)
    back = lax.all_to_all(summed, "ctx", 0, 0, tiled=True).reshape(n * per, width)
    state_out = back[: heads * feat].reshape(heads, feat, width)
    total_out = back[heads * feat : heads * (feat + total_rows)].reshape(heads, total_rows * width)
    return state_out, total_out[:, :feat]


def sketch_parts(tokens, projector, pattern):
    inverse = tokens.shape[-1] ** (-0.5)
    sketch_one = jnp.einsum(pattern, tokens, projector[0], preferred_element_type=f32) * inverse
    sketch_two = jnp.einsum(pattern, tokens, projector[1], preferred_element_type=f32) * inverse
    return (sketch_one, sketch_two)


def tri_features(sketch_one, sketch_two, take_a, take_b):
    width = sketch_one.shape[-1]
    sketch = sketch_one * sketch_two
    first = take_exact(sketch, take_a)
    second = take_exact(sketch, take_b)
    return (first * second * (1.0 / width)).astype(bf16)


def tri_feature_back(cotangent, sketch_one, sketch_two, proj_wide, take_a, take_b, off):
    width = sketch_one.shape[-1]
    sketch = sketch_one * sketch_two
    first = take_exact(sketch, take_a)
    second = take_exact(sketch, take_b)
    spread = jnp.concatenate([cotangent * second, cotangent * first * off], axis=-1)
    gather = jnp.concatenate([take_a.T, take_b.T], axis=0).astype(bf16)
    dsketch = dot_parts("...k,ka->...a", spread, gather, 2) * (2.0 / width)
    back_one = jnp.einsum("...f,df->...d", dsketch * sketch_two, proj_wide[0], precision=highest)
    back_two = jnp.einsum("...f,df->...d", dsketch * sketch_one, proj_wide[1], precision=highest)
    return (back_one + back_two) * proj_wide.shape[1] ** (-0.5)


def body(queries, keys, values, dout, signs):
    projector = (2 * signs - 1).astype(bf16)
    proj_wide = projector.astype(f32)
    width = signs.shape[-1]
    take_a_np, take_b_np, weight_np, off_np = triangle(width)
    take_a = jnp.asarray(take_a_np, bf16)
    take_b = jnp.asarray(take_b_np, bf16)
    weight = jnp.asarray(weight_np, bf16)
    off = jnp.asarray(off_np, f32)
    heads_all = keys.shape[1]
    owned = heads_all // lax.axis_size("head")
    offset = lax.axis_index("head") * owned
    key_part = lax.dynamic_slice_in_dim(keys, offset, owned, 1)
    value_part = lax.dynamic_slice_in_dim(values, offset, owned, 1)
    both = lax.all_to_all(
        jnp.stack([queries, dout]), "head", split_axis=3, concat_axis=2, tiled=True
    )
    query_part, grad_part = both[0], both[1]
    key_one, key_two = sketch_parts(key_part, projector, "thd,df->htf")
    key_feat = tri_features(key_one, key_two, take_a, take_b)
    key_wfeat = key_feat * weight
    value_heads = value_part.transpose(1, 0, 2)
    block_state = jnp.einsum("htf,htd->hfd", key_feat, value_heads, preferred_element_type=f32)
    block_total = jnp.sum(key_feat, 1, dtype=f32)
    state_in, total_in = ctx_scan(block_state, block_total, False)

    query_one, query_two = sketch_parts(query_part, projector, "tmhd,df->hmtf")
    query_feat = tri_features(query_one, query_two, take_a, take_b)
    query_wfeat = query_feat * weight
    grad_heads = grad_part.transpose(2, 1, 0, 3).astype(f32)
    length = key_feat.shape[1]
    causal = lax.broadcasted_iota(jnp.int32, (length, length), 0) >= lax.broadcasted_iota(
        jnp.int32, (length, length), 1
    )
    scores = jnp.where(
        causal,
        jnp.einsum("hmif,hjf->hmij", query_wfeat, key_feat, preferred_element_type=f32),
        0.0,
    )
    weights = scores.astype(bf16)
    numerator = jnp.einsum(
        "hmij,hjd->hmid", weights, value_heads, preferred_element_type=f32
    ) + dot_split("hmif,hfd->hmid", query_wfeat, state_in)
    denominator = 1.0 + jnp.sum(scores, -1) + dot_split("hmif,hf->hmi", query_wfeat, total_in)
    output_rows = numerator / denominator[..., None]
    grad_rows = grad_heads / denominator[..., None]
    grad_low = grad_rows.astype(bf16)
    correction = -jnp.sum(grad_rows * output_rows, -1)
    suffix_part = jnp.einsum("hmif,hmid->hfd", query_feat, grad_low, preferred_element_type=f32)
    suffix_sum = dot_split("hmif,hmi->hf", query_feat, correction)
    merged_state, merged_total = ctx_scan(suffix_part, suffix_sum, True)

    dscores = jnp.where(
        causal,
        jnp.einsum("hmid,hjd->hmij", grad_low, value_heads, preferred_element_type=f32)
        + correction[..., None],
        0.0,
    ).astype(bf16)
    grad_qfeat = (
        jnp.einsum("hmij,hjf->hmif", dscores, key_feat, preferred_element_type=f32)
        + dot_split3("hmid,hfd->hmif", grad_rows, state_in)
        + correction[..., None] * total_in[:, None, None, :]
    )
    query_grad = tri_feature_back(
        grad_qfeat, query_one, query_two, proj_wide, take_a, take_b, off
    )
    query_low = query_grad.transpose(2, 1, 0, 3).astype(bf16)
    query_out = lax.all_to_all(query_low, "head", split_axis=1, concat_axis=2, tiled=True)

    grad_kfeat = jnp.einsum("hmij,hmif->hjf", dscores, query_feat, preferred_element_type=f32)
    grad_value = jnp.einsum("hmij,hmid->hjd", weights, grad_low, preferred_element_type=f32)
    kfeat_total = (
        grad_kfeat
        + dot_split("htd,hfd->htf", value_heads, merged_state)
        + merged_total[:, None, :]
    )
    value_total = grad_value + dot_split("htf,hfd->htd", key_wfeat, merged_state)
    key_sum = tri_feature_back(kfeat_total, key_one, key_two, proj_wide, take_a, take_b, off)
    key_out = key_sum.transpose(1, 0, 2).astype(bf16)
    value_out = value_total.transpose(1, 0, 2).astype(bf16)
    return (query_out, key_out, value_out)


def solution(mesh):
    in_specs = (
        P("ctx", "head", None, None),
        P("ctx", None, None),
        P("ctx", None, None),
        P("ctx", "head", None, None),
        P(),
    )
    out_specs = (P("ctx", "head", None, None), P("ctx", "head", None), P("ctx", "head", None))
    return jax.shard_map(body, mesh=mesh, in_specs=in_specs, out_specs=out_specs, check_vma=False)
```

time: 191 us -> 163 us (0.85)
  local copies, waits for them, and re-layouts: 32.4 us -> 18.7 us
  waiting for transfers between devices: 45.7 us -> 36.9 us
  starting transfers between devices: 44.8 us -> 39.6 us
  other arithmetic: 12.6 us -> 7.43 us
  matrix products: 53 us -> 57.9 us
    unnamed x50 -> x73, local copies, waits for them, and re-layouts: 23.2 us -> 5.08 us
    dot_general x15 -> x31, matrix products: 15.1 us -> 28.7 us  [the longest x26 23.7 us: dot_parts(): term = jnp.einsum(pattern, *args, preferred_element_type=f32)]
    all_to_all x6 -> x5, waiting for transfers between devices: 40.5 us -> 30.6 us  [the longest x1 12.6 us: body(): lax.all_to_all(jnp.stack([queries, dout]), 'head', split_axis=3, concat_a...]
    unnamed x3 -> x0, other arithmetic: 6.75 us -> none
    dot_general x1, matrix products: 9.18 us -> 2.88 us  [dot_split3(): jnp.einsum(pattern, fl, sh, preferred_element_type=f32)]
    dot_general x1, matrix products: 2.83 us -> 8.6 us  [body(): jnp.einsum('hmij,hjf->hmif', dscores, key_feat, preferred_element_type=f32)]
    all_to_all x6 -> x5, starting transfers between devices: 40.6 us -> 35.5 us  [the longest x2 16.1 us: ctx_scan(): got = lax.all_to_all(flat.reshape(n, per, width), 'ctx', 0, 0, tiled=True)]
    slice x1 -> x5, local copies, waits for them, and re-layouts: 1.05 us -> 4.44 us  [the longest x2 2.16 us: ctx_scan(): state_out = back[:heads * feat].reshape(heads, feat, width)]
  transfers between devices with their start and end apart: 7 -> 6, of which waited for: 6 -> 4; matrix products, arithmetic and copies ran while one was open for 32% -> 26% of each run, Pallas kernels for 0% -> 0%
where the time goes in v2:
time: 163 us; the launch traced here: 162 us
  matrix products  57.9 us (36%)
  starting transfers between devices  39.6 us (24%)
  waiting for transfers between devices  36.9 us (23%)
  local copies, waits for them, and re-layouts  18.7 us (11%)
  other arithmetic  7.43 us (5%)
    dot_general x26, matrix products, dot_parts(): term = jnp.einsum(pattern, *args, preferred_element_type=f32)  23.7 us
    all_to_all x2, starting transfers between devices, ctx_scan(): got = lax.all_to_all(flat.reshape(n, per, width), 'ctx', 0, 0, tiled=True)  16.1 us
    all_to_all x2, starting transfers between devices, ctx_scan(): lax.all_to_all(summed, 'ctx', 0, 0, tiled=True).reshape(n * per, width)  14.4 us
    all_to_all x1, waiting for transfers between devices, body(): lax.all_to_all(jnp.stack([queries, dout]), 'head', split_axis=3, concat_a...  12.6 us
    all_to_all x2, waiting for transfers between devices, ctx_scan(): got = lax.all_to_all(flat.reshape(n, per, width), 'ctx', 0, 0, tiled=True)  11.6 us
    dot_general x1, matrix products, body(): jnp.einsum('hmij,hjf->hmif', dscores, key_feat, preferred_element_type=f32)  8.6 us
    all_to_all x2, waiting for transfers between devices, ctx_scan(): lax.all_to_all(summed, 'ctx', 0, 0, tiled=True).reshape(n * per, width)  6.4 us
    all_to_all x1, waiting for transfers between devices, body(): lax.all_to_all(query_low, 'head', split_axis=1, concat_axis=2, tiled=True)  6.33 us
  transfers between devices with their start and end apart: 6, of which 4 were waited for; matrix products, arithmetic and copies ran while one was open for 26% of the time, Pallas kernels for 0%

profile of v2, /device:TPU:1, one launch (start us, length us, event | category | flops | bytes accessed | tf_op | source)
XLA Modules:
  0.0 161.9 jit_solution(4072367906151150819)
XLA Ops:
  0.6 0.8 add_convert_fusion
  1.4 1.5 constant_dynamic-slice_fusion
  3.0 0.8 fusion.156
  3.9 1.1 fusion.107
  6.5 1.4 convert_reduce_fusion
  8.2 0.9 select_maximum_fusion.1
  9.1 8.6 %all-to-all-start.1 = ((f32[32,40,128]{2,1,0:T(8,128)}), f32[32,40,128]{2,1,0:T(8,128)S(1)}, u32[]{:S(2)}, u32[]{:S(2)}) async-start(f32[32,40,128]{2,1,0:T(8,128)} %bitcast.30), calls=%async_computation.1 | async-start | bytes 1310720 | tf_op jit(solution)/shard_map/all_to_all | solution.py:75
  17.9 1.1 pad_maximum_fusion.2
  19.0 11.6 %all-to-all-done.1 = f32[32,40,128]{2,1,0:T(8,128)S(1)} async-done(((f32[32,40,128]{2,1,0:T(8,128)}), f32[32,40,128]{2,1,0:T(8,128)S(1)}, u32[]{:S(2)}, u32[]{:S(2)}) %all-to-all-start.1) | async-done | bytes 655392 | tf_op jit(solution)/shard_map/all_to_all | solution.py:75
  30.6 5.0 %all-to-all-start = ((bf16[2,256,1,8,128]{4,1,2,0,3:T(8,128)(2,1)}), bf16[2,256,1,8,128]{4,1,2,0,3:T(8,128)(2,1)S(1)}, u32[]{:S(2)}, u32[]{:S(2)}) async-start(bf16[2,256,1,8,128]{4,1,2,0,3:T(8,128)(2,1)} %pad_maximum_fusion.2), calls=%async_computation | async-start | bytes 2097152 | tf_op jit(solution)/shard_map/all_to_all | solution.py:128
  36.1 1.2 copy.85
  37.3 12.6 %all-to-all-done = bf16[2,256,1,8,128]{4,1,2,0,3:T(8,128)(2,1)S(1)} async-done(((bf16[2,256,1,8,128]{4,1,2,0,3:T(8,128)(2,1)}), bf16[2,256,1,8,128]{4,1,2,0,3:T(8,128)(2,1)S(1)}, u32[]{:S(2)}, u32[]{:S(2)}) %all-to-all-start) | async-done | bytes 1048608 | tf_op jit(solution)/shard_map/all_to_all | solution.py:128
  49.9 5.9 %all-to-all-start.2 = ((f32[32,40,128]{2,1,0:T(8,128)}), f32[32,40,128]{2,1,0:T(8,128)}, u32[]{:S(2)}, u32[]{:S(2)}) async-start(f32[32,40,128]{2,1,0:T(8,128)} %copy.85), calls=%async_computation.2 | async-start | bytes 1310720 | tf_op jit(solution)/shard_map/all_to_all | solution.py:80
  55.9 0.9 fusion.153
  57.0 1.0 fusion.65
  58.0 0.8 fusion.82
  58.8 0.8 fusion.84
  59.6 0.8 fusion.86
  60.3 0.8 fusion.88
  61.1 1.1 add_add_fusion
  62.2 3.6 %multiply_convert_fusion = (bf16[2,4,256,528]{2,3,1,0:T(8,128)(2,1)S(1)}, f32[2,4,256,528]{2,3,1,0:T(8,128)}) fusion(f32[2,4,256,528]{2,3,1,0:T(8,128)S(1)} %add_add_fusion, bf16[32,528,1,1]{1,0,3,2:T(8,128)(2,1)S(1)} %copy-done.16, bf16[2,4,256,32]{2,3,0,1:T(8,128)(2,1)S(1)} %get-tuple-element.22, f32[2,4,256,528]{2,3,1,0:T(8,128)S(1)} %fusion.88, ...), kind=kOutput, calls=%fused_computation.10 | convolution fusion | flops 74612736 | bytes 19629056 | tf_op jit(solution)/shard_map/...a,ak->...k/dot_general | solution.py:36
  65.8 2.3 %copy.75 = f32[256,4,2,128]{0,3,1,2:T(8,128)} copy(bf16[256,4,2,128]{3,0,2,1:T(8,128)(2,1)} %bitcast.212) | data formatting | bytes 1572864 | tf_op jit(solution)/shard_map/convert_element_type | solution.py:143
  68.1 2.2 %select_reduce_fusion = (f32[2,4,256]{2,1,0:T(4,128)S(1)}, bf16[2,4,256,256]{2,3,1,0:T(8,128)(2,1)}) fusion(pred[256,256]{0,1:T(8,128)(4,1)S(1)} %iota_compare_fusion.1, bf16[2,256,528]{1,2,0:T(8,128)(2,1)S(1)} %get-tuple-element.13, bf16[2,4,256,528]{2,3,1,0:T(8,128)(2,1)S(1)} %get-tuple-element.34, bf16[528]{0:T(1024)(128)(2,1)S(1)} %copy-done.25), kind=kOutput, calls=%fused_computation.19 | convolution fusion | flops 556300288 | bytes 3826720 | tf_op jit(solution)/shard_map/hmif,hjf->hmij/dot_general | solution.py:150
  70.3 0.7 slice.53
  71.0 1.1 slice.55
  72.1 0.6 fusion.155
  73.7 0.7 fusion.29
  74.9 1.6 fusion.143
  76.5 2.8 %fusion.70 = f32[2,4,256,528]{2,3,1,0:T(8,128)} fusion(f32[2,528,128]{2,1,0:T(8,128)S(1)} %bitcast.200, f32[256,4,2,128]{0,3,1,2:T(8,128)S(1)} %copy-done.1, f32[2,4,256]{2,1,0:T(4,128)S(1)} %fusion.114), kind=kOutput, calls=%fused_computation.116 | convolution fusion | flops 278016000 | bytes 5922816 | tf_op jit(solution)/shard_map/hmid,hfd->hmif/dot_general | solution.py:50
  79.3 2.9 %fusion.56 = f32[2,4,256,528]{2,3,1,0:T(8,128)} fusion(f32[2,528,128]{2,1,0:T(8,128)S(1)} %bitcast.201, f32[256,4,2,128]{0,3,1,2:T(8,128)S(1)} %copy-done.1, f32[2,4,256]{2,1,0:T(4,128)S(1)} %fusion.114), kind=kOutput, calls=%fused_computation.96 | convolution fusion | flops 278142976 | bytes 5922816 | tf_op jit(solution)/shard_map/hmid,hfd->hmif/dot_general | solution.py:51
  82.2 2.7 %fusion.69 = f32[2,4,256,528]{2,3,1,0:T(8,128)} fusion(f32[2,528,128]{2,1,0:T(8,128)S(1)} %bitcast.202, f32[256,4,2,128]{0,3,1,2:T(8,128)S(1)} %copy-done.1, f32[2,4,256]{2,1,0:T(4,128)S(1)} %fusion.114), kind=kOutput, calls=%fused_computation.115 | convolution fusion | flops 277880832 | bytes 5922816 | tf_op jit(solution)/shard_map/hmid,hfd->hmif/dot_general | solution.py:49
  84.9 0.7 convolution_add_fusion.7
  86.5 0.6 fusion.135
  87.1 0.7 fusion.121
  87.8 0.7 fusion.119
  88.5 0.6 pad.16
  89.1 1.3 reshape.73
  90.4 1.9 %select_maximum_fusion = f32[1280,128]{1,0:T(8,128)} fusion(f32[10,128]{1,0:T(8,128)} %reshape.73, f32[1056,128]{1,0:T(8,128)} %bitcast.213), kind=kLoop, calls=%fused_computation.85 | loop fusion | flops 655360 | bytes 1201152 | tf_op jit(solution)/shard_map/concatenate | solution.py:63
  92.3 7.6 %all-to-all-start.4 = ((f32[32,40,128]{2,1,0:T(8,128)}), f32[32,40,128]{2,1,0:T(8,128)}, u32[]{:S(2)}, u32[]{:S(2)}) async-start(f32[32,40,128]{2,1,0:T(8,128)} %bitcast.210), calls=%async_computation.4 | async-start | bytes 1310720 | tf_op jit(solution)/shard_map/all_to_all | solution.py:75
  99.9 1.4 select_convert_fusion
  101.4 8.6 %fusion.151 = (f32[2,4,256,528]{2,3,1,0:T(8,128)S(1)}, f32[2,4,256,528]{2,3,1,0:T(8,128)S(1)}) fusion(f32[2,4,256,528]{2,3,1,0:T(8,128)} %copy-done, f32[528]{0:T(1024)S(1)} %copy-done.30, f32[2,4,256,528]{2,3,1,0:T(8,128)} %get-tuple-element.35, f32[2,528]{1,0:T(2,128)S(1)} %copy-done.29, f32[2,4,256]{2,1,0:T(4,128)S(1)} %copy-done.32, ...), kind=kOutput, calls=%fused_computation.201 | convolution fusion | flops 562298880 | bytes 31881408 | tf_op jit(solution)/shard_map/hmij,hjf->hmif/dot_general | solution.py:173
  110.1 1.5 reduce-precision_convert_fusion
  111.6 0.9 fusion.1
  112.5 0.9 fusion.154
  113.4 1.0 fusion.67
  114.4 1.0 fusion.13
  115.5 0.8 copy.98
  116.3 4.1 %all-to-all-start.3 = ((bf16[256,4,2,128]{3,0,2,1:T(8,128)(2,1)}), bf16[256,4,2,128]{3,0,2,1:T(8,128)(2,1)}, u32[]{:S(2)}, u32[]{:S(2)}) async-start(bf16[256,4,2,128]{3,0,2,1:T(8,128)(2,1)} %copy.98), calls=%async_computation.3 | async-start | bytes 1048576 | tf_op jit(solution)/shard_map/all_to_all | solution.py:181
  120.5 1.6 fusion.48
  122.0 1.2 copy.102
  123.3 6.3 %all-to-all-done.3 = bf16[256,4,2,128]{3,0,2,1:T(8,128)(2,1)} async-done(((bf16[256,4,2,128]{3,0,2,1:T(8,128)(2,1)}), bf16[256,4,2,128]{3,0,2,1:T(8,128)(2,1)}, u32[]{:S(2)}, u32[]{:S(2)}) %all-to-all-start.3) | async-done | bytes 524320 | tf_op jit(solution)/shard_map/all_to_all | solution.py:181
  129.6 8.4 %all-to-all-start.5 = ((f32[32,40,128]{2,1,0:T(8,128)}), f32[32,40,128]{2,1,0:T(8,128)}, u32[]{:S(2)}, u32[]{:S(2)}) async-start(f32[32,40,128]{2,1,0:T(8,128)} %copy.102), calls=%async_computation.5 | async-start | bytes 1310720 | tf_op jit(solution)/shard_map/all_to_all | solution.py:80
  138.1 3.1 %convolution_bitcast_fusion = f32[2,256,528]{1,2,0:T(8,128)} fusion(bf16[2,4,256,256]{2,3,1,0:T(8,128)(2,1)} %copy-done.10, bf16[2,4,256,528]{2,3,1,0:T(8,128)(2,1)S(1)} %get-tuple-element.34), kind=kOutput, calls=%fused_computation.22 | convolution fusion | flops 553648128 | bytes 4292608 | tf_op jit(solution)/shard_map/hmij,hmif->hjf/dot_general | solution.py:183
  141.2 1.2 convolution_bitcast_fusion.1
  142.3 2.2 %copy.104 = bf16[256,1,8,128]{3,2,1,0:T(8,128)(2,1)} copy(bf16[256,1,8,128]{3,0,2,1:T(8,128)(2,1)} %bitcast.50) | data formatting | bytes 1048576
  144.6 6.4 %all-to-all-done.5 = f32[32,40,128]{2,1,0:T(8,128)} async-done(((f32[32,40,128]{2,1,0:T(8,128)}), f32[32,40,128]{2,1,0:T(8,128)}, u32[]{:S(2)}, u32[]{:S(2)}) %all-to-all-start.5) | async-done | bytes 655392 | tf_op jit(solution)/shard_map/all_to_all | solution.py:80
  151.0 0.7 slice.57
  151.7 1.1 slice.56
  152.8 1.2 fusion.59
  154.0 1.3 fusion.74
  155.3 1.6 %fusion.27 = bf16[256,2,128]{2,0,1:T(8,128)(2,1)S(1)} fusion(f32[2,256,128]{2,1,0:T(8,128)} %convolution_bitcast_fusion.1, f32[2,256,128]{2,1,0:T(8,128)} %fusion.59, bf16[2,256,528]{1,2,0:T(8,128)(2,1)S(1)} %copy-done.5, bf16[528]{0:T(1024)(128)(2,1)S(1)} %copy-done.26, f32[2,528,128]{2,1,0:T(8,128)S(1)} %bitcast.206), kind=kOutput, calls=%fused_computation.53 | convolution fusion | flops 70078464 | bytes 1737760 | tf_op jit(solution)/shard_map/htf,hfd->htd/dot_general | solution.py:36
  157.0 0.8 copy.106
  157.8 1.8 %fusion.152 = (f32[2,256,528]{1,2,0:T(8,128)S(1)}, f32[2,256,528]{1,2,0:T(8,128)S(1)}) fusion(f32[2,256,528]{1,2,0:T(8,128)S(1)} %copy-done.7, f32[528]{0:T(1024)S(1)} %copy-done.31, f32[2,256,528]{1,2,0:T(8,128)S(1)} %copy-done.8, f32[2,528]{1,0:T(2,128)S(1)} %bitcast.214, f32[2,256,528]{1,2,0:T(8,128)} %convolution_bitcast_fusion, ...), kind=kOutput, calls=%fused_computation.202 | convolution fusion | flops 71233536 | bytes 7166144 | tf_op jit(solution)/shard_map/htd,hfd->htf/dot_general | solution.py:36
  161.1 0.8 copy.105
  (95 shorter events, 7.0 us)
Async XLA Ops:
  0.6 4.3 %copy-start.18 = (bf16[32,528,1]{1,0,2:T(8,128)(2,1)S(1)}, bf16[32,528,1]{1,0,2:T(8,128)(2,1)}, u32[]{:S(2)}) copy-start(bf16[32,528,1]{1,0,2:T(8,128)(2,1)} %constant.58) | copy-start | bytes 101380
  2.9 82.7 %copy-start.11 = (bf16[256,2,128]{2,1,0:T(2,128)(2,1)}, bf16[256,2,128]{2,1,0:T(2,128)(2,1)S(1)}, u32[]{:S(2)}) copy-start(bf16[256,2,128]{2,1,0:T(2,128)(2,1)S(1)} %get-tuple-element.44) | copy-start | bytes 393220
  5.0 0.8 copy-start.17
  5.8 2.1 %copy-start.6 = (f32[2,256,528]{1,2,0:T(8,128)}, f32[2,256,528]{1,2,0:T(8,128)S(1)}, u32[]{:S(2)}) copy-start(f32[2,256,528]{1,2,0:T(8,128)S(1)} %convolution_add_fusion) | copy-start | bytes 3244036
  7.8 60.2 %copy-start.3 = (bf16[2,256,528]{1,2,0:T(8,128)(2,1)}, bf16[2,256,528]{1,2,0:T(8,128)(2,1)S(1)}, u32[]{:S(2)}) copy-start(bf16[2,256,528]{1,2,0:T(8,128)(2,1)S(1)} %get-tuple-element.13) | copy-start | bytes 1622020
  7.9 9.8 %copy-start.14 = (bf16[256,1,8,128]{3,2,1,0:T(8,128)(2,1)S(1)}, bf16[256,1,8,128]{3,2,1,0:T(8,128)(2,1)}, u32[]{:S(2)}) copy-start(bf16[256,1,8,128]{3,2,1,0:T(8,128)(2,1)} %param.12) | copy-start | bytes 1572868
  7.9 9.8 %copy-start.15 = (bf16[256,1,8,128]{3,2,1,0:T(8,128)(2,1)S(1)}, bf16[256,1,8,128]{3,2,1,0:T(8,128)(2,1)}, u32[]{:S(2)}) copy-start(bf16[256,1,8,128]{3,2,1,0:T(8,128)(2,1)} %param.9) | copy-start | bytes 1572868
  9.1 21.5 %all-to-all-start.1 = ((f32[32,40,128]{2,1,0:T(8,128)}), f32[32,40,128]{2,1,0:T(8,128)S(1)}, u32[]{:S(2)}, u32[]{:S(2)}) async-start(f32[32,40,128]{2,1,0:T(8,128)} %bitcast.30), calls=%async_computation.1 | async-start | bytes 1310720 | tf_op jit(solution)/shard_map/all_to_all | solution.py:75
  30.6 19.4 %all-to-all-start = ((bf16[2,256,1,8,128]{4,1,2,0,3:T(8,128)(2,1)}), bf16[2,256,1,8,128]{4,1,2,0,3:T(8,128)(2,1)S(1)}, u32[]{:S(2)}, u32[]{:S(2)}) async-start(bf16[2,256,1,8,128]{4,1,2,0,3:T(8,128)(2,1)} %pad_maximum_fusion.2), calls=%async_computation | async-start | bytes 2097152 | tf_op jit(solution)/shard_map/all_to_all | solution.py:128
  35.6 50.0 %copy-start.27 = (pred[256,256]{0,1:T(8,128)(4,1)}, pred[256,256]{0,1:T(8,128)(4,1)S(1)}, u32[]{:S(2)}) copy-start(pred[256,256]{0,1:T(8,128)(4,1)S(1)} %iota_compare_fusion.1) | copy-start | bytes 196612
  49.9 20.4 %all-to-all-start.2 = ((f32[32,40,128]{2,1,0:T(8,128)}), f32[32,40,128]{2,1,0:T(8,128)}, u32[]{:S(2)}, u32[]{:S(2)}) async-start(f32[32,40,128]{2,1,0:T(8,128)} %copy.85), calls=%async_computation.2 | async-start | bytes 1310720 | tf_op jit(solution)/shard_map/all_to_all | solution.py:80
  55.8 2.2 %copy-start.19 = (bf16[32,528,1,1]{1,0,3,2:T(8,128)(2,1)S(1)}, bf16[32,528,1,1]{1,0,3,2:T(8,128)(2,1)}, u32[]{:S(2)}) copy-start(bf16[32,528,1,1]{1,0,3,2:T(8,128)(2,1)} %constant.56) | copy-start | bytes 101380
  58.0 0.8 copy-start.16
  62.2 3.6 %copy-start = (f32[2,4,256,528]{2,3,1,0:T(8,128)}, f32[2,4,256,528]{2,3,1,0:T(8,128)S(1)}, u32[]{:S(2)}) copy-start(f32[2,4,256,528]{2,3,1,0:T(8,128)S(1)} %add_add_fusion) | copy-start | bytes 12976132
  62.2 5.8 %copy-start.25 = (bf16[528]{0:T(1024)(128)(2,1)S(1)}, bf16[528]{0:T(1024)(128)(2,1)}, u32[]{:S(2)}) copy-start(bf16[528]{0:T(1024)(128)(2,1)} %constant.12.clone) | copy-start | bytes 3172
  73.7 1.2 copy-start.1
  74.9 10.7 %copy-start.22 = (f32[2,4,256]{2,1,0:T(4,128)}, f32[2,4,256]{2,1,0:T(4,128)S(1)}, u32[]{:S(2)}) copy-start(f32[2,4,256]{2,1,0:T(4,128)S(1)} %fusion.114) | copy-start | bytes 24580
  84.9 1.2 copy-start.33
  87.8 12.1 %copy-start.2 = (f32[256,4,2,128]{0,3,1,2:T(8,128)S(1)}, f32[256,4,2,128]{0,3,1,2:T(8,128)}, u32[]{:S(2)}) copy-start(f32[256,4,2,128]{0,3,1,2:T(8,128)} %copy.75) | copy-start | bytes 3145732
  92.3 24.0 %all-to-all-start.4 = ((f32[32,40,128]{2,1,0:T(8,128)}), f32[32,40,128]{2,1,0:T(8,128)}, u32[]{:S(2)}, u32[]{:S(2)}) async-start(f32[32,40,128]{2,1,0:T(8,128)} %bitcast.210), calls=%async_computation.4 | async-start | bytes 1310720 | tf_op jit(solution)/shard_map/all_to_all | solution.py:75
  99.9 1.5 copy-start.4
  99.9 1.5 copy-start.29
  99.9 1.5 copy-start.30
  99.9 1.5 copy-start.32
  101.4 8.7 %copy-start.10 = (bf16[2,4,256,256]{2,3,1,0:T(8,128)(2,1)}, bf16[2,4,256,256]{2,3,1,0:T(8,128)(2,1)S(1)}, u32[]{:S(2)}) copy-start(bf16[2,4,256,256]{2,3,1,0:T(8,128)(2,1)S(1)} %select_convert_fusion) | copy-start | bytes 3145732
  110.0 1.5 copy-start.20
  111.6 1.0 copy-start.13
  116.3 13.3 %all-to-all-start.3 = ((bf16[256,4,2,128]{3,0,2,1:T(8,128)(2,1)}), bf16[256,4,2,128]{3,0,2,1:T(8,128)(2,1)}, u32[]{:S(2)}, u32[]{:S(2)}) async-start(bf16[256,4,2,128]{3,0,2,1:T(8,128)(2,1)} %copy.98), calls=%async_computation.3 | async-start | bytes 1048576 | tf_op jit(solution)/shard_map/all_to_all | solution.py:181
  129.6 21.4 %all-to-all-start.5 = ((f32[32,40,128]{2,1,0:T(8,128)}), f32[32,40,128]{2,1,0:T(8,128)}, u32[]{:S(2)}, u32[]{:S(2)}) async-start(f32[32,40,128]{2,1,0:T(8,128)} %copy.102), calls=%async_computation.5 | async-start | bytes 1310720 | tf_op jit(solution)/shard_map/all_to_all | solution.py:80
  138.0 3.1 %copy-start.23 = (f32[2,4,256]{2,1,0:T(4,128)S(1)}, f32[2,4,256]{2,1,0:T(4,128)}, u32[]{:S(2)}) copy-start(f32[2,4,256]{2,1,0:T(4,128)} %copy-done.22) | copy-start | bytes 24580
  138.0 3.1 %copy-start.28 = (pred[256,256]{0,1:T(8,128)(4,1)S(1)}, pred[256,256]{0,1:T(8,128)(4,1)}, u32[]{:S(2)}) copy-start(pred[256,256]{0,1:T(8,128)(4,1)} %copy-done.27) | copy-start | bytes 196612
  138.0 3.1 %copy-start.34 = (bf16[2,4,256,256]{2,3,1,0:T(8,128)(2,1)S(1)}, bf16[2,4,256,256]{2,3,1,0:T(8,128)(2,1)}, u32[]{:S(2)}) copy-start(bf16[2,4,256,256]{2,3,1,0:T(8,128)(2,1)} %get-tuple-element.40) | copy-start | bytes 3145732
  141.1 11.6 %copy-start.26 = (bf16[528]{0:T(1024)(128)(2,1)S(1)}, bf16[528]{0:T(1024)(128)(2,1)}, u32[]{:S(2)}) copy-start(bf16[528]{0:T(1024)(128)(2,1)} %constant.12.clone) | copy-start | bytes 3172
  142.3 10.4 %copy-start.5 = (bf16[2,256,528]{1,2,0:T(8,128)(2,1)S(1)}, bf16[2,256,528]{1,2,0:T(8,128)(2,1)}, u32[]{:S(2)}) copy-start(bf16[2,256,528]{1,2,0:T(8,128)(2,1)} %copy-done.3) | copy-start | bytes 1622020
  142.3 11.7 %copy-start.12 = (bf16[256,2,128]{2,1,0:T(2,128)(2,1)S(1)}, bf16[256,2,128]{2,1,0:T(2,128)(2,1)}, u32[]{:S(2)}) copy-start(bf16[256,2,128]{2,1,0:T(2,128)(2,1)} %copy-done.11) | copy-start | bytes 393220
  154.0 3.8 %copy-start.7 = (f32[2,256,528]{1,2,0:T(8,128)S(1)}, f32[2,256,528]{1,2,0:T(8,128)}, u32[]{:S(2)}) copy-start(f32[2,256,528]{1,2,0:T(8,128)} %copy-done.6) | copy-start | bytes 3244036
  154.0 3.8 %copy-start.8 = (f32[2,256,528]{1,2,0:T(8,128)S(1)}, f32[2,256,528]{1,2,0:T(8,128)}, u32[]{:S(2)}) copy-start(f32[2,256,528]{1,2,0:T(8,128)} %get-tuple-element.38) | copy-start | bytes 3244036
  154.0 3.8 %copy-start.31 = (f32[528]{0:T(1024)S(1)}, f32[528]{0:T(1024)}, u32[]{:S(2)}) copy-start(f32[528]{0:T(1024)} %constant.13.clone) | copy-start | bytes 6340
  155.3 2.4 %copy-start.9 = (f32[2,256,528]{1,2,0:T(8,128)S(1)}, f32[2,256,528]{1,2,0:T(8,128)}, u32[]{:S(2)}) copy-start(f32[2,256,528]{1,2,0:T(8,128)} %fusion.74) | copy-start | bytes 3244036
  157.8 1.8 %copy-start.24 = (bf16[1056,32,1]{0,1,2:T(8,128)(2,1)S(1)}, bf16[1056,32,1]{0,1,2:T(8,128)(2,1)}, u32[]{:S(2)}) copy-start(bf16[1056,32,1]{0,1,2:T(8,128)(2,1)} %constant.60) | copy-start | bytes 202756
  159.6 1.1 copy-start.21

commit v3 on v2

--- a/solution.py
+++ b/solution.py
@@ -81,6 +81,32 @@
     state_out = back[: heads * feat].reshape(heads, feat, width)
     total_out = back[heads * feat : heads * (feat + total_rows)].reshape(heads, total_rows * width)
     return state_out, total_out[:, :feat]
+
+
+def head_exchange(stacked, owned):
+    count = lax.axis_size("head")
+    me = lax.axis_index("head")
+    pieces = []
+    for k in range(count):
+        target = (me + k) % count
+        piece = lax.dynamic_slice_in_dim(stacked, target * owned, owned, axis=3)
+        if k:
+            piece = lax.ppermute(piece, "head", [(j, (j + k) % count) for j in range(count)])
+        pieces.append(piece)
+    return jnp.concatenate(pieces, axis=2)
+
+
+def head_return(grads, heads_all):
+    count = lax.axis_size("head")
+    me = lax.axis_index("head")
+    owned = grads.shape[2]
+    out = jnp.zeros((grads.shape[0], 1, heads_all, grads.shape[3]), grads.dtype)
+    for k in range(count):
+        piece = grads[:, k : k + 1]
+        if k:
+            piece = lax.ppermute(piece, "head", [(j, (j - k) % count) for j in range(count)])
+        out = lax.dynamic_update_slice_in_dim(out, piece, ((me + k) % count) * owned, axis=2)
+    return out
 
 
 def sketch_parts(tokens, projector, pattern):
@@ -125,9 +151,7 @@
     offset = lax.axis_index("head") * owned
     key_part = lax.dynamic_slice_in_dim(keys, offset, owned, 1)
     value_part = lax.dynamic_slice_in_dim(values, offset, owned, 1)
-    both = lax.all_to_all(
-        jnp.stack([queries, dout]), "head", split_axis=3, concat_axis=2, tiled=True
-    )
+    both = head_exchange(jnp.stack([queries, dout]), owned)
     query_part, grad_part = both[0], both[1]
     key_one, key_two = sketch_parts(key_part, projector, "thd,df->htf")
     key_feat = tri_features(key_one, key_two, take_a, take_b)
@@ -178,7 +202,7 @@
         grad_qfeat, query_one, query_two, proj_wide, take_a, take_b, off
     )
     query_low = query_grad.transpose(2, 1, 0, 3).astype(bf16)
-    query_out = lax.all_to_all(query_low, "head", split_axis=1, concat_axis=2, tiled=True)
+    query_out = head_return(query_low, heads_all)
 
     grad_kfeat = jnp.einsum("hmij,hmif->hjf", dscores, query_feat, preferred_element_type=f32)
     grad_value = jnp.einsum("hmij,hmid->hjd", weights, grad_low, preferred_element_type=f32)

time: 163 us -> 140 us (0.86)
  waiting for transfers between devices: 36.9 us -> 14.2 us
  matrix products: 57.9 us -> 64.4 us
  starting transfers between devices: 39.6 us -> 36.8 us
  local copies, waits for them, and re-layouts: 18.7 us -> 16.2 us
    all_to_all x2 -> x0, waiting for transfers between devices: 18.9 us -> none  [the longest x1 12.6 us: body(): lax.all_to_all(jnp.stack([queries, dout]), 'head', split_axis=3, concat_a...]
    dot_general x26, matrix products: 23.7 us -> 34.1 us  [dot_parts(): term = jnp.einsum(pattern, *args, preferred_element_type=f32)]
    all_to_all x2, waiting for transfers between devices: 11.6 us -> 1.43 us  [ctx_scan(): got = lax.all_to_all(flat.reshape(n, per, width), 'ctx', 0, 0, tiled=True)]
    all_to_all x2 -> x0, starting transfers between devices: 9.16 us -> none  [the longest x1 5.02 us: body(): lax.all_to_all(jnp.stack([queries, dout]), 'head', split_axis=3, concat_a...]
    ppermute x0 -> x6, starting transfers between devices: none -> 9.09 us  [the longest x3 6.57 us: head_exchange(): lax.ppermute(piece, 'head', [(j, (j + k) % count) for j in range(count)])]
    all_to_all x2, waiting for transfers between devices: 6.4 us -> 12.8 us  [ctx_scan(): lax.all_to_all(summed, 'ctx', 0, 0, tiled=True).reshape(n * per, width)]
    convert_element_type x2 -> x0, local copies, waits for them, and re-layouts: 3.11 us -> none  [the longest x1 2.28 us: body(): grad_heads = grad_part.transpose(2, 1, 0, 3).astype(f32)]
    dynamic_update_slice x0 -> x4, local copies, waits for them, and re-layouts: none -> 2.73 us  [head_return(): lax.dynamic_update_slice_in_dim(out, piece, (me + k) % count * owned, axi...]
  transfers between devices with their start and end apart: 6 -> 10, of which waited for: 4 -> 3; matrix products, arithmetic and copies ran while one was open for 26% -> 38% of each run, Pallas kernels for 0% -> 0%
where the time goes in v3:
time: 140 us; the launch traced here: 139 us
  matrix products  64.4 us (46%)
  starting transfers between devices  36.8 us (26%)
  local copies, waits for them, and re-layouts  16.2 us (12%)
  waiting for transfers between devices  14.2 us (10%)
  other arithmetic  6.02 us (4%)
  between operations  1.42 us (1%)
    dot_general x26, matrix products, dot_parts(): term = jnp.einsum(pattern, *args, preferred_element_type=f32)  34.1 us
    all_to_all x2, starting transfers between devices, ctx_scan(): lax.all_to_all(summed, 'ctx', 0, 0, tiled=True).reshape(n * per, width)  14.1 us
    all_to_all x2, starting transfers between devices, ctx_scan(): got = lax.all_to_all(flat.reshape(n, per, width), 'ctx', 0, 0, tiled=True)  13.6 us
    all_to_all x2, waiting for transfers between devices, ctx_scan(): lax.all_to_all(summed, 'ctx', 0, 0, tiled=True).reshape(n * per, width)  12.8 us
    dot_general x1, matrix products, body(): jnp.einsum('hmij,hjf->hmif', dscores, key_feat, preferred_element_type=f32)  7.19 us
    ppermute x3, starting transfers between devices, head_exchange(): lax.ppermute(piece, 'head', [(j, (j + k) % count) for j in range(count)])  6.57 us
    unnamed x68, local copies, waits for them, and re-layouts  2.96 us
    dot_general x1, matrix products, dot_split3(): jnp.einsum(pattern, fh, sl, preferred_element_type=f32)  2.86 us
  transfers between devices with their start and end apart: 10, of which 3 were waited for; matrix products, arithmetic and copies ran while one was open for 38% of the time, Pallas kernels for 0%

profile of v3, /device:TPU:1, one launch (start us, length us, event | category | flops | bytes accessed | tf_op | source)
XLA Modules:
  0.0 139.0 jit_solution(11634572894272692122)
XLA Ops:
  0.7 1.4 %copy_bitcast_fusion = (bf16[1,256,1,8,128]{4,1,3,2,0:T(8,128)(2,1)S(1)}, bf16[1,256,1,8,128]{4,1,3,2,0:T(8,128)(2,1)S(1)}) fusion(bf16[256,1,8,128]{3,2,1,0:T(8,128)(2,1)} %param.12, bf16[256,1,8,128]{3,2,1,0:T(8,128)(2,1)} %param.9), kind=kLoop, calls=%fused_computation.102 | loop fusion | bytes 2097152 | tf_op jit(solution)/shard_map/stack | solution.py:154
  2.3 2.5 %collective-permute-start = (bf16[2,256,1,2,128]{4,1,3,2,0:T(8,128)(2,1)S(1)}, bf16[2,256,1,2,128]{4,1,3,2,0:T(8,128)(2,1)S(1)}, u32[]{:S(2)}, u32[]{:S(2)}) collective-permute-start(bf16[2,256,1,2,128]{4,1,3,2,0:T(8,128)(2,1)S(1)} %get-tuple-element.26), channel_id=1, source_target_pairs={{0,1},{1,2},{2,3},{3,0},{4,5},{5,6},{6,7},{7,4},{8,9},{9,10},{10,1... | collective-permute-start | bytes 786440 | tf_op jit(solution)/shard_map/ppermute | solution.py:94
  4.8 3.3 %collective-permute-start.1 = (bf16[2,256,1,2,128]{4,1,3,2,0:T(8,128)(2,1)S(1)}, bf16[2,256,1,2,128]{4,1,3,2,0:T(8,128)(2,1)S(1)}, u32[]{:S(2)}, u32[]{:S(2)}) collective-permute-start(bf16[2,256,1,2,128]{4,1,3,2,0:T(8,128)(2,1)S(1)} %get-tuple-element.27), channel_id=1, source_target_pairs={{0,2},{1,3},{2,0},{3,1},{4,6},{5,7},{6,4},{7,5},{8,10},{9,11},{10,... | collective-permute-start | bytes 786440 | tf_op jit(solution)/shard_map/ppermute | solution.py:94
  8.1 0.7 collective-permute-start.2
  9.2 0.8 fusion.159
  11.8 1.2 constant_dynamic-slice_fusion
  13.0 1.4 convert_reduce_fusion
  14.7 0.9 select_maximum_fusion.1
  15.6 8.6 %all-to-all-start = ((f32[32,40,128]{2,1,0:T(8,128)}), f32[32,40,128]{2,1,0:T(8,128)S(1)}, u32[]{:S(2)}, u32[]{:S(2)}) async-start(f32[32,40,128]{2,1,0:T(8,128)} %bitcast.30), calls=%async_computation | async-start | bytes 1310720 | tf_op jit(solution)/shard_map/all_to_all | solution.py:75
  24.7 1.0 fusion.72
  25.7 0.8 fusion.91
  26.5 0.8 fusion.95
  27.3 2.8 %fusion.93 = f32[2,4,256,528]{2,3,1,0:T(8,128)} fusion(bf16[32,528,1,1]{1,0,3,2:T(8,128)(2,1)S(1)} %copy-done.22, bf16[2,4,256,32]{2,3,0,1:T(8,128)(2,1)S(1)} %get-tuple-element.34), kind=kOutput, calls=%fused_computation.152 | convolution fusion | flops 69206016 | bytes 4490240 | tf_op jit(solution)/shard_map/...a,ak->...k/dot_general | solution.py:36
  30.1 2.7 %fusion.97 = f32[2,4,256,528]{2,3,1,0:T(8,128)} fusion(bf16[32,528,1,1]{1,0,3,2:T(8,128)(2,1)S(1)} %copy-done.22, bf16[2,4,256,32]{2,3,0,1:T(8,128)(2,1)S(1)} %get-tuple-element.35), kind=kOutput, calls=%fused_computation.156 | convolution fusion | flops 69206016 | bytes 4490240 | tf_op jit(solution)/shard_map/...a,ak->...k/dot_general | solution.py:36
  32.9 2.8 %add_add_fusion = f32[2,4,256,528]{2,3,1,0:T(8,128)} fusion(f32[2,4,256,528]{2,3,1,0:T(8,128)S(1)} %fusion.95, f32[2,4,256,528]{2,3,1,0:T(8,128)S(1)} %fusion.91, bf16[32,528,1,1]{1,0,3,2:T(8,128)(2,1)S(1)} %copy-done.25, bf16[2,4,256,32]{2,3,0,1:T(8,128)(2,1)S(1)} %get-tuple-element.33), kind=kOutput, calls=%fused_computation.11 | convolution fusion | flops 71368704 | bytes 13140992 | tf_op jit(solution)/shard_map/...a,ak->...k/dot_general | solution.py:36
  35.7 1.4 %all-to-all-done = f32[32,40,128]{2,1,0:T(8,128)S(1)} async-done(((f32[32,40,128]{2,1,0:T(8,128)}), f32[32,40,128]{2,1,0:T(8,128)S(1)}, u32[]{:S(2)}, u32[]{:S(2)}) %all-to-all-start) | async-done | bytes 655392 | tf_op jit(solution)/shard_map/all_to_all | solution.py:75
  37.6 1.2 copy.95
  38.8 6.0 %all-to-all-start.1 = ((f32[32,40,128]{2,1,0:T(8,128)}), f32[32,40,128]{2,1,0:T(8,128)}, u32[]{:S(2)}, u32[]{:S(2)}) async-start(f32[32,40,128]{2,1,0:T(8,128)} %copy.95), calls=%async_computation.1 | async-start | bytes 1310720 | tf_op jit(solution)/shard_map/all_to_all | solution.py:80
  44.8 8.2 %broadcast_multiply_fusion = (bf16[2,4,256,528]{2,3,1,0:T(8,128)(2,1)S(1)}, bf16[2,4,256,528]{2,3,1,0:T(8,128)(2,1)S(1)}, f32[2,4,256,528]{2,3,1,0:T(8,128)}) fusion(bf16[528]{0:T(1024)(128)(2,1)S(1)} %copy-done.32, f32[2,4,256,528]{2,3,1,0:T(8,128)} %add_add_fusion, bf16[32,528,1,1]{1,0,3,2:T(8,128)(2,1)S(1)} %copy-done.22, ...), kind=kOutput, calls=%fused_computation.75 | convolution fusion | flops 75694080 | bytes 21792800 | tf_op jit(solution)/shard_map/...a,ak->...k/dot_general | solution.py:36
  53.1 2.1 %select_convert_fusion.1 = (bf16[2,4,256,256]{2,3,1,0:T(8,128)(2,1)}, f32[2,4,256,256]{2,3,1,0:T(8,128)S(1)}) fusion(pred[256,256]{0,1:T(8,128)(4,1)S(1)} %iota_compare_fusion.1, bf16[2,4,256,528]{2,3,1,0:T(8,128)(2,1)S(1)} %get-tuple-element.14, bf16[2,256,528]{1,2,0:T(8,128)(2,1)S(1)} %get-tuple-element.13), kind=kOutput, calls=%fused_computation.18 | convolution fusion | flops 554172416 | bytes 5914624 | tf_op jit(solution)/shard_map/hmif,hjf->hmij/dot_general | solution.py:174
  55.4 2.4 %all-to-all-done.1 = f32[32,40,128]{2,1,0:T(8,128)} async-done(((f32[32,40,128]{2,1,0:T(8,128)}), f32[32,40,128]{2,1,0:T(8,128)}, u32[]{:S(2)}, u32[]{:S(2)}) %all-to-all-start.1) | async-done | bytes 655392 | tf_op jit(solution)/shard_map/all_to_all | solution.py:80
  57.8 0.7 slice.66
  58.5 1.1 slice.68
  59.6 0.6 reshape.58
  60.2 0.8 fusion.158
  61.0 2.0 %fusion.143 = f32[2,1,4,256]{3,1,2,0:T(1,128)S(1)} fusion(bf16[2,4,256,528]{2,3,1,0:T(8,128)(2,1)} %copy-done.2, bf16[2,528,1,1]{1,0,2,3:T(2,128)(2,1)S(1)} %get-tuple-element.42), kind=kOutput, calls=%fused_computation.209 | convolution fusion | flops 2162688 | bytes 2172992 | tf_op jit(solution)/shard_map/hmif,hf->hmi/dot_general | solution.py:36
  63.5 1.2 fusion.6
  64.7 1.3 fusion.153
  66.0 2.9 %fusion.57 = f32[2,4,256,528]{2,3,1,0:T(8,128)} fusion(bf16[2,4,256,128]{3,2,0,1:T(8,128)(2,1)S(1)} %get-tuple-element.23, f32[2,528,128]{2,1,0:T(8,128)S(1)} %bitcast.210), kind=kOutput, calls=%fused_computation.107 | convolution fusion | flops 277229568 | bytes 5390336 | tf_op jit(solution)/shard_map/hmid,hfd->hmif/dot_general | solution.py:50
  68.9 2.8 %fusion.59 = f32[2,4,256,528]{2,3,1,0:T(8,128)} fusion(bf16[2,4,256,128]{3,2,0,1:T(8,128)(2,1)S(1)} %get-tuple-element.23, f32[2,528,128]{2,1,0:T(8,128)S(1)} %bitcast.211), kind=kOutput, calls=%fused_computation.109 | convolution fusion | flops 277094400 | bytes 5390336 | tf_op jit(solution)/shard_map/hmid,hfd->hmif/dot_general | solution.py:49
  71.6 1.2 fusion.14
  72.9 1.1 fusion.19
  74.0 0.7 fusion.128
  74.7 0.7 fusion.130
  75.4 0.6 pad.16
  76.0 0.7 reshape.61
  76.7 1.8 %fusion.62 = f32[2,528,128,1]{2,1,3,0:T(8,128)S(1)} fusion(bf16[2,4,256,528]{2,3,1,0:T(8,128)(2,1)S(1)} %get-tuple-element.15, bf16[2,4,256,128]{3,2,0,1:T(8,128)(2,1)} %get-tuple-element.22), kind=kOutput, calls=%fused_computation.112 | convolution fusion | flops 276824064 | bytes 3227648 | tf_op jit(solution)/shard_map/hmif,hmid->hfd/dot_general | solution.py:186
  78.4 0.9 select_maximum_fusion
  79.4 5.0 %all-to-all-start.2 = ((f32[32,40,128]{2,1,0:T(8,128)}), f32[32,40,128]{2,1,0:T(8,128)}, u32[]{:S(2)}, u32[]{:S(2)}) async-start(f32[32,40,128]{2,1,0:T(8,128)} %bitcast.214), calls=%async_computation.2 | async-start | bytes 1310720 | tf_op jit(solution)/shard_map/all_to_all | solution.py:75
  84.4 1.6 %select_convert_fusion = bf16[2,4,256,256]{2,3,1,0:T(8,128)(2,1)S(1)} fusion(f32[2,4,256]{2,1,0:T(4,128)S(1)} %copy.103, pred[256,256]{0,1:T(8,128)(4,1)} %copy-done.15, bf16[2,4,256,128]{3,2,0,1:T(8,128)(2,1)} %get-tuple-element.22, bf16[256,2,128]{2,1,0:T(2,128)(2,1)} %copy-done.10), kind=kOutput, calls=%fused_computation.17 | convolution fusion | flops 135790592 | bytes 1777664 | tf_op jit(solution)/shard_map/hmid,hjd->hmij/dot_general | solution.py:192
  86.1 0.7 fusion.52
  86.8 7.2 %fusion.154 = (f32[2,4,256,528]{2,3,1,0:T(8,128)S(1)}, f32[2,4,256,528]{2,3,1,0:T(8,128)S(1)}) fusion(f32[2,4,256,528]{2,3,1,0:T(8,128)} %add_add_fusion, f32[528]{0:T(1024)S(1)} %copy-done.30, f32[2,4,256,528]{2,3,1,0:T(8,128)} %get-tuple-element.45, f32[2,528]{1,0:T(2,128)S(1)} %get-tuple-element.41, f32[2,4,256]{2,1,0:T(4,128)S(1)} %copy.103, ...), kind=kOutput, calls=%fused_computation.220 | convolution fusion | flops 562298880 | bytes 31881408 | tf_op jit(solution)/shard_map/hmij,hjf->hmif/dot_general | solution.py:197
  94.0 1.5 %reduce-precision_convert_fusion = (bf16[2,4,256,1056]{2,3,1,0:T(8,128)(2,1)S(1)}, bf16[2,4,256,1056]{2,3,1,0:T(8,128)(2,1)S(1)}) fusion(f32[2,4,256,528]{2,3,1,0:T(8,128)S(1)} %get-tuple-element.19, f32[2,4,256,528]{2,3,1,0:T(8,128)S(1)} %get-tuple-element.18), kind=kLoop, calls=%fused_computation.1 | loop fusion | flops 10813440 | bytes 17301504 | tf_op jit(solution)/shard_map/convert_element_type | solution.py:26
  95.6 0.9 fusion.1
  96.5 0.9 fusion.157
  97.5 1.0 fusion.78
  98.5 1.0 fusion.20
  99.5 0.8 fusion.156
  100.2 2.5 %collective-permute-start.4 = (bf16[256,1,2,128]{3,0,1,2:T(8,128)(2,1)}, bf16[256,1,2,128]{3,0,1,2:T(8,128)(2,1)}, u32[]{:S(2)}, u32[]{:S(2)}) collective-permute-start(bf16[256,1,2,128]{3,0,1,2:T(8,128)(2,1)} %get-tuple-element.30), channel_id=1, source_target_pairs={{0,2},{1,3},{2,0},{3,1},{4,6},{5,7},{6,4},{7,5},{8,10},{9,11},{10,... | collective-permute-start | bytes 393224 | tf_op jit(solution)/shard_map/ppermute | solution.py:107
  102.8 1.1 convolution_bitcast_fusion.1
  104.2 1.8 %convolution_bitcast_fusion = f32[2,256,528]{1,2,0:T(8,128)} fusion(bf16[2,4,256,256]{2,3,1,0:T(8,128)(2,1)S(1)} %select_convert_fusion, bf16[2,4,256,528]{2,3,1,0:T(8,128)(2,1)S(1)} %get-tuple-element.15), kind=kOutput, calls=%fused_computation.34 | convolution fusion | flops 553648128 | bytes 4292608 | tf_op jit(solution)/shard_map/hmij,hmif->hjf/dot_general | solution.py:207
  106.0 1.6 %fusion.43 = f32[32,40,128]{2,0,1:T(8,128)S(1)} fusion(f32[32,40,128]{2,1,0:T(8,128)} %all-to-all-done.2), kind=kOutput, calls=%fused_computation.89 | convolution fusion | flops 62915584 | bytes 1310720 | tf_op jit(solution)/shard_map/ij,jrc->irc/dot_general | solution.py:79
  107.6 1.2 copy.121
  108.8 8.1 %all-to-all-start.3 = ((f32[32,40,128]{2,1,0:T(8,128)}), f32[32,40,128]{2,1,0:T(8,128)S(1)}, u32[]{:S(2)}, u32[]{:S(2)}) async-start(f32[32,40,128]{2,1,0:T(8,128)} %copy.121), calls=%async_computation.3 | async-start | bytes 1310720 | tf_op jit(solution)/shard_map/all_to_all | solution.py:80
  116.9 1.1 copy_dynamic-update-slice_fusion.2
  118.0 1.1 copy_dynamic-update-slice_fusion.1
  119.4 10.3 %all-to-all-done.3 = f32[32,40,128]{2,1,0:T(8,128)S(1)} async-done(((f32[32,40,128]{2,1,0:T(8,128)}), f32[32,40,128]{2,1,0:T(8,128)S(1)}, u32[]{:S(2)}, u32[]{:S(2)}) %all-to-all-start.3) | async-done | bytes 655392 | tf_op jit(solution)/shard_map/all_to_all | solution.py:80
  129.8 0.8 copy-done.9
  131.2 1.3 fusion.83
  132.5 0.7 slice.74
  133.2 0.5 fusion.34
  133.7 0.8 copy.124
  134.5 2.1 %fusion.155 = (f32[2,256,528]{1,2,0:T(8,128)S(1)}, f32[2,256,528]{1,2,0:T(8,128)S(1)}) fusion(f32[2,256,528]{1,2,0:T(8,128)S(1)} %copy-done.5, f32[528]{0:T(1024)S(1)} %copy-done.30, f32[2,256,528]{1,2,0:T(8,128)S(1)} %copy-done.8, f32[2,528]{1,0:T(2,128)S(1)} %bitcast.219, f32[2,256,528]{1,2,0:T(8,128)} %convolution_bitcast_fusion, ...), kind=kOutput, calls=%fused_computation.221 | convolution fusion | flops 71233536 | bytes 7166144 | tf_op jit(solution)/shard_map/htd,hfd->htf/dot_general | solution.py:36
  138.2 0.8 copy.123
  (107 shorter events, 7.1 us)
Async XLA Ops:
  0.6 8.2 %copy-start = (bf16[256,8,128]{2,1,0:T(8,128)(2,1)S(1)}, bf16[256,8,128]{2,1,0:T(8,128)(2,1)}, u32[]{:S(2)}) copy-start(bf16[256,8,128]{2,1,0:T(8,128)(2,1)} %param.10) | copy-start | bytes 1572868
  0.7 8.2 %copy-start.31 = (s32[2,128,32]{1,2,0:T(8,128)S(1)}, s32[2,128,32]{1,2,0:T(8,128)}, u32[]{:S(2)}) copy-start(s32[2,128,32]{1,2,0:T(8,128)} %param.13) | copy-start | bytes 98308
  0.7 9.3 %copy-start.24 = (bf16[32,528,1]{1,0,2:T(8,128)(2,1)S(1)}, bf16[32,528,1]{1,0,2:T(8,128)(2,1)}, u32[]{:S(2)}) copy-start(bf16[32,528,1]{1,0,2:T(8,128)(2,1)} %constant.95) | copy-start | bytes 101380
  2.3 22.0 %collective-permute-start = (bf16[2,256,1,2,128]{4,1,3,2,0:T(8,128)(2,1)S(1)}, bf16[2,256,1,2,128]{4,1,3,2,0:T(8,128)(2,1)S(1)}, u32[]{:S(2)}, u32[]{:S(2)}) collective-permute-start(bf16[2,256,1,2,128]{4,1,3,2,0:T(8,128)(2,1)S(1)} %get-tuple-element.26), channel_id=1, source_target_pairs={{0,1},{1,2},{2,3},{3,0},{4,5},{5,6},{6,7},{7,4},{8,9},{9,10},{10,1... | collective-permute-start | bytes 786440 | tf_op jit(solution)/shard_map/ppermute | solution.py:94
  4.8 19.4 %collective-permute-start.1 = (bf16[2,256,1,2,128]{4,1,3,2,0:T(8,128)(2,1)S(1)}, bf16[2,256,1,2,128]{4,1,3,2,0:T(8,128)(2,1)S(1)}, u32[]{:S(2)}, u32[]{:S(2)}) collective-permute-start(bf16[2,256,1,2,128]{4,1,3,2,0:T(8,128)(2,1)S(1)} %get-tuple-element.27), channel_id=1, source_target_pairs={{0,2},{1,3},{2,0},{3,1},{4,6},{5,7},{6,4},{7,5},{8,10},{9,11},{10,... | collective-permute-start | bytes 786440 | tf_op jit(solution)/shard_map/ppermute | solution.py:94
  8.1 16.1 %collective-permute-start.2 = (bf16[2,256,1,2,128]{4,1,3,2,0:T(8,128)(2,1)S(1)}, bf16[2,256,1,2,128]{4,1,3,2,0:T(8,128)(2,1)S(1)}, u32[]{:S(2)}, u32[]{:S(2)}) collective-permute-start(bf16[2,256,1,2,128]{4,1,3,2,0:T(8,128)(2,1)S(1)} %get-tuple-element.28), channel_id=1, source_target_pairs={{0,3},{1,0},{2,1},{3,2},{4,7},{5,4},{6,5},{7,6},{8,11},{9,8},{10,9... | collective-permute-start | bytes 786440 | tf_op jit(solution)/shard_map/ppermute | solution.py:94
  9.2 1.9 %copy-start.19 = (f32[2,256,32]{1,2,0:T(8,128)}, f32[2,256,32]{1,2,0:T(8,128)S(1)}, u32[]{:S(2)}) copy-start(f32[2,256,32]{1,2,0:T(8,128)S(1)} %fusion.36) | copy-start | bytes 196612
  10.3 0.8 copy-start.23
  11.1 3.3 %copy-start.4 = (f32[2,256,528]{1,2,0:T(8,128)}, f32[2,256,528]{1,2,0:T(8,128)S(1)}, u32[]{:S(2)}) copy-start(f32[2,256,528]{1,2,0:T(8,128)S(1)} %convolution_add_fusion) | copy-start | bytes 3244036
  13.0 1.7 %copy-start.10 = (bf16[256,2,128]{2,1,0:T(2,128)(2,1)}, bf16[256,2,128]{2,1,0:T(2,128)(2,1)S(1)}, u32[]{:S(2)}) copy-start(bf16[256,2,128]{2,1,0:T(2,128)(2,1)S(1)} %constant_dynamic-slice_fusion) | copy-start | bytes 393220
  15.6 21.5 %all-to-all-start = ((f32[32,40,128]{2,1,0:T(8,128)}), f32[32,40,128]{2,1,0:T(8,128)S(1)}, u32[]{:S(2)}, u32[]{:S(2)}) async-start(f32[32,40,128]{2,1,0:T(8,128)} %bitcast.30), calls=%async_computation | async-start | bytes 1310720 | tf_op jit(solution)/shard_map/all_to_all | solution.py:75
  24.2 30.9 %copy-start.15 = (pred[256,256]{0,1:T(8,128)(4,1)}, pred[256,256]{0,1:T(8,128)(4,1)S(1)}, u32[]{:S(2)}) copy-start(pred[256,256]{0,1:T(8,128)(4,1)S(1)} %iota_compare_fusion.1) | copy-start | bytes 196612
  24.3 1.4 %copy-start.25 = (bf16[32,528,1,1]{1,0,3,2:T(8,128)(2,1)S(1)}, bf16[32,528,1,1]{1,0,3,2:T(8,128)(2,1)}, u32[]{:S(2)}) copy-start(bf16[32,528,1,1]{1,0,3,2:T(8,128)(2,1)} %constant.93) | copy-start | bytes 101380
  24.4 2.1 %copy-start.6 = (bf16[2,256,4,2,128]{4,1,3,2,0:T(8,128)(2,1)}, bf16[2,256,4,2,128]{4,1,3,2,0:T(8,128)(2,1)S(1)}, u32[]{:S(2)}) copy-start(bf16[2,256,4,2,128]{4,1,3,2,0:T(8,128)(2,1)S(1)} %pad_maximum_fusion.2) | copy-start | bytes 3145732
  26.5 0.8 copy-start.22
  35.7 9.1 %copy-start.32 = (bf16[528]{0:T(1024)(128)(2,1)S(1)}, bf16[528]{0:T(1024)(128)(2,1)}, u32[]{:S(2)}) copy-start(bf16[528]{0:T(1024)(128)(2,1)} %constant.77.clone) | copy-start | bytes 3172
  38.8 19.0 %all-to-all-start.1 = ((f32[32,40,128]{2,1,0:T(8,128)}), f32[32,40,128]{2,1,0:T(8,128)}, u32[]{:S(2)}, u32[]{:S(2)}) async-start(f32[32,40,128]{2,1,0:T(8,128)} %copy.95), calls=%async_computation.1 | async-start | bytes 1310720 | tf_op jit(solution)/shard_map/all_to_all | solution.py:80
  53.1 2.1 %copy-start.2 = (bf16[2,4,256,528]{2,3,1,0:T(8,128)(2,1)}, bf16[2,4,256,528]{2,3,1,0:T(8,128)(2,1)S(1)}, u32[]{:S(2)}) copy-start(bf16[2,4,256,528]{2,3,1,0:T(8,128)(2,1)S(1)} %get-tuple-element.14) | copy-start | bytes 6488068
  60.2 2.8 %copy-start.3 = (bf16[2,4,256,528]{2,3,1,0:T(8,128)(2,1)S(1)}, bf16[2,4,256,528]{2,3,1,0:T(8,128)(2,1)}, u32[]{:S(2)}) copy-start(bf16[2,4,256,528]{2,3,1,0:T(8,128)(2,1)} %copy-done.2) | copy-start | bytes 6488068
  63.4 1.2 copy-start.7
  71.6 1.2 copy-start.11
  71.6 1.3 copy-start.17
  79.4 26.6 %all-to-all-start.2 = ((f32[32,40,128]{2,1,0:T(8,128)}), f32[32,40,128]{2,1,0:T(8,128)}, u32[]{:S(2)}, u32[]{:S(2)}) async-start(f32[32,40,128]{2,1,0:T(8,128)} %bitcast.214), calls=%async_computation.2 | async-start | bytes 1310720 | tf_op jit(solution)/shard_map/all_to_all | solution.py:75
  84.4 1.6 %copy-start.14 = (bf16[2,4,256,128]{3,2,0,1:T(8,128)(2,1)S(1)}, bf16[2,4,256,128]{3,2,0,1:T(8,128)(2,1)}, u32[]{:S(2)}) copy-start(bf16[2,4,256,128]{3,2,0,1:T(8,128)(2,1)} %get-tuple-element.24) | copy-start | bytes 1572868
  86.0 0.7 copy-start.30
  94.0 1.6 %copy-start.26 = (bf16[1056,32,1,1]{0,1,2,3:T(8,128)(2,1)S(1)}, bf16[1056,32,1,1]{0,1,2,3:T(8,128)(2,1)}, u32[]{:S(2)}) copy-start(bf16[1056,32,1,1]{0,1,2,3:T(8,128)(2,1)} %constant.96) | copy-start | bytes 202756
  95.6 1.0 copy-start.16
  97.4 5.3 %copy-start.13 = (bf16[2,4,256,128]{3,2,0,1:T(8,128)(2,1)S(1)}, bf16[2,4,256,128]{3,2,0,1:T(8,128)(2,1)}, u32[]{:S(2)}) copy-start(bf16[2,4,256,128]{3,2,0,1:T(8,128)(2,1)} %get-tuple-element.22) | copy-start | bytes 1572868
  97.4 5.3 %copy-start.18 = (bf16[2,4,256,256]{2,3,1,0:T(8,128)(2,1)S(1)}, bf16[2,4,256,256]{2,3,1,0:T(8,128)(2,1)}, u32[]{:S(2)}) copy-start(bf16[2,4,256,256]{2,3,1,0:T(8,128)(2,1)} %get-tuple-element.49) | copy-start | bytes 3145732
  100.2 16.6 %collective-permute-start.3 = (bf16[256,1,2,128]{3,0,1,2:T(8,128)(2,1)}, bf16[256,1,2,128]{3,0,1,2:T(8,128)(2,1)}, u32[]{:S(2)}, u32[]{:S(2)}) collective-permute-start(bf16[256,1,2,128]{3,0,1,2:T(8,128)(2,1)} %get-tuple-element.31), channel_id=1, source_target_pairs={{0,3},{1,0},{2,1},{3,2},{4,7},{5,4},{6,5},{7,6},{8,11},{9,8},{10,9... | collective-permute-start | bytes 393224 | tf_op jit(solution)/shard_map/ppermute | solution.py:107
  100.2 17.8 %collective-permute-start.4 = (bf16[256,1,2,128]{3,0,1,2:T(8,128)(2,1)}, bf16[256,1,2,128]{3,0,1,2:T(8,128)(2,1)}, u32[]{:S(2)}, u32[]{:S(2)}) collective-permute-start(bf16[256,1,2,128]{3,0,1,2:T(8,128)(2,1)} %get-tuple-element.30), channel_id=1, source_target_pairs={{0,2},{1,3},{2,0},{3,1},{4,6},{5,7},{6,4},{7,5},{8,10},{9,11},{10,... | collective-permute-start | bytes 393224 | tf_op jit(solution)/shard_map/ppermute | solution.py:107
  102.8 16.4 %collective-permute-start.5 = (bf16[256,1,2,128]{3,0,1,2:T(8,128)(2,1)}, bf16[256,1,2,128]{3,0,1,2:T(8,128)(2,1)S(1)}, u32[]{:S(2)}, u32[]{:S(2)}) collective-permute-start(bf16[256,1,2,128]{3,0,1,2:T(8,128)(2,1)} %get-tuple-element.29), channel_id=1, source_target_pairs={{0,1},{1,2},{2,3},{3,0},{4,5},{5,6},{6,7},{7,4},{8,9},{9,10},{10,1... | collective-permute-start | bytes 393224 | tf_op jit(solution)/shard_map/ppermute | solution.py:107
  108.8 22.3 %copy-start.12 = (bf16[256,2,128]{2,1,0:T(2,128)(2,1)S(1)}, bf16[256,2,128]{2,1,0:T(2,128)(2,1)}, u32[]{:S(2)}) copy-start(bf16[256,2,128]{2,1,0:T(2,128)(2,1)} %copy-done.10) | copy-start | bytes 393220
  108.8 21.0 %all-to-all-start.3 = ((f32[32,40,128]{2,1,0:T(8,128)}), f32[32,40,128]{2,1,0:T(8,128)S(1)}, u32[]{:S(2)}, u32[]{:S(2)}) async-start(f32[32,40,128]{2,1,0:T(8,128)} %copy.121), calls=%async_computation.3 | async-start | bytes 1310720 | tf_op jit(solution)/shard_map/all_to_all | solution.py:80
  119.4 10.4 %copy-start.21 = (bf16[256,1,8,128]{3,2,1,0:T(8,128)(2,1)}, bf16[256,1,8,128]{3,2,1,0:T(8,128)(2,1)S(1)}, u32[]{:S(2)}) copy-start(bf16[256,1,8,128]{3,2,1,0:T(8,128)(2,1)S(1)} %copy_dynamic-update-slice_fusion) | copy-start | bytes 1572868
  129.8 0.8 copy-start.9
  129.8 3.4 %copy-start.27 = (f32[2,256,128]{2,1,0:T(8,128)S(1)}, f32[2,256,128]{2,1,0:T(8,128)}, u32[]{:S(2)}) copy-start(f32[2,256,128]{2,1,0:T(8,128)} %convolution_bitcast_fusion.1) | copy-start | bytes 786436
  131.1 3.3 %copy-start.5 = (f32[2,256,528]{1,2,0:T(8,128)S(1)}, f32[2,256,528]{1,2,0:T(8,128)}, u32[]{:S(2)}) copy-start(f32[2,256,528]{1,2,0:T(8,128)} %copy-done.4) | copy-start | bytes 3244036
  131.2 3.3 %copy-start.8 = (f32[2,256,528]{1,2,0:T(8,128)S(1)}, f32[2,256,528]{1,2,0:T(8,128)}, u32[]{:S(2)}) copy-start(f32[2,256,528]{1,2,0:T(8,128)} %get-tuple-element.48) | copy-start | bytes 3244036
  134.5 2.1 %copy-start.29 = (bf16[1056,32,1]{0,1,2:T(8,128)(2,1)S(1)}, bf16[1056,32,1]{0,1,2:T(8,128)(2,1)}, u32[]{:S(2)}) copy-start(bf16[1056,32,1]{0,1,2:T(8,128)(2,1)} %constant.97) | copy-start | bytes 202756
  136.6 0.8 copy-start.20
  136.6 1.2 copy-start.28
  136.6 2.4 %copy-start.1 = (bf16[256,8,128]{2,1,0:T(8,128)(2,1)S(1)}, bf16[256,8,128]{2,1,0:T(8,128)(2,1)}, u32[]{:S(2)}) copy-start(bf16[256,8,128]{2,1,0:T(8,128)(2,1)} %param.10) | copy-start | bytes 1572868

commit v4 on v3

--- a/solution.py
+++ b/solution.py
@@ -9,13 +9,12 @@
 bf16 = jnp.bfloat16
 
 
-def triangle(width):
-    rows, cols = np.triu_indices(width)
-    take_a = np.eye(width, dtype=np.float32)[:, rows]
-    take_b = np.eye(width, dtype=np.float32)[:, cols]
-    weight = np.where(rows == cols, 1.0, 2.0).astype(np.float32)
-    off = (rows != cols).astype(np.float32)
-    return take_a, take_b, weight, off
+def half_blocks(width):
+    half, quarter = width // 2, width // 4
+    blocks = [((0, half), (half, width), 2.0)]
+    blocks += [((lo, lo + quarter), (lo + quarter, lo + half), 2.0) for lo in (0, half)]
+    blocks += [((lo, lo + quarter), (lo, lo + quarter), 1.0) for lo in range(0, width, quarter)]
+    return blocks
 
 
 def split_parts(x, count):
@@ -50,10 +49,6 @@
         + jnp.einsum(pattern, fh, sl, preferred_element_type=f32)
         + jnp.einsum(pattern, fl, sh, preferred_element_type=f32)
     )
-
-
-def take_exact(x, select):
-    return dot_parts("...a,ak->...k", x, select, 3)
 
 
 def ctx_scan(state, total, reverse):
@@ -116,22 +111,44 @@
     return (sketch_one, sketch_two)
 
 
-def tri_features(sketch_one, sketch_two, take_a, take_b):
+def half_features(sketch_one, sketch_two):
     width = sketch_one.shape[-1]
     sketch = sketch_one * sketch_two
-    first = take_exact(sketch, take_a)
-    second = take_exact(sketch, take_b)
-    return (first * second * (1.0 / width)).astype(bf16)
-
-
-def tri_feature_back(cotangent, sketch_one, sketch_two, proj_wide, take_a, take_b, off):
+    pieces = []
+    for (r0, r1), (c0, c1), _ in half_blocks(width):
+        outer = sketch[..., r0:r1, None] * sketch[..., None, c0:c1] * (1.0 / width)
+        pieces.append(outer.reshape(sketch.shape[:-1] + ((r1 - r0) * (c1 - c0),)))
+    return jnp.concatenate(pieces, axis=-1).astype(bf16)
+
+
+def half_weight(width):
+    parts = [np.full((r1 - r0) * (c1 - c0), w, np.float32) for (r0, r1), (c0, c1), w in half_blocks(width)]
+    return np.concatenate(parts)
+
+
+def half_feature_back(cotangent, sketch_one, sketch_two, proj_wide):
     width = sketch_one.shape[-1]
     sketch = sketch_one * sketch_two
-    first = take_exact(sketch, take_a)
-    second = take_exact(sketch, take_b)
-    spread = jnp.concatenate([cotangent * second, cotangent * first * off], axis=-1)
-    gather = jnp.concatenate([take_a.T, take_b.T], axis=0).astype(bf16)
-    dsketch = dot_parts("...k,ka->...a", spread, gather, 2) * (2.0 / width)
+    quarter = width // 4
+    segments = [[] for _ in range(4)]
+    place = 0
+    for (r0, r1), (c0, c1), w in half_blocks(width):
+        size = (r1 - r0) * (c1 - c0)
+        block = cotangent[..., place : place + size].reshape(
+            cotangent.shape[:-1] + (r1 - r0, c1 - c0)
+        )
+        place += size
+        rows_part = jnp.einsum("...rc,...c->...r", block, sketch[..., c0:c1], precision=highest)
+        for k in range(r0 // quarter, r1 // quarter):
+            lo = k * quarter - r0
+            segments[k].append(rows_part[..., lo : lo + quarter])
+        if w != 1.0:
+            cols_part = jnp.einsum("...rc,...r->...c", block, sketch[..., r0:r1], precision=highest)
+            for k in range(c0 // quarter, c1 // quarter):
+                lo = k * quarter - c0
+                segments[k].append(cols_part[..., lo : lo + quarter])
+    dsketch = jnp.concatenate([sum(parts[1:], parts[0]) for parts in segments], axis=-1)
+    dsketch = dsketch * (2.0 / width)
     back_one = jnp.einsum("...f,df->...d", dsketch * sketch_two, proj_wide[0], precision=highest)
     back_two = jnp.einsum("...f,df->...d", dsketch * sketch_one, proj_wide[1], precision=highest)
     return (back_one + back_two) * proj_wide.shape[1] ** (-0.5)
@@ -141,11 +158,7 @@
     projector = (2 * signs - 1).astype(bf16)
     proj_wide = projector.astype(f32)
     width = signs.shape[-1]
-    take_a_np, take_b_np, weight_np, off_np = triangle(width)
-    take_a = jnp.asarray(take_a_np, bf16)
-    take_b = jnp.asarray(take_b_np, bf16)
-    weight = jnp.asarray(weight_np, bf16)
-    off = jnp.asarray(off_np, f32)
+    weight = jnp.asarray(half_weight(width), bf16)
     heads_all = keys.shape[1]
     owned = heads_all // lax.axis_size("head")
     offset = lax.axis_index("head") * owned
@@ -154,7 +167,7 @@
     both = head_exchange(jnp.stack([queries, dout]), owned)
     query_part, grad_part = both[0], both[1]
     key_one, key_two = sketch_parts(key_part, projector, "thd,df->htf")
-    key_feat = tri_features(key_one, key_two, take_a, take_b)
+    key_feat = half_features(key_one, key_two)
     key_wfeat = key_feat * weight
     value_heads = value_part.transpose(1, 0, 2)
     block_state = jnp.einsum("htf,htd->hfd", key_feat, value_heads, preferred_element_type=f32)
@@ -162,7 +175,7 @@
     state_in, total_in = ctx_scan(block_state, block_total, False)
 
     query_one, query_two = sketch_parts(query_part, projector, "tmhd,df->hmtf")
-    query_feat = tri_features(query_one, query_two, take_a, take_b)
+    query_feat = half_features(query_one, query_two)
     query_wfeat = query_feat * weight
     grad_heads = grad_part.transpose(2, 1, 0, 3).astype(f32)
     length = key_feat.shape[1]
@@ -198,9 +211,7 @@
         + dot_split3("hmid,hfd->hmif", grad_rows, state_in)
         + correction[..., None] * total_in[:, None, None, :]
     )
-    query_grad = tri_feature_back(
-        grad_qfeat, query_one, query_two, proj_wide, take_a, take_b, off
-    )
+    query_grad = half_feature_back(grad_qfeat, query_one, query_two, proj_wide)
     query_low = query_grad.transpose(2, 1, 0, 3).astype(bf16)
     query_out = head_return(query_low, heads_all)
 
@@ -212,7 +223,7 @@
         + merged_total[:, None, :]
     )
     value_total = grad_value + dot_split("htf,hfd->htd", key_wfeat, merged_state)
-    key_sum = tri_feature_back(kfeat_total, key_one, key_two, proj_wide, take_a, take_b, off)
+    key_sum = half_feature_back(kfeat_total, key_one, key_two, proj_wide)
     key_out = key_sum.transpose(1, 0, 2).astype(bf16)
     value_out = value_total.transpose(1, 0, 2).astype(bf16)
     return (query_out, key_out, value_out)

time: 140 us -> 186 us (1.33)
  local copies, waits for them, and re-layouts: 16.2 us -> 65.1 us
  matrix products: 64.4 us -> 34.9 us
  other arithmetic: 6.02 us -> 23.9 us
  waiting for transfers between devices: 14.2 us -> 20.1 us
    unnamed x68 -> x130, local copies, waits for them, and re-layouts: 2.96 us -> 25.3 us
    dot_general x26 -> x10, matrix products: 34.1 us -> 12.4 us  [dot_parts(): term = jnp.einsum(pattern, *args, preferred_element_type=f32)]
    unnamed x0 -> x8, other arithmetic: none -> 15 us
    mul x0 -> x14, local copies, waits for them, and re-layouts: none -> 8.27 us  [half_features(): outer = sketch[..., r0:r1, None] * sketch[..., None, c0:c1] * (1.0 / width)]
    all_to_all x2, waiting for transfers between devices: 12.8 us -> 20.1 us  [ctx_scan(): lax.all_to_all(summed, 'ctx', 0, 0, tiled=True).reshape(n * per, width)]
    slice x0 -> x10, local copies, waits for them, and re-layouts: none -> 6.91 us  [the longest x4 6.19 us: half_feature_back(): cotangent[..., place:place + size]]
    concatenate x0 -> x2, local copies, waits for them, and re-layouts: none -> 6.16 us  [half_features(): return jnp.concatenate(pieces, axis=-1).astype(bf16)]
    dot_general x1, matrix products: 7.19 us -> 1.7 us  [body(): jnp.einsum('hmij,hjf->hmif', dscores, key_feat, preferred_element_type=f32)]
  transfers between devices with their start and end apart: 10 -> 10, of which waited for: 3 -> 2; matrix products, arithmetic and copies ran while one was open for 38% -> 39% of each run, Pallas kernels for 0% -> 0%
where the time goes in v4:
time: 186 us; the launch traced here: 184 us
  local copies, waits for them, and re-layouts  65.1 us (35%)
  starting transfers between devices  38 us (20%)
  matrix products  34.9 us (19%)
  other arithmetic  23.9 us (13%)
  waiting for transfers between devices  20.1 us (11%)
  between operations  1.92 us (1%)
    unnamed x130, local copies, waits for them, and re-layouts  25.3 us
    all_to_all x2, waiting for transfers between devices, ctx_scan(): lax.all_to_all(summed, 'ctx', 0, 0, tiled=True).reshape(n * per, width)  20.1 us
    all_to_all x2, starting transfers between devices, ctx_scan(): lax.all_to_all(summed, 'ctx', 0, 0, tiled=True).reshape(n * per, width)  15.5 us
    unnamed x8, other arithmetic  15 us
    all_to_all x2, starting transfers between devices, ctx_scan(): got = lax.all_to_all(flat.reshape(n, per, width), 'ctx', 0, 0, tiled=True)  13.4 us
    dot_general x10, matrix products, dot_parts(): term = jnp.einsum(pattern, *args, preferred_element_type=f32)  12.4 us
    mul x14, local copies, waits for them, and re-layouts, half_features(): outer = sketch[..., r0:r1, None] * sketch[..., None, c0:c1] * (1.0 / width)  8.27 us
    ppermute x3, starting transfers between devices, head_exchange(): lax.ppermute(piece, 'head', [(j, (j + k) % count) for j in range(count)])  6.57 us
  transfers between devices with their start and end apart: 10, of which 2 were waited for; matrix products, arithmetic and copies ran while one was open for 39% of the time, Pallas kernels for 0%

profile of v4, /device:TPU:1, one launch (start us, length us, event | category | flops | bytes accessed | tf_op | source)
XLA Modules:
  0.0 184.0 jit_solution(16537575312258147018)
XLA Ops:
  0.7 1.2 copy.538
  1.9 1.1 copy.539
  3.1 2.5 %collective-permute-start = (bf16[2,256,1,2,128]{4,1,3,2,0:T(8,128)(2,1)S(1)}, bf16[2,256,1,2,128]{4,1,3,2,0:T(8,128)(2,1)S(1)}, u32[]{:S(2)}, u32[]{:S(2)}) collective-permute-start(bf16[2,256,1,2,128]{4,1,3,2,0:T(8,128)(2,1)S(1)} %get-tuple-element.36), channel_id=1, source_target_pairs={{0,1},{1,2},{2,3},{3,0},{4,5},{5,6},{6,7},{7,4},{8,9},{9,10},{10,1... | collective-permute-start | bytes 786440 | tf_op jit(solution)/shard_map/ppermute | solution.py:89
  5.7 3.3 %collective-permute-start.1 = (bf16[2,256,1,2,128]{4,1,3,2,0:T(8,128)(2,1)S(1)}, bf16[2,256,1,2,128]{4,1,3,2,0:T(8,128)(2,1)S(1)}, u32[]{:S(2)}, u32[]{:S(2)}) collective-permute-start(bf16[2,256,1,2,128]{4,1,3,2,0:T(8,128)(2,1)S(1)} %get-tuple-element.37), channel_id=1, source_target_pairs={{0,2},{1,3},{2,0},{3,1},{4,6},{5,7},{6,4},{7,5},{8,10},{9,11},{10,... | collective-permute-start | bytes 786440 | tf_op jit(solution)/shard_map/ppermute | solution.py:89
  12.0 1.2 constant_dynamic-slice_fusion
  15.1 8.6 %all-to-all-start = ((f32[32,48,128]{2,1,0:T(8,128)}), f32[32,48,128]{2,1,0:T(8,128)}, u32[]{:S(2)}, u32[]{:S(2)}) async-start(f32[32,48,128]{2,1,0:T(8,128)} %bitcast.50), calls=%async_computation | async-start | bytes 1572864 | tf_op jit(solution)/shard_map/all_to_all | solution.py:70
  24.4 1.1 pad_maximum_fusion
  27.8 1.3 copy.145
  31.6 1.0 copy.148
  32.6 1.0 copy.149
  33.6 1.0 copy.150
  34.6 1.0 copy.151
  35.6 5.7 %concatenate.24 = bf16[2,4,256,640]{3,2,1,0:T(8,128)(2,1)S(1)} concatenate(bf16[2,4,256,256]{3,2,1,0:T(8,128)(2,1)} %copy.145, bf16[2,4,256,64]{3,2,1,0:T(8,128)(2,1)} %copy.146, bf16[2,4,256,64]{3,2,1,0:T(8,128)(2,1)} %copy.147, bf16[2,4,256,64]{3,2,1,0:T(8,128)(2,1)} %copy.148, bf16[2,4,256,64]{3,2,1,0:T(8,128)(2,1)} %copy.149, bf16[2,4,256,64]{3,2,1,0:T(8,128)(2,1)} %copy.150, ...), dimensions={3} | concatenate | bytes 5242880 | tf_op jit(solution)/shard_map/concatenate | solution.py:121
  41.4 1.9 %fusion.33 = f32[32,48,128]{2,0,1:T(8,128)S(1)} fusion(f32[32,48,128]{2,1,0:T(8,128)} %all-to-all-done), kind=kOutput, calls=%fused_computation.66 | convolution fusion | flops 75498496 | bytes 1572864 | tf_op jit(solution)/shard_map/ij,jrc->irc/dot_general | solution.py:74
  43.3 1.4 copy.163
  44.6 7.4 %all-to-all-start.1 = ((f32[32,48,128]{2,1,0:T(8,128)}), f32[32,48,128]{2,1,0:T(8,128)}, u32[]{:S(2)}, u32[]{:S(2)}) async-start(f32[32,48,128]{2,1,0:T(8,128)} %copy.163), calls=%async_computation.1 | async-start | bytes 1572864 | tf_op jit(solution)/shard_map/all_to_all | solution.py:75
  52.1 1.9 %select_convert_fusion.1 = (bf16[2,4,256,256]{2,3,1,0:T(8,128)(2,1)S(1)}, f32[2,4,256,256]{2,3,1,0:T(8,128)S(1)}) fusion(pred[256,256]{0,1:T(8,128)(4,1)} %iota_compare_fusion.1, bf16[2,256,640]{2,1,0:T(8,128)(2,1)S(1)} %concatenate.25, bf16[2,4,256,640]{3,2,1,0:T(8,128)(2,1)S(1)} %concatenate.24, bf16[640]{0:T(1024)(128)(2,1)} %constant.71.clone), kind=kOutput, calls=%fused_computation.9 | convolution fusion | flops 672923648 | bytes 6489344 | tf_op jit(solution)/shard_map/hmif,hjf->hmij/dot_general | solution.py:187
  55.1 1.5 fusion.27
  56.6 9.8 %all-to-all-done.1 = f32[32,48,128]{2,1,0:T(8,128)} async-done(((f32[32,48,128]{2,1,0:T(8,128)}), f32[32,48,128]{2,1,0:T(8,128)}, u32[]{:S(2)}, u32[]{:S(2)}) %all-to-all-start.1) | async-done | bytes 786464 | tf_op jit(solution)/shard_map/all_to_all | solution.py:75
  66.4 2.0 %slice.243 = f32[1280,128]{1,0:T(8,128)} slice(f32[1536,128]{1,0:T(8,128)} %bitcast.51), slice={[0:1280], [0:128]} | slice | bytes 1310720 | tf_op jit(solution)/shard_map/slice | solution.py:76
  68.3 1.3 slice.242
  69.6 2.2 %copy.168 = f32[2,640,128]{1,2,0:T(8,128)} copy(f32[2,640,128]{2,1,0:T(8,128)} %bitcast.319) | data formatting | bytes 1310720 | tf_op jit(solution)/shard_map/reshape | solution.py:76
  71.8 3.0 %fusion = f32[2,4,256,128]{3,2,0,1:T(8,128)} fusion(f32[2,640,128]{1,2,0:T(8,128)} %copy.168, bf16[2,4,256,640]{3,2,1,0:T(8,128)(2,1)S(1)} %concatenate.24, bf16[640]{0:T(1024)(128)(2,1)} %constant.71.clone), kind=kOutput, calls=%fused_computation.1 | convolution fusion | flops 337346560 | bytes 4326656 | tf_op jit(solution)/shard_map/hmif,hfd->hmid/dot_general | solution.py:35
  74.7 1.3 reshape.213
  76.8 1.5 fusion.157
  82.0 1.1 multiply_reduce_fusion.2
  83.1 2.0 %fusion.58 = f32[2,640,128,1]{2,1,3,0:T(8,128)} fusion(bf16[2,4,256,640]{3,2,1,0:T(8,128)(2,1)S(1)} %concatenate.24, bf16[2,4,256,128]{3,2,0,1:T(8,128)(2,1)S(1)} %get-tuple-element.32), kind=kOutput, calls=%fused_computation.112 | convolution fusion | flops 335544320 | bytes 3801088 | tf_op jit(solution)/shard_map/hmif,hmid->hfd/dot_general | solution.py:199
  86.5 1.7 multiply_add_fusion
  88.3 3.7 %fusion.168 = (f32[2,4,256,64]{3,2,1,0:T(8,128)}, f32[2,4,256,64]{3,2,1,0:T(8,128)}, f32[2,4,256,64]{3,2,1,0:T(8,128)}, f32[2,4,256,64]{3,2,1,0:T(8,128)}, f32[2...) fusion(f32[2,4,256,640]{3,2,1,0:T(8,128)S(1)} %multiply_add_fusion), kind=kLoop, calls=%fused_computation.256 | loop fusion | bytes 6291456 | tf_op jit(solution)/shard_map/slice | solution.py:137
  91.9 1.5 slice.244
  95.0 1.3 reshape.223
  96.3 2.1 %select_maximum_fusion = f32[1536,128]{1,0:T(8,128)} fusion(f32[10,128]{1,0:T(8,128)} %reshape.223, f32[1280,128]{1,0:T(8,128)} %bitcast.320), kind=kLoop, calls=%fused_computation.61 | loop fusion | flops 786432 | bytes 1446912 | tf_op jit(solution)/shard_map/concatenate | solution.py:58
  98.3 4.8 %all-to-all-start.2 = ((f32[32,48,128]{2,1,0:T(8,128)}), f32[32,48,128]{2,1,0:T(8,128)}, u32[]{:S(2)}, u32[]{:S(2)}) async-start(f32[32,48,128]{2,1,0:T(8,128)} %bitcast.315), calls=%async_computation.2 | async-start | bytes 1572864 | tf_op jit(solution)/shard_map/all_to_all | solution.py:70
  103.1 2.3 %copy.371 = f32[2,4,256,64]{2,3,1,0:T(8,128)} copy(f32[2,4,256,64]{3,2,1,0:T(8,128)} %get-tuple-element.25) | data formatting | bytes 1048576
  105.5 2.3 %copy.373 = f32[2,4,256,64]{2,3,1,0:T(8,128)} copy(f32[2,4,256,64]{3,2,1,0:T(8,128)} %get-tuple-element.24) | data formatting | bytes 1048576
  107.8 1.7 fusion.50
  109.5 2.2 %fusion.49 = (f32[2,4,256,8]{2,3,1,0:T(8,128)}, f32[2,4,256,8]{2,3,1,0:T(8,128)}) fusion(f32[2,4,256,64]{2,3,1,0:T(8,128)} %copy.371, f32[2,4,256,64]{2,3,1,0:T(8,128)} %copy.373, f32[2,4,256,8]{2,3,0,1:T(8,128)} %copy-done.24), kind=kLoop, calls=%fused_computation.91 | loop fusion | flops 491520 | bytes 1245184
  111.7 2.3 %copy.372 = f32[2,4,256,64]{2,3,1,0:T(8,128)} copy(f32[2,4,256,64]{3,2,1,0:T(8,128)} %get-tuple-element.20) | data formatting | bytes 1048576
  114.0 1.8 fusion.48
  115.9 2.9 %copy.370 = f32[2,4,256,256]{2,3,1,0:T(8,128)} copy(f32[2,4,256,256]{3,2,1,0:T(8,128)} %slice.244) | data formatting | bytes 4194304
  118.7 2.1 %multiply_reduce_fusion.1 = f32[2,4,256,16]{2,3,1,0:T(8,128)S(1)} fusion(f32[2,4,256,256]{2,3,1,0:T(8,128)} %copy.370, f32[2,4,256,16]{2,3,0,1:T(8,128)} %copy-done.15), kind=kLoop, calls=%fused_computation.6 | loop fusion | flops 1015808 | bytes 2359296
  121.5 2.3 %copy.375 = f32[2,4,256,64]{2,3,1,0:T(8,128)} copy(f32[2,4,256,64]{3,2,1,0:T(8,128)} %get-tuple-element.22) | data formatting | bytes 1048576
  123.8 1.8 fusion.44
  125.7 2.3 %copy.374 = f32[2,4,256,64]{2,3,1,0:T(8,128)} copy(f32[2,4,256,64]{3,2,1,0:T(8,128)} %get-tuple-element.23) | data formatting | bytes 1048576
  128.0 1.7 fusion.46
  129.7 2.4 %copy.376 = f32[2,4,256,64]{2,3,1,0:T(8,128)} copy(f32[2,4,256,64]{3,2,1,0:T(8,128)} %get-tuple-element.21) | data formatting | bytes 1048576
  132.2 1.6 fusion.45
  133.8 1.9 %multiply_reduce_fusion = f32[2,4,256,16]{2,3,1,0:T(8,128)S(1)} fusion(f32[2,4,256,16,16]{2,4,3,1,0:T(8,128)} %bitcast.308, f32[2,4,256,16]{2,3,0,1:T(8,128)S(1)} %get-tuple-element.49), kind=kLoop, calls=%fused_computation.5 | loop fusion | flops 1015808 | bytes 2359296
  137.1 1.0 fusion.14
  138.8 2.5 %collective-permute-start.4 = (bf16[256,1,2,128]{3,0,1,2:T(8,128)(2,1)}, bf16[256,1,2,128]{3,0,1,2:T(8,128)(2,1)}, u32[]{:S(2)}, u32[]{:S(2)}) collective-permute-start(bf16[256,1,2,128]{3,0,1,2:T(8,128)(2,1)} %get-tuple-element.40), channel_id=1, source_target_pairs={{0,2},{1,3},{2,0},{3,1},{4,6},{5,7},{6,4},{7,5},{8,10},{9,11},{10,... | collective-permute-start | bytes 393224 | tf_op jit(solution)/shard_map/ppermute | solution.py:102
  141.4 1.1 convolution_bitcast_fusion.1
  142.5 2.1 %convolution_bitcast_fusion = f32[2,256,640]{2,1,0:T(8,128)} fusion(bf16[2,4,256,256]{2,3,1,0:T(8,128)(2,1)S(1)} %copy-done.7, bf16[2,4,256,640]{3,2,1,0:T(8,128)(2,1)S(1)} %concatenate.24), kind=kOutput, calls=%fused_computation.23 | convolution fusion | flops 671088640 | bytes 4980736 | tf_op jit(solution)/shard_map/hmij,hmif->hjf/dot_general | solution.py:218
  144.6 1.9 %fusion.31 = f32[32,48,128]{2,0,1:T(8,128)S(1)} fusion(f32[32,48,128]{2,1,0:T(8,128)} %all-to-all-done.2), kind=kOutput, calls=%fused_computation.64 | convolution fusion | flops 75498496 | bytes 1572864 | tf_op jit(solution)/shard_map/ij,jrc->irc/dot_general | solution.py:74
  146.5 1.3 copy.199
  147.8 8.1 %all-to-all-start.3 = ((f32[32,48,128]{2,1,0:T(8,128)}), f32[32,48,128]{2,1,0:T(8,128)S(1)}, u32[]{:S(2)}, u32[]{:S(2)}) async-start(f32[32,48,128]{2,1,0:T(8,128)} %copy.199), calls=%async_computation.3 | async-start | bytes 1572864 | tf_op jit(solution)/shard_map/all_to_all | solution.py:75
  156.2 1.1 copy_dynamic-update-slice_fusion.2
  157.4 1.1 copy_dynamic-update-slice_fusion.1
  158.5 1.2 copy_dynamic-update-slice_fusion
  159.8 10.3 %all-to-all-done.3 = f32[32,48,128]{2,1,0:T(8,128)S(1)} async-done(((f32[32,48,128]{2,1,0:T(8,128)}), f32[32,48,128]{2,1,0:T(8,128)S(1)}, u32[]{:S(2)}, u32[]{:S(2)}) %all-to-all-start.3) | async-done | bytes 786464 | tf_op jit(solution)/shard_map/all_to_all | solution.py:75
  171.0 1.1 slice.259
  172.1 1.7 fusion.41
  173.8 1.4 fusion.94
  175.9 1.7 fusion.5
  179.9 1.1 copy.378
  (201 shorter events, 27.9 us)
Async XLA Ops:
  0.6 9.1 %copy-start = (bf16[256,8,128]{2,1,0:T(8,128)(2,1)S(1)}, bf16[256,8,128]{2,1,0:T(8,128)(2,1)}, u32[]{:S(2)}) copy-start(bf16[256,8,128]{2,1,0:T(8,128)(2,1)} %param.7) | copy-start | bytes 1572868
  0.6 9.0 %copy-start.52 = (s32[2,128,32]{1,2,0:T(8,128)S(1)}, s32[2,128,32]{1,2,0:T(8,128)}, u32[]{:S(2)}) copy-start(s32[2,128,32]{1,2,0:T(8,128)} %param.10) | copy-start | bytes 98308
  3.1 21.3 %collective-permute-start = (bf16[2,256,1,2,128]{4,1,3,2,0:T(8,128)(2,1)S(1)}, bf16[2,256,1,2,128]{4,1,3,2,0:T(8,128)(2,1)S(1)}, u32[]{:S(2)}, u32[]{:S(2)}) collective-permute-start(bf16[2,256,1,2,128]{4,1,3,2,0:T(8,128)(2,1)S(1)} %get-tuple-element.36), channel_id=1, source_target_pairs={{0,1},{1,2},{2,3},{3,0},{4,5},{5,6},{6,7},{7,4},{8,9},{9,10},{10,1... | collective-permute-start | bytes 786440 | tf_op jit(solution)/shard_map/ppermute | solution.py:89
  5.7 18.8 %collective-permute-start.1 = (bf16[2,256,1,2,128]{4,1,3,2,0:T(8,128)(2,1)S(1)}, bf16[2,256,1,2,128]{4,1,3,2,0:T(8,128)(2,1)S(1)}, u32[]{:S(2)}, u32[]{:S(2)}) collective-permute-start(bf16[2,256,1,2,128]{4,1,3,2,0:T(8,128)(2,1)S(1)} %get-tuple-element.37), channel_id=1, source_target_pairs={{0,2},{1,3},{2,0},{3,1},{4,6},{5,7},{6,4},{7,5},{8,10},{9,11},{10,... | collective-permute-start | bytes 786440 | tf_op jit(solution)/shard_map/ppermute | solution.py:89
  9.0 15.5 %collective-permute-start.2 = (bf16[2,256,1,2,128]{4,1,3,2,0:T(8,128)(2,1)S(1)}, bf16[2,256,1,2,128]{4,1,3,2,0:T(8,128)(2,1)}, u32[]{:S(2)}, u32[]{:S(2)}) collective-permute-start(bf16[2,256,1,2,128]{4,1,3,2,0:T(8,128)(2,1)S(1)} %get-tuple-element.38), channel_id=1, source_target_pairs={{0,3},{1,0},{2,1},{3,2},{4,7},{5,4},{6,5},{7,6},{8,11},{9,8},{10,9... | collective-permute-start | bytes 786440 | tf_op jit(solution)/shard_map/ppermute | solution.py:89
  10.0 1.7 copy-start.25
  10.8 1.0 copy-start.28
  10.8 1.0 copy-start.46
  10.8 1.0 copy-start.48
  10.9 1.0 copy-start.32
  10.9 1.0 copy-start.34
  15.1 26.3 %all-to-all-start = ((f32[32,48,128]{2,1,0:T(8,128)}), f32[32,48,128]{2,1,0:T(8,128)}, u32[]{:S(2)}, u32[]{:S(2)}) async-start(f32[32,48,128]{2,1,0:T(8,128)} %bitcast.50), calls=%async_computation | async-start | bytes 1572864 | tf_op jit(solution)/shard_map/all_to_all | solution.py:70
  25.5 1.0 copy-start.3
  26.5 1.0 copy-start.11
  27.5 2.8 %copy-start.15 = (f32[2,4,256,16]{2,3,0,1:T(8,128)}, f32[2,4,256,16]{2,3,0,1:T(8,128)S(1)}, u32[]{:S(2)}) copy-start(f32[2,4,256,16]{2,3,0,1:T(8,128)S(1)} %get-tuple-element.50) | copy-start | bytes 393220
  29.1 1.2 copy-start.24
  29.1 5.5 %copy-start.17 = (f32[2,4,256,8]{2,3,0,1:T(8,128)}, f32[2,4,256,8]{2,3,0,1:T(8,128)S(1)}, u32[]{:S(2)}) copy-start(f32[2,4,256,8]{2,3,0,1:T(8,128)S(1)} %get-tuple-element.45) | copy-start | bytes 196612
  29.2 5.5 %copy-start.18 = (f32[2,4,256,8]{2,3,0,1:T(8,128)}, f32[2,4,256,8]{2,3,0,1:T(8,128)S(1)}, u32[]{:S(2)}) copy-start(f32[2,4,256,8]{2,3,0,1:T(8,128)S(1)} %get-tuple-element.48) | copy-start | bytes 196612
  29.2 5.5 %copy-start.23 = (f32[2,4,256,8]{2,3,0,1:T(8,128)}, f32[2,4,256,8]{2,3,0,1:T(8,128)S(1)}, u32[]{:S(2)}) copy-start(f32[2,4,256,8]{2,3,0,1:T(8,128)S(1)} %get-tuple-element.46) | copy-start | bytes 196612
  44.6 21.7 %all-to-all-start.1 = ((f32[32,48,128]{2,1,0:T(8,128)}), f32[32,48,128]{2,1,0:T(8,128)}, u32[]{:S(2)}, u32[]{:S(2)}) async-start(f32[32,48,128]{2,1,0:T(8,128)} %copy.163), calls=%async_computation.1 | async-start | bytes 1572864 | tf_op jit(solution)/shard_map/all_to_all | solution.py:75
  52.1 2.0 %copy-start.19 = (pred[256,256]{0,1:T(8,128)(4,1)S(1)}, pred[256,256]{0,1:T(8,128)(4,1)}, u32[]{:S(2)}) copy-start(pred[256,256]{0,1:T(8,128)(4,1)} %iota_compare_fusion.1) | copy-start | bytes 196612
  54.0 1.0 copy-start.8
  76.0 2.3 %copy-start.53 = (bf16[640]{0:T(1024)(128)(2,1)S(1)}, bf16[640]{0:T(1024)(128)(2,1)}, u32[]{:S(2)}) copy-start(bf16[640]{0:T(1024)(128)(2,1)} %constant.71.clone) | copy-start | bytes 3844
  76.8 2.4 %copy-start.51 = (f32[2,4,256]{2,1,0:T(4,128)S(1)}, f32[2,4,256]{2,1,0:T(4,128)}, u32[]{:S(2)}) copy-start(f32[2,4,256]{2,1,0:T(4,128)} %select_reduce_fusion) | copy-start | bytes 24580
  76.8 2.4 %copy-start.4 = (bf16[2,256,4,2,128]{4,1,3,2,0:T(8,128)(2,1)S(1)}, bf16[2,256,4,2,128]{4,1,3,2,0:T(8,128)(2,1)}, u32[]{:S(2)}) copy-start(bf16[2,256,4,2,128]{4,1,3,2,0:T(8,128)(2,1)} %copy-done.3) | copy-start | bytes 3145732
  78.3 1.3 copy-start.2
  79.6 5.5 %copy-start.13 = (bf16[2,4,256,128]{3,2,0,1:T(8,128)(2,1)}, bf16[2,4,256,128]{3,2,0,1:T(8,128)(2,1)S(1)}, u32[]{:S(2)}) copy-start(bf16[2,4,256,128]{3,2,0,1:T(8,128)(2,1)S(1)} %get-tuple-element.32) | copy-start | bytes 1572868
  80.4 1.2 copy-start.21
  80.4 1.5 copy-start.55
  83.1 2.0 %copy-start.20 = (pred[256,256]{0,1:T(8,128)(4,1)S(1)}, pred[256,256]{0,1:T(8,128)(4,1)}, u32[]{:S(2)}) copy-start(pred[256,256]{0,1:T(8,128)(4,1)} %iota_compare_fusion.1) | copy-start | bytes 196612
  85.6 1.0 copy-start.6
  85.6 1.0 copy-start.50
  98.3 46.3 %all-to-all-start.2 = ((f32[32,48,128]{2,1,0:T(8,128)}), f32[32,48,128]{2,1,0:T(8,128)}, u32[]{:S(2)}, u32[]{:S(2)}) async-start(f32[32,48,128]{2,1,0:T(8,128)} %bitcast.315), calls=%async_computation.2 | async-start | bytes 1572864 | tf_op jit(solution)/shard_map/all_to_all | solution.py:70
  132.1 3.7 %copy-start.37 = (f32[2,4,256,8]{2,3,1,0:T(8,128)S(1)}, f32[2,4,256,8]{2,3,1,0:T(8,128)}, u32[]{:S(2)}) copy-start(f32[2,4,256,8]{2,3,1,0:T(8,128)} %fusion.50) | copy-start | bytes 196612
  132.1 3.7 %copy-start.38 = (f32[2,4,256,8]{2,3,1,0:T(8,128)S(1)}, f32[2,4,256,8]{2,3,1,0:T(8,128)}, u32[]{:S(2)}) copy-start(f32[2,4,256,8]{2,3,1,0:T(8,128)} %get-tuple-element.12) | copy-start | bytes 196612
  132.1 3.7 %copy-start.39 = (f32[2,4,256,8]{2,3,1,0:T(8,128)S(1)}, f32[2,4,256,8]{2,3,1,0:T(8,128)}, u32[]{:S(2)}) copy-start(f32[2,4,256,8]{2,3,1,0:T(8,128)} %get-tuple-element.13) | copy-start | bytes 196612
  132.1 3.7 %copy-start.40 = (f32[2,4,256,8]{2,3,1,0:T(8,128)S(1)}, f32[2,4,256,8]{2,3,1,0:T(8,128)}, u32[]{:S(2)}) copy-start(f32[2,4,256,8]{2,3,1,0:T(8,128)} %fusion.48) | copy-start | bytes 196612
  132.1 3.7 %copy-start.44 = (f32[2,4,256,8]{2,3,1,0:T(8,128)S(1)}, f32[2,4,256,8]{2,3,1,0:T(8,128)}, u32[]{:S(2)}) copy-start(f32[2,4,256,8]{2,3,1,0:T(8,128)} %get-tuple-element.51) | copy-start | bytes 196612
  132.1 3.7 %copy-start.45 = (f32[2,4,256,8]{2,3,1,0:T(8,128)S(1)}, f32[2,4,256,8]{2,3,1,0:T(8,128)}, u32[]{:S(2)}) copy-start(f32[2,4,256,8]{2,3,1,0:T(8,128)} %get-tuple-element.52) | copy-start | bytes 196612
  132.1 3.8 %copy-start.41 = (f32[2,4,256,8]{2,3,1,0:T(8,128)S(1)}, f32[2,4,256,8]{2,3,1,0:T(8,128)}, u32[]{:S(2)}) copy-start(f32[2,4,256,8]{2,3,1,0:T(8,128)} %fusion.44) | copy-start | bytes 196612
  132.1 3.7 %copy-start.42 = (f32[2,4,256,8]{2,3,1,0:T(8,128)S(1)}, f32[2,4,256,8]{2,3,1,0:T(8,128)}, u32[]{:S(2)}) copy-start(f32[2,4,256,8]{2,3,1,0:T(8,128)} %fusion.46) | copy-start | bytes 196612
  132.1 3.8 %copy-start.12 = (f32[2,4,256,32]{2,3,0,1:T(8,128)S(1)}, f32[2,4,256,32]{2,3,0,1:T(8,128)}, u32[]{:S(2)}) copy-start(f32[2,4,256,32]{2,3,0,1:T(8,128)} %copy-done.11) | copy-start | bytes 786436
  132.2 3.8 %copy-start.16 = (f32[2,4,256,32]{2,3,0,1:T(8,128)S(1)}, f32[2,4,256,32]{2,3,0,1:T(8,128)}, u32[]{:S(2)}) copy-start(f32[2,4,256,32]{2,3,0,1:T(8,128)} %get-tuple-element.85) | copy-start | bytes 786436
  135.9 5.4 %copy-start.9 = (bf16[2,4,256,256]{2,3,1,0:T(8,128)(2,1)S(1)}, bf16[2,4,256,256]{2,3,1,0:T(8,128)(2,1)}, u32[]{:S(2)}) copy-start(bf16[2,4,256,256]{2,3,1,0:T(8,128)(2,1)} %copy-done.8) | copy-start | bytes 3145732
  136.0 5.4 %copy-start.14 = (bf16[2,4,256,128]{3,2,0,1:T(8,128)(2,1)S(1)}, bf16[2,4,256,128]{3,2,0,1:T(8,128)(2,1)}, u32[]{:S(2)}) copy-start(bf16[2,4,256,128]{3,2,0,1:T(8,128)(2,1)} %copy-done.13) | copy-start | bytes 1572868
  137.0 5.5 %copy-start.7 = (bf16[2,4,256,256]{2,3,1,0:T(8,128)(2,1)S(1)}, bf16[2,4,256,256]{2,3,1,0:T(8,128)(2,1)}, u32[]{:S(2)}) copy-start(bf16[2,4,256,256]{2,3,1,0:T(8,128)(2,1)} %copy-done.6) | copy-start | bytes 3145732
  138.8 17.4 %collective-permute-start.3 = (bf16[256,1,2,128]{3,0,1,2:T(8,128)(2,1)}, bf16[256,1,2,128]{3,0,1,2:T(8,128)(2,1)}, u32[]{:S(2)}, u32[]{:S(2)}) collective-permute-start(bf16[256,1,2,128]{3,0,1,2:T(8,128)(2,1)} %get-tuple-element.41), channel_id=1, source_target_pairs={{0,3},{1,0},{2,1},{3,2},{4,7},{5,4},{6,5},{7,6},{8,11},{9,8},{10,9... | collective-permute-start | bytes 393224 | tf_op jit(solution)/shard_map/ppermute | solution.py:102
  138.8 18.5 %collective-permute-start.4 = (bf16[256,1,2,128]{3,0,1,2:T(8,128)(2,1)}, bf16[256,1,2,128]{3,0,1,2:T(8,128)(2,1)}, u32[]{:S(2)}, u32[]{:S(2)}) collective-permute-start(bf16[256,1,2,128]{3,0,1,2:T(8,128)(2,1)} %get-tuple-element.40), channel_id=1, source_target_pairs={{0,2},{1,3},{2,0},{3,1},{4,6},{5,7},{6,4},{7,5},{8,10},{9,11},{10,... | collective-permute-start | bytes 393224 | tf_op jit(solution)/shard_map/ppermute | solution.py:102
  141.4 17.2 %collective-permute-start.5 = (bf16[256,1,2,128]{3,0,1,2:T(8,128)(2,1)}, bf16[256,1,2,128]{3,0,1,2:T(8,128)(2,1)}, u32[]{:S(2)}, u32[]{:S(2)}) collective-permute-start(bf16[256,1,2,128]{3,0,1,2:T(8,128)(2,1)} %get-tuple-element.39), channel_id=1, source_target_pairs={{0,1},{1,2},{2,3},{3,0},{4,5},{5,6},{6,7},{7,4},{8,9},{9,10},{10,1... | collective-permute-start | bytes 393224 | tf_op jit(solution)/shard_map/ppermute | solution.py:102
  147.8 22.3 %all-to-all-start.3 = ((f32[32,48,128]{2,1,0:T(8,128)}), f32[32,48,128]{2,1,0:T(8,128)S(1)}, u32[]{:S(2)}, u32[]{:S(2)}) async-start(f32[32,48,128]{2,1,0:T(8,128)} %copy.199), calls=%async_computation.3 | async-start | bytes 1572864 | tf_op jit(solution)/shard_map/all_to_all | solution.py:75
  158.5 17.4 %copy-start.5 = (f32[2,256,640]{2,1,0:T(8,128)S(1)}, f32[2,256,640]{2,1,0:T(8,128)}, u32[]{:S(2)}) copy-start(f32[2,256,640]{2,1,0:T(8,128)} %convolution_bitcast_fusion) | copy-start | bytes 3932164
  159.8 16.2 %copy-start.27 = (bf16[256,1,8,128]{3,2,1,0:T(8,128)(2,1)}, bf16[256,1,8,128]{3,2,1,0:T(8,128)(2,1)S(1)}, u32[]{:S(2)}) copy-start(bf16[256,1,8,128]{3,2,1,0:T(8,128)(2,1)S(1)} %copy_dynamic-update-slice_fusion) | copy-start | bytes 1572868
  177.6 1.0 copy-start.22
  177.6 1.0 copy-start.36
  177.6 1.0 copy-start.54
  178.7 2.9 %copy-start.35 = (f32[2,256,16]{1,2,0:T(8,128)S(1)}, f32[2,256,16]{1,2,0:T(8,128)}, u32[]{:S(2)}) copy-start(f32[2,256,16]{1,2,0:T(8,128)} %copy-done.34) | copy-start | bytes 98308
  179.0 2.9 %copy-start.33 = (f32[2,256,16]{1,2,0:T(8,128)S(1)}, f32[2,256,16]{1,2,0:T(8,128)}, u32[]{:S(2)}) copy-start(f32[2,256,16]{1,2,0:T(8,128)} %copy-done.32) | copy-start | bytes 98308
  179.0 2.9 %copy-start.29 = (f32[2,256,8]{1,2,0:T(8,128)S(1)}, f32[2,256,8]{1,2,0:T(8,128)}, u32[]{:S(2)}) copy-start(f32[2,256,8]{1,2,0:T(8,128)} %copy-done.28) | copy-start | bytes 49156
  179.0 2.9 %copy-start.31 = (f32[2,256,8]{1,2,0:T(8,128)S(1)}, f32[2,256,8]{1,2,0:T(8,128)}, u32[]{:S(2)}) copy-start(f32[2,256,8]{1,2,0:T(8,128)} %copy-done.30) | copy-start | bytes 49156
  179.1 3.0 %copy-start.49 = (f32[2,256,8]{1,2,0:T(8,128)S(1)}, f32[2,256,8]{1,2,0:T(8,128)}, u32[]{:S(2)}) copy-start(f32[2,256,8]{1,2,0:T(8,128)} %copy-done.48) | copy-start | bytes 49156
  179.9 2.3 %copy-start.47 = (f32[2,256,8]{1,2,0:T(8,128)S(1)}, f32[2,256,8]{1,2,0:T(8,128)}, u32[]{:S(2)}) copy-start(f32[2,256,8]{1,2,0:T(8,128)} %copy-done.46) | copy-start | bytes 49156
  181.1 1.3 copy-start.26
  181.2 1.6 copy-start.43
  181.3 2.6 %copy-start.1 = (bf16[256,8,128]{2,1,0:T(8,128)(2,1)S(1)}, bf16[256,8,128]{2,1,0:T(8,128)(2,1)}, u32[]{:S(2)}) copy-start(bf16[256,8,128]{2,1,0:T(8,128)(2,1)} %param.7) | copy-start | bytes 1572868
  (2 other events, 1.8 us)

commit v5 on v3

--- a/solution.py
+++ b/solution.py
@@ -11,11 +11,11 @@
 
 def triangle(width):
     rows, cols = np.triu_indices(width)
-    take_a = np.eye(width, dtype=np.float32)[:, rows]
-    take_b = np.eye(width, dtype=np.float32)[:, cols]
-    weight = np.where(rows == cols, 1.0, 2.0).astype(np.float32)
-    off = (rows != cols).astype(np.float32)
-    return take_a, take_b, weight, off
+    keep = (rows * width + cols).astype(np.int32)
+    place = np.zeros((width, width), np.int32)
+    place[rows, cols] = np.arange(rows.size)
+    place[cols, rows] = np.arange(rows.size)
+    return keep, place.reshape(-1)
 
 
 def split_parts(x, count):
@@ -50,10 +50,6 @@
         + jnp.einsum(pattern, fh, sl, preferred_element_type=f32)
         + jnp.einsum(pattern, fl, sh, preferred_element_type=f32)
     )
-
-
-def take_exact(x, select):
-    return dot_parts("...a,ak->...k", x, select, 3)
 
 
 def ctx_scan(state, total, reverse):
@@ -116,36 +112,40 @@
     return (sketch_one, sketch_two)
 
 
-def tri_features(sketch_one, sketch_two, take_a, take_b):
+def features(sketch_one, sketch_two):
     width = sketch_one.shape[-1]
     sketch = sketch_one * sketch_two
-    first = take_exact(sketch, take_a)
-    second = take_exact(sketch, take_b)
-    return (first * second * (1.0 / width)).astype(bf16)
-
-
-def tri_feature_back(cotangent, sketch_one, sketch_two, proj_wide, take_a, take_b, off):
+    outer = sketch[..., :, None] * sketch[..., None, :] * (1.0 / width)
+    return outer.reshape(sketch.shape[:-1] + (width * width,)).astype(bf16)
+
+
+def feature_back(cotangent, sketch_one, sketch_two, proj_wide):
     width = sketch_one.shape[-1]
     sketch = sketch_one * sketch_two
-    first = take_exact(sketch, take_a)
-    second = take_exact(sketch, take_b)
-    spread = jnp.concatenate([cotangent * second, cotangent * first * off], axis=-1)
-    gather = jnp.concatenate([take_a.T, take_b.T], axis=0).astype(bf16)
-    dsketch = dot_parts("...k,ka->...a", spread, gather, 2) * (2.0 / width)
+    square = cotangent.reshape(cotangent.shape[:-1] + (width, width))
+    dsketch = (
+        jnp.einsum("...ab,...b->...a", square, sketch, precision=highest)
+        + jnp.einsum("...ab,...a->...b", square, sketch, precision=highest)
+    ) * (1.0 / width)
     back_one = jnp.einsum("...f,df->...d", dsketch * sketch_two, proj_wide[0], precision=highest)
     back_two = jnp.einsum("...f,df->...d", dsketch * sketch_one, proj_wide[1], precision=highest)
     return (back_one + back_two) * proj_wide.shape[1] ** (-0.5)
+
+
+def sym_scan(state, total, keep, place, reverse):
+    half_state, half_total = ctx_scan(
+        jnp.take(state, keep, axis=1), jnp.take(total, keep, axis=1), reverse
+    )
+    return jnp.take(half_state, place, axis=1), jnp.take(half_total, place, axis=1)
 
 
 def body(queries, keys, values, dout, signs):
     projector = (2 * signs - 1).astype(bf16)
     proj_wide = projector.astype(f32)
     width = signs.shape[-1]
-    take_a_np, take_b_np, weight_np, off_np = triangle(width)
-    take_a = jnp.asarray(take_a_np, bf16)
-    take_b = jnp.asarray(take_b_np, bf16)
-    weight = jnp.asarray(weight_np, bf16)
-    off = jnp.asarray(off_np, f32)
+    keep_np, place_np = triangle(width)
+    keep = jnp.asarray(keep_np)
+    place = jnp.asarray(place_np)
     heads_all = keys.shape[1]
     owned = heads_all // lax.axis_size("head")
     offset = lax.axis_index("head") * owned
@@ -154,16 +154,14 @@
     both = head_exchange(jnp.stack([queries, dout]), owned)
     query_part, grad_part = both[0], both[1]
     key_one, key_two = sketch_parts(key_part, projector, "thd,df->htf")
-    key_feat = tri_features(key_one, key_two, take_a, take_b)
-    key_wfeat = key_feat * weight
+    key_feat = features(key_one, key_two)
     value_heads = value_part.transpose(1, 0, 2)
     block_state = jnp.einsum("htf,htd->hfd", key_feat, value_heads, preferred_element_type=f32)
     block_total = jnp.sum(key_feat, 1, dtype=f32)
-    state_in, total_in = ctx_scan(block_state, block_total, False)
+    state_in, total_in = sym_scan(block_state, block_total, keep, place, False)
 
     query_one, query_two = sketch_parts(query_part, projector, "tmhd,df->hmtf")
-    query_feat = tri_features(query_one, query_two, take_a, take_b)
-    query_wfeat = query_feat * weight
+    query_feat = features(query_one, query_two)
     grad_heads = grad_part.transpose(2, 1, 0, 3).astype(f32)
     length = key_feat.shape[1]
     causal = lax.broadcasted_iota(jnp.int32, (length, length), 0) >= lax.broadcasted_iota(
@@ -171,21 +169,21 @@
     )
     scores = jnp.where(
         causal,
-        jnp.einsum("hmif,hjf->hmij", query_wfeat, key_feat, preferred_element_type=f32),
+        jnp.einsum("hmif,hjf->hmij", query_feat, key_feat, preferred_element_type=f32),
         0.0,
     )
     weights = scores.astype(bf16)
     numerator = jnp.einsum(
         "hmij,hjd->hmid", weights, value_heads, preferred_element_type=f32
-    ) + dot_split("hmif,hfd->hmid", query_wfeat, state_in)
-    denominator = 1.0 + jnp.sum(scores, -1) + dot_split("hmif,hf->hmi", query_wfeat, total_in)
+    ) + dot_split("hmif,hfd->hmid", query_feat, state_in)
+    denominator = 1.0 + jnp.sum(scores, -1) + dot_split("hmif,hf->hmi", query_feat, total_in)
     output_rows = numerator / denominator[..., None]
     grad_rows = grad_heads / denominator[..., None]
     grad_low = grad_rows.astype(bf16)
     correction = -jnp.sum(grad_rows * output_rows, -1)
     suffix_part = jnp.einsum("hmif,hmid->hfd", query_feat, grad_low, preferred_element_type=f32)
     suffix_sum = dot_split("hmif,hmi->hf", query_feat, correction)
-    merged_state, merged_total = ctx_scan(suffix_part, suffix_sum, True)
+    merged_state, merged_total = sym_scan(suffix_part, suffix_sum, keep, place, True)
 
     dscores = jnp.where(
         causal,
@@ -198,9 +196,7 @@
         + dot_split3("hmid,hfd->hmif", grad_rows, state_in)
         + correction[..., None] * total_in[:, None, None, :]
     )
-    query_grad = tri_feature_back(
-        grad_qfeat, query_one, query_two, proj_wide, take_a, take_b, off
-    )
+    query_grad = feature_back(grad_qfeat, query_one, query_two, proj_wide)
     query_low = query_grad.transpose(2, 1, 0, 3).astype(bf16)
     query_out = head_return(query_low, heads_all)
 
@@ -211,8 +207,8 @@
         + dot_split("htd,hfd->htf", value_heads, merged_state)
         + merged_total[:, None, :]
     )
-    value_total = grad_value + dot_split("htf,hfd->htd", key_wfeat, merged_state)
-    key_sum = tri_feature_back(kfeat_total, key_one, key_two, proj_wide, take_a, take_b, off)
+    value_total = grad_value + dot_split("htf,hfd->htd", key_feat, merged_state)
+    key_sum = feature_back(kfeat_total, key_one, key_two, proj_wide)
     key_out = key_sum.transpose(1, 0, 2).astype(bf16)
     value_out = value_total.transpose(1, 0, 2).astype(bf16)
     return (query_out, key_out, value_out)

time: 140 us -> 213 us (1.52)
  local copies, waits for them, and re-layouts: 16.2 us -> 54.5 us
  other arithmetic: 6.02 us -> 19 us
  waiting for transfers between devices: 14.2 us -> 25.3 us
  starting transfers between devices: 36.8 us -> 44.5 us
    gather x0 -> x12, local copies, waits for them, and re-layouts: none -> 26.1 us  [the longest x4 7.63 us: sym_scan(): jnp.take(state, keep, axis=1)]
    dot_general x26 -> x10, matrix products: 34.1 us -> 20.8 us  [dot_parts(): term = jnp.einsum(pattern, *args, preferred_element_type=f32)]
    unnamed x68 -> x98, local copies, waits for them, and re-layouts: 2.96 us -> 14.6 us
    dot_general x1, matrix products: 0.73 us -> 9.38 us  [dot_split3(): jnp.einsum(pattern, fl, sh, preferred_element_type=f32)]
    all_to_all x2, starting transfers between devices: 13.6 us -> 22 us  [ctx_scan(): got = lax.all_to_all(flat.reshape(n, per, width), 'ctx', 0, 0, tiled=True)]
    all_to_all x2, waiting for transfers between devices: 12.8 us -> 19.7 us  [ctx_scan(): lax.all_to_all(summed, 'ctx', 0, 0, tiled=True).reshape(n * per, width)]
    unnamed x0 -> x2, other arithmetic: none -> 6.73 us
    dot_general x1, matrix products: 7.19 us -> 2.79 us  [body(): jnp.einsum('hmij,hjf->hmif', dscores, key_feat, preferred_element_type=f32)]
  transfers between devices with their start and end apart: 10 -> 10, of which waited for: 3 -> 3; matrix products, arithmetic and copies ran while one was open for 38% -> 28% of each run, Pallas kernels for 0% -> 0%
where the time goes in v5:
time: 213 us; the launch traced here: 210 us
  matrix products  65.1 us (31%)
  local copies, waits for them, and re-layouts  54.5 us (26%)
  starting transfers between devices  44.5 us (21%)
  waiting for transfers between devices  25.3 us (12%)
  other arithmetic  19 us (9%)
    all_to_all x2, starting transfers between devices, ctx_scan(): got = lax.all_to_all(flat.reshape(n, per, width), 'ctx', 0, 0, tiled=True)  22 us
    dot_general x10, matrix products, dot_parts(): term = jnp.einsum(pattern, *args, preferred_element_type=f32)  20.8 us
    all_to_all x2, waiting for transfers between devices, ctx_scan(): lax.all_to_all(summed, 'ctx', 0, 0, tiled=True).reshape(n * per, width)  19.7 us
    unnamed x98, local copies, waits for them, and re-layouts  14.6 us
    all_to_all x2, starting transfers between devices, ctx_scan(): lax.all_to_all(summed, 'ctx', 0, 0, tiled=True).reshape(n * per, width)  12.7 us
    dot_general x1, matrix products, dot_split3(): jnp.einsum(pattern, fl, sh, preferred_element_type=f32)  9.38 us
    gather x4, local copies, waits for them, and re-layouts, sym_scan(): jnp.take(state, keep, axis=1)  7.63 us
    gather x2, local copies, waits for them, and re-layouts, sym_scan(): jnp.take(half_state, place, axis=1)  7.6 us
  transfers between devices with their start and end apart: 10, of which 3 were waited for; matrix products, arithmetic and copies ran while one was open for 28% of the time, Pallas kernels for 0%

profile of v5, /device:TPU:1, one launch (start us, length us, event | category | flops | bytes accessed | tf_op | source)
XLA Modules:
  0.0 210.3 jit_solution(8603057643490138300)
XLA Ops:
  0.7 1.4 copy_bitcast_fusion
  2.2 0.9 fusion.50
  3.1 2.5 %collective-permute-start = (bf16[2,256,1,2,128]{4,1,3,2,0:T(8,128)(2,1)}, bf16[2,256,1,2,128]{4,1,3,2,0:T(8,128)(2,1)}, u32[]{:S(2)}, u32[]{:S(2)}) collective-permute-start(bf16[2,256,1,2,128]{4,1,3,2,0:T(8,128)(2,1)} %get-tuple-element.26), channel_id=1, source_target_pairs={{0,1},{1,2},{2,3},{3,0},{4,5},{5,6},{6,7},{7,4},{8,9},{9,10},{10,1... | collective-permute-start | bytes 786440 | tf_op jit(solution)/shard_map/ppermute | solution.py:90
  5.6 3.3 %collective-permute-start.1 = (bf16[2,256,1,2,128]{4,1,3,2,0:T(8,128)(2,1)}, bf16[2,256,1,2,128]{4,1,3,2,0:T(8,128)(2,1)}, u32[]{:S(2)}, u32[]{:S(2)}) collective-permute-start(bf16[2,256,1,2,128]{4,1,3,2,0:T(8,128)(2,1)} %get-tuple-element.27), channel_id=1, source_target_pairs={{0,2},{1,3},{2,0},{3,1},{4,6},{5,7},{6,4},{7,5},{8,10},{9,11},{10,... | collective-permute-start | bytes 786440 | tf_op jit(solution)/shard_map/ppermute | solution.py:90
  9.8 1.2 constant_dynamic-slice_fusion.1
  11.2 0.8 fusion.114
  12.6 1.6 gather_fusion.1
  14.8 0.8 copy.242
  15.6 2.9 %gather_fusion = f32[528,2,128]{2,1,0:T(2,128)S(1)} fusion(f32[2,1024,128]{2,0,1:T(2,128)S(1)} %copy.242, s32[1024]{0:T(1024)} %copy-done.34), kind=kCustom, calls=%fused_computation.clone | custom fusion | bytes 1083456 | tf_op jit(solution)/shard_map/jit(_take)/gather | solution.py:137
  18.6 0.9 select_maximum_fusion.1
  19.5 8.6 %all-to-all-start = ((f32[32,40,128]{2,1,0:T(8,128)}), f32[32,40,128]{2,1,0:T(8,128)S(1)}, u32[]{:S(2)}, u32[]{:S(2)}) async-start(f32[32,40,128]{2,1,0:T(8,128)} %bitcast.28), calls=%async_computation | async-start | bytes 1310720 | tf_op jit(solution)/shard_map/all_to_all | solution.py:71
  28.8 1.2 pad_maximum_fusion
  31.1 1.0 fusion.113
  32.1 3.4 %multiply_convert_fusion = bf16[2,4,256,32,32]{2,4,3,1,0:T(8,128)(2,1)} fusion(f32[2,4,256,32]{2,3,0,1:T(8,128)S(1)} %get-tuple-element.42), kind=kLoop, calls=%fused_computation.11 | loop fusion | flops 6291456 | bytes 4456448 | tf_op jit(solution)/shard_map/convert_element_type | solution.py:119
  35.5 5.6 %all-to-all-done = f32[32,40,128]{2,1,0:T(8,128)S(1)} async-done(((f32[32,40,128]{2,1,0:T(8,128)}), f32[32,40,128]{2,1,0:T(8,128)S(1)}, u32[]{:S(2)}, u32[]{:S(2)}) %all-to-all-start) | async-done | bytes 655392 | tf_op jit(solution)/shard_map/all_to_all | solution.py:71
  41.5 1.2 copy.247
  42.8 4.5 %all-to-all-start.1 = ((f32[32,40,128]{2,1,0:T(8,128)}), f32[32,40,128]{2,1,0:T(8,128)S(1)}, u32[]{:S(2)}, u32[]{:S(2)}) async-start(f32[32,40,128]{2,1,0:T(8,128)} %copy.247), calls=%async_computation.1 | async-start | bytes 1310720 | tf_op jit(solution)/shard_map/all_to_all | solution.py:76
  47.2 4.6 %select_convert_fusion.1 = (bf16[2,4,256,256]{2,3,1,0:T(8,128)(2,1)}, f32[2,4,256,256]{2,3,1,0:T(8,128)S(1)}) fusion(pred[256,256]{0,1:T(8,128)(4,1)S(1)} %iota_compare_fusion.1, bf16[2,4,256,1024]{2,3,1,0:T(8,128)(2,1)} %bitcast.228, bf16[2,256,1024,1]{1,2,3,0:T(8,128)(2,1)S(1)} %bitcast.239), kind=kOutput, calls=%fused_computation.23 | convolution fusion | flops 1074266112 | bytes 8454144 | tf_op jit(solution)/shard_map/hmif,hjf->hmij/dot_general | solution.py:172
  52.6 7.6 %all-to-all-done.1 = f32[32,40,128]{2,1,0:T(8,128)S(1)} async-done(((f32[32,40,128]{2,1,0:T(8,128)}), f32[32,40,128]{2,1,0:T(8,128)S(1)}, u32[]{:S(2)}, u32[]{:S(2)}) %all-to-all-start.1) | async-done | bytes 655392 | tf_op jit(solution)/shard_map/all_to_all | solution.py:76
  60.2 0.8 slice.84
  61.0 1.3 copy.253
  62.5 2.8 %gather_fusion.2 = f32[1024,2]{1,0:T(8,128)S(1)} fusion(f32[2,528]{0,1:T(8,128)S(1)} %copy.366, s32[1024]{0:T(1024)S(1)} %copy-done.32), kind=kCustom, calls=%fused_computation.2.clone | custom fusion | bytes 20480 | tf_op jit(solution)/shard_map/jit(_take)/gather | solution.py:139
  65.4 4.0 %gather_fusion.3 = f32[1024,2,128]{2,1,0:T(2,128)S(1)} fusion(f32[2,528,128]{2,0,1:T(2,128)S(1)} %copy.253, s32[1024]{0:T(1024)} %broadcast_clamp_fusion), kind=kCustom, calls=%fused_computation.3.clone | custom fusion | bytes 2101248 | tf_op jit(solution)/shard_map/jit(_take)/gather | solution.py:139
  70.0 3.0 %fusion.116 = f32[2,1,4,256]{3,1,2,0:T(1,128)S(1)} fusion(bf16[2,4,256,1024]{2,3,1,0:T(8,128)(2,1)} %bitcast.229, bf16[2,1024,1,1]{1,2,3,0:T(2,128)(2,1)S(1)} %copy.301), kind=kOutput, calls=%fused_computation.181 | convolution fusion | flops 4194304 | bytes 4206592 | tf_op jit(solution)/shard_map/hmif,hf->hmi/dot_general | solution.py:36
  74.1 2.8 %fusion = f32[2,4,256,128]{3,2,0,1:T(8,128)} fusion(bf16[2,4,256,1024]{2,3,1,0:T(8,128)(2,1)S(1)} %bitcast.233, f32[1024,2,128]{2,1,0:T(2,128)S(1)} %gather_fusion.3), kind=kOutput, calls=%fused_computation.12 | convolution fusion | flops 537657344 | bytes 6291456 | tf_op jit(solution)/shard_map/hmif,hfd->hmid/dot_general | solution.py:36
  76.9 1.4 fusion.25
  78.3 4.5 %fusion.34 = f32[2,4,256,1024]{3,2,1,0:T(8,128)} fusion(bf16[2,4,256,128]{3,2,0,1:T(8,128)(2,1)S(1)} %get-tuple-element.23, f32[1024,2,128]{2,1,0:T(2,128)S(1)} %gather_fusion.3), kind=kOutput, calls=%fused_computation.85 | convolution fusion | flops 537657344 | bytes 9961472 | tf_op jit(solution)/shard_map/hmid,hfd->hmif/dot_general | solution.py:50
  82.9 4.5 %fusion.37 = f32[2,4,256,1024]{3,2,1,0:T(8,128)} fusion(bf16[2,4,256,128]{3,2,0,1:T(8,128)(2,1)S(1)} %get-tuple-element.23, f32[1024,2,128]{2,1,0:T(2,128)S(1)} %gather_fusion.3), kind=kOutput, calls=%fused_computation.89 | convolution fusion | flops 537395200 | bytes 9961472 | tf_op jit(solution)/shard_map/hmid,hfd->hmif/dot_general | solution.py:49
  88.2 4.1 %fusion.8 = f32[2,4,256,128]{3,2,0,1:T(8,128)S(1)} fusion(f32[2,4,256,128]{3,2,0,1:T(8,128)} %fusion, bf16[2,4,256,1024]{2,3,1,0:T(8,128)(2,1)} %bitcast.230, f32[1024,2,128]{2,1,0:T(2,128)S(1)} %gather_fusion.3), kind=kOutput, calls=%fused_computation.45 | convolution fusion | flops 537657344 | bytes 7340032 | tf_op jit(solution)/shard_map/hmif,hfd->hmid/dot_general | solution.py:36
  92.3 2.2 %fusion.12 = f32[2,4,256]{2,0,1:T(2,128)S(1)} fusion(f32[2,4,256,128]{3,2,0,1:T(8,128)S(1)} %fusion.8, bf16[2,4,256,256]{2,3,1,0:T(8,128)(2,1)S(1)} %copy-done.22, f32[2,4,256]{2,0,1:T(2,128)S(1)} %copy.249, bf16[256,2,128]{2,1,0:T(2,128)(2,1)S(1)} %constant_dynamic-slice_fusion, bf16[2,256,4,2,128]{4,1,3,2,0:T(8,128)(2,1)} %copy-done.7), kind=kOutput, calls=%fused_computation.47 | convolution fusion | flops 135788544 | bytes 2768896 | tf_op jit(solution)/shard_map/hmij,hjd->hmid/dot_general | solution.py:176
  94.6 1.8 fusion.97
  97.0 1.2 fusion.95
  98.7 0.9 bitcast_add_fusion.1
  99.5 2.7 %gather_fusion.5 = f32[528,2]{1,0:T(8,128)S(1)} fusion(f32[2,1024]{0,1:T(8,128)} %bitcast_add_fusion.1, s32[1024]{0:T(1024)S(1)} %copy-done.35), kind=kCustom, calls=%fused_computation.5.clone | custom fusion | bytes 10560 | tf_op jit(solution)/shard_map/jit(_take)/gather | solution.py:137
  103.0 3.5 %convolution_bitcast_fusion = f32[2,1024,128]{2,1,0:T(8,128)S(1)} fusion(bf16[2,4,256,1024]{2,3,1,0:T(8,128)(2,1)} %bitcast.231, bf16[2,4,256,128]{3,2,0,1:T(8,128)(2,1)} %get-tuple-element.24), kind=kOutput, calls=%fused_computation.39 | convolution fusion | flops 536870912 | bytes 5767168 | tf_op jit(solution)/shard_map/hmif,hmid->hfd/dot_general | solution.py:184
  106.6 1.4 select_convert_fusion
  108.0 1.8 copy.280
  109.8 3.6 %gather_fusion.4 = f32[528,2,128]{2,1,0:T(2,128)} fusion(f32[2,1024,128]{2,0,1:T(2,128)} %copy.280, s32[1024]{0:T(1024)S(1)} %copy-done.35), kind=kCustom, calls=%fused_computation.4.clone | custom fusion | bytes 1083456 | tf_op jit(solution)/shard_map/jit(_take)/gather | solution.py:137
  113.4 1.1 copy.281
  114.5 0.9 select_maximum_fusion
  115.4 13.4 %all-to-all-start.2 = ((f32[32,40,128]{2,1,0:T(8,128)}), f32[32,40,128]{2,1,0:T(8,128)}, u32[]{:S(2)}, u32[]{:S(2)}) async-start(f32[32,40,128]{2,1,0:T(8,128)} %bitcast.244), calls=%async_computation.2 | async-start | bytes 1310720 | tf_op jit(solution)/shard_map/all_to_all | solution.py:71
  128.8 2.8 %fusion.117 = f32[2,4,256,1024]{3,2,1,0:T(8,128)S(1)} fusion(bf16[2,4,256,256]{2,3,1,0:T(8,128)(2,1)} %select_convert_fusion, bf16[2,256,1024,1]{1,2,3,0:T(8,128)(2,1)S(1)} %bitcast.240), kind=kOutput, calls=%fused_computation.182 | convolution fusion | flops 1073741824 | bytes 10485760 | tf_op jit(solution)/shard_map/hmij,hjf->hmif/dot_general | solution.py:195
  131.6 9.4 %multiply_add_fusion = f32[2,4,256,1024]{3,2,1,0:T(8,128)} fusion(f32[2,4,256,1024]{3,2,1,0:T(8,128)S(1)} %fusion.117, f32[2,4,256,1024]{3,2,1,0:T(8,128)} %fusion.37, f32[2,4,256,1024]{3,2,1,0:T(8,128)} %fusion.34, f32[2,1024]{1,0:T(2,128)S(1)} %copy-done.36, f32[2,4,256]{2,1,0:T(4,128)S(1)} %copy-done.39, bf16[2,4,256,128]{3,2,0,1:T(8,128)(2,1)S(1)} %copy-done.14, ...), kind=kOutput, calls=%fused_computation.10 | convolution fusion | flops 547880960 | bytes 35143680 | tf_op jit(solution)/shard_map/hmid,hfd->hmif/dot_general | solution.py:51
  141.0 8.7 %copy.362 = f32[2,4,256,1024]{2,3,1,0:T(8,128)} copy(f32[2,4,256,1024]{3,2,1,0:T(8,128)} %multiply_add_fusion) | data formatting | bytes 16777216
  149.8 5.4 %multiply_reduce_fusion.1 = f32[2,4,256,32]{2,3,1,0:T(8,128)S(1)} fusion(f32[2,4,256,1024]{2,3,1,0:T(8,128)} %copy.362, f32[2,4,256,32]{2,3,0,1:T(8,128)S(1)} %get-tuple-element.42), kind=kLoop, calls=%fused_computation.9 | loop fusion | flops 4128768 | bytes 8912896
  155.5 1.4 multiply_reduce_fusion
  157.0 1.0 fusion.55
  158.0 1.0 fusion.13
  159.1 0.8 collective-permute-start.5
  160.1 2.3 %collective-permute-start.3 = (bf16[256,1,2,128]{3,0,1,2:T(8,128)(2,1)S(1)}, bf16[256,1,2,128]{3,0,1,2:T(8,128)(2,1)S(1)}, u32[]{:S(2)}, u32[]{:S(2)}) collective-permute-start(bf16[256,1,2,128]{3,0,1,2:T(8,128)(2,1)S(1)} %get-tuple-element.31), channel_id=1, source_target_pairs={{0,3},{1,0},{2,1},{3,2},{4,7},{5,4},{6,5},{7,6},{8,11},{9,8},{10,9... | collective-permute-start | bytes 393224 | tf_op jit(solution)/shard_map/ppermute | solution.py:103
  162.7 1.1 convolution_bitcast_fusion.1
  163.9 2.6 %fusion.118 = f32[2,256,1024,1]{2,1,3,0:T(8,128)} fusion(bf16[2,4,256,256]{2,3,1,0:T(8,128)(2,1)S(1)} %copy-done.9, bf16[2,4,256,1024]{2,3,1,0:T(8,128)(2,1)S(1)} %bitcast.236), kind=kOutput, calls=%fused_computation.183 | convolution fusion | flops 1073741824 | bytes 7340032 | tf_op jit(solution)/shard_map/hmij,hmif->hjf/dot_general | solution.py:203
  166.5 1.6 fusion.29
  168.1 1.2 copy.284
  169.3 8.3 %all-to-all-start.3 = ((f32[32,40,128]{2,1,0:T(8,128)}), f32[32,40,128]{2,1,0:T(8,128)S(1)}, u32[]{:S(2)}, u32[]{:S(2)}) async-start(f32[32,40,128]{2,1,0:T(8,128)} %copy.284), calls=%async_computation.3 | async-start | bytes 1310720 | tf_op jit(solution)/shard_map/all_to_all | solution.py:76
  178.3 12.2 %all-to-all-done.3 = f32[32,40,128]{2,1,0:T(8,128)S(1)} async-done(((f32[32,40,128]{2,1,0:T(8,128)}), f32[32,40,128]{2,1,0:T(8,128)S(1)}, u32[]{:S(2)}, u32[]{:S(2)}) %all-to-all-start.3) | async-done | bytes 655392 | tf_op jit(solution)/shard_map/all_to_all | solution.py:76
  190.8 3.6 %gather_fusion.6 = f32[1024,2,128]{2,1,0:T(2,128)S(1)} fusion(f32[2,528,128]{2,0,1:T(2,128)S(1)} %copy.285, s32[1024]{0:T(1024)S(1)} %copy-done.33), kind=kCustom, calls=%fused_computation.7.clone | custom fusion | bytes 2101248 | tf_op jit(solution)/shard_map/jit(_take)/gather | solution.py:139
  194.9 1.8 fusion.58
  196.9 2.8 %gather_fusion.7 = f32[1024,2]{1,0:T(8,128)S(1)} fusion(f32[2,528]{0,1:T(8,128)S(1)} %copy.367, s32[1024]{0:T(1024)S(1)} %copy-done.33), kind=kCustom, calls=%fused_computation.6.clone | custom fusion | bytes 20480 | tf_op jit(solution)/shard_map/jit(_take)/gather | solution.py:139
  199.9 1.6 fusion.21
  201.5 0.8 copy.294
  202.3 3.5 %fusion.4 = f32[2,256,1024]{2,1,0:T(8,128)} fusion(f32[2,256,1024,1]{2,1,3,0:T(8,128)S(1)} %copy-done.6, f32[2,256,1024]{2,1,0:T(8,128)} %fusion.58, f32[2,1024]{1,0:T(2,128)S(1)} %copy.288, f32[1024,2,128]{2,1,0:T(2,128)S(1)} %gather_fusion.6, bf16[256,2,128]{2,1,0:T(2,128)(2,1)S(1)} %constant_dynamic-slice_fusion), kind=kOutput, calls=%fused_computation.17 | convolution fusion | flops 136577024 | bytes 7479296 | tf_op jit(solution)/shard_map/htd,hfd->htf/dot_general | solution.py:36
  205.8 2.0 copy.363
  209.2 0.8 copy.293
  (150 shorter events, 14.1 us)
Async XLA Ops:
  0.6 9.0 %copy-start = (bf16[256,8,128]{2,1,0:T(8,128)(2,1)S(1)}, bf16[256,8,128]{2,1,0:T(8,128)(2,1)}, u32[]{:S(2)}) copy-start(bf16[256,8,128]{2,1,0:T(8,128)(2,1)} %param.17) | copy-start | bytes 1572868
  0.6 9.0 %copy-start.44 = (s32[528]{0:T(1024)S(1)}, s32[528]{0:T(1024)}, u32[]{:S(2)}) copy-start(s32[528]{0:T(1024)} %constant.194) | copy-start | bytes 6340
  0.7 9.0 %copy-start.42 = (s32[2,128,32]{1,2,0:T(8,128)S(1)}, s32[2,128,32]{1,2,0:T(8,128)}, u32[]{:S(2)}) copy-start(s32[2,128,32]{1,2,0:T(8,128)} %param.19) | copy-start | bytes 98308
  3.1 25.7 %collective-permute-start = (bf16[2,256,1,2,128]{4,1,3,2,0:T(8,128)(2,1)}, bf16[2,256,1,2,128]{4,1,3,2,0:T(8,128)(2,1)}, u32[]{:S(2)}, u32[]{:S(2)}) collective-permute-start(bf16[2,256,1,2,128]{4,1,3,2,0:T(8,128)(2,1)} %get-tuple-element.26), channel_id=1, source_target_pairs={{0,1},{1,2},{2,3},{3,0},{4,5},{5,6},{6,7},{7,4},{8,9},{9,10},{10,1... | collective-permute-start | bytes 786440 | tf_op jit(solution)/shard_map/ppermute | solution.py:90
  5.6 23.2 %collective-permute-start.1 = (bf16[2,256,1,2,128]{4,1,3,2,0:T(8,128)(2,1)}, bf16[2,256,1,2,128]{4,1,3,2,0:T(8,128)(2,1)}, u32[]{:S(2)}, u32[]{:S(2)}) collective-permute-start(bf16[2,256,1,2,128]{4,1,3,2,0:T(8,128)(2,1)} %get-tuple-element.27), channel_id=1, source_target_pairs={{0,2},{1,3},{2,0},{3,1},{4,6},{5,7},{6,4},{7,5},{8,10},{9,11},{10,... | collective-permute-start | bytes 786440 | tf_op jit(solution)/shard_map/ppermute | solution.py:90
  8.9 19.9 %collective-permute-start.2 = (bf16[2,256,1,2,128]{4,1,3,2,0:T(8,128)(2,1)}, bf16[2,256,1,2,128]{4,1,3,2,0:T(8,128)(2,1)}, u32[]{:S(2)}, u32[]{:S(2)}) collective-permute-start(bf16[2,256,1,2,128]{4,1,3,2,0:T(8,128)(2,1)} %get-tuple-element.28), channel_id=1, source_target_pairs={{0,3},{1,0},{2,1},{3,2},{4,7},{5,4},{6,5},{7,6},{8,11},{9,8},{10,9... | collective-permute-start | bytes 786440 | tf_op jit(solution)/shard_map/ppermute | solution.py:90
  9.6 4.7 %copy-start.34 = (s32[1024]{0:T(1024)}, s32[1024]{0:T(1024)S(1)}, u32[]{:S(2)}) copy-start(s32[1024]{0:T(1024)S(1)} %pad_clamp_fusion) | copy-start | bytes 12292
  9.6 2.3 %copy-start.27 = (bf16[2,128,32]{1,2,0:T(8,128)(2,1)}, bf16[2,128,32]{1,2,0:T(8,128)(2,1)S(1)}, u32[]{:S(2)}) copy-start(bf16[2,128,32]{1,2,0:T(8,128)(2,1)S(1)} %add_convert_fusion) | copy-start | bytes 49156
  11.1 7.5 %copy-start.24 = (f32[2,256,32]{1,2,0:T(8,128)}, f32[2,256,32]{1,2,0:T(8,128)S(1)}, u32[]{:S(2)}) copy-start(f32[2,256,32]{1,2,0:T(8,128)S(1)} %fusion.22) | copy-start | bytes 196612
  12.0 6.7 %copy-start.17 = (f32[2,256,32]{1,2,0:T(8,128)}, f32[2,256,32]{1,2,0:T(8,128)S(1)}, u32[]{:S(2)}) copy-start(f32[2,256,32]{1,2,0:T(8,128)S(1)} %get-tuple-element.44) | copy-start | bytes 196612
  14.4 13.8 %copy-start.43 = (s32[1024]{0:T(1024)S(1)}, s32[1024]{0:T(1024)}, u32[]{:S(2)}) copy-start(s32[1024]{0:T(1024)} %constant.196) | copy-start | bytes 12292
  14.8 15.3 %copy-start.28 = (bf16[2,128,32]{1,2,0:T(8,128)(2,1)S(1)}, bf16[2,128,32]{1,2,0:T(8,128)(2,1)}, u32[]{:S(2)}) copy-start(bf16[2,128,32]{1,2,0:T(8,128)(2,1)} %copy-done.27) | copy-start | bytes 49156
  19.5 21.5 %all-to-all-start = ((f32[32,40,128]{2,1,0:T(8,128)}), f32[32,40,128]{2,1,0:T(8,128)S(1)}, u32[]{:S(2)}, u32[]{:S(2)}) async-start(f32[32,40,128]{2,1,0:T(8,128)} %bitcast.28), calls=%async_computation | async-start | bytes 1310720 | tf_op jit(solution)/shard_map/all_to_all | solution.py:71
  28.2 23.6 %copy-start.19 = (pred[256,256]{0,1:T(8,128)(4,1)}, pred[256,256]{0,1:T(8,128)(4,1)S(1)}, u32[]{:S(2)}) copy-start(pred[256,256]{0,1:T(8,128)(4,1)S(1)} %iota_compare_fusion.1) | copy-start | bytes 196612
  30.1 1.0 copy-start.7
  31.1 11.7 %copy-start.10 = (f32[2,4,256,32]{2,3,0,1:T(8,128)}, f32[2,4,256,32]{2,3,0,1:T(8,128)S(1)}, u32[]{:S(2)}) copy-start(f32[2,4,256,32]{2,3,0,1:T(8,128)S(1)} %fusion.15) | copy-start | bytes 786436
  42.8 17.4 %all-to-all-start.1 = ((f32[32,40,128]{2,1,0:T(8,128)}), f32[32,40,128]{2,1,0:T(8,128)S(1)}, u32[]{:S(2)}, u32[]{:S(2)}) async-start(f32[32,40,128]{2,1,0:T(8,128)} %copy.247), calls=%async_computation.1 | async-start | bytes 1310720 | tf_op jit(solution)/shard_map/all_to_all | solution.py:76
  51.8 10.7 %copy-start.32 = (s32[1024]{0:T(1024)S(1)}, s32[1024]{0:T(1024)}, u32[]{:S(2)}) copy-start(s32[1024]{0:T(1024)} %broadcast_clamp_fusion) | copy-start | bytes 12292
  65.4 8.7 %copy-start.12 = (f32[1024,2]{1,0:T(8,128)}, f32[1024,2]{1,0:T(8,128)S(1)}, u32[]{:S(2)}) copy-start(f32[1024,2]{1,0:T(8,128)S(1)} %gather_fusion.2) | copy-start | bytes 24580
  70.0 3.5 %copy-start.2 = (bf16[2,4,256,32,32]{2,4,3,1,0:T(8,128)(2,1)S(1)}, bf16[2,4,256,32,32]{2,4,3,1,0:T(8,128)(2,1)}, u32[]{:S(2)}) copy-start(bf16[2,4,256,32,32]{2,4,3,1,0:T(8,128)(2,1)} %multiply_convert_fusion) | copy-start | bytes 12582916
  74.1 2.8 %copy-start.41 = (f32[2,4,256]{2,1,0:T(4,128)S(1)}, f32[2,4,256]{2,1,0:T(4,128)}, u32[]{:S(2)}) copy-start(f32[2,4,256]{2,1,0:T(4,128)} %select_reduce_fusion) | copy-start | bytes 24580
  74.1 2.8 %copy-start.8 = (bf16[2,256,4,2,128]{4,1,3,2,0:T(8,128)(2,1)S(1)}, bf16[2,256,4,2,128]{4,1,3,2,0:T(8,128)(2,1)}, u32[]{:S(2)}) copy-start(bf16[2,256,4,2,128]{4,1,3,2,0:T(8,128)(2,1)} %copy-done.7) | copy-start | bytes 3145732
  82.9 4.5 %copy-start.13 = (f32[1024,2]{1,0:T(8,128)S(1)}, f32[1024,2]{1,0:T(8,128)}, u32[]{:S(2)}) copy-start(f32[1024,2]{1,0:T(8,128)} %copy-done.12) | copy-start | bytes 24580
  88.2 4.1 %copy-start.22 = (bf16[2,4,256,256]{2,3,1,0:T(8,128)(2,1)S(1)}, bf16[2,4,256,256]{2,3,1,0:T(8,128)(2,1)}, u32[]{:S(2)}) copy-start(bf16[2,4,256,256]{2,3,1,0:T(8,128)(2,1)} %get-tuple-element.46) | copy-start | bytes 3145732
  92.2 2.3 %copy-start.3 = (bf16[2,4,256,32,32]{2,4,3,1,0:T(8,128)(2,1)S(1)}, bf16[2,4,256,32,32]{2,4,3,1,0:T(8,128)(2,1)}, u32[]{:S(2)}) copy-start(bf16[2,4,256,32,32]{2,4,3,1,0:T(8,128)(2,1)} %multiply_convert_fusion) | copy-start | bytes 12582916
  96.4 2.0 copy-start.37
  96.4 3.1 %copy-start.35 = (s32[1024]{0:T(1024)S(1)}, s32[1024]{0:T(1024)}, u32[]{:S(2)}) copy-start(s32[1024]{0:T(1024)} %copy-done.34) | copy-start | bytes 12292
  98.6 7.9 %copy-start.38 = (f32[2,4,256]{2,1,0:T(4,128)S(1)}, f32[2,4,256]{2,1,0:T(4,128)}, u32[]{:S(2)}) copy-start(f32[2,4,256]{2,1,0:T(4,128)} %copy.262) | copy-start | bytes 24580
  99.5 7.0 %copy-start.15 = (bf16[2,4,256,128]{3,2,0,1:T(8,128)(2,1)S(1)}, bf16[2,4,256,128]{3,2,0,1:T(8,128)(2,1)}, u32[]{:S(2)}) copy-start(bf16[2,4,256,128]{3,2,0,1:T(8,128)(2,1)} %get-tuple-element.24) | copy-start | bytes 1572868
  99.5 7.0 %copy-start.20 = (pred[256,256]{0,1:T(8,128)(4,1)S(1)}, pred[256,256]{0,1:T(8,128)(4,1)}, u32[]{:S(2)}) copy-start(pred[256,256]{0,1:T(8,128)(4,1)} %copy-done.19) | copy-start | bytes 196612
  108.0 6.5 %copy-start.40 = (f32[10,128]{1,0:T(8,128)S(1)}, f32[10,128]{1,0:T(8,128)}, u32[]{:S(2)}) copy-start(f32[10,128]{1,0:T(8,128)} %reshape.103) | copy-start | bytes 15364
  115.4 51.1 %all-to-all-start.2 = ((f32[32,40,128]{2,1,0:T(8,128)}), f32[32,40,128]{2,1,0:T(8,128)}, u32[]{:S(2)}, u32[]{:S(2)}) async-start(f32[32,40,128]{2,1,0:T(8,128)} %bitcast.244), calls=%async_computation.2 | async-start | bytes 1310720 | tf_op jit(solution)/shard_map/all_to_all | solution.py:71
  128.8 2.8 %copy-start.14 = (bf16[2,4,256,128]{3,2,0,1:T(8,128)(2,1)S(1)}, bf16[2,4,256,128]{3,2,0,1:T(8,128)(2,1)}, u32[]{:S(2)}) copy-start(bf16[2,4,256,128]{3,2,0,1:T(8,128)(2,1)} %get-tuple-element.22) | copy-start | bytes 1572868
  128.8 2.8 %copy-start.36 = (f32[2,1024]{1,0:T(2,128)S(1)}, f32[2,1024]{1,0:T(2,128)}, u32[]{:S(2)}) copy-start(f32[2,1024]{1,0:T(2,128)} %copy.270) | copy-start | bytes 24580
  128.8 2.8 %copy-start.39 = (f32[2,4,256]{2,1,0:T(4,128)S(1)}, f32[2,4,256]{2,1,0:T(4,128)}, u32[]{:S(2)}) copy-start(f32[2,4,256]{2,1,0:T(4,128)} %copy.262) | copy-start | bytes 24580
  149.8 5.8 %copy-start.5 = (f32[2,4,256,1024]{2,3,1,0:T(8,128)S(1)}, f32[2,4,256,1024]{2,3,1,0:T(8,128)}, u32[]{:S(2)}) copy-start(f32[2,4,256,1024]{2,3,1,0:T(8,128)} %copy.362) | copy-start | bytes 25165828
  155.5 1.4 copy-start.11
  155.5 1.4 copy-start.21
  155.5 1.5 copy-start.29
  156.9 5.8 %copy-start.16 = (bf16[2,4,256,128]{3,2,0,1:T(8,128)(2,1)S(1)}, bf16[2,4,256,128]{3,2,0,1:T(8,128)(2,1)}, u32[]{:S(2)}) copy-start(bf16[2,4,256,128]{3,2,0,1:T(8,128)(2,1)} %get-tuple-element.24) | copy-start | bytes 1572868
  156.9 5.8 %copy-start.23 = (bf16[2,4,256,256]{2,3,1,0:T(8,128)(2,1)S(1)}, bf16[2,4,256,256]{2,3,1,0:T(8,128)(2,1)}, u32[]{:S(2)}) copy-start(bf16[2,4,256,256]{2,3,1,0:T(8,128)(2,1)} %get-tuple-element.46) | copy-start | bytes 3145732
  156.9 6.9 %copy-start.4 = (bf16[2,4,256,32,32]{2,4,3,1,0:T(8,128)(2,1)S(1)}, bf16[2,4,256,32,32]{2,4,3,1,0:T(8,128)(2,1)}, u32[]{:S(2)}) copy-start(bf16[2,4,256,32,32]{2,4,3,1,0:T(8,128)(2,1)} %multiply_convert_fusion) | copy-start | bytes 12582916
  156.9 6.9 %copy-start.9 = (bf16[2,4,256,256]{2,3,1,0:T(8,128)(2,1)S(1)}, bf16[2,4,256,256]{2,3,1,0:T(8,128)(2,1)}, u32[]{:S(2)}) copy-start(bf16[2,4,256,256]{2,3,1,0:T(8,128)(2,1)} %select_convert_fusion) | copy-start | bytes 3145732
  159.1 19.0 %collective-permute-start.5 = (bf16[256,1,2,128]{3,0,1,2:T(8,128)(2,1)S(1)}, bf16[256,1,2,128]{3,0,1,2:T(8,128)(2,1)S(1)}, u32[]{:S(2)}, u32[]{:S(2)}) collective-permute-start(bf16[256,1,2,128]{3,0,1,2:T(8,128)(2,1)S(1)} %get-tuple-element.29), channel_id=1, source_target_pairs={{0,1},{1,2},{2,3},{3,0},{4,5},{5,6},{6,7},{7,4},{8,9},{9,10},{10,1... | collective-permute-start | bytes 393224 | tf_op jit(solution)/shard_map/ppermute | solution.py:103
  159.9 17.9 %collective-permute-start.4 = (bf16[256,1,2,128]{3,0,1,2:T(8,128)(2,1)S(1)}, bf16[256,1,2,128]{3,0,1,2:T(8,128)(2,1)S(1)}, u32[]{:S(2)}, u32[]{:S(2)}) collective-permute-start(bf16[256,1,2,128]{3,0,1,2:T(8,128)(2,1)S(1)} %get-tuple-element.30), channel_id=1, source_target_pairs={{0,2},{1,3},{2,0},{3,1},{4,6},{5,7},{6,4},{7,5},{8,10},{9,11},{10,... | collective-permute-start | bytes 393224 | tf_op jit(solution)/shard_map/ppermute | solution.py:103
  160.1 17.5 %collective-permute-start.3 = (bf16[256,1,2,128]{3,0,1,2:T(8,128)(2,1)S(1)}, bf16[256,1,2,128]{3,0,1,2:T(8,128)(2,1)S(1)}, u32[]{:S(2)}, u32[]{:S(2)}) collective-permute-start(bf16[256,1,2,128]{3,0,1,2:T(8,128)(2,1)S(1)} %get-tuple-element.31), channel_id=1, source_target_pairs={{0,3},{1,0},{2,1},{3,2},{4,7},{5,4},{6,5},{7,6},{8,11},{9,8},{10,9... | collective-permute-start | bytes 393224 | tf_op jit(solution)/shard_map/ppermute | solution.py:103
  166.5 24.3 %copy-start.33 = (s32[1024]{0:T(1024)S(1)}, s32[1024]{0:T(1024)}, u32[]{:S(2)}) copy-start(s32[1024]{0:T(1024)} %broadcast_clamp_fusion) | copy-start | bytes 12292
  169.3 21.2 %all-to-all-start.3 = ((f32[32,40,128]{2,1,0:T(8,128)}), f32[32,40,128]{2,1,0:T(8,128)S(1)}, u32[]{:S(2)}, u32[]{:S(2)}) async-start(f32[32,40,128]{2,1,0:T(8,128)} %copy.284), calls=%async_computation.3 | async-start | bytes 1310720 | tf_op jit(solution)/shard_map/all_to_all | solution.py:76
  178.3 12.5 %copy-start.26 = (bf16[256,1,8,128]{3,2,1,0:T(8,128)(2,1)}, bf16[256,1,8,128]{3,2,1,0:T(8,128)(2,1)S(1)}, u32[]{:S(2)}) copy-start(bf16[256,1,8,128]{3,2,1,0:T(8,128)(2,1)S(1)} %copy_dynamic-update-slice_fusion) | copy-start | bytes 1572868
  199.9 2.4 %copy-start.6 = (f32[2,256,1024,1]{2,1,3,0:T(8,128)S(1)}, f32[2,256,1024,1]{2,1,3,0:T(8,128)}, u32[]{:S(2)}) copy-start(f32[2,256,1024,1]{2,1,3,0:T(8,128)} %fusion.118) | copy-start | bytes 6291460
  202.3 5.5 %copy-start.18 = (f32[2,256,32]{1,2,0:T(8,128)S(1)}, f32[2,256,32]{1,2,0:T(8,128)}, u32[]{:S(2)}) copy-start(f32[2,256,32]{1,2,0:T(8,128)} %copy-done.17) | copy-start | bytes 196612
  202.3 7.8 %copy-start.1 = (bf16[256,8,128]{2,1,0:T(8,128)(2,1)S(1)}, bf16[256,8,128]{2,1,0:T(8,128)(2,1)}, u32[]{:S(2)}) copy-start(bf16[256,8,128]{2,1,0:T(8,128)(2,1)} %param.17) | copy-start | bytes 1572868
  205.8 2.6 %copy-start.25 = (f32[2,256,32]{1,2,0:T(8,128)S(1)}, f32[2,256,32]{1,2,0:T(8,128)}, u32[]{:S(2)}) copy-start(f32[2,256,32]{1,2,0:T(8,128)} %copy-done.24) | copy-start | bytes 196612
  205.8 2.6 %copy-start.30 = (bf16[2,128,32]{1,2,0:T(8,128)(2,1)S(1)}, bf16[2,128,32]{1,2,0:T(8,128)(2,1)}, u32[]{:S(2)}) copy-start(bf16[2,128,32]{1,2,0:T(8,128)(2,1)} %copy-done.27) | copy-start | bytes 49156
  205.8 3.0 %copy-start.31 = (f32[2,256,32]{1,2,0:T(8,128)S(1)}, f32[2,256,32]{1,2,0:T(8,128)}, u32[]{:S(2)}) copy-start(f32[2,256,32]{1,2,0:T(8,128)} %get-tuple-element.45) | copy-start | bytes 196612

commit v6 on v3

--- a/solution.py
+++ b/solution.py
@@ -42,18 +42,13 @@
     return dot_parts(pattern, wide, exact, 2, wide_first=False)
 
 
-def dot_split3(pattern, first, second):
-    fh, fl = split_parts(first, 2)
-    sh, sl = split_parts(second, 2)
-    return (
-        jnp.einsum(pattern, fh, sh, preferred_element_type=f32)
-        + jnp.einsum(pattern, fh, sl, preferred_element_type=f32)
-        + jnp.einsum(pattern, fl, sh, preferred_element_type=f32)
-    )
-
-
-def take_exact(x, select):
-    return dot_parts("...a,ak->...k", x, select, 3)
+def take_pair(x, take_a, take_b):
+    lhs = jnp.concatenate(split_parts(x, 3), axis=-1)
+    both = jnp.concatenate([take_a, take_b], axis=1)
+    rhs = jnp.concatenate([both, both, both], axis=0)
+    out = jnp.einsum("...k,kn->...n", lhs, rhs, preferred_element_type=f32)
+    size = take_a.shape[1]
+    return out[..., :size], out[..., size:]
 
 
 def ctx_scan(state, total, reverse):
@@ -119,16 +114,14 @@
 def tri_features(sketch_one, sketch_two, take_a, take_b):
     width = sketch_one.shape[-1]
     sketch = sketch_one * sketch_two
-    first = take_exact(sketch, take_a)
-    second = take_exact(sketch, take_b)
+    first, second = take_pair(sketch, take_a, take_b)
     return (first * second * (1.0 / width)).astype(bf16)
 
 
 def tri_feature_back(cotangent, sketch_one, sketch_two, proj_wide, take_a, take_b, off):
     width = sketch_one.shape[-1]
     sketch = sketch_one * sketch_two
-    first = take_exact(sketch, take_a)
-    second = take_exact(sketch, take_b)
+    first, second = take_pair(sketch, take_a, take_b)
     spread = jnp.concatenate([cotangent * second, cotangent * first * off], axis=-1)
     gather = jnp.concatenate([take_a.T, take_b.T], axis=0).astype(bf16)
     dsketch = dot_parts("...k,ka->...a", spread, gather, 2) * (2.0 / width)
@@ -193,10 +186,17 @@
         + correction[..., None],
         0.0,
     ).astype(bf16)
-    grad_qfeat = (
-        jnp.einsum("hmij,hjf->hmif", dscores, key_feat, preferred_element_type=f32)
-        + dot_split3("hmid,hfd->hmif", grad_rows, state_in)
-        + correction[..., None] * total_in[:, None, None, :]
+    grad_hi, grad_lo = split_parts(grad_rows, 2)
+    state_hi, state_lo = split_parts(state_in.transpose(0, 2, 1), 2)
+    corr_hi, corr_lo = split_parts(correction[..., None], 2)
+    total_hi, total_lo = split_parts(total_in[:, None, :], 2)
+    grad_qfeat = jnp.einsum(
+        "hmik,hkf->hmif",
+        jnp.concatenate([dscores, grad_hi, grad_hi, grad_lo, corr_hi, corr_hi, corr_lo], axis=-1),
+        jnp.concatenate(
+            [key_feat, state_hi, state_lo, state_hi, total_hi, total_lo, total_hi], axis=1
+        ),
+        preferred_element_type=f32,
     )
     query_grad = tri_feature_back(
         grad_qfeat, query_one, query_two, proj_wide, take_a, take_b, off
@@ -206,9 +206,15 @@
 
     grad_kfeat = jnp.einsum("hmij,hmif->hjf", dscores, query_feat, preferred_element_type=f32)
     grad_value = jnp.einsum("hmij,hmid->hjd", weights, grad_low, preferred_element_type=f32)
+    merged_hi, merged_lo = split_parts(merged_state.transpose(0, 2, 1), 2)
     kfeat_total = (
         grad_kfeat
-        + dot_split("htd,hfd->htf", value_heads, merged_state)
+        + jnp.einsum(
+            "htk,hkf->htf",
+            jnp.concatenate([value_heads, value_heads], axis=-1),
+            jnp.concatenate([merged_hi, merged_lo], axis=1),
+            preferred_element_type=f32,
+        )
         + merged_total[:, None, :]
     )
     value_total = grad_value + dot_split("htf,hfd->htd", key_wfeat, merged_state)

time: 140 us -> 149 us (1.064)
  matrix products: 64.4 us -> 39 us
  local copies, waits for them, and re-layouts: 16.2 us -> 38 us
  other arithmetic: 6.02 us -> 13.8 us
  waiting for transfers between devices: 14.2 us -> 20.3 us
  starting transfers between devices: 36.8 us -> 35.3 us
    dot_general x26 -> x12, matrix products: 34.1 us -> 9.62 us  [dot_parts(): term = jnp.einsum(pattern, *args, preferred_element_type=f32)]
    concatenate x0 -> x2, local copies, waits for them, and re-layouts: none -> 15.6 us  [the longest x1 11.8 us: body(): jnp.concatenate([dscores, grad_hi, grad_hi, grad_lo, corr_hi, corr_hi, co...]
    convert_element_type x0 -> x4, local copies, waits for them, and re-layouts: none -> 5.09 us  [the longest x2 2.95 us: split_parts(): parts.append(rest.astype(bf16))]
    mul x0 -> x1, other arithmetic: none -> 4.22 us  [body(): query_wfeat = query_feat * weight]
    all_to_all x2, waiting for transfers between devices: 12.8 us -> 16 us  [ctx_scan(): lax.all_to_all(summed, 'ctx', 0, 0, tiled=True).reshape(n * per, width)]
    all_to_all x2, waiting for transfers between devices: 1.43 us -> 4.24 us  [ctx_scan(): got = lax.all_to_all(flat.reshape(n, per, width), 'ctx', 0, 0, tiled=True)]
    convert_element_type x1 -> x3, other arithmetic: 1.34 us -> 3.29 us  [split_parts(): parts.append(rest.astype(bf16))]
    unnamed x68 -> x61, local copies, waits for them, and re-layouts: 2.96 us -> 4.89 us
  transfers between devices with their start and end apart: 10 -> 10, of which waited for: 3 -> 3; matrix products, arithmetic and copies ran while one was open for 38% -> 42% of each run, Pallas kernels for 0% -> 0%
where the time goes in v6:
time: 149 us; the launch traced here: 148 us
  matrix products  39 us (26%)
  local copies, waits for them, and re-layouts  38 us (26%)
  starting transfers between devices  35.3 us (24%)
  waiting for transfers between devices  20.3 us (14%)
  other arithmetic  13.8 us (9%)
    all_to_all x2, waiting for transfers between devices, ctx_scan(): lax.all_to_all(summed, 'ctx', 0, 0, tiled=True).reshape(n * per, width)  16 us
    all_to_all x2, starting transfers between devices, ctx_scan(): got = lax.all_to_all(flat.reshape(n, per, width), 'ctx', 0, 0, tiled=True)  13.3 us
    all_to_all x2, starting transfers between devices, ctx_scan(): lax.all_to_all(summed, 'ctx', 0, 0, tiled=True).reshape(n * per, width)  12.8 us
    concatenate x1, local copies, waits for them, and re-layouts, body(): jnp.concatenate([dscores, grad_hi, grad_hi, grad_lo, corr_hi, corr_hi, co...  11.8 us
    dot_general x12, matrix products, dot_parts(): term = jnp.einsum(pattern, *args, preferred_element_type=f32)  9.62 us
    dot_general x1, matrix products, body(): jnp.einsum('hmik,hkf->hmif', jnp.concatenate([dscores, grad_hi, grad_hi,...  6.83 us
    ppermute x3, starting transfers between devices, head_exchange(): lax.ppermute(piece, 'head', [(j, (j + k) % count) for j in range(count)])  6.57 us
    dot_general x2, matrix products, take_pair(): out = jnp.einsum('...k,kn->...n', lhs, rhs, preferred_element_type=f32)  5.2 us
  transfers between devices with their start and end apart: 10, of which 3 were waited for; matrix products, arithmetic and copies ran while one was open for 42% of the time, Pallas kernels for 0%

profile of v6, /device:TPU:1, one launch (start us, length us, event | category | flops | bytes accessed | tf_op | source)
XLA Modules:
  0.0 147.6 jit_solution(14454803908674853649)
XLA Ops:
  0.7 1.4 copy_bitcast_fusion
  2.3 2.5 %collective-permute-start = (bf16[2,256,1,2,128]{4,1,3,2,0:T(8,128)(2,1)S(1)}, bf16[2,256,1,2,128]{4,1,3,2,0:T(8,128)(2,1)S(1)}, u32[]{:S(2)}, u32[]{:S(2)}) collective-permute-start(bf16[2,256,1,2,128]{4,1,3,2,0:T(8,128)(2,1)S(1)} %get-tuple-element.29), channel_id=1, source_target_pairs={{0,1},{1,2},{2,3},{3,0},{4,5},{5,6},{6,7},{7,4},{8,9},{9,10},{10,1... | collective-permute-start | bytes 786440 | tf_op jit(solution)/shard_map/ppermute | solution.py:89
  4.8 3.3 %collective-permute-start.1 = (bf16[2,256,1,2,128]{4,1,3,2,0:T(8,128)(2,1)S(1)}, bf16[2,256,1,2,128]{4,1,3,2,0:T(8,128)(2,1)}, u32[]{:S(2)}, u32[]{:S(2)}) collective-permute-start(bf16[2,256,1,2,128]{4,1,3,2,0:T(8,128)(2,1)S(1)} %get-tuple-element.30), channel_id=1, source_target_pairs={{0,2},{1,3},{2,0},{3,1},{4,6},{5,7},{6,4},{7,5},{8,10},{9,11},{10,... | collective-permute-start | bytes 786440 | tf_op jit(solution)/shard_map/ppermute | solution.py:89
  8.1 0.7 collective-permute-start.2
  9.2 0.8 reduce-precision_convert_fusion.12
  10.0 0.5 fusion.90
  10.5 1.4 copy-done.4
  12.1 1.2 constant_dynamic-slice_fusion
  13.6 0.9 select_maximum_fusion.1
  14.5 8.6 %all-to-all-start = ((f32[32,40,128]{2,1,0:T(8,128)}), f32[32,40,128]{2,1,0:T(8,128)S(1)}, u32[]{:S(2)}, u32[]{:S(2)}) async-start(f32[32,40,128]{2,1,0:T(8,128)} %bitcast.25), calls=%async_computation | async-start | bytes 1310720 | tf_op jit(solution)/shard_map/all_to_all | solution.py:70
  23.1 0.7 copy.248
  23.9 1.2 pad_maximum_fusion.2
  25.4 0.7 copy-done.6
  26.1 1.0 reduce-precision_convert_fusion.9
  27.1 4.7 %fusion.64 = f32[2,4,256,1056]{2,3,1,0:T(8,128)} fusion(bf16[96,1056,1,1]{1,0,3,2:T(8,128)(2,1)S(1)} %copy-done.24, bf16[2,4,256,32]{2,3,0,1:T(8,128)(2,1)S(1)} %get-tuple-element.42, bf16[2,4,256,32]{2,3,0,1:T(8,128)(2,1)S(1)} %get-tuple-element.41, bf16[2,4,256,32]{2,3,0,1:T(8,128)(2,1)S(1)} %get-tuple-element.40), kind=kOutput, calls=%fused_computation.114 | convolution fusion | flops 416415744 | bytes 9246720 | tf_op jit(solution)/shard_map/...k,kn->...n/dot_general | solution.py:49
  31.8 4.2 %all-to-all-done = f32[32,40,128]{2,1,0:T(8,128)S(1)} async-done(((f32[32,40,128]{2,1,0:T(8,128)}), f32[32,40,128]{2,1,0:T(8,128)S(1)}, u32[]{:S(2)}, u32[]{:S(2)}) %all-to-all-start) | async-done | bytes 655392 | tf_op jit(solution)/shard_map/all_to_all | solution.py:70
  36.1 0.5 fusion.46
  36.5 1.2 copy.113
  37.8 4.8 %all-to-all-start.1 = ((f32[32,40,128]{2,1,0:T(8,128)}), f32[32,40,128]{2,1,0:T(8,128)}, u32[]{:S(2)}, u32[]{:S(2)}) async-start(f32[32,40,128]{2,1,0:T(8,128)} %copy.113), calls=%async_computation.1 | async-start | bytes 1310720 | tf_op jit(solution)/shard_map/all_to_all | solution.py:75
  42.5 4.2 %broadcast_multiply_fusion = (bf16[2,4,256,528]{2,3,1,0:T(8,128)(2,1)S(1)}, bf16[2,4,256,528]{2,3,1,0:T(8,128)(2,1)S(1)}) fusion(bf16[528]{0:T(1024)(128)(2,1)S(1)} %copy-done.28, f32[2,4,256,1056]{2,3,1,0:T(8,128)} %fusion.64), kind=kLoop, calls=%fused_computation.70 | loop fusion | flops 4325376 | bytes 12977184 | tf_op jit(solution)/shard_map/mul | solution.py:159
  46.8 2.1 %select_convert_fusion.1 = (bf16[2,4,256,256]{2,3,1,0:T(8,128)(2,1)}, f32[2,4,256,256]{2,3,1,0:T(8,128)S(1)}) fusion(pred[256,256]{0,1:T(8,128)(4,1)S(1)} %iota_compare_fusion.1, bf16[2,4,256,528]{2,3,1,0:T(8,128)(2,1)S(1)} %get-tuple-element.17, bf16[2,256,528]{1,2,0:T(8,128)(2,1)S(1)} %get-tuple-element.16), kind=kOutput, calls=%fused_computation.16 | convolution fusion | flops 554172416 | bytes 5914624 | tf_op jit(solution)/shard_map/hmif,hjf->hmij/dot_general | solution.py:167
  49.0 6.6 %all-to-all-done.1 = f32[32,40,128]{2,1,0:T(8,128)} async-done(((f32[32,40,128]{2,1,0:T(8,128)}), f32[32,40,128]{2,1,0:T(8,128)}, u32[]{:S(2)}, u32[]{:S(2)}) %all-to-all-start.1) | async-done | bytes 655392 | tf_op jit(solution)/shard_map/all_to_all | solution.py:75
  55.6 0.7 slice.90
  56.3 1.9 %slice.92 = f32[1056,128]{1,0:T(8,128)} slice(f32[1280,128]{1,0:T(8,128)} %bitcast.26), slice={[0:1056], [0:128]} | slice | bytes 1081344 | tf_op jit(solution)/shard_map/slice | solution.py:76
  58.2 2.2 %fusion.128 = f32[2,1,4,256]{3,1,2,0:T(1,128)S(1)} fusion(bf16[2,4,256,528]{2,3,1,0:T(8,128)(2,1)} %copy-done.2, bf16[2,528,1,1]{1,0,2,3:T(2,128)(2,1)S(1)} %bitcast.197), kind=kOutput, calls=%fused_computation.199 | convolution fusion | flops 2162688 | bytes 2172992 | tf_op jit(solution)/shard_map/hmif,hf->hmi/dot_general | solution.py:36
  60.9 1.2 fusion.6
  62.1 1.2 fusion.15
  63.3 1.4 fusion.41
  64.7 1.1 fusion.20
  65.9 1.4 select_convert_fusion
  67.3 1.5 %fusion.61 = f32[2,528,128,1]{2,1,3,0:T(8,128)} fusion(bf16[2,4,256,528]{2,3,1,0:T(8,128)(2,1)S(1)} %get-tuple-element.18, bf16[2,4,256,128]{3,2,0,1:T(8,128)(2,1)S(1)} %get-tuple-element.27), kind=kOutput, calls=%fused_computation.110 | convolution fusion | flops 276824064 | bytes 3227648 | tf_op jit(solution)/shard_map/hmif,hmid->hfd/dot_general | solution.py:179
  68.8 0.7 fusion.115
  69.5 0.7 fusion.117
  70.2 2.0 %select_maximum_fusion = f32[1280,128]{1,0:T(8,128)} fusion(f32[10,128]{1,0:T(8,128)S(1)} %reshape.91, f32[1056,128]{1,0:T(8,128)} %bitcast.194), kind=kLoop, calls=%fused_computation.86 | loop fusion | flops 655360 | bytes 1201152 | tf_op jit(solution)/shard_map/concatenate | solution.py:58
  72.1 4.7 %all-to-all-start.2 = ((f32[32,40,128]{2,1,0:T(8,128)}), f32[32,40,128]{2,1,0:T(8,128)}, u32[]{:S(2)}, u32[]{:S(2)}) async-start(f32[32,40,128]{2,1,0:T(8,128)} %bitcast.191), calls=%async_computation.2 | async-start | bytes 1310720 | tf_op jit(solution)/shard_map/all_to_all | solution.py:70
  76.9 1.8 %fusion.49 = (bf16[2,128,528]{1,2,0:T(8,128)(2,1)}, bf16[2,128,528]{1,2,0:T(8,128)(2,1)S(1)}) fusion(f32[2,128,528]{1,2,0:T(8,128)} %bitcast.188), kind=kLoop, calls=%fused_computation.94 | loop fusion | flops 540672 | bytes 1081344 | tf_op jit(solution)/shard_map/convert_element_type | solution.py:28
  78.7 0.9 copy.125
  79.6 0.9 copy.126
  80.5 1.2 copy.122
  81.8 2.0 %copy.124 = bf16[2,4,256,128]{2,3,1,0:T(8,128)(2,1)} copy(bf16[2,4,256,128]{3,2,0,1:T(8,128)(2,1)} %get-tuple-element.25) | data formatting | bytes 1048576 | tf_op jit(solution)/shard_map/convert_element_type | solution.py:28
  83.8 3.8 %concatenate.58 = bf16[2,643,528]{1,2,0:T(8,128)(2,1)} concatenate(bf16[2,256,528]{1,2,0:T(8,128)(2,1)S(1)} %get-tuple-element.16, bf16[2,128,528]{1,2,0:T(8,128)(2,1)S(1)} %get-tuple-element.35, bf16[2,128,528]{1,2,0:T(8,128)(2,1)} %get-tuple-element.34, bf16[2,128,528]{1,2,0:T(8,128)(2,1)S(1)} %get-tuple-element.35, bf16[2,1,528]{1,2,0:T(8,128)(2,1)} %copy.125, ...), dimensions={1} | concatenate | bytes 2716032 | tf_op jit(solution)/shard_map/concatenate | solution.py:196
  87.6 11.8 %concatenate.57 = bf16[2,4,256,643]{2,3,1,0:T(8,128)(2,1)} concatenate(bf16[2,4,256,256]{2,3,1,0:T(8,128)(2,1)} %select_convert_fusion, bf16[2,4,256,128]{2,3,1,0:T(8,128)(2,1)S(1)} %copy.122, bf16[2,4,256,128]{2,3,1,0:T(8,128)(2,1)S(1)} %copy.122, bf16[2,4,256,128]{2,3,1,0:T(8,128)(2,1)} %copy.124, bf16[2,4,256,1]{2,3,1,0:T(2,128)(2,1)S(1)} %get-tuple-element.52, ...), dimensions={3} | concatenate | bytes 5267456 | tf_op jit(solution)/shard_map/concatenate | solution.py:195
  99.4 6.8 %slice_multiply_fusion = (f32[2,4,256,528]{2,3,1,0:T(8,128)S(1)}, f32[2,4,256,528]{2,3,1,0:T(8,128)S(1)}) fusion(f32[2,4,256,1056]{2,3,1,0:T(8,128)} %fusion.64, f32[528]{0:T(1024)S(1)} %copy-done.26, bf16[2,4,256,643]{2,3,1,0:T(8,128)(2,1)} %concatenate.57, bf16[2,643,528]{1,2,0:T(8,128)(2,1)} %concatenate.58), kind=kOutput, calls=%fused_computation.10 | convolution fusion | flops 1393852416 | bytes 21295360 | tf_op jit(solution)/shard_map/hmik,hkf->hmif/dot_general | solution.py:193
  106.3 1.5 %reduce-precision_convert_fusion = (bf16[2,4,256,1056]{2,3,1,0:T(8,128)(2,1)S(1)}, bf16[2,4,256,1056]{2,3,1,0:T(8,128)(2,1)S(1)}) fusion(f32[2,4,256,528]{2,3,1,0:T(8,128)S(1)} %get-tuple-element.20, f32[2,4,256,528]{2,3,1,0:T(8,128)S(1)} %get-tuple-element.19), kind=kLoop, calls=%fused_computation.1 | loop fusion | flops 10813440 | bytes 17301504 | tf_op jit(solution)/shard_map/convert_element_type | solution.py:26
  107.9 0.9 fusion.1
  108.9 0.9 fusion.143
  109.8 1.0 fusion.82
  110.8 1.0 fusion.21
  111.8 0.8 fusion.142
  112.6 2.5 %collective-permute-start.4 = (bf16[256,1,2,128]{3,0,1,2:T(8,128)(2,1)}, bf16[256,1,2,128]{3,0,1,2:T(8,128)(2,1)}, u32[]{:S(2)}, u32[]{:S(2)}) collective-permute-start(bf16[256,1,2,128]{3,0,1,2:T(8,128)(2,1)} %get-tuple-element.37), channel_id=1, source_target_pairs={{0,2},{1,3},{2,0},{3,1},{4,6},{5,7},{6,4},{7,5},{8,10},{9,11},{10,... | collective-permute-start | bytes 393224 | tf_op jit(solution)/shard_map/ppermute | solution.py:102
  115.1 0.4 convolution_bitcast_fusion.1
  115.9 1.8 %convolution_bitcast_fusion = f32[2,256,528]{1,2,0:T(8,128)} fusion(bf16[2,4,256,256]{2,3,1,0:T(8,128)(2,1)S(1)} %copy-done.9, bf16[2,4,256,528]{2,3,1,0:T(8,128)(2,1)S(1)} %get-tuple-element.18), kind=kOutput, calls=%fused_computation.36 | convolution fusion | flops 553648128 | bytes 4292608 | tf_op jit(solution)/shard_map/hmij,hmif->hjf/dot_general | solution.py:207
  117.7 1.6 %fusion.44 = f32[32,40,128]{2,0,1:T(8,128)S(1)} fusion(f32[32,40,128]{2,1,0:T(8,128)} %all-to-all-done.2), kind=kOutput, calls=%fused_computation.89 | convolution fusion | flops 62915584 | bytes 1310720 | tf_op jit(solution)/shard_map/ij,jrc->irc/dot_general | solution.py:74
  119.2 1.2 copy.139
  120.5 8.1 %all-to-all-start.3 = ((f32[32,40,128]{2,1,0:T(8,128)}), f32[32,40,128]{2,1,0:T(8,128)S(1)}, u32[]{:S(2)}, u32[]{:S(2)}) async-start(f32[32,40,128]{2,1,0:T(8,128)} %copy.139), calls=%async_computation.3 | async-start | bytes 1310720 | tf_op jit(solution)/shard_map/all_to_all | solution.py:75
  128.5 1.1 copy_dynamic-update-slice_fusion.2
  129.7 1.1 copy_dynamic-update-slice_fusion.1
  130.8 1.1 copy_dynamic-update-slice_fusion
  132.0 9.4 %all-to-all-done.3 = f32[32,40,128]{2,1,0:T(8,128)S(1)} async-done(((f32[32,40,128]{2,1,0:T(8,128)}), f32[32,40,128]{2,1,0:T(8,128)S(1)}, u32[]{:S(2)}, u32[]{:S(2)}) %all-to-all-start.3) | async-done | bytes 655392 | tf_op jit(solution)/shard_map/all_to_all | solution.py:75
  141.5 0.5 fusion.58
  142.0 0.5 fusion.35
  142.5 0.8 copy.142
  143.5 1.7 %slice_multiply_fusion.1 = (f32[2,256,528]{1,2,0:T(8,128)S(1)}, f32[2,256,528]{1,2,0:T(8,128)S(1)}) fusion(f32[2,256,1056]{1,2,0:T(8,128)S(1)} %copy-done.5, f32[528]{0:T(1024)S(1)} %copy-done.26, f32[2,528]{1,0:T(2,128)S(1)} %bitcast.199, f32[2,256,528]{1,2,0:T(8,128)} %convolution_bitcast_fusion, bf16[2,128,528]{1,2,0:T(8,128)(2,1)S(1)} %get-tuple-element.33, ...), kind=kOutput, calls=%fused_computation.77 | convolution fusion | flops 141369344 | bytes 6084800 | tf_op jit(solution)/shard_map/htk,hkf->htf/dot_general | solution.py:212
  146.8 0.8 copy.141
  (96 shorter events, 4.4 us)
Async XLA Ops:
  0.6 8.2 %copy-start = (bf16[256,8,128]{2,1,0:T(8,128)(2,1)S(1)}, bf16[256,8,128]{2,1,0:T(8,128)(2,1)}, u32[]{:S(2)}) copy-start(bf16[256,8,128]{2,1,0:T(8,128)(2,1)} %param.10) | copy-start | bytes 1572868
  0.7 8.2 %copy-start.27 = (s32[2,128,32]{1,2,0:T(8,128)S(1)}, s32[2,128,32]{1,2,0:T(8,128)}, u32[]{:S(2)}) copy-start(s32[2,128,32]{1,2,0:T(8,128)} %param.13) | copy-start | bytes 98308
  0.7 9.3 %copy-start.23 = (bf16[96,1056,1]{1,0,2:T(8,128)(2,1)S(1)}, bf16[96,1056,1]{1,0,2:T(8,128)(2,1)}, u32[]{:S(2)}) copy-start(bf16[96,1056,1]{1,0,2:T(8,128)(2,1)} %constant.95) | copy-start | bytes 608260
  2.3 21.5 %collective-permute-start = (bf16[2,256,1,2,128]{4,1,3,2,0:T(8,128)(2,1)S(1)}, bf16[2,256,1,2,128]{4,1,3,2,0:T(8,128)(2,1)S(1)}, u32[]{:S(2)}, u32[]{:S(2)}) collective-permute-start(bf16[2,256,1,2,128]{4,1,3,2,0:T(8,128)(2,1)S(1)} %get-tuple-element.29), channel_id=1, source_target_pairs={{0,1},{1,2},{2,3},{3,0},{4,5},{5,6},{6,7},{7,4},{8,9},{9,10},{10,1... | collective-permute-start | bytes 786440 | tf_op jit(solution)/shard_map/ppermute | solution.py:89
  4.8 19.0 %collective-permute-start.1 = (bf16[2,256,1,2,128]{4,1,3,2,0:T(8,128)(2,1)S(1)}, bf16[2,256,1,2,128]{4,1,3,2,0:T(8,128)(2,1)}, u32[]{:S(2)}, u32[]{:S(2)}) collective-permute-start(bf16[2,256,1,2,128]{4,1,3,2,0:T(8,128)(2,1)S(1)} %get-tuple-element.30), channel_id=1, source_target_pairs={{0,2},{1,3},{2,0},{3,1},{4,6},{5,7},{6,4},{7,5},{8,10},{9,11},{10,... | collective-permute-start | bytes 786440 | tf_op jit(solution)/shard_map/ppermute | solution.py:89
  8.1 15.7 %collective-permute-start.2 = (bf16[2,256,1,2,128]{4,1,3,2,0:T(8,128)(2,1)S(1)}, bf16[2,256,1,2,128]{4,1,3,2,0:T(8,128)(2,1)}, u32[]{:S(2)}, u32[]{:S(2)}) collective-permute-start(bf16[2,256,1,2,128]{4,1,3,2,0:T(8,128)(2,1)S(1)} %get-tuple-element.31), channel_id=1, source_target_pairs={{0,3},{1,0},{2,1},{3,2},{4,7},{5,4},{6,5},{7,6},{8,11},{9,8},{10,9... | collective-permute-start | bytes 786440 | tf_op jit(solution)/shard_map/ppermute | solution.py:89
  9.2 2.9 %copy-start.17 = (f32[2,256,32]{1,2,0:T(8,128)}, f32[2,256,32]{1,2,0:T(8,128)S(1)}, u32[]{:S(2)}) copy-start(f32[2,256,32]{1,2,0:T(8,128)S(1)} %fusion.37) | copy-start | bytes 196612
  10.5 1.4 copy-start.4
  14.5 21.5 %all-to-all-start = ((f32[32,40,128]{2,1,0:T(8,128)}), f32[32,40,128]{2,1,0:T(8,128)S(1)}, u32[]{:S(2)}, u32[]{:S(2)}) async-start(f32[32,40,128]{2,1,0:T(8,128)} %bitcast.25), calls=%async_computation | async-start | bytes 1310720 | tf_op jit(solution)/shard_map/all_to_all | solution.py:70
  23.9 3.2 %copy-start.24 = (bf16[96,1056,1,1]{1,0,3,2:T(8,128)(2,1)S(1)}, bf16[96,1056,1,1]{1,0,3,2:T(8,128)(2,1)}, u32[]{:S(2)}) copy-start(bf16[96,1056,1,1]{1,0,3,2:T(8,128)(2,1)} %constant.94) | copy-start | bytes 608260
  25.1 1.0 copy-start.6
  26.1 5.7 %copy-start.10 = (f32[2,4,256,32]{2,3,0,1:T(8,128)}, f32[2,4,256,32]{2,3,0,1:T(8,128)S(1)}, u32[]{:S(2)}) copy-start(f32[2,4,256,32]{2,3,0,1:T(8,128)S(1)} %fusion.22) | copy-start | bytes 786436
  31.8 10.7 %copy-start.28 = (bf16[528]{0:T(1024)(128)(2,1)S(1)}, bf16[528]{0:T(1024)(128)(2,1)}, u32[]{:S(2)}) copy-start(bf16[528]{0:T(1024)(128)(2,1)} %constant.77.clone) | copy-start | bytes 3172
  37.8 17.8 %all-to-all-start.1 = ((f32[32,40,128]{2,1,0:T(8,128)}), f32[32,40,128]{2,1,0:T(8,128)}, u32[]{:S(2)}, u32[]{:S(2)}) async-start(f32[32,40,128]{2,1,0:T(8,128)} %copy.113), calls=%async_computation.1 | async-start | bytes 1310720 | tf_op jit(solution)/shard_map/all_to_all | solution.py:75
  46.8 2.1 %copy-start.2 = (bf16[2,4,256,528]{2,3,1,0:T(8,128)(2,1)}, bf16[2,4,256,528]{2,3,1,0:T(8,128)(2,1)S(1)}, u32[]{:S(2)}) copy-start(bf16[2,4,256,528]{2,3,1,0:T(8,128)(2,1)S(1)} %get-tuple-element.17) | copy-start | bytes 6488068
  58.2 2.3 %copy-start.3 = (bf16[2,4,256,528]{2,3,1,0:T(8,128)(2,1)S(1)}, bf16[2,4,256,528]{2,3,1,0:T(8,128)(2,1)}, u32[]{:S(2)}) copy-start(bf16[2,4,256,528]{2,3,1,0:T(8,128)(2,1)} %copy-done.2) | copy-start | bytes 6488068
  58.2 2.7 %copy-start.8 = (f32[1056,128]{1,0:T(8,128)S(1)}, f32[1056,128]{1,0:T(8,128)}, u32[]{:S(2)}) copy-start(f32[1056,128]{1,0:T(8,128)} %slice.92) | copy-start | bytes 1622020
  62.1 1.2 copy-start.7
  62.1 2.7 %copy-start.15 = (bf16[2,4,256,256]{2,3,1,0:T(8,128)(2,1)S(1)}, bf16[2,4,256,256]{2,3,1,0:T(8,128)(2,1)}, u32[]{:S(2)}) copy-start(bf16[2,4,256,256]{2,3,1,0:T(8,128)(2,1)} %get-tuple-element.58) | copy-start | bytes 3145732
  64.7 2.6 %copy-start.12 = (bf16[2,4,256,128]{3,2,0,1:T(8,128)(2,1)}, bf16[2,4,256,128]{3,2,0,1:T(8,128)(2,1)S(1)}, u32[]{:S(2)}) copy-start(bf16[2,4,256,128]{3,2,0,1:T(8,128)(2,1)S(1)} %get-tuple-element.27) | copy-start | bytes 1572868
  72.1 45.5 %all-to-all-start.2 = ((f32[32,40,128]{2,1,0:T(8,128)}), f32[32,40,128]{2,1,0:T(8,128)}, u32[]{:S(2)}, u32[]{:S(2)}) async-start(f32[32,40,128]{2,1,0:T(8,128)} %bitcast.191), calls=%async_computation.2 | async-start | bytes 1310720 | tf_op jit(solution)/shard_map/all_to_all | solution.py:70
  87.6 11.8 %copy-start.26 = (f32[528]{0:T(1024)S(1)}, f32[528]{0:T(1024)}, u32[]{:S(2)}) copy-start(f32[528]{0:T(1024)} %constant.78.clone) | copy-start | bytes 6340
  106.3 1.6 %copy-start.21 = (bf16[1056,32,1,1]{0,1,2,3:T(8,128)(2,1)S(1)}, bf16[1056,32,1,1]{0,1,2,3:T(8,128)(2,1)}, u32[]{:S(2)}) copy-start(bf16[1056,32,1,1]{0,1,2,3:T(8,128)(2,1)} %constant.96) | copy-start | bytes 202756
  107.8 1.0 copy-start.11
  107.9 1.0 copy-start.14
  109.8 5.4 %copy-start.13 = (bf16[2,4,256,128]{3,2,0,1:T(8,128)(2,1)S(1)}, bf16[2,4,256,128]{3,2,0,1:T(8,128)(2,1)}, u32[]{:S(2)}) copy-start(bf16[2,4,256,128]{3,2,0,1:T(8,128)(2,1)} %copy-done.12) | copy-start | bytes 1572868
  109.8 5.3 %copy-start.16 = (bf16[2,4,256,256]{2,3,1,0:T(8,128)(2,1)S(1)}, bf16[2,4,256,256]{2,3,1,0:T(8,128)(2,1)}, u32[]{:S(2)}) copy-start(bf16[2,4,256,256]{2,3,1,0:T(8,128)(2,1)} %get-tuple-element.58) | copy-start | bytes 3145732
  111.8 4.0 %copy-start.9 = (bf16[2,4,256,256]{2,3,1,0:T(8,128)(2,1)S(1)}, bf16[2,4,256,256]{2,3,1,0:T(8,128)(2,1)}, u32[]{:S(2)}) copy-start(bf16[2,4,256,256]{2,3,1,0:T(8,128)(2,1)} %select_convert_fusion) | copy-start | bytes 3145732
  112.6 15.9 %collective-permute-start.3 = (bf16[256,1,2,128]{3,0,1,2:T(8,128)(2,1)}, bf16[256,1,2,128]{3,0,1,2:T(8,128)(2,1)}, u32[]{:S(2)}, u32[]{:S(2)}) collective-permute-start(bf16[256,1,2,128]{3,0,1,2:T(8,128)(2,1)} %get-tuple-element.38), channel_id=1, source_target_pairs={{0,3},{1,0},{2,1},{3,2},{4,7},{5,4},{6,5},{7,6},{8,11},{9,8},{10,9... | collective-permute-start | bytes 393224 | tf_op jit(solution)/shard_map/ppermute | solution.py:102
  112.6 17.1 %collective-permute-start.4 = (bf16[256,1,2,128]{3,0,1,2:T(8,128)(2,1)}, bf16[256,1,2,128]{3,0,1,2:T(8,128)(2,1)}, u32[]{:S(2)}, u32[]{:S(2)}) collective-permute-start(bf16[256,1,2,128]{3,0,1,2:T(8,128)(2,1)} %get-tuple-element.37), channel_id=1, source_target_pairs={{0,2},{1,3},{2,0},{3,1},{4,6},{5,7},{6,4},{7,5},{8,10},{9,11},{10,... | collective-permute-start | bytes 393224 | tf_op jit(solution)/shard_map/ppermute | solution.py:102
  115.1 15.7 %collective-permute-start.5 = (bf16[256,1,2,128]{3,0,1,2:T(8,128)(2,1)}, bf16[256,1,2,128]{3,0,1,2:T(8,128)(2,1)}, u32[]{:S(2)}, u32[]{:S(2)}) collective-permute-start(bf16[256,1,2,128]{3,0,1,2:T(8,128)(2,1)} %get-tuple-element.36), channel_id=1, source_target_pairs={{0,1},{1,2},{2,3},{3,0},{4,5},{5,6},{6,7},{7,4},{8,9},{9,10},{10,1... | collective-permute-start | bytes 393224 | tf_op jit(solution)/shard_map/ppermute | solution.py:102
  120.5 21.0 %all-to-all-start.3 = ((f32[32,40,128]{2,1,0:T(8,128)}), f32[32,40,128]{2,1,0:T(8,128)S(1)}, u32[]{:S(2)}, u32[]{:S(2)}) async-start(f32[32,40,128]{2,1,0:T(8,128)} %copy.139), calls=%async_computation.3 | async-start | bytes 1310720 | tf_op jit(solution)/shard_map/all_to_all | solution.py:75
  132.0 9.5 %copy-start.20 = (bf16[256,1,8,128]{3,2,1,0:T(8,128)(2,1)}, bf16[256,1,8,128]{3,2,1,0:T(8,128)(2,1)S(1)}, u32[]{:S(2)}) copy-start(bf16[256,1,8,128]{3,2,1,0:T(8,128)(2,1)S(1)} %copy_dynamic-update-slice_fusion) | copy-start | bytes 1572868
  141.5 2.0 %copy-start.5 = (f32[2,256,1056]{1,2,0:T(8,128)S(1)}, f32[2,256,1056]{1,2,0:T(8,128)}, u32[]{:S(2)}) copy-start(f32[2,256,1056]{1,2,0:T(8,128)} %copy-done.4) | copy-start | bytes 6488068
  141.5 2.0 %copy-start.19 = (bf16[256,2,128]{2,0,1:T(8,128)(2,1)S(1)}, bf16[256,2,128]{2,0,1:T(8,128)(2,1)}, u32[]{:S(2)}) copy-start(bf16[256,2,128]{2,0,1:T(8,128)(2,1)} %copy.248) | copy-start | bytes 393220
  143.5 1.7 %copy-start.25 = (bf16[1056,32,1]{0,1,2:T(8,128)(2,1)S(1)}, bf16[1056,32,1]{0,1,2:T(8,128)(2,1)}, u32[]{:S(2)}) copy-start(bf16[1056,32,1]{0,1,2:T(8,128)(2,1)} %constant.97) | copy-start | bytes 202756
  145.2 0.8 copy-start.18
  145.2 1.2 copy-start.22
  145.2 2.4 %copy-start.1 = (bf16[256,8,128]{2,1,0:T(8,128)(2,1)S(1)}, bf16[256,8,128]{2,1,0:T(8,128)(2,1)}, u32[]{:S(2)}) copy-start(bf16[256,8,128]{2,1,0:T(8,128)(2,1)} %param.10) | copy-start | bytes 1572868

commit v7 on v6

--- a/solution.py
+++ b/solution.py
@@ -188,15 +188,14 @@
     ).astype(bf16)
     grad_hi, grad_lo = split_parts(grad_rows, 2)
     state_hi, state_lo = split_parts(state_in.transpose(0, 2, 1), 2)
-    corr_hi, corr_lo = split_parts(correction[..., None], 2)
-    total_hi, total_lo = split_parts(total_in[:, None, :], 2)
-    grad_qfeat = jnp.einsum(
-        "hmik,hkf->hmif",
-        jnp.concatenate([dscores, grad_hi, grad_hi, grad_lo, corr_hi, corr_hi, corr_lo], axis=-1),
-        jnp.concatenate(
-            [key_feat, state_hi, state_lo, state_hi, total_hi, total_lo, total_hi], axis=1
-        ),
-        preferred_element_type=f32,
+    grad_qfeat = (
+        jnp.einsum(
+            "hmik,hkf->hmif",
+            jnp.concatenate([dscores, grad_hi, grad_hi, grad_lo], axis=-1),
+            jnp.concatenate([key_feat, state_hi, state_lo, state_hi], axis=1),
+            preferred_element_type=f32,
+        )
+        + correction[..., None] * total_in[:, None, None, :]
     )
     query_grad = tri_feature_back(
         grad_qfeat, query_one, query_two, proj_wide, take_a, take_b, off

time: 149 us -> 131 us (0.88)
  local copies, waits for them, and re-layouts: 38 us -> 19.5 us
  other arithmetic: 13.8 us -> 10.7 us
  waiting for transfers between devices: 20.3 us -> 22.3 us
  matrix products: 39 us -> 40.8 us
    concatenate x2 -> x0, local copies, waits for them, and re-layouts: 15.6 us -> none  [the longest x1 11.8 us: body(): jnp.concatenate([dscores, grad_hi, grad_hi, grad_lo, corr_hi, corr_hi, co...]
    convert_element_type x3 -> x1, other arithmetic: 3.29 us -> 0.09 us  [split_parts(): parts.append(rest.astype(bf16))]
    convert_element_type x0 -> x1, other arithmetic: none -> 1.63 us  [body(): grad_low = grad_rows.astype(bf16)]
  transfers between devices with their start and end apart: 10 -> 10, of which waited for: 3 -> 3; matrix products, arithmetic and copies ran while one was open for 42% -> 34% of each run, Pallas kernels for 0% -> 0%
where the time goes in v7:
time: 131 us; the launch traced here: 130 us
  matrix products  40.8 us (31%)
  starting transfers between devices  35.2 us (27%)
  waiting for transfers between devices  22.3 us (17%)
  local copies, waits for them, and re-layouts  19.5 us (15%)
  other arithmetic  10.7 us (8%)
  between operations  1.39 us (1%)
    all_to_all x2, waiting for transfers between devices, ctx_scan(): lax.all_to_all(summed, 'ctx', 0, 0, tiled=True).reshape(n * per, width)  16.9 us
    all_to_all x2, starting transfers between devices, ctx_scan(): got = lax.all_to_all(flat.reshape(n, per, width), 'ctx', 0, 0, tiled=True)  13.4 us
    all_to_all x2, starting transfers between devices, ctx_scan(): lax.all_to_all(summed, 'ctx', 0, 0, tiled=True).reshape(n * per, width)  12.8 us
    dot_general x12, matrix products, dot_parts(): term = jnp.einsum(pattern, *args, preferred_element_type=f32)  10.6 us
    ppermute x3, starting transfers between devices, head_exchange(): lax.ppermute(piece, 'head', [(j, (j + k) % count) for j in range(count)])  6.57 us
    dot_general x1, matrix products, body(): jnp.einsum('hmik,hkf->hmif', jnp.concatenate([dscores, grad_hi, grad_hi,...  5.54 us
    all_to_all x2, waiting for transfers between devices, ctx_scan(): got = lax.all_to_all(flat.reshape(n, per, width), 'ctx', 0, 0, tiled=True)  5.33 us
    dot_general x2, matrix products, take_pair(): out = jnp.einsum('...k,kn->...n', lhs, rhs, preferred_element_type=f32)  5.2 us
  transfers between devices with their start and end apart: 10, of which 3 were waited for; matrix products, arithmetic and copies ran while one was open for 34% of the time, Pallas kernels for 0%

profile of v7, /device:TPU:1, one launch (start us, length us, event | category | flops | bytes accessed | tf_op | source)
XLA Modules:
  0.0 129.8 jit_solution(5927316383527608643)
XLA Ops:
  0.7 1.4 %copy_bitcast_fusion = (bf16[1,256,1,8,128]{4,1,3,2,0:T(8,128)(2,1)S(1)}, bf16[1,256,1,8,128]{4,1,3,2,0:T(8,128)(2,1)S(1)}) fusion(bf16[256,1,8,128]{3,2,1,0:T(8,128)(2,1)} %param.12, bf16[256,1,8,128]{3,2,1,0:T(8,128)(2,1)} %param.9), kind=kLoop, calls=%fused_computation.118 | loop fusion | bytes 2097152 | tf_op jit(solution)/shard_map/stack | solution.py:147
  2.3 2.5 %collective-permute-start = (bf16[2,256,1,2,128]{4,1,3,2,0:T(8,128)(2,1)S(1)}, bf16[2,256,1,2,128]{4,1,3,2,0:T(8,128)(2,1)S(1)}, u32[]{:S(2)}, u32[]{:S(2)}) collective-permute-start(bf16[2,256,1,2,128]{4,1,3,2,0:T(8,128)(2,1)S(1)} %get-tuple-element.26), channel_id=1, source_target_pairs={{0,1},{1,2},{2,3},{3,0},{4,5},{5,6},{6,7},{7,4},{8,9},{9,10},{10,1... | collective-permute-start | bytes 786440 | tf_op jit(solution)/shard_map/ppermute | solution.py:89
  4.8 3.3 %collective-permute-start.1 = (bf16[2,256,1,2,128]{4,1,3,2,0:T(8,128)(2,1)S(1)}, bf16[2,256,1,2,128]{4,1,3,2,0:T(8,128)(2,1)S(1)}, u32[]{:S(2)}, u32[]{:S(2)}) collective-permute-start(bf16[2,256,1,2,128]{4,1,3,2,0:T(8,128)(2,1)S(1)} %get-tuple-element.27), channel_id=1, source_target_pairs={{0,2},{1,3},{2,0},{3,1},{4,6},{5,7},{6,4},{7,5},{8,10},{9,11},{10,... | collective-permute-start | bytes 786440 | tf_op jit(solution)/shard_map/ppermute | solution.py:89
  8.1 0.7 collective-permute-start.2
  9.2 0.8 reduce-precision_convert_fusion.12
  10.0 0.5 fusion.102
  10.5 1.3 %copy-done.4 = f32[2,256,1056]{1,2,0:T(8,128)} copy-done((f32[2,256,1056]{1,2,0:T(8,128)}, f32[2,256,1056]{1,2,0:T(8,128)S(1)}, u32[]{:S(2)}) %copy-start.4) | copy-done | bytes 2162712
  12.1 1.2 constant_dynamic-slice_fusion
  13.3 0.3 fusion.152
  13.6 0.9 select_maximum_fusion.1
  14.5 8.6 %all-to-all-start = ((f32[32,40,128]{2,1,0:T(8,128)}), f32[32,40,128]{2,1,0:T(8,128)S(1)}, u32[]{:S(2)}, u32[]{:S(2)}) async-start(f32[32,40,128]{2,1,0:T(8,128)} %bitcast.25), calls=%async_computation | async-start | bytes 1310720 | tf_op jit(solution)/shard_map/all_to_all | solution.py:70
  23.1 0.7 copy.208
  24.3 0.7 copy-done.6
  25.0 1.0 reduce-precision_convert_fusion.9
  26.0 4.7 %fusion.76 = f32[2,4,256,1056]{2,3,1,0:T(8,128)} fusion(bf16[96,1056,1,1]{1,0,3,2:T(8,128)(2,1)S(1)} %copy-done.23, bf16[2,4,256,32]{2,3,0,1:T(8,128)(2,1)S(1)} %get-tuple-element.39, bf16[2,4,256,32]{2,3,0,1:T(8,128)(2,1)S(1)} %get-tuple-element.38, bf16[2,4,256,32]{2,3,0,1:T(8,128)(2,1)S(1)} %get-tuple-element.37), kind=kOutput, calls=%fused_computation.128 | convolution fusion | flops 416415744 | bytes 9246720 | tf_op jit(solution)/shard_map/...k,kn->...n/dot_general | solution.py:49
  30.7 5.3 %all-to-all-done = f32[32,40,128]{2,1,0:T(8,128)S(1)} async-done(((f32[32,40,128]{2,1,0:T(8,128)}), f32[32,40,128]{2,1,0:T(8,128)S(1)}, u32[]{:S(2)}, u32[]{:S(2)}) %all-to-all-start) | async-done | bytes 655392 | tf_op jit(solution)/shard_map/all_to_all | solution.py:70
  36.0 0.5 fusion.58
  36.5 1.2 copy.78
  37.7 4.8 %all-to-all-start.1 = ((f32[32,40,128]{2,1,0:T(8,128)}), f32[32,40,128]{2,1,0:T(8,128)}, u32[]{:S(2)}, u32[]{:S(2)}) async-start(f32[32,40,128]{2,1,0:T(8,128)} %copy.78), calls=%async_computation.1 | async-start | bytes 1310720 | tf_op jit(solution)/shard_map/all_to_all | solution.py:75
  42.5 4.2 %broadcast_multiply_fusion = (bf16[2,4,256,528]{2,3,1,0:T(8,128)(2,1)S(1)}, bf16[2,4,256,528]{2,3,1,0:T(8,128)(2,1)S(1)}) fusion(bf16[528]{0:T(1024)(128)(2,1)S(1)} %copy-done.26, f32[2,4,256,1056]{2,3,1,0:T(8,128)} %fusion.76), kind=kLoop, calls=%fused_computation.84 | loop fusion | flops 4325376 | bytes 12977184 | tf_op jit(solution)/shard_map/mul | solution.py:159
  46.7 2.1 %select_convert_fusion.1 = (bf16[2,4,256,256]{2,3,1,0:T(8,128)(2,1)}, f32[2,4,256,256]{2,3,1,0:T(8,128)S(1)}) fusion(pred[256,256]{0,1:T(8,128)(4,1)S(1)} %iota_compare_fusion.1, bf16[2,4,256,528]{2,3,1,0:T(8,128)(2,1)S(1)} %get-tuple-element.14, bf16[2,256,528]{1,2,0:T(8,128)(2,1)S(1)} %get-tuple-element.13), kind=kOutput, calls=%fused_computation.25 | convolution fusion | flops 554172416 | bytes 5914624 | tf_op jit(solution)/shard_map/hmif,hjf->hmij/dot_general | solution.py:167
  49.0 6.6 %all-to-all-done.1 = f32[32,40,128]{2,1,0:T(8,128)} async-done(((f32[32,40,128]{2,1,0:T(8,128)}), f32[32,40,128]{2,1,0:T(8,128)}, u32[]{:S(2)}, u32[]{:S(2)}) %all-to-all-start.1) | async-done | bytes 655392 | tf_op jit(solution)/shard_map/all_to_all | solution.py:75
  55.5 0.7 slice.91
  56.2 1.1 slice.86
  57.3 0.6 fusion.156
  57.9 2.0 %fusion.139 = f32[2,1,4,256]{3,1,2,0:T(1,128)S(1)} fusion(bf16[2,4,256,528]{2,3,1,0:T(8,128)(2,1)} %copy-done.2, bf16[2,528,1,1]{1,0,2,3:T(2,128)(2,1)S(1)} %get-tuple-element.50), kind=kOutput, calls=%fused_computation.209 | convolution fusion | flops 2162688 | bytes 2172992 | tf_op jit(solution)/shard_map/hmif,hf->hmi/dot_general | solution.py:36
  60.0 0.4 fusion.141
  60.4 1.2 fusion.14
  61.6 1.2 fusion.21
  62.8 1.6 %fusion.153 = (bf16[2,4,256,128]{3,2,0,1:T(8,128)(2,1)}, bf16[2,4,256,128]{3,2,0,1:T(8,128)(2,1)}, bf16[2,4,256,128]{3,2,0,1:T(8,128)(2,1)}) fusion(f32[2,4,256]{2,0,1:T(2,128)S(1)} %copy.79, bf16[2,256,4,2,128]{4,1,3,2,0:T(8,128)(2,1)S(1)} %copy-done.7), kind=kLoop, calls=%fused_computation.225 | loop fusion | flops 1835008 | bytes 2105344 | tf_op jit(solution)/shard_map/convert_element_type | solution.py:177
  64.5 1.1 fusion.32
  65.6 0.7 fusion.126
  66.2 0.7 fusion.128
  66.9 1.8 %fusion.73 = f32[2,528,128,1]{2,1,3,0:T(8,128)S(1)} fusion(bf16[2,4,256,528]{2,3,1,0:T(8,128)(2,1)S(1)} %get-tuple-element.15, bf16[2,4,256,128]{3,2,0,1:T(8,128)(2,1)} %get-tuple-element.22), kind=kOutput, calls=%fused_computation.124 | convolution fusion | flops 276824064 | bytes 3227648 | tf_op jit(solution)/shard_map/hmif,hmid->hfd/dot_general | solution.py:179
  68.7 0.9 select_maximum_fusion
  69.6 4.8 %all-to-all-start.2 = ((f32[32,40,128]{2,1,0:T(8,128)}), f32[32,40,128]{2,1,0:T(8,128)}, u32[]{:S(2)}, u32[]{:S(2)}) async-start(f32[32,40,128]{2,1,0:T(8,128)} %bitcast.188), calls=%async_computation.2 | async-start | bytes 1310720 | tf_op jit(solution)/shard_map/all_to_all | solution.py:70
  74.4 2.6 %select_convert_fusion = bf16[2,4,256,256]{2,3,1,0:T(8,128)(2,1)} fusion(f32[2,4,256]{2,1,0:T(4,128)S(1)} %copy.86, pred[256,256]{0,1:T(8,128)(4,1)} %copy-done.11, bf16[2,4,256,128]{3,2,0,1:T(8,128)(2,1)} %get-tuple-element.22, bf16[256,2,128]{2,1,0:T(2,128)(2,1)} %copy-done.9), kind=kOutput, calls=%fused_computation.24 | convolution fusion | flops 135790592 | bytes 1777664 | tf_op jit(solution)/shard_map/hmid,hjd->hmij/dot_general | solution.py:185
  76.9 2.1 %copy.87 = bf16[2,4,256,128]{2,3,1,0:T(8,128)(2,1)} copy(bf16[2,4,256,128]{3,2,0,1:T(8,128)(2,1)} %get-tuple-element.23) | data formatting | bytes 1048576 | tf_op jit(solution)/shard_map/convert_element_type | solution.py:26
  79.0 2.1 %copy.89 = bf16[2,4,256,128]{2,3,1,0:T(8,128)(2,1)} copy(bf16[2,4,256,128]{3,2,0,1:T(8,128)(2,1)} %get-tuple-element.24) | data formatting | bytes 1048576 | tf_op jit(solution)/shard_map/convert_element_type | solution.py:28
  81.2 5.5 %slice_multiply_fusion = (f32[2,4,256,528]{2,3,1,0:T(8,128)S(1)}, f32[2,4,256,528]{2,3,1,0:T(8,128)S(1)}) fusion(f32[2,4,256,1056]{2,3,1,0:T(8,128)} %fusion.76, f32[2,528]{1,0:T(2,128)S(1)} %copy-done.27, f32[2,4,256]{2,1,0:T(4,128)S(1)} %copy.86, f32[528]{0:T(1024)S(1)} %copy-done.28, bf16[2,4,256,128]{2,3,1,0:T(8,128)(2,1)} %copy.89, ...), kind=kOutput, calls=%fused_computation.11 | convolution fusion | flops 1405419520 | bytes 20494528 | tf_op jit(solution)/shard_map/hmik,hkf->hmif/dot_general | solution.py:192
  86.7 1.5 %reduce-precision_convert_fusion = (bf16[2,4,256,1056]{2,3,1,0:T(8,128)(2,1)S(1)}, bf16[2,4,256,1056]{2,3,1,0:T(8,128)(2,1)S(1)}) fusion(f32[2,4,256,528]{2,3,1,0:T(8,128)S(1)} %get-tuple-element.17, f32[2,4,256,528]{2,3,1,0:T(8,128)S(1)} %get-tuple-element.16), kind=kLoop, calls=%fused_computation.1 | loop fusion | flops 10813440 | bytes 17301504 | tf_op jit(solution)/shard_map/convert_element_type | solution.py:26
  88.3 0.9 fusion.1
  89.2 0.9 fusion.155
  90.2 1.0 fusion.94
  91.2 1.0 fusion.33
  92.2 0.8 fusion.154
  93.0 2.5 %collective-permute-start.4 = (bf16[256,1,2,128]{3,0,1,2:T(8,128)(2,1)}, bf16[256,1,2,128]{3,0,1,2:T(8,128)(2,1)}, u32[]{:S(2)}, u32[]{:S(2)}) collective-permute-start(bf16[256,1,2,128]{3,0,1,2:T(8,128)(2,1)} %get-tuple-element.34), channel_id=1, source_target_pairs={{0,2},{1,3},{2,0},{3,1},{4,6},{5,7},{6,4},{7,5},{8,10},{9,11},{10,... | collective-permute-start | bytes 393224 | tf_op jit(solution)/shard_map/ppermute | solution.py:102
  95.5 1.1 convolution_bitcast_fusion.1
  96.9 1.8 %convolution_bitcast_fusion = f32[2,256,528]{1,2,0:T(8,128)} fusion(bf16[2,4,256,256]{2,3,1,0:T(8,128)(2,1)S(1)} %copy-done.15, bf16[2,4,256,528]{2,3,1,0:T(8,128)(2,1)S(1)} %get-tuple-element.15), kind=kOutput, calls=%fused_computation.43 | convolution fusion | flops 553648128 | bytes 4292608 | tf_op jit(solution)/shard_map/hmij,hmif->hjf/dot_general | solution.py:206
  98.7 1.6 %fusion.56 = f32[32,40,128]{2,0,1:T(8,128)S(1)} fusion(f32[32,40,128]{2,1,0:T(8,128)} %all-to-all-done.2), kind=kOutput, calls=%fused_computation.103 | convolution fusion | flops 62915584 | bytes 1310720 | tf_op jit(solution)/shard_map/ij,jrc->irc/dot_general | solution.py:74
  100.3 1.2 copy.103
  101.5 8.1 %all-to-all-start.3 = ((f32[32,40,128]{2,1,0:T(8,128)}), f32[32,40,128]{2,1,0:T(8,128)S(1)}, u32[]{:S(2)}, u32[]{:S(2)}) async-start(f32[32,40,128]{2,1,0:T(8,128)} %copy.103), calls=%async_computation.3 | async-start | bytes 1310720 | tf_op jit(solution)/shard_map/all_to_all | solution.py:75
  109.6 1.1 copy_dynamic-update-slice_fusion.2
  110.7 1.1 copy_dynamic-update-slice_fusion.1
  112.1 10.3 %all-to-all-done.3 = f32[32,40,128]{2,1,0:T(8,128)S(1)} async-done(((f32[32,40,128]{2,1,0:T(8,128)}), f32[32,40,128]{2,1,0:T(8,128)S(1)}, u32[]{:S(2)}, u32[]{:S(2)}) %all-to-all-start.3) | async-done | bytes 655392 | tf_op jit(solution)/shard_map/all_to_all | solution.py:75
  122.6 0.5 fusion.70
  123.1 1.6 %fusion.47 = bf16[256,2,128]{2,0,1:T(8,128)(2,1)S(1)} fusion(f32[2,256,128]{2,1,0:T(8,128)} %convolution_bitcast_fusion.1, f32[2,256,128]{2,1,0:T(8,128)S(1)} %fusion.70, bf16[2,256,528]{1,2,0:T(8,128)(2,1)S(1)} %get-tuple-element.13, f32[2,528,128]{2,1,0:T(8,128)S(1)} %bitcast.183, bf16[528]{0:T(1024)(128)(2,1)S(1)} %copy-done.26), kind=kOutput, calls=%fused_computation.74 | convolution fusion | flops 70078464 | bytes 1737760 | tf_op jit(solution)/shard_map/htf,hfd->htd/dot_general | solution.py:36
  124.7 0.8 copy.106
  125.6 1.7 %slice_multiply_fusion.1 = (f32[2,256,528]{1,2,0:T(8,128)S(1)}, f32[2,256,528]{1,2,0:T(8,128)S(1)}) fusion(f32[2,256,1056]{1,2,0:T(8,128)S(1)} %copy-done.5, f32[528]{0:T(1024)S(1)} %copy-done.28, f32[2,528]{1,0:T(2,128)S(1)} %bitcast.194, f32[2,256,528]{1,2,0:T(8,128)} %convolution_bitcast_fusion, bf16[2,128,528]{1,2,0:T(8,128)(2,1)S(1)} %get-tuple-element.30, ...), kind=kOutput, calls=%fused_computation.91 | convolution fusion | flops 141369344 | bytes 6084800 | tf_op jit(solution)/shard_map/htk,hkf->htf/dot_general | solution.py:211
  127.4 0.3 fusion.51
  127.7 0.3 fusion.48
  128.2 0.4 fusion.110
  128.6 0.4 fusion.46
  129.0 0.8 copy.105
  (92 shorter events, 2.5 us)
Async XLA Ops:
  0.6 8.2 %copy-start = (bf16[256,8,128]{2,1,0:T(8,128)(2,1)S(1)}, bf16[256,8,128]{2,1,0:T(8,128)(2,1)}, u32[]{:S(2)}) copy-start(bf16[256,8,128]{2,1,0:T(8,128)(2,1)} %param.10) | copy-start | bytes 1572868
  0.7 8.2 %copy-start.25 = (s32[2,128,32]{1,2,0:T(8,128)S(1)}, s32[2,128,32]{1,2,0:T(8,128)}, u32[]{:S(2)}) copy-start(s32[2,128,32]{1,2,0:T(8,128)} %param.13) | copy-start | bytes 98308
  0.7 9.3 %copy-start.22 = (bf16[96,1056,1]{1,0,2:T(8,128)(2,1)S(1)}, bf16[96,1056,1]{1,0,2:T(8,128)(2,1)}, u32[]{:S(2)}) copy-start(bf16[96,1056,1]{1,0,2:T(8,128)(2,1)} %constant.95) | copy-start | bytes 608260
  2.3 21.5 %collective-permute-start = (bf16[2,256,1,2,128]{4,1,3,2,0:T(8,128)(2,1)S(1)}, bf16[2,256,1,2,128]{4,1,3,2,0:T(8,128)(2,1)S(1)}, u32[]{:S(2)}, u32[]{:S(2)}) collective-permute-start(bf16[2,256,1,2,128]{4,1,3,2,0:T(8,128)(2,1)S(1)} %get-tuple-element.26), channel_id=1, source_target_pairs={{0,1},{1,2},{2,3},{3,0},{4,5},{5,6},{6,7},{7,4},{8,9},{9,10},{10,1... | collective-permute-start | bytes 786440 | tf_op jit(solution)/shard_map/ppermute | solution.py:89
  4.8 19.0 %collective-permute-start.1 = (bf16[2,256,1,2,128]{4,1,3,2,0:T(8,128)(2,1)S(1)}, bf16[2,256,1,2,128]{4,1,3,2,0:T(8,128)(2,1)S(1)}, u32[]{:S(2)}, u32[]{:S(2)}) collective-permute-start(bf16[2,256,1,2,128]{4,1,3,2,0:T(8,128)(2,1)S(1)} %get-tuple-element.27), channel_id=1, source_target_pairs={{0,2},{1,3},{2,0},{3,1},{4,6},{5,7},{6,4},{7,5},{8,10},{9,11},{10,... | collective-permute-start | bytes 786440 | tf_op jit(solution)/shard_map/ppermute | solution.py:89
  8.1 15.7 %collective-permute-start.2 = (bf16[2,256,1,2,128]{4,1,3,2,0:T(8,128)(2,1)S(1)}, bf16[2,256,1,2,128]{4,1,3,2,0:T(8,128)(2,1)S(1)}, u32[]{:S(2)}, u32[]{:S(2)}) collective-permute-start(bf16[2,256,1,2,128]{4,1,3,2,0:T(8,128)(2,1)S(1)} %get-tuple-element.28), channel_id=1, source_target_pairs={{0,3},{1,0},{2,1},{3,2},{4,7},{5,4},{6,5},{7,6},{8,11},{9,8},{10,9... | collective-permute-start | bytes 786440 | tf_op jit(solution)/shard_map/ppermute | solution.py:89
  9.2 0.8 copy-start.16
  10.5 1.3 %copy-start.4 = (f32[2,256,1056]{1,2,0:T(8,128)}, f32[2,256,1056]{1,2,0:T(8,128)S(1)}, u32[]{:S(2)}) copy-start(f32[2,256,1056]{1,2,0:T(8,128)S(1)} %fusion.102) | copy-start | bytes 6488068
  13.3 10.7 %copy-start.9 = (bf16[256,2,128]{2,1,0:T(2,128)(2,1)}, bf16[256,2,128]{2,1,0:T(2,128)(2,1)S(1)}, u32[]{:S(2)}) copy-start(bf16[256,2,128]{2,1,0:T(2,128)(2,1)S(1)} %constant_dynamic-slice_fusion) | copy-start | bytes 393220
  14.5 21.5 %all-to-all-start = ((f32[32,40,128]{2,1,0:T(8,128)}), f32[32,40,128]{2,1,0:T(8,128)S(1)}, u32[]{:S(2)}, u32[]{:S(2)}) async-start(f32[32,40,128]{2,1,0:T(8,128)} %bitcast.25), calls=%async_computation | async-start | bytes 1310720 | tf_op jit(solution)/shard_map/all_to_all | solution.py:70
  23.8 25.0 %copy-start.11 = (pred[256,256]{0,1:T(8,128)(4,1)}, pred[256,256]{0,1:T(8,128)(4,1)S(1)}, u32[]{:S(2)}) copy-start(pred[256,256]{0,1:T(8,128)(4,1)S(1)} %iota_compare_fusion.1) | copy-start | bytes 196612
  23.8 2.1 %copy-start.23 = (bf16[96,1056,1,1]{1,0,3,2:T(8,128)(2,1)S(1)}, bf16[96,1056,1,1]{1,0,3,2:T(8,128)(2,1)}, u32[]{:S(2)}) copy-start(bf16[96,1056,1,1]{1,0,3,2:T(8,128)(2,1)} %constant.94) | copy-start | bytes 608260
  24.0 1.0 copy-start.6
  30.7 11.8 %copy-start.26 = (bf16[528]{0:T(1024)(128)(2,1)S(1)}, bf16[528]{0:T(1024)(128)(2,1)}, u32[]{:S(2)}) copy-start(bf16[528]{0:T(1024)(128)(2,1)} %constant.77.clone) | copy-start | bytes 3172
  37.7 17.8 %all-to-all-start.1 = ((f32[32,40,128]{2,1,0:T(8,128)}), f32[32,40,128]{2,1,0:T(8,128)}, u32[]{:S(2)}, u32[]{:S(2)}) async-start(f32[32,40,128]{2,1,0:T(8,128)} %copy.78), calls=%async_computation.1 | async-start | bytes 1310720 | tf_op jit(solution)/shard_map/all_to_all | solution.py:75
  46.7 2.1 %copy-start.2 = (bf16[2,4,256,528]{2,3,1,0:T(8,128)(2,1)}, bf16[2,4,256,528]{2,3,1,0:T(8,128)(2,1)S(1)}, u32[]{:S(2)}) copy-start(bf16[2,4,256,528]{2,3,1,0:T(8,128)(2,1)S(1)} %get-tuple-element.14) | copy-start | bytes 6488068
  57.3 2.7 %copy-start.3 = (bf16[2,4,256,528]{2,3,1,0:T(8,128)(2,1)S(1)}, bf16[2,4,256,528]{2,3,1,0:T(8,128)(2,1)}, u32[]{:S(2)}) copy-start(bf16[2,4,256,528]{2,3,1,0:T(8,128)(2,1)} %copy-done.2) | copy-start | bytes 6488068
  61.6 1.2 copy-start.7
  61.6 2.8 %copy-start.10 = (bf16[256,2,128]{2,1,0:T(2,128)(2,1)S(1)}, bf16[256,2,128]{2,1,0:T(2,128)(2,1)}, u32[]{:S(2)}) copy-start(bf16[256,2,128]{2,1,0:T(2,128)(2,1)} %copy-done.9) | copy-start | bytes 393220
  61.6 2.8 %copy-start.13 = (bf16[2,4,256,256]{2,3,1,0:T(8,128)(2,1)S(1)}, bf16[2,4,256,256]{2,3,1,0:T(8,128)(2,1)}, u32[]{:S(2)}) copy-start(bf16[2,4,256,256]{2,3,1,0:T(8,128)(2,1)} %get-tuple-element.53) | copy-start | bytes 3145732
  69.6 29.1 %all-to-all-start.2 = ((f32[32,40,128]{2,1,0:T(8,128)}), f32[32,40,128]{2,1,0:T(8,128)}, u32[]{:S(2)}, u32[]{:S(2)}) async-start(f32[32,40,128]{2,1,0:T(8,128)} %bitcast.188), calls=%async_computation.2 | async-start | bytes 1310720 | tf_op jit(solution)/shard_map/all_to_all | solution.py:70
  76.9 4.2 %copy-start.27 = (f32[2,528]{1,0:T(2,128)S(1)}, f32[2,528]{1,0:T(2,128)}, u32[]{:S(2)}) copy-start(f32[2,528]{1,0:T(2,128)} %get-tuple-element.48) | copy-start | bytes 12676
  76.9 4.2 %copy-start.28 = (f32[528]{0:T(1024)S(1)}, f32[528]{0:T(1024)}, u32[]{:S(2)}) copy-start(f32[528]{0:T(1024)} %constant.78.clone) | copy-start | bytes 6340
  86.7 1.6 %copy-start.20 = (bf16[1056,32,1,1]{0,1,2,3:T(8,128)(2,1)S(1)}, bf16[1056,32,1,1]{0,1,2,3:T(8,128)(2,1)}, u32[]{:S(2)}) copy-start(bf16[1056,32,1,1]{0,1,2,3:T(8,128)(2,1)} %constant.96) | copy-start | bytes 202756
  88.3 1.0 copy-start.12
  90.1 5.3 %copy-start.8 = (bf16[2,4,256,128]{3,2,0,1:T(8,128)(2,1)S(1)}, bf16[2,4,256,128]{3,2,0,1:T(8,128)(2,1)}, u32[]{:S(2)}) copy-start(bf16[2,4,256,128]{3,2,0,1:T(8,128)(2,1)} %get-tuple-element.22) | copy-start | bytes 1572868
  90.2 5.3 %copy-start.14 = (bf16[2,4,256,256]{2,3,1,0:T(8,128)(2,1)S(1)}, bf16[2,4,256,256]{2,3,1,0:T(8,128)(2,1)}, u32[]{:S(2)}) copy-start(bf16[2,4,256,256]{2,3,1,0:T(8,128)(2,1)} %get-tuple-element.53) | copy-start | bytes 3145732
  92.2 4.7 %copy-start.15 = (bf16[2,4,256,256]{2,3,1,0:T(8,128)(2,1)S(1)}, bf16[2,4,256,256]{2,3,1,0:T(8,128)(2,1)}, u32[]{:S(2)}) copy-start(bf16[2,4,256,256]{2,3,1,0:T(8,128)(2,1)} %select_convert_fusion) | copy-start | bytes 3145732
  93.0 16.6 %collective-permute-start.3 = (bf16[256,1,2,128]{3,0,1,2:T(8,128)(2,1)}, bf16[256,1,2,128]{3,0,1,2:T(8,128)(2,1)}, u32[]{:S(2)}, u32[]{:S(2)}) collective-permute-start(bf16[256,1,2,128]{3,0,1,2:T(8,128)(2,1)} %get-tuple-element.35), channel_id=1, source_target_pairs={{0,3},{1,0},{2,1},{3,2},{4,7},{5,4},{6,5},{7,6},{8,11},{9,8},{10,9... | collective-permute-start | bytes 393224 | tf_op jit(solution)/shard_map/ppermute | solution.py:102
  93.0 17.8 %collective-permute-start.4 = (bf16[256,1,2,128]{3,0,1,2:T(8,128)(2,1)}, bf16[256,1,2,128]{3,0,1,2:T(8,128)(2,1)}, u32[]{:S(2)}, u32[]{:S(2)}) collective-permute-start(bf16[256,1,2,128]{3,0,1,2:T(8,128)(2,1)} %get-tuple-element.34), channel_id=1, source_target_pairs={{0,2},{1,3},{2,0},{3,1},{4,6},{5,7},{6,4},{7,5},{8,10},{9,11},{10,... | collective-permute-start | bytes 393224 | tf_op jit(solution)/shard_map/ppermute | solution.py:102
  95.5 16.4 %collective-permute-start.5 = (bf16[256,1,2,128]{3,0,1,2:T(8,128)(2,1)}, bf16[256,1,2,128]{3,0,1,2:T(8,128)(2,1)S(1)}, u32[]{:S(2)}, u32[]{:S(2)}) collective-permute-start(bf16[256,1,2,128]{3,0,1,2:T(8,128)(2,1)} %get-tuple-element.33), channel_id=1, source_target_pairs={{0,1},{1,2},{2,3},{3,0},{4,5},{5,6},{6,7},{7,4},{8,9},{9,10},{10,1... | collective-permute-start | bytes 393224 | tf_op jit(solution)/shard_map/ppermute | solution.py:102
  101.5 21.0 %all-to-all-start.3 = ((f32[32,40,128]{2,1,0:T(8,128)}), f32[32,40,128]{2,1,0:T(8,128)S(1)}, u32[]{:S(2)}, u32[]{:S(2)}) async-start(f32[32,40,128]{2,1,0:T(8,128)} %copy.103), calls=%async_computation.3 | async-start | bytes 1310720 | tf_op jit(solution)/shard_map/all_to_all | solution.py:75
  112.1 13.4 %copy-start.19 = (bf16[256,1,8,128]{3,2,1,0:T(8,128)(2,1)}, bf16[256,1,8,128]{3,2,1,0:T(8,128)(2,1)S(1)}, u32[]{:S(2)}) copy-start(bf16[256,1,8,128]{3,2,1,0:T(8,128)(2,1)S(1)} %copy_dynamic-update-slice_fusion) | copy-start | bytes 1572868
  122.5 3.1 %copy-start.5 = (f32[2,256,1056]{1,2,0:T(8,128)S(1)}, f32[2,256,1056]{1,2,0:T(8,128)}, u32[]{:S(2)}) copy-start(f32[2,256,1056]{1,2,0:T(8,128)} %copy-done.4) | copy-start | bytes 6488068
  122.5 3.1 %copy-start.18 = (bf16[256,2,128]{2,0,1:T(8,128)(2,1)S(1)}, bf16[256,2,128]{2,0,1:T(8,128)(2,1)}, u32[]{:S(2)}) copy-start(bf16[256,2,128]{2,0,1:T(8,128)(2,1)} %copy.208) | copy-start | bytes 393220
  125.6 1.7 %copy-start.24 = (bf16[1056,32,1]{0,1,2:T(8,128)(2,1)S(1)}, bf16[1056,32,1]{0,1,2:T(8,128)(2,1)}, u32[]{:S(2)}) copy-start(bf16[1056,32,1]{0,1,2:T(8,128)(2,1)} %constant.97) | copy-start | bytes 202756
  127.3 0.8 copy-start.17
  127.4 1.2 copy-start.21
  127.4 2.4 %copy-start.1 = (bf16[256,8,128]{2,1,0:T(8,128)(2,1)S(1)}, bf16[256,8,128]{2,1,0:T(8,128)(2,1)}, u32[]{:S(2)}) copy-start(bf16[256,8,128]{2,1,0:T(8,128)(2,1)} %param.10) | copy-start | bytes 1572868

commit v8 on v7

--- a/solution.py
+++ b/solution.py
@@ -51,7 +51,7 @@
     return out[..., :size], out[..., size:]
 
 
-def ctx_scan(state, total, reverse):
+def scan_send(state, total):
     n = lax.axis_size("ctx")
     heads, feat, width = state.shape
     total_rows = -(-feat // width)
@@ -67,15 +67,34 @@
     rows = flat.shape[0]
     per = -(-rows // (n * 8)) * 8
     flat = jnp.pad(flat, ((0, n * per - rows), (0, 0)))
-    got = lax.all_to_all(flat.reshape(n, per, width), "ctx", 0, 0, tiled=True)
+    return lax.all_to_all(flat.reshape(n, per, width), "ctx", 0, 0, tiled=True)
+
+
+def scan_sum(got, reverse):
+    n = got.shape[0]
     src = lax.broadcasted_iota(jnp.int32, (n, n), 1)
     dst = lax.broadcasted_iota(jnp.int32, (n, n), 0)
-    mask = (src > dst if reverse else src < dst).astype(f32)
-    summed = jnp.einsum("ij,jrc->irc", mask, got, precision=highest)
+    mask = (src > dst if reverse else src < dst).astype(bf16)
+    return jnp.einsum(
+        "ij,jrc->irc",
+        jnp.concatenate([mask, mask, mask], axis=1),
+        jnp.concatenate(split_parts(got, 3), axis=0),
+        preferred_element_type=f32,
+    )
+
+
+def scan_return(summed, heads, feat):
+    n, per, width = summed.shape
+    total_rows = -(-feat // width)
     back = lax.all_to_all(summed, "ctx", 0, 0, tiled=True).reshape(n * per, width)
     state_out = back[: heads * feat].reshape(heads, feat, width)
     total_out = back[heads * feat : heads * (feat + total_rows)].reshape(heads, total_rows * width)
     return state_out, total_out[:, :feat]
+
+
+def ctx_scan(state, total, reverse):
+    summed = scan_sum(scan_send(state, total), reverse)
+    return scan_return(summed, state.shape[0], state.shape[1])
 
 
 def head_exchange(stacked, owned):
@@ -178,7 +197,7 @@
     correction = -jnp.sum(grad_rows * output_rows, -1)
     suffix_part = jnp.einsum("hmif,hmid->hfd", query_feat, grad_low, preferred_element_type=f32)
     suffix_sum = dot_split("hmif,hmi->hf", query_feat, correction)
-    merged_state, merged_total = ctx_scan(suffix_part, suffix_sum, True)
+    suffix_got = scan_send(suffix_part, suffix_sum)
 
     dscores = jnp.where(
         causal,
@@ -197,14 +216,19 @@
         )
         + correction[..., None] * total_in[:, None, None, :]
     )
+    grad_kfeat = jnp.einsum("hmij,hmif->hjf", dscores, query_feat, preferred_element_type=f32)
+    grad_value = jnp.einsum("hmij,hmid->hjd", weights, grad_low, preferred_element_type=f32)
+    suffix_summed = scan_sum(suffix_got, True)
+    suffix_summed, grad_qfeat, grad_kfeat, grad_value = lax.optimization_barrier(
+        (suffix_summed, grad_qfeat, grad_kfeat, grad_value)
+    )
+    merged_state, merged_total = scan_return(suffix_summed, suffix_part.shape[0], suffix_part.shape[1])
     query_grad = tri_feature_back(
         grad_qfeat, query_one, query_two, proj_wide, take_a, take_b, off
     )
     query_low = query_grad.transpose(2, 1, 0, 3).astype(bf16)
     query_out = head_return(query_low, heads_all)
 
-    grad_kfeat = jnp.einsum("hmij,hmif->hjf", dscores, query_feat, preferred_element_type=f32)
-    grad_value = jnp.einsum("hmij,hmid->hjd", weights, grad_low, preferred_element_type=f32)
     merged_hi, merged_lo = split_parts(merged_state.transpose(0, 2, 1), 2)
     kfeat_total = (
         grad_kfeat

time: 131 us -> 135 us (1.031)
  waiting for transfers between devices: 22.3 us -> 29.6 us
  local copies, waits for them, and re-layouts: 19.5 us -> 12.4 us
  other arithmetic: 10.7 us -> 17.6 us
  matrix products: 40.8 us -> 39.3 us
    all_to_all x4, waiting for transfers between devices: 22.2 us -> 11.2 us  [the longest x2 6.44 us: scan_return(): lax.all_to_all(summed, 'ctx', 0, 0, tiled=True).reshape(n * per, width)]
    ppermute x3, waiting for transfers between devices: 0.01 us -> 10.4 us  [head_exchange(): lax.ppermute(piece, 'head', [(j, (j + k) % count) for j in range(count)])]
    ppermute x3, waiting for transfers between devices: 0.01 us -> 8.02 us  [head_return(): lax.ppermute(piece, 'head', [(j, (j - k) % count) for j in range(count)])]
    mul x0 -> x1, other arithmetic: none -> 5.95 us  [tri_feature_back(): cotangent * second]
    dot_general x1, matrix products: 2.56 us -> 0.44 us  [body(): jnp.einsum('hmid,hjd->hmij', grad_low, value_heads, preferred_element_typ...]
    convert_element_type x1, local copies, waits for them, and re-layouts: 2.08 us -> 0.21 us  [split_parts(): parts.append(hi.astype(bf16))]
    convert_element_type x1, local copies, waits for them, and re-layouts: 2.06 us -> 0.21 us  [split_parts(): parts.append(rest.astype(bf16))]
    dynamic_update_slice x4, local copies, waits for them, and re-layouts: 2.73 us -> 0.9 us  [head_return(): lax.dynamic_update_slice_in_dim(out, piece, (me + k) % count * owned, axi...]
  transfers between devices with their start and end apart: 10 -> 10, of which waited for: 3 -> 7; matrix products, arithmetic and copies ran while one was open for 34% -> 25% of each run, Pallas kernels for 0% -> 0%
where the time goes in v8:
time: 135 us; the launch traced here: 134 us
  matrix products  39.3 us (29%)
  starting transfers between devices  33.9 us (25%)
  waiting for transfers between devices  29.6 us (22%)
  other arithmetic  17.6 us (13%)
  local copies, waits for them, and re-layouts  12.4 us (9%)
  between operations  1.4 us (1%)
    all_to_all x2, starting transfers between devices, scan_send(): return lax.all_to_all(flat.reshape(n, per, width), 'ctx', 0, 0, tiled=True)  12.8 us
    all_to_all x2, starting transfers between devices, scan_return(): lax.all_to_all(summed, 'ctx', 0, 0, tiled=True).reshape(n * per, width)  12.4 us
    dot_general x12, matrix products, dot_parts(): term = jnp.einsum(pattern, *args, preferred_element_type=f32)  10.9 us
    ppermute x3, waiting for transfers between devices, head_exchange(): lax.ppermute(piece, 'head', [(j, (j + k) % count) for j in range(count)])  10.4 us
    ppermute x3, waiting for transfers between devices, head_return(): lax.ppermute(piece, 'head', [(j, (j - k) % count) for j in range(count)])  8.02 us
    all_to_all x2, waiting for transfers between devices, scan_return(): lax.all_to_all(summed, 'ctx', 0, 0, tiled=True).reshape(n * per, width)  6.44 us
    dot_general x2, matrix products, take_pair(): out = jnp.einsum('...k,kn->...n', lhs, rhs, preferred_element_type=f32)  6.15 us
    mul x1, other arithmetic, tri_feature_back(): cotangent * second  5.95 us
  transfers between devices with their start and end apart: 10, of which 7 were waited for; matrix products, arithmetic and copies ran while one was open for 25% of the time, Pallas kernels for 0%

profile of v8, /device:TPU:1, one launch (start us, length us, event | category | flops | bytes accessed | tf_op | source)
XLA Modules:
  0.0 134.2 jit_solution(1462276045792468739)
XLA Ops:
  0.6 0.8 add_convert_fusion
  1.4 1.5 %constant_dynamic-slice_fusion = (bf16[256,2,128]{2,1,0:T(2,128)(2,1)S(1)}, bf16[256,2,128]{2,1,0:T(2,128)(2,1)S(1)}) fusion(bf16[256,8,128]{2,1,0:T(8,128)(2,1)} %param.11, s32[]{:T(128)S(6)} %select_n.62, bf16[256,8,128]{2,1,0:T(8,128)(2,1)} %param.10), kind=kLoop, calls=%fused_computation.243 | loop fusion | bytes 524292 | tf_op jit(solution)/shard_map/dynamic_slice | solution.py:165
  3.0 0.8 reduce-precision_convert_fusion.16
  3.8 1.4 %fusion.117 = f32[2,256,1056]{1,2,0:T(8,128)S(1)} fusion(bf16[96,1056,1]{1,0,2:T(8,128)(2,1)} %constant.95, bf16[2,256,32]{1,2,0:T(8,128)(2,1)S(1)} %get-tuple-element.58, bf16[2,256,32]{1,2,0:T(8,128)(2,1)S(1)} %get-tuple-element.57, bf16[2,256,32]{1,2,0:T(8,128)(2,1)S(1)} %get-tuple-element.56), kind=kOutput, calls=%fused_computation.181 | convolution fusion | flops 104103936 | bytes 2463744 | tf_op jit(solution)/shard_map/...k,kn->...n/dot_general | solution.py:49
  5.3 1.3 copy-done.2
  6.9 0.3 fusion.175
  7.2 0.9 fusion.74
  8.1 8.6 %all-to-all-start = ((f32[32,40,128]{2,1,0:T(8,128)}), f32[32,40,128]{2,1,0:T(8,128)S(1)}, u32[]{:S(2)}, u32[]{:S(2)}) async-start(f32[32,40,128]{2,1,0:T(8,128)} %bitcast.26), calls=%async_computation | async-start | bytes 1310720 | tf_op jit(solution)/shard_map/all_to_all | solution.py:70
  17.1 1.7 %collective-permute-start = (bf16[2,256,1,2,128]{4,1,3,2,0:T(8,128)(2,1)S(1)}, bf16[2,256,1,2,128]{4,1,3,2,0:T(8,128)(2,1)S(1)}, u32[]{:S(2)}, u32[]{:S(2)}) collective-permute-start(bf16[2,256,1,2,128]{4,1,3,2,0:T(8,128)(2,1)S(1)} %get-tuple-element.34), channel_id=1, source_target_pairs={{0,1},{1,2},{2,3},{3,0},{4,5},{5,6},{6,7},{7,4},{8,9},{9,10},{10,1... | collective-permute-start | bytes 786440 | tf_op jit(solution)/shard_map/ppermute | solution.py:108
  18.8 3.3 %collective-permute-start.1 = (bf16[2,256,1,2,128]{4,1,3,2,0:T(8,128)(2,1)S(1)}, bf16[2,256,1,2,128]{4,1,3,2,0:T(8,128)(2,1)S(1)}, u32[]{:S(2)}, u32[]{:S(2)}) collective-permute-start(bf16[2,256,1,2,128]{4,1,3,2,0:T(8,128)(2,1)S(1)} %get-tuple-element.35), channel_id=1, source_target_pairs={{0,2},{1,3},{2,0},{3,1},{4,6},{5,7},{6,4},{7,5},{8,10},{9,11},{10,... | collective-permute-start | bytes 786440 | tf_op jit(solution)/shard_map/ppermute | solution.py:108
  22.1 0.7 collective-permute-start.2
  22.8 0.7 copy.218
  23.6 3.9 %collective-permute-done = bf16[2,256,1,2,128]{4,1,3,2,0:T(8,128)(2,1)S(1)} collective-permute-done((bf16[2,256,1,2,128]{4,1,3,2,0:T(8,128)(2,1)S(1)}, bf16[2,256,1,2,128]{4,1,3,2,0:T(8,128)(2,1)S(1)}, u32[]{:S(2)}, u32[]{:S(2)}) %collective-permute-start) | collective-permute-done | bytes 262176 | tf_op jit(solution)/shard_map/ppermute | solution.py:108
  27.4 6.5 %collective-permute-done.1 = bf16[2,256,1,2,128]{4,1,3,2,0:T(8,128)(2,1)S(1)} collective-permute-done((bf16[2,256,1,2,128]{4,1,3,2,0:T(8,128)(2,1)S(1)}, bf16[2,256,1,2,128]{4,1,3,2,0:T(8,128)(2,1)S(1)}, u32[]{:S(2)}, u32[]{:S(2)}) %collective-permute-start.1) | collective-permute-done | bytes 262176 | tf_op jit(solution)/shard_map/ppermute | solution.py:108
  34.3 0.8 copy-done.4
  35.1 1.0 reduce-precision_convert_fusion.13
  36.1 4.7 %fusion.91 = f32[2,4,256,1056]{2,3,1,0:T(8,128)} fusion(bf16[96,1056,1,1]{1,0,3,2:T(8,128)(2,1)S(1)} %copy-done.27, bf16[2,4,256,32]{2,3,0,1:T(8,128)(2,1)S(1)} %get-tuple-element.53, bf16[2,4,256,32]{2,3,0,1:T(8,128)(2,1)S(1)} %get-tuple-element.52, bf16[2,4,256,32]{2,3,0,1:T(8,128)(2,1)S(1)} %get-tuple-element.51), kind=kOutput, calls=%fused_computation.148 | convolution fusion | flops 416415744 | bytes 9246720 | tf_op jit(solution)/shard_map/...k,kn->...n/dot_general | solution.py:49
  41.1 0.3 fusion.58
  41.4 1.2 copy.79
  42.6 8.1 %all-to-all-start.1 = ((f32[32,40,128]{2,1,0:T(8,128)}), f32[32,40,128]{2,1,0:T(8,128)}, u32[]{:S(2)}, u32[]{:S(2)}) async-start(f32[32,40,128]{2,1,0:T(8,128)} %copy.79), calls=%async_computation.1 | async-start | bytes 1310720 | tf_op jit(solution)/shard_map/all_to_all | solution.py:89
  50.8 4.2 %broadcast_multiply_fusion = (bf16[2,4,256,528]{2,3,1,0:T(8,128)(2,1)S(1)}, bf16[2,4,256,528]{2,3,1,0:T(8,128)(2,1)S(1)}) fusion(bf16[528]{0:T(1024)(128)(2,1)S(1)} %copy-done.29, f32[2,4,256,1056]{2,3,1,0:T(8,128)} %fusion.91), kind=kLoop, calls=%fused_computation.84 | loop fusion | flops 4325376 | bytes 12977184 | tf_op jit(solution)/shard_map/mul | solution.py:178
  55.0 2.1 %select_convert_fusion.1 = (bf16[2,4,256,256]{2,3,1,0:T(8,128)(2,1)}, f32[2,4,256,256]{2,3,1,0:T(8,128)S(1)}) fusion(pred[256,256]{0,1:T(8,128)(4,1)S(1)} %iota_compare_fusion.1, bf16[2,4,256,528]{2,3,1,0:T(8,128)(2,1)S(1)} %get-tuple-element.22, bf16[2,256,528]{1,2,0:T(8,128)(2,1)S(1)} %get-tuple-element.21), kind=kOutput, calls=%fused_computation.25 | convolution fusion | flops 554172416 | bytes 5914624 | tf_op jit(solution)/shard_map/hmif,hjf->hmij/dot_general | solution.py:186
  57.3 6.4 %all-to-all-done.1 = f32[32,40,128]{2,1,0:T(8,128)} async-done(((f32[32,40,128]{2,1,0:T(8,128)}), f32[32,40,128]{2,1,0:T(8,128)}, u32[]{:S(2)}, u32[]{:S(2)}) %all-to-all-start.1) | async-done | bytes 655392 | tf_op jit(solution)/shard_map/all_to_all | solution.py:89
  63.7 0.7 slice.90
  64.4 1.1 slice.92
  65.5 2.2 %fusion.160 = f32[2,1,4,256]{3,1,2,0:T(1,128)S(1)} fusion(bf16[2,4,256,528]{2,3,1,0:T(8,128)(2,1)} %copy-done, bf16[2,528,1,1]{1,0,2,3:T(2,128)(2,1)S(1)} %get-tuple-element.63), kind=kOutput, calls=%fused_computation.239 | convolution fusion | flops 2162688 | bytes 2172992 | tf_op jit(solution)/shard_map/hmif,hf->hmi/dot_general | solution.py:36
  67.8 0.4 fusion.158
  68.2 1.3 %reduce-precision_convert_fusion.2 = (bf16[2,4,256,128]{3,2,0,1:T(8,128)(2,1)}, bf16[2,4,256,128]{3,2,0,1:T(8,128)(2,1)}, bf16[2,4,256,128]{3,2,0,1:T(8,128)(2,1)S(1)}) fusion(f32[2,4,256]{2,0,1:T(2,128)S(1)} %copy.80, bf16[2,256,4,2,128]{4,1,3,2,0:T(8,128)(2,1)S(1)} %copy-done.5), kind=kLoop, calls=%fused_computation.32 | loop fusion | flops 1835008 | bytes 2105344 | tf_op jit(solution)/shard_map/convert_element_type | solution.py:26
  69.5 1.2 fusion.16
  70.7 1.2 fusion.23
  72.0 1.1 fusion.34
  73.2 0.4 select_convert_fusion
  73.6 1.6 %fusion.89 = f32[2,528,128,1]{2,1,3,0:T(8,128)} fusion(bf16[2,4,256,528]{2,3,1,0:T(8,128)(2,1)S(1)} %get-tuple-element.23, bf16[2,4,256,128]{3,2,0,1:T(8,128)(2,1)S(1)} %get-tuple-element.32), kind=kOutput, calls=%fused_computation.145 | convolution fusion | flops 276824064 | bytes 3227648 | tf_op jit(solution)/shard_map/hmif,hmid->hfd/dot_general | solution.py:198
  75.2 1.7 %convolution_bitcast_fusion = f32[2,256,528]{1,2,0:T(8,128)} fusion(bf16[2,4,256,256]{2,3,1,0:T(8,128)(2,1)S(1)} %select_convert_fusion, bf16[2,4,256,528]{2,3,1,0:T(8,128)(2,1)S(1)} %get-tuple-element.23), kind=kOutput, calls=%fused_computation.43 | convolution fusion | flops 553648128 | bytes 4292608 | tf_op jit(solution)/shard_map/hmij,hmif->hjf/dot_general | solution.py:219
  76.9 0.9 fusion.76
  77.8 0.7 fusion.147
  78.5 0.7 fusion.145
  79.2 0.9 select_maximum_fusion
  80.1 4.2 %all-to-all-start.2 = ((f32[32,40,128]{2,1,0:T(8,128)}), f32[32,40,128]{2,1,0:T(8,128)S(1)}, u32[]{:S(2)}, u32[]{:S(2)}) async-start(f32[32,40,128]{2,1,0:T(8,128)} %bitcast.43), calls=%async_computation.2 | async-start | bytes 1310720 | tf_op jit(solution)/shard_map/all_to_all | solution.py:70
  84.4 2.4 %convolution_bitcast_fusion.1 = f32[2,256,128]{2,1,0:T(8,128)} fusion(bf16[2,4,256,256]{2,3,1,0:T(8,128)(2,1)} %get-tuple-element.67, bf16[2,4,256,128]{3,2,0,1:T(8,128)(2,1)S(1)} %copy-done.8), kind=kOutput, calls=%fused_computation.69 | convolution fusion | flops 134217728 | bytes 1835008 | tf_op jit(solution)/shard_map/hmij,hmid->hjd/dot_general | solution.py:220
  87.3 5.4 %multiply_add_fusion = f32[2,4,256,528]{2,3,1,0:T(8,128)} fusion(f32[2,528]{1,0:T(2,128)S(1)} %get-tuple-element.62, f32[2,4,256]{2,1,0:T(4,128)S(1)} %copy.90, bf16[2,4,256,128]{2,3,1,0:T(8,128)(2,1)S(1)} %copy.93, bf16[2,4,256,128]{2,3,1,0:T(8,128)(2,1)S(1)} %copy.91, bf16[2,4,256,256]{2,3,1,0:T(8,128)(2,1)} %copy-done.17, ...), kind=kOutput, calls=%fused_computation.9 | convolution fusion | flops 1402175488 | bytes 7516288 | tf_op jit(solution)/shard_map/hmik,hkf->hmif/dot_general | solution.py:211
  92.6 4.7 %all-to-all-done.2 = f32[32,40,128]{2,1,0:T(8,128)S(1)} async-done(((f32[32,40,128]{2,1,0:T(8,128)}), f32[32,40,128]{2,1,0:T(8,128)S(1)}, u32[]{:S(2)}, u32[]{:S(2)}) %all-to-all-start.2) | async-done | bytes 655392 | tf_op jit(solution)/shard_map/all_to_all | solution.py:70
  97.6 0.3 fusion.64
  97.9 1.3 copy.106
  99.2 4.3 %all-to-all-start.3 = ((f32[32,40,128]{2,1,0:T(8,128)}), f32[32,40,128]{2,1,0:T(8,128)S(1)}, u32[]{:S(2)}, u32[]{:S(2)}) async-start(f32[32,40,128]{2,1,0:T(8,128)} %copy.106), calls=%async_computation.3 | async-start | bytes 1310720 | tf_op jit(solution)/shard_map/all_to_all | solution.py:89
  103.5 5.9 %slice_multiply_fusion = (f32[2,4,256,528]{2,3,1,0:T(8,128)S(1)}, f32[2,4,256,528]{2,3,1,0:T(8,128)S(1)}) fusion(f32[2,4,256,528]{2,3,1,0:T(8,128)} %multiply_add_fusion, f32[2,4,256,1056]{2,3,1,0:T(8,128)} %fusion.91, f32[528]{0:T(1024)S(1)} %copy-done.30), kind=kLoop, calls=%fused_computation.11 | loop fusion | flops 3244032 | bytes 21628992 | tf_op jit(solution)/shard_map/mul | solution.py:144
  109.5 1.4 %reduce-precision_convert_fusion = (bf16[2,4,256,1056]{2,3,1,0:T(8,128)(2,1)S(1)}, bf16[2,4,256,1056]{2,3,1,0:T(8,128)(2,1)S(1)}) fusion(f32[2,4,256,528]{2,3,1,0:T(8,128)S(1)} %get-tuple-element.25, f32[2,4,256,528]{2,3,1,0:T(8,128)S(1)} %get-tuple-element.24), kind=kLoop, calls=%fused_computation.1 | loop fusion | flops 10813440 | bytes 17301504 | tf_op jit(solution)/shard_map/convert_element_type | solution.py:26
  110.9 0.9 fusion.1
  111.8 0.9 fusion.178
  112.7 1.0 fusion.109
  113.8 1.0 fusion.35
  114.8 1.9 %collective-permute-start.3 = (bf16[256,1,2,128]{3,0,1,2:T(8,128)(2,1)S(1)}, bf16[256,1,2,128]{3,0,1,2:T(8,128)(2,1)S(1)}, u32[]{:S(2)}, u32[]{:S(2)}) collective-permute-start(bf16[256,1,2,128]{3,0,1,2:T(8,128)(2,1)S(1)} %get-tuple-element.49), channel_id=1, source_target_pairs={{0,3},{1,0},{2,1},{3,2},{4,7},{5,4},{6,5},{7,6},{8,11},{9,8},{10,9... | collective-permute-start | bytes 393224 | tf_op jit(solution)/shard_map/ppermute | solution.py:121
  116.8 0.9 collective-permute-start.4
  118.0 1.6 %collective-permute-done.3 = bf16[256,1,2,128]{3,0,1,2:T(8,128)(2,1)S(1)} collective-permute-done((bf16[256,1,2,128]{3,0,1,2:T(8,128)(2,1)S(1)}, bf16[256,1,2,128]{3,0,1,2:T(8,128)(2,1)S(1)}, u32[]{:S(2)}, u32[]{:S(2)}) %collective-permute-start.3) | collective-permute-done | bytes 131104 | tf_op jit(solution)/shard_map/ppermute | solution.py:121
  119.9 2.8 %collective-permute-done.4 = bf16[256,1,2,128]{3,0,1,2:T(8,128)(2,1)S(1)} collective-permute-done((bf16[256,1,2,128]{3,0,1,2:T(8,128)(2,1)S(1)}, bf16[256,1,2,128]{3,0,1,2:T(8,128)(2,1)S(1)}, u32[]{:S(2)}, u32[]{:S(2)}) %collective-permute-start.4) | collective-permute-done | bytes 131104 | tf_op jit(solution)/shard_map/ppermute | solution.py:121
  122.9 3.6 %collective-permute-done.5 = bf16[256,1,2,128]{3,0,1,2:T(8,128)(2,1)S(1)} collective-permute-done((bf16[256,1,2,128]{3,0,1,2:T(8,128)(2,1)S(1)}, bf16[256,1,2,128]{3,0,1,2:T(8,128)(2,1)S(1)}, u32[]{:S(2)}, u32[]{:S(2)}) %collective-permute-start.5) | collective-permute-done | bytes 131104 | tf_op jit(solution)/shard_map/ppermute | solution.py:121
  126.8 0.5 fusion.85
  127.3 1.7 %fusion.49 = bf16[256,2,128]{2,0,1:T(8,128)(2,1)S(1)} fusion(f32[2,256,128]{2,1,0:T(8,128)} %convolution_bitcast_fusion.1, f32[2,256,128]{2,1,0:T(8,128)S(1)} %fusion.85, bf16[2,256,528]{1,2,0:T(8,128)(2,1)S(1)} %get-tuple-element.21, f32[2,528,128]{2,1,0:T(8,128)S(1)} %bitcast.181, bf16[528]{0:T(1024)(128)(2,1)S(1)} %copy-done.29), kind=kOutput, calls=%fused_computation.74 | convolution fusion | flops 70078464 | bytes 1737760 | tf_op jit(solution)/shard_map/htf,hfd->htd/dot_general | solution.py:36
  129.1 0.8 copy.108
  130.0 1.7 %slice_multiply_fusion.1 = (f32[2,256,528]{1,2,0:T(8,128)S(1)}, f32[2,256,528]{1,2,0:T(8,128)S(1)}) fusion(f32[2,256,1056]{1,2,0:T(8,128)S(1)} %copy-done.3, f32[528]{0:T(1024)S(1)} %copy-done.30, f32[2,528]{1,0:T(2,128)S(1)} %bitcast.191, f32[2,256,528]{1,2,0:T(8,128)} %convolution_bitcast_fusion, bf16[2,128,528]{1,2,0:T(8,128)(2,1)S(1)} %get-tuple-element.44, ...), kind=kOutput, calls=%fused_computation.91 | convolution fusion | flops 141369344 | bytes 6084800 | tf_op jit(solution)/shard_map/htk,hkf->htf/dot_general | solution.py:235
  132.0 0.3 fusion.50
  132.6 0.4 fusion.125
  133.0 0.4 fusion.48
  133.4 0.8 copy.107
  (100 shorter events, 4.3 us)
Async XLA Ops:
  2.9 20.0 %copy-start.11 = (bf16[256,2,128]{2,1,0:T(2,128)(2,1)}, bf16[256,2,128]{2,1,0:T(2,128)(2,1)S(1)}, u32[]{:S(2)}) copy-start(bf16[256,2,128]{2,1,0:T(2,128)(2,1)S(1)} %get-tuple-element.72) | copy-start | bytes 393220
  3.0 0.8 copy-start.18
  5.3 1.3 copy-start.2
  6.9 9.9 %copy-start.22 = (bf16[256,1,8,128]{3,2,1,0:T(8,128)(2,1)S(1)}, bf16[256,1,8,128]{3,2,1,0:T(8,128)(2,1)}, u32[]{:S(2)}) copy-start(bf16[256,1,8,128]{3,2,1,0:T(8,128)(2,1)} %param.12) | copy-start | bytes 1572868
  6.9 9.9 %copy-start.23 = (bf16[256,1,8,128]{3,2,1,0:T(8,128)(2,1)S(1)}, bf16[256,1,8,128]{3,2,1,0:T(8,128)(2,1)}, u32[]{:S(2)}) copy-start(bf16[256,1,8,128]{3,2,1,0:T(8,128)(2,1)} %param.9) | copy-start | bytes 1572868
  8.1 32.7 %all-to-all-start = ((f32[32,40,128]{2,1,0:T(8,128)}), f32[32,40,128]{2,1,0:T(8,128)S(1)}, u32[]{:S(2)}, u32[]{:S(2)}) async-start(f32[32,40,128]{2,1,0:T(8,128)} %bitcast.26), calls=%async_computation | async-start | bytes 1310720 | tf_op jit(solution)/shard_map/all_to_all | solution.py:70
  17.1 10.4 %collective-permute-start = (bf16[2,256,1,2,128]{4,1,3,2,0:T(8,128)(2,1)S(1)}, bf16[2,256,1,2,128]{4,1,3,2,0:T(8,128)(2,1)S(1)}, u32[]{:S(2)}, u32[]{:S(2)}) collective-permute-start(bf16[2,256,1,2,128]{4,1,3,2,0:T(8,128)(2,1)S(1)} %get-tuple-element.34), channel_id=1, source_target_pairs={{0,1},{1,2},{2,3},{3,0},{4,5},{5,6},{6,7},{7,4},{8,9},{9,10},{10,1... | collective-permute-start | bytes 786440 | tf_op jit(solution)/shard_map/ppermute | solution.py:108
  18.8 15.1 %collective-permute-start.1 = (bf16[2,256,1,2,128]{4,1,3,2,0:T(8,128)(2,1)S(1)}, bf16[2,256,1,2,128]{4,1,3,2,0:T(8,128)(2,1)S(1)}, u32[]{:S(2)}, u32[]{:S(2)}) collective-permute-start(bf16[2,256,1,2,128]{4,1,3,2,0:T(8,128)(2,1)S(1)} %get-tuple-element.35), channel_id=1, source_target_pairs={{0,2},{1,3},{2,0},{3,1},{4,6},{5,7},{6,4},{7,5},{8,10},{9,11},{10,... | collective-permute-start | bytes 786440 | tf_op jit(solution)/shard_map/ppermute | solution.py:108
  22.1 11.8 %collective-permute-start.2 = (bf16[2,256,1,2,128]{4,1,3,2,0:T(8,128)(2,1)S(1)}, bf16[2,256,1,2,128]{4,1,3,2,0:T(8,128)(2,1)S(1)}, u32[]{:S(2)}, u32[]{:S(2)}) collective-permute-start(bf16[2,256,1,2,128]{4,1,3,2,0:T(8,128)(2,1)S(1)} %get-tuple-element.36), channel_id=1, source_target_pairs={{0,3},{1,0},{2,1},{3,2},{4,7},{5,4},{6,5},{7,6},{8,11},{9,8},{10,9... | collective-permute-start | bytes 786440 | tf_op jit(solution)/shard_map/ppermute | solution.py:108
  23.5 33.5 %copy-start.13 = (pred[256,256]{0,1:T(8,128)(4,1)}, pred[256,256]{0,1:T(8,128)(4,1)S(1)}, u32[]{:S(2)}) copy-start(pred[256,256]{0,1:T(8,128)(4,1)S(1)} %iota_compare_fusion.1) | copy-start | bytes 196612
  33.9 2.2 %copy-start.27 = (bf16[96,1056,1,1]{1,0,3,2:T(8,128)(2,1)S(1)}, bf16[96,1056,1,1]{1,0,3,2:T(8,128)(2,1)}, u32[]{:S(2)}) copy-start(bf16[96,1056,1,1]{1,0,3,2:T(8,128)(2,1)} %constant.94) | copy-start | bytes 608260
  34.1 1.1 copy-start.4
  41.1 9.7 %copy-start.29 = (bf16[528]{0:T(1024)(128)(2,1)S(1)}, bf16[528]{0:T(1024)(128)(2,1)}, u32[]{:S(2)}) copy-start(bf16[528]{0:T(1024)(128)(2,1)} %constant.77.clone) | copy-start | bytes 3172
  42.6 21.1 %all-to-all-start.1 = ((f32[32,40,128]{2,1,0:T(8,128)}), f32[32,40,128]{2,1,0:T(8,128)}, u32[]{:S(2)}, u32[]{:S(2)}) async-start(f32[32,40,128]{2,1,0:T(8,128)} %copy.79), calls=%async_computation.1 | async-start | bytes 1310720 | tf_op jit(solution)/shard_map/all_to_all | solution.py:89
  55.0 2.1 %copy-start = (bf16[2,4,256,528]{2,3,1,0:T(8,128)(2,1)}, bf16[2,4,256,528]{2,3,1,0:T(8,128)(2,1)S(1)}, u32[]{:S(2)}) copy-start(bf16[2,4,256,528]{2,3,1,0:T(8,128)(2,1)S(1)} %get-tuple-element.22) | copy-start | bytes 6488068
  65.5 2.3 %copy-start.1 = (bf16[2,4,256,528]{2,3,1,0:T(8,128)(2,1)S(1)}, bf16[2,4,256,528]{2,3,1,0:T(8,128)(2,1)}, u32[]{:S(2)}) copy-start(bf16[2,4,256,528]{2,3,1,0:T(8,128)(2,1)} %copy-done) | copy-start | bytes 6488068
  65.5 2.7 %copy-start.5 = (bf16[2,256,4,2,128]{4,1,3,2,0:T(8,128)(2,1)S(1)}, bf16[2,256,4,2,128]{4,1,3,2,0:T(8,128)(2,1)}, u32[]{:S(2)}) copy-start(bf16[2,256,4,2,128]{4,1,3,2,0:T(8,128)(2,1)} %copy-done.4) | copy-start | bytes 3145732
  69.5 4.1 %copy-start.7 = (bf16[2,4,256,128]{3,2,0,1:T(8,128)(2,1)}, bf16[2,4,256,128]{3,2,0,1:T(8,128)(2,1)S(1)}, u32[]{:S(2)}) copy-start(bf16[2,4,256,128]{3,2,0,1:T(8,128)(2,1)S(1)} %get-tuple-element.32) | copy-start | bytes 1572868
  70.7 1.2 copy-start.12
  70.7 1.3 copy-start.16
  72.0 1.1 copy-start.14
  73.6 3.3 %copy-start.17 = (bf16[2,4,256,256]{2,3,1,0:T(8,128)(2,1)}, bf16[2,4,256,256]{2,3,1,0:T(8,128)(2,1)S(1)}, u32[]{:S(2)}) copy-start(bf16[2,4,256,256]{2,3,1,0:T(8,128)(2,1)S(1)} %select_convert_fusion) | copy-start | bytes 3145732
  77.8 1.4 %copy-start.6 = (f32[2,528,128,1]{2,1,3,0:T(8,128)S(1)}, f32[2,528,128,1]{2,1,3,0:T(8,128)}, u32[]{:S(2)}) copy-start(f32[2,528,128,1]{2,1,3,0:T(8,128)} %fusion.89) | copy-start | bytes 1622020
  79.2 5.2 %copy-start.8 = (bf16[2,4,256,128]{3,2,0,1:T(8,128)(2,1)S(1)}, bf16[2,4,256,128]{3,2,0,1:T(8,128)(2,1)}, u32[]{:S(2)}) copy-start(bf16[2,4,256,128]{3,2,0,1:T(8,128)(2,1)} %copy-done.7) | copy-start | bytes 1572868
  80.1 6.7 %copy-start.10 = (bf16[2,4,256,128]{3,2,0,1:T(8,128)(2,1)S(1)}, bf16[2,4,256,128]{3,2,0,1:T(8,128)(2,1)}, u32[]{:S(2)}) copy-start(bf16[2,4,256,128]{3,2,0,1:T(8,128)(2,1)} %get-tuple-element.30) | copy-start | bytes 1572868
  80.1 6.9 %copy-start.9 = (bf16[2,4,256,128]{3,2,0,1:T(8,128)(2,1)S(1)}, bf16[2,4,256,128]{3,2,0,1:T(8,128)(2,1)}, u32[]{:S(2)}) copy-start(bf16[2,4,256,128]{3,2,0,1:T(8,128)(2,1)} %get-tuple-element.31) | copy-start | bytes 1572868
  80.1 17.3 %all-to-all-start.2 = ((f32[32,40,128]{2,1,0:T(8,128)}), f32[32,40,128]{2,1,0:T(8,128)S(1)}, u32[]{:S(2)}, u32[]{:S(2)}) async-start(f32[32,40,128]{2,1,0:T(8,128)} %bitcast.43), calls=%async_computation.2 | async-start | bytes 1310720 | tf_op jit(solution)/shard_map/all_to_all | solution.py:70
  84.4 2.9 %copy-start.25 = (bf16[2,128,528]{1,2,0:T(8,128)(2,1)S(1)}, bf16[2,128,528]{1,2,0:T(8,128)(2,1)}, u32[]{:S(2)}) copy-start(bf16[2,128,528]{1,2,0:T(8,128)(2,1)} %get-tuple-element.45) | copy-start | bytes 811012
  97.6 5.9 %copy-start.30 = (f32[528]{0:T(1024)S(1)}, f32[528]{0:T(1024)}, u32[]{:S(2)}) copy-start(f32[528]{0:T(1024)} %constant.78.clone) | copy-start | bytes 6340
  99.2 27.5 %all-to-all-start.3 = ((f32[32,40,128]{2,1,0:T(8,128)}), f32[32,40,128]{2,1,0:T(8,128)S(1)}, u32[]{:S(2)}, u32[]{:S(2)}) async-start(f32[32,40,128]{2,1,0:T(8,128)} %copy.106), calls=%async_computation.3 | async-start | bytes 1310720 | tf_op jit(solution)/shard_map/all_to_all | solution.py:89
  109.5 1.4 %copy-start.24 = (bf16[1056,32,1,1]{0,1,2,3:T(8,128)(2,1)S(1)}, bf16[1056,32,1,1]{0,1,2,3:T(8,128)(2,1)}, u32[]{:S(2)}) copy-start(bf16[1056,32,1,1]{0,1,2,3:T(8,128)(2,1)} %constant.96) | copy-start | bytes 202756
  110.9 1.0 copy-start.15
  114.8 4.8 %collective-permute-start.3 = (bf16[256,1,2,128]{3,0,1,2:T(8,128)(2,1)S(1)}, bf16[256,1,2,128]{3,0,1,2:T(8,128)(2,1)S(1)}, u32[]{:S(2)}, u32[]{:S(2)}) collective-permute-start(bf16[256,1,2,128]{3,0,1,2:T(8,128)(2,1)S(1)} %get-tuple-element.49), channel_id=1, source_target_pairs={{0,3},{1,0},{2,1},{3,2},{4,7},{5,4},{6,5},{7,6},{8,11},{9,8},{10,9... | collective-permute-start | bytes 393224 | tf_op jit(solution)/shard_map/ppermute | solution.py:121
  116.8 5.9 %collective-permute-start.4 = (bf16[256,1,2,128]{3,0,1,2:T(8,128)(2,1)S(1)}, bf16[256,1,2,128]{3,0,1,2:T(8,128)(2,1)S(1)}, u32[]{:S(2)}, u32[]{:S(2)}) collective-permute-start(bf16[256,1,2,128]{3,0,1,2:T(8,128)(2,1)S(1)} %get-tuple-element.48), channel_id=1, source_target_pairs={{0,2},{1,3},{2,0},{3,1},{4,6},{5,7},{6,4},{7,5},{8,10},{9,11},{10,... | collective-permute-start | bytes 393224 | tf_op jit(solution)/shard_map/ppermute | solution.py:121
  117.6 8.9 %collective-permute-start.5 = (bf16[256,1,2,128]{3,0,1,2:T(8,128)(2,1)S(1)}, bf16[256,1,2,128]{3,0,1,2:T(8,128)(2,1)S(1)}, u32[]{:S(2)}, u32[]{:S(2)}) collective-permute-start(bf16[256,1,2,128]{3,0,1,2:T(8,128)(2,1)S(1)} %get-tuple-element.47), channel_id=1, source_target_pairs={{0,1},{1,2},{2,3},{3,0},{4,5},{5,6},{6,7},{7,4},{8,9},{9,10},{10,1... | collective-permute-start | bytes 393224 | tf_op jit(solution)/shard_map/ppermute | solution.py:121
  126.7 3.2 %copy-start.21 = (bf16[256,1,8,128]{3,2,1,0:T(8,128)(2,1)}, bf16[256,1,8,128]{3,2,1,0:T(8,128)(2,1)S(1)}, u32[]{:S(2)}) copy-start(bf16[256,1,8,128]{3,2,1,0:T(8,128)(2,1)S(1)} %copy_dynamic-update-slice_fusion) | copy-start | bytes 1572868
  126.8 3.2 %copy-start.3 = (f32[2,256,1056]{1,2,0:T(8,128)S(1)}, f32[2,256,1056]{1,2,0:T(8,128)}, u32[]{:S(2)}) copy-start(f32[2,256,1056]{1,2,0:T(8,128)} %copy-done.2) | copy-start | bytes 6488068
  126.8 3.2 %copy-start.20 = (bf16[256,2,128]{2,0,1:T(8,128)(2,1)S(1)}, bf16[256,2,128]{2,0,1:T(8,128)(2,1)}, u32[]{:S(2)}) copy-start(bf16[256,2,128]{2,0,1:T(8,128)(2,1)} %copy.218) | copy-start | bytes 393220
  130.0 1.7 %copy-start.28 = (bf16[1056,32,1]{0,1,2:T(8,128)(2,1)S(1)}, bf16[1056,32,1]{0,1,2:T(8,128)(2,1)}, u32[]{:S(2)}) copy-start(bf16[1056,32,1]{0,1,2:T(8,128)(2,1)} %constant.97) | copy-start | bytes 202756
  131.7 0.8 copy-start.19
  131.7 1.2 copy-start.26

commit v9 on v7

--- a/solution.py
+++ b/solution.py
@@ -70,8 +70,13 @@
     got = lax.all_to_all(flat.reshape(n, per, width), "ctx", 0, 0, tiled=True)
     src = lax.broadcasted_iota(jnp.int32, (n, n), 1)
     dst = lax.broadcasted_iota(jnp.int32, (n, n), 0)
-    mask = (src > dst if reverse else src < dst).astype(f32)
-    summed = jnp.einsum("ij,jrc->irc", mask, got, precision=highest)
+    mask = (src > dst if reverse else src < dst).astype(bf16)
+    summed = jnp.einsum(
+        "ij,jrc->irc",
+        jnp.concatenate([mask, mask, mask], axis=1),
+        jnp.concatenate(split_parts(got, 3), axis=0),
+        preferred_element_type=f32,
+    )
     back = lax.all_to_all(summed, "ctx", 0, 0, tiled=True).reshape(n * per, width)
     state_out = back[: heads * feat].reshape(heads, feat, width)
     total_out = back[heads * feat : heads * (feat + total_rows)].reshape(heads, total_rows * width)

time: 131 us -> 140 us (1.069)
  waiting for transfers between devices: 22.3 us -> 27.2 us
  starting transfers between devices: 35.2 us -> 38.4 us
  other arithmetic: 10.7 us -> 13 us
    ppermute x3, waiting for transfers between devices: 0.01 us -> 10.4 us  [head_exchange(): lax.ppermute(piece, 'head', [(j, (j + k) % count) for j in range(count)])]
    all_to_all x2, waiting for transfers between devices: 5.33 us -> 0.01 us  [ctx_scan(): got = lax.all_to_all(flat.reshape(n, per, width), 'ctx', 0, 0, tiled=True)]
    all_to_all x2, starting transfers between devices: 12.8 us -> 16.5 us  [ctx_scan(): lax.all_to_all(summed, 'ctx', 0, 0, tiled=True).reshape(n * per, width)]
    convert_element_type x3 -> x5, other arithmetic: 1.65 us -> 3.16 us  [split_parts(): parts.append(hi.astype(bf16))]
  transfers between devices with their start and end apart: 10 -> 10, of which waited for: 3 -> 4; matrix products, arithmetic and copies ran while one was open for 34% -> 29% of each run, Pallas kernels for 0% -> 0%
where the time goes in v9:
time: 140 us; the launch traced here: 139 us
  matrix products  40.3 us (29%)
  starting transfers between devices  38.4 us (27%)
  waiting for transfers between devices  27.2 us (19%)
  local copies, waits for them, and re-layouts  18.5 us (13%)
  other arithmetic  13 us (9%)
    all_to_all x2, waiting for transfers between devices, ctx_scan(): lax.all_to_all(summed, 'ctx', 0, 0, tiled=True).reshape(n * per, width)  16.8 us
    all_to_all x2, starting transfers between devices, ctx_scan(): lax.all_to_all(summed, 'ctx', 0, 0, tiled=True).reshape(n * per, width)  16.5 us
    all_to_all x2, starting transfers between devices, ctx_scan(): got = lax.all_to_all(flat.reshape(n, per, width), 'ctx', 0, 0, tiled=True)  13.4 us
    dot_general x12, matrix products, dot_parts(): term = jnp.einsum(pattern, *args, preferred_element_type=f32)  10.6 us
    ppermute x3, waiting for transfers between devices, head_exchange(): lax.ppermute(piece, 'head', [(j, (j + k) % count) for j in range(count)])  10.4 us
    dot_general x2, matrix products, take_pair(): out = jnp.einsum('...k,kn->...n', lhs, rhs, preferred_element_type=f32)  6.12 us
    ppermute x3, starting transfers between devices, head_exchange(): lax.ppermute(piece, 'head', [(j, (j + k) % count) for j in range(count)])  5.73 us
    dot_general x1, matrix products, body(): jnp.einsum('hmik,hkf->hmif', jnp.concatenate([dscores, grad_hi, grad_hi,...  5.54 us
  transfers between devices with their start and end apart: 10, of which 4 were waited for; matrix products, arithmetic and copies ran while one was open for 29% of the time, Pallas kernels for 0%

profile of v9, /device:TPU:1, one launch (start us, length us, event | category | flops | bytes accessed | tf_op | source)
XLA Modules:
  0.0 138.7 jit_solution(9711095646685781980)
XLA Ops:
  0.7 0.8 add_convert_fusion
  2.0 0.8 reduce-precision_convert_fusion.16
  2.8 1.4 %fusion.112 = f32[2,256,1056]{1,2,0:T(8,128)S(1)} fusion(bf16[96,1056,1]{1,0,2:T(8,128)(2,1)} %constant.95, bf16[2,256,32]{1,2,0:T(8,128)(2,1)S(1)} %get-tuple-element.50, bf16[2,256,32]{1,2,0:T(8,128)(2,1)S(1)} %get-tuple-element.49, bf16[2,256,32]{1,2,0:T(8,128)(2,1)S(1)} %get-tuple-element.48), kind=kOutput, calls=%fused_computation.179 | convolution fusion | flops 104103936 | bytes 2463744 | tf_op jit(solution)/shard_map/...k,kn->...n/dot_general | solution.py:49
  4.2 1.3 copy-done.4
  5.8 1.3 constant_dynamic-slice_fusion
  7.4 0.9 select_maximum_fusion.1
  8.3 8.6 %all-to-all-start = ((f32[32,40,128]{2,1,0:T(8,128)}), f32[32,40,128]{2,1,0:T(8,128)S(1)}, u32[]{:S(2)}, u32[]{:S(2)}) async-start(f32[32,40,128]{2,1,0:T(8,128)} %bitcast.25), calls=%async_computation | async-start | bytes 1310720 | tf_op jit(solution)/shard_map/all_to_all | solution.py:70
  17.3 1.7 %collective-permute-start = (bf16[2,256,1,2,128]{4,1,3,2,0:T(8,128)(2,1)S(1)}, bf16[2,256,1,2,128]{4,1,3,2,0:T(8,128)(2,1)S(1)}, u32[]{:S(2)}, u32[]{:S(2)}) collective-permute-start(bf16[2,256,1,2,128]{4,1,3,2,0:T(8,128)(2,1)S(1)} %get-tuple-element.26), channel_id=1, source_target_pairs={{0,1},{1,2},{2,3},{3,0},{4,5},{5,6},{6,7},{7,4},{8,9},{9,10},{10,1... | collective-permute-start | bytes 786440 | tf_op jit(solution)/shard_map/ppermute | solution.py:94
  19.0 3.3 %collective-permute-start.1 = (bf16[2,256,1,2,128]{4,1,3,2,0:T(8,128)(2,1)S(1)}, bf16[2,256,1,2,128]{4,1,3,2,0:T(8,128)(2,1)S(1)}, u32[]{:S(2)}, u32[]{:S(2)}) collective-permute-start(bf16[2,256,1,2,128]{4,1,3,2,0:T(8,128)(2,1)S(1)} %get-tuple-element.27), channel_id=1, source_target_pairs={{0,2},{1,3},{2,0},{3,1},{4,6},{5,7},{6,4},{7,5},{8,10},{9,11},{10,... | collective-permute-start | bytes 786440 | tf_op jit(solution)/shard_map/ppermute | solution.py:94
  22.3 0.7 collective-permute-start.2
  23.1 0.7 copy.218
  23.8 3.9 %collective-permute-done = bf16[2,256,1,2,128]{4,1,3,2,0:T(8,128)(2,1)S(1)} collective-permute-done((bf16[2,256,1,2,128]{4,1,3,2,0:T(8,128)(2,1)S(1)}, bf16[2,256,1,2,128]{4,1,3,2,0:T(8,128)(2,1)S(1)}, u32[]{:S(2)}, u32[]{:S(2)}) %collective-permute-start) | collective-permute-done | bytes 262176 | tf_op jit(solution)/shard_map/ppermute | solution.py:94
  27.7 6.5 %collective-permute-done.1 = bf16[2,256,1,2,128]{4,1,3,2,0:T(8,128)(2,1)S(1)} collective-permute-done((bf16[2,256,1,2,128]{4,1,3,2,0:T(8,128)(2,1)S(1)}, bf16[2,256,1,2,128]{4,1,3,2,0:T(8,128)(2,1)S(1)}, u32[]{:S(2)}, u32[]{:S(2)}) %collective-permute-start.1) | collective-permute-done | bytes 262176 | tf_op jit(solution)/shard_map/ppermute | solution.py:94
  34.5 0.7 copy-done.6
  35.3 1.0 reduce-precision_convert_fusion.13
  36.2 4.7 %fusion.86 = f32[2,4,256,1056]{2,3,1,0:T(8,128)} fusion(bf16[96,1056,1,1]{1,0,3,2:T(8,128)(2,1)S(1)} %copy-done.24, bf16[2,4,256,32]{2,3,0,1:T(8,128)(2,1)S(1)} %get-tuple-element.45, bf16[2,4,256,32]{2,3,0,1:T(8,128)(2,1)S(1)} %get-tuple-element.44, bf16[2,4,256,32]{2,3,0,1:T(8,128)(2,1)S(1)} %get-tuple-element.43), kind=kOutput, calls=%fused_computation.146 | convolution fusion | flops 416415744 | bytes 9246720 | tf_op jit(solution)/shard_map/...k,kn->...n/dot_general | solution.py:49
  41.2 0.3 fusion.56
  41.5 1.2 copy.79
  42.8 8.1 %all-to-all-start.1 = ((f32[32,40,128]{2,1,0:T(8,128)}), f32[32,40,128]{2,1,0:T(8,128)}, u32[]{:S(2)}, u32[]{:S(2)}) async-start(f32[32,40,128]{2,1,0:T(8,128)} %copy.79), calls=%async_computation.1 | async-start | bytes 1310720 | tf_op jit(solution)/shard_map/all_to_all | solution.py:80
  50.9 4.2 %broadcast_multiply_fusion = (bf16[2,4,256,528]{2,3,1,0:T(8,128)(2,1)S(1)}, bf16[2,4,256,528]{2,3,1,0:T(8,128)(2,1)S(1)}) fusion(bf16[528]{0:T(1024)(128)(2,1)S(1)} %copy-done.26, f32[2,4,256,1056]{2,3,1,0:T(8,128)} %fusion.86), kind=kLoop, calls=%fused_computation.84 | loop fusion | flops 4325376 | bytes 12977184 | tf_op jit(solution)/shard_map/mul | solution.py:164
  55.1 2.1 %select_convert_fusion.1 = (bf16[2,4,256,256]{2,3,1,0:T(8,128)(2,1)}, f32[2,4,256,256]{2,3,1,0:T(8,128)S(1)}) fusion(pred[256,256]{0,1:T(8,128)(4,1)S(1)} %iota_compare_fusion.1, bf16[2,4,256,528]{2,3,1,0:T(8,128)(2,1)S(1)} %get-tuple-element.14, bf16[2,256,528]{1,2,0:T(8,128)(2,1)S(1)} %get-tuple-element.13), kind=kOutput, calls=%fused_computation.25 | convolution fusion | flops 554172416 | bytes 5914624 | tf_op jit(solution)/shard_map/hmif,hjf->hmij/dot_general | solution.py:172
  57.4 6.4 %all-to-all-done.1 = f32[32,40,128]{2,1,0:T(8,128)} async-done(((f32[32,40,128]{2,1,0:T(8,128)}), f32[32,40,128]{2,1,0:T(8,128)}, u32[]{:S(2)}, u32[]{:S(2)}) %all-to-all-start.1) | async-done | bytes 655392 | tf_op jit(solution)/shard_map/all_to_all | solution.py:80
  63.8 0.7 slice.91
  64.5 1.1 slice.86
  65.6 0.6 fusion.174
  66.2 2.0 %fusion.155 = f32[2,1,4,256]{3,1,2,0:T(1,128)S(1)} fusion(bf16[2,4,256,528]{2,3,1,0:T(8,128)(2,1)} %copy-done.2, bf16[2,528,1,1]{1,0,2,3:T(2,128)(2,1)S(1)} %get-tuple-element.55), kind=kOutput, calls=%fused_computation.237 | convolution fusion | flops 2162688 | bytes 2172992 | tf_op jit(solution)/shard_map/hmif,hf->hmi/dot_general | solution.py:36
  68.3 0.4 fusion.153
  68.7 1.2 fusion.14
  69.9 1.2 fusion.21
  71.1 1.6 %fusion.171 = (bf16[2,4,256,128]{3,2,0,1:T(8,128)(2,1)}, bf16[2,4,256,128]{3,2,0,1:T(8,128)(2,1)}, bf16[2,4,256,128]{3,2,0,1:T(8,128)(2,1)}) fusion(f32[2,4,256]{2,0,1:T(2,128)S(1)} %copy.80, bf16[2,256,4,2,128]{4,1,3,2,0:T(8,128)(2,1)S(1)} %copy-done.7), kind=kLoop, calls=%fused_computation.255 | loop fusion | flops 1835008 | bytes 2105344 | tf_op jit(solution)/shard_map/convert_element_type | solution.py:182
  72.7 1.1 fusion.32
  73.8 0.7 fusion.140
  74.5 0.7 fusion.142
  75.2 1.8 %fusion.83 = f32[2,528,128,1]{2,1,3,0:T(8,128)S(1)} fusion(bf16[2,4,256,528]{2,3,1,0:T(8,128)(2,1)S(1)} %get-tuple-element.15, bf16[2,4,256,128]{3,2,0,1:T(8,128)(2,1)} %get-tuple-element.22), kind=kOutput, calls=%fused_computation.142 | convolution fusion | flops 276824064 | bytes 3227648 | tf_op jit(solution)/shard_map/hmif,hmid->hfd/dot_general | solution.py:184
  77.0 0.9 select_maximum_fusion
  77.9 4.8 %all-to-all-start.2 = ((f32[32,40,128]{2,1,0:T(8,128)}), f32[32,40,128]{2,1,0:T(8,128)}, u32[]{:S(2)}, u32[]{:S(2)}) async-start(f32[32,40,128]{2,1,0:T(8,128)} %bitcast.188), calls=%async_computation.2 | async-start | bytes 1310720 | tf_op jit(solution)/shard_map/all_to_all | solution.py:70
  82.7 2.6 %select_convert_fusion = bf16[2,4,256,256]{2,3,1,0:T(8,128)(2,1)} fusion(f32[2,4,256]{2,1,0:T(4,128)S(1)} %copy.87, pred[256,256]{0,1:T(8,128)(4,1)} %copy-done.11, bf16[2,4,256,128]{3,2,0,1:T(8,128)(2,1)} %get-tuple-element.22, bf16[256,2,128]{2,1,0:T(2,128)(2,1)} %copy-done.9), kind=kOutput, calls=%fused_computation.24 | convolution fusion | flops 135790592 | bytes 1777664 | tf_op jit(solution)/shard_map/hmid,hjd->hmij/dot_general | solution.py:190
  85.2 2.1 %copy.88 = bf16[2,4,256,128]{2,3,1,0:T(8,128)(2,1)} copy(bf16[2,4,256,128]{3,2,0,1:T(8,128)(2,1)} %get-tuple-element.23) | data formatting | bytes 1048576 | tf_op jit(solution)/shard_map/convert_element_type | solution.py:26
  87.3 2.0 %copy.90 = bf16[2,4,256,128]{2,3,1,0:T(8,128)(2,1)} copy(bf16[2,4,256,128]{3,2,0,1:T(8,128)(2,1)} %get-tuple-element.24) | data formatting | bytes 1048576 | tf_op jit(solution)/shard_map/convert_element_type | solution.py:28
  89.5 5.5 %slice_multiply_fusion = (f32[2,4,256,528]{2,3,1,0:T(8,128)S(1)}, f32[2,4,256,528]{2,3,1,0:T(8,128)S(1)}) fusion(f32[2,4,256,1056]{2,3,1,0:T(8,128)} %fusion.86, f32[2,528]{1,0:T(2,128)S(1)} %copy-done.27, f32[2,4,256]{2,1,0:T(4,128)S(1)} %copy.87, f32[528]{0:T(1024)S(1)} %copy-done.28, bf16[2,4,256,128]{2,3,1,0:T(8,128)(2,1)} %copy.90, ...), kind=kOutput, calls=%fused_computation.11 | convolution fusion | flops 1405419520 | bytes 20494528 | tf_op jit(solution)/shard_map/hmik,hkf->hmif/dot_general | solution.py:197
  95.0 1.5 %reduce-precision_convert_fusion = (bf16[2,4,256,1056]{2,3,1,0:T(8,128)(2,1)S(1)}, bf16[2,4,256,1056]{2,3,1,0:T(8,128)(2,1)S(1)}) fusion(f32[2,4,256,528]{2,3,1,0:T(8,128)S(1)} %get-tuple-element.17, f32[2,4,256,528]{2,3,1,0:T(8,128)S(1)} %get-tuple-element.16), kind=kLoop, calls=%fused_computation.1 | loop fusion | flops 10813440 | bytes 17301504 | tf_op jit(solution)/shard_map/convert_element_type | solution.py:26
  96.6 0.9 fusion.1
  97.5 0.9 fusion.173
  98.4 1.0 fusion.104
  99.5 1.0 fusion.33
  100.5 0.7 fusion.172
  101.2 1.9 %collective-permute-start.3 = (bf16[256,1,2,128]{3,0,1,2:T(8,128)(2,1)}, bf16[256,1,2,128]{3,0,1,2:T(8,128)(2,1)}, u32[]{:S(2)}, u32[]{:S(2)}) collective-permute-start(bf16[256,1,2,128]{3,0,1,2:T(8,128)(2,1)} %get-tuple-element.41), channel_id=1, source_target_pairs={{0,3},{1,0},{2,1},{3,2},{4,7},{5,4},{6,5},{7,6},{8,11},{9,8},{10,9... | collective-permute-start | bytes 393224 | tf_op jit(solution)/shard_map/ppermute | solution.py:107
  103.1 0.9 collective-permute-start.4
  104.1 1.1 convolution_bitcast_fusion.1
  105.5 1.8 %convolution_bitcast_fusion = f32[2,256,528]{1,2,0:T(8,128)} fusion(bf16[2,4,256,256]{2,3,1,0:T(8,128)(2,1)S(1)} %copy-done.15, bf16[2,4,256,528]{2,3,1,0:T(8,128)(2,1)S(1)} %get-tuple-element.15), kind=kOutput, calls=%fused_computation.43 | convolution fusion | flops 553648128 | bytes 4292608 | tf_op jit(solution)/shard_map/hmij,hmif->hjf/dot_general | solution.py:211
  107.3 1.3 reduce-precision_convert_fusion.5
  108.9 1.2 copy.105
  110.2 8.3 %all-to-all-start.3 = ((f32[32,40,128]{2,1,0:T(8,128)}), f32[32,40,128]{2,1,0:T(8,128)S(1)}, u32[]{:S(2)}, u32[]{:S(2)}) async-start(f32[32,40,128]{2,1,0:T(8,128)} %copy.105), calls=%async_computation.3 | async-start | bytes 1310720 | tf_op jit(solution)/shard_map/all_to_all | solution.py:80
  118.5 1.1 copy_dynamic-update-slice_fusion.2
  119.7 1.1 copy_dynamic-update-slice_fusion.1
  121.1 10.3 %all-to-all-done.3 = f32[32,40,128]{2,1,0:T(8,128)S(1)} async-done(((f32[32,40,128]{2,1,0:T(8,128)}), f32[32,40,128]{2,1,0:T(8,128)S(1)}, u32[]{:S(2)}, u32[]{:S(2)}) %all-to-all-start.3) | async-done | bytes 655392 | tf_op jit(solution)/shard_map/all_to_all | solution.py:80
  131.5 0.5 fusion.80
  132.0 1.6 %fusion.47 = bf16[256,2,128]{2,0,1:T(8,128)(2,1)S(1)} fusion(f32[2,256,128]{2,1,0:T(8,128)} %convolution_bitcast_fusion.1, f32[2,256,128]{2,1,0:T(8,128)S(1)} %fusion.80, bf16[2,256,528]{1,2,0:T(8,128)(2,1)S(1)} %get-tuple-element.13, f32[2,528,128]{2,1,0:T(8,128)S(1)} %bitcast.183, bf16[528]{0:T(1024)(128)(2,1)S(1)} %copy-done.26), kind=kOutput, calls=%fused_computation.74 | convolution fusion | flops 70078464 | bytes 1737760 | tf_op jit(solution)/shard_map/htf,hfd->htd/dot_general | solution.py:36
  133.6 0.8 copy.108
  134.5 1.7 %slice_multiply_fusion.1 = (f32[2,256,528]{1,2,0:T(8,128)S(1)}, f32[2,256,528]{1,2,0:T(8,128)S(1)}) fusion(f32[2,256,1056]{1,2,0:T(8,128)S(1)} %copy-done.5, f32[528]{0:T(1024)S(1)} %copy-done.28, f32[2,528]{1,0:T(2,128)S(1)} %bitcast.194, f32[2,256,528]{1,2,0:T(8,128)} %convolution_bitcast_fusion, bf16[2,128,528]{1,2,0:T(8,128)(2,1)S(1)} %get-tuple-element.36, ...), kind=kOutput, calls=%fused_computation.91 | convolution fusion | flops 141369344 | bytes 6084800 | tf_op jit(solution)/shard_map/htk,hkf->htf/dot_general | solution.py:216
  136.6 0.3 fusion.48
  137.1 0.4 fusion.120
  137.5 0.4 fusion.46
  137.9 0.8 copy.107
  (96 shorter events, 4.1 us)
Async XLA Ops:
  0.6 1.1 copy-start
  2.0 0.8 copy-start.16
  4.2 1.3 copy-start.4
  5.8 11.2 %copy-start.20 = (bf16[256,1,8,128]{3,2,1,0:T(8,128)(2,1)S(1)}, bf16[256,1,8,128]{3,2,1,0:T(8,128)(2,1)}, u32[]{:S(2)}) copy-start(bf16[256,1,8,128]{3,2,1,0:T(8,128)(2,1)} %param.12) | copy-start | bytes 1572868
  5.8 11.2 %copy-start.21 = (bf16[256,1,8,128]{3,2,1,0:T(8,128)(2,1)S(1)}, bf16[256,1,8,128]{3,2,1,0:T(8,128)(2,1)}, u32[]{:S(2)}) copy-start(bf16[256,1,8,128]{3,2,1,0:T(8,128)(2,1)} %param.9) | copy-start | bytes 1572868
  7.1 16.0 %copy-start.9 = (bf16[256,2,128]{2,1,0:T(2,128)(2,1)}, bf16[256,2,128]{2,1,0:T(2,128)(2,1)S(1)}, u32[]{:S(2)}) copy-start(bf16[256,2,128]{2,1,0:T(2,128)(2,1)S(1)} %constant_dynamic-slice_fusion) | copy-start | bytes 393220
  8.3 32.6 %all-to-all-start = ((f32[32,40,128]{2,1,0:T(8,128)}), f32[32,40,128]{2,1,0:T(8,128)S(1)}, u32[]{:S(2)}, u32[]{:S(2)}) async-start(f32[32,40,128]{2,1,0:T(8,128)} %bitcast.25), calls=%async_computation | async-start | bytes 1310720 | tf_op jit(solution)/shard_map/all_to_all | solution.py:70
  17.3 10.3 %collective-permute-start = (bf16[2,256,1,2,128]{4,1,3,2,0:T(8,128)(2,1)S(1)}, bf16[2,256,1,2,128]{4,1,3,2,0:T(8,128)(2,1)S(1)}, u32[]{:S(2)}, u32[]{:S(2)}) collective-permute-start(bf16[2,256,1,2,128]{4,1,3,2,0:T(8,128)(2,1)S(1)} %get-tuple-element.26), channel_id=1, source_target_pairs={{0,1},{1,2},{2,3},{3,0},{4,5},{5,6},{6,7},{7,4},{8,9},{9,10},{10,1... | collective-permute-start | bytes 786440 | tf_op jit(solution)/shard_map/ppermute | solution.py:94
  19.0 15.1 %collective-permute-start.1 = (bf16[2,256,1,2,128]{4,1,3,2,0:T(8,128)(2,1)S(1)}, bf16[2,256,1,2,128]{4,1,3,2,0:T(8,128)(2,1)S(1)}, u32[]{:S(2)}, u32[]{:S(2)}) collective-permute-start(bf16[2,256,1,2,128]{4,1,3,2,0:T(8,128)(2,1)S(1)} %get-tuple-element.27), channel_id=1, source_target_pairs={{0,2},{1,3},{2,0},{3,1},{4,6},{5,7},{6,4},{7,5},{8,10},{9,11},{10,... | collective-permute-start | bytes 786440 | tf_op jit(solution)/shard_map/ppermute | solution.py:94
  22.3 11.8 %collective-permute-start.2 = (bf16[2,256,1,2,128]{4,1,3,2,0:T(8,128)(2,1)S(1)}, bf16[2,256,1,2,128]{4,1,3,2,0:T(8,128)(2,1)S(1)}, u32[]{:S(2)}, u32[]{:S(2)}) collective-permute-start(bf16[2,256,1,2,128]{4,1,3,2,0:T(8,128)(2,1)S(1)} %get-tuple-element.28), channel_id=1, source_target_pairs={{0,3},{1,0},{2,1},{3,2},{4,7},{5,4},{6,5},{7,6},{8,11},{9,8},{10,9... | collective-permute-start | bytes 786440 | tf_op jit(solution)/shard_map/ppermute | solution.py:94
  23.8 33.5 %copy-start.11 = (pred[256,256]{0,1:T(8,128)(4,1)}, pred[256,256]{0,1:T(8,128)(4,1)S(1)}, u32[]{:S(2)}) copy-start(pred[256,256]{0,1:T(8,128)(4,1)S(1)} %iota_compare_fusion.1) | copy-start | bytes 196612
  34.1 2.1 %copy-start.24 = (bf16[96,1056,1,1]{1,0,3,2:T(8,128)(2,1)S(1)}, bf16[96,1056,1,1]{1,0,3,2:T(8,128)(2,1)}, u32[]{:S(2)}) copy-start(bf16[96,1056,1,1]{1,0,3,2:T(8,128)(2,1)} %constant.94) | copy-start | bytes 608260
  34.3 1.0 copy-start.6
  41.2 9.7 %copy-start.26 = (bf16[528]{0:T(1024)(128)(2,1)S(1)}, bf16[528]{0:T(1024)(128)(2,1)}, u32[]{:S(2)}) copy-start(bf16[528]{0:T(1024)(128)(2,1)} %constant.77.clone) | copy-start | bytes 3172
  42.8 21.1 %all-to-all-start.1 = ((f32[32,40,128]{2,1,0:T(8,128)}), f32[32,40,128]{2,1,0:T(8,128)}, u32[]{:S(2)}, u32[]{:S(2)}) async-start(f32[32,40,128]{2,1,0:T(8,128)} %copy.79), calls=%async_computation.1 | async-start | bytes 1310720 | tf_op jit(solution)/shard_map/all_to_all | solution.py:80
  55.1 2.1 %copy-start.2 = (bf16[2,4,256,528]{2,3,1,0:T(8,128)(2,1)}, bf16[2,4,256,528]{2,3,1,0:T(8,128)(2,1)S(1)}, u32[]{:S(2)}) copy-start(bf16[2,4,256,528]{2,3,1,0:T(8,128)(2,1)S(1)} %get-tuple-element.14) | copy-start | bytes 6488068
  65.6 2.7 %copy-start.3 = (bf16[2,4,256,528]{2,3,1,0:T(8,128)(2,1)S(1)}, bf16[2,4,256,528]{2,3,1,0:T(8,128)(2,1)}, u32[]{:S(2)}) copy-start(bf16[2,4,256,528]{2,3,1,0:T(8,128)(2,1)} %copy-done.2) | copy-start | bytes 6488068
  69.9 1.2 copy-start.7
  69.9 2.8 %copy-start.10 = (bf16[256,2,128]{2,1,0:T(2,128)(2,1)S(1)}, bf16[256,2,128]{2,1,0:T(2,128)(2,1)}, u32[]{:S(2)}) copy-start(bf16[256,2,128]{2,1,0:T(2,128)(2,1)} %copy-done.9) | copy-start | bytes 393220
  69.9 2.8 %copy-start.13 = (bf16[2,4,256,256]{2,3,1,0:T(8,128)(2,1)S(1)}, bf16[2,4,256,256]{2,3,1,0:T(8,128)(2,1)}, u32[]{:S(2)}) copy-start(bf16[2,4,256,256]{2,3,1,0:T(8,128)(2,1)} %get-tuple-element.59) | copy-start | bytes 3145732
  77.9 29.4 %all-to-all-start.2 = ((f32[32,40,128]{2,1,0:T(8,128)}), f32[32,40,128]{2,1,0:T(8,128)}, u32[]{:S(2)}, u32[]{:S(2)}) async-start(f32[32,40,128]{2,1,0:T(8,128)} %bitcast.188), calls=%async_computation.2 | async-start | bytes 1310720 | tf_op jit(solution)/shard_map/all_to_all | solution.py:70
  85.2 4.2 %copy-start.27 = (f32[2,528]{1,0:T(2,128)S(1)}, f32[2,528]{1,0:T(2,128)}, u32[]{:S(2)}) copy-start(f32[2,528]{1,0:T(2,128)} %get-tuple-element.54) | copy-start | bytes 12676
  85.2 4.2 %copy-start.28 = (f32[528]{0:T(1024)S(1)}, f32[528]{0:T(1024)}, u32[]{:S(2)}) copy-start(f32[528]{0:T(1024)} %constant.78.clone) | copy-start | bytes 6340
  95.0 1.6 %copy-start.22 = (bf16[1056,32,1,1]{0,1,2,3:T(8,128)(2,1)S(1)}, bf16[1056,32,1,1]{0,1,2,3:T(8,128)(2,1)}, u32[]{:S(2)}) copy-start(bf16[1056,32,1,1]{0,1,2,3:T(8,128)(2,1)} %constant.96) | copy-start | bytes 202756
  96.6 1.0 copy-start.12
  98.4 5.6 %copy-start.8 = (bf16[2,4,256,128]{3,2,0,1:T(8,128)(2,1)S(1)}, bf16[2,4,256,128]{3,2,0,1:T(8,128)(2,1)}, u32[]{:S(2)}) copy-start(bf16[2,4,256,128]{3,2,0,1:T(8,128)(2,1)} %get-tuple-element.22) | copy-start | bytes 1572868
  98.4 5.6 %copy-start.14 = (bf16[2,4,256,256]{2,3,1,0:T(8,128)(2,1)S(1)}, bf16[2,4,256,256]{2,3,1,0:T(8,128)(2,1)}, u32[]{:S(2)}) copy-start(bf16[2,4,256,256]{2,3,1,0:T(8,128)(2,1)} %get-tuple-element.59) | copy-start | bytes 3145732
  100.5 5.0 %copy-start.15 = (bf16[2,4,256,256]{2,3,1,0:T(8,128)(2,1)S(1)}, bf16[2,4,256,256]{2,3,1,0:T(8,128)(2,1)}, u32[]{:S(2)}) copy-start(bf16[2,4,256,256]{2,3,1,0:T(8,128)(2,1)} %select_convert_fusion) | copy-start | bytes 3145732
  101.2 17.3 %collective-permute-start.3 = (bf16[256,1,2,128]{3,0,1,2:T(8,128)(2,1)}, bf16[256,1,2,128]{3,0,1,2:T(8,128)(2,1)}, u32[]{:S(2)}, u32[]{:S(2)}) collective-permute-start(bf16[256,1,2,128]{3,0,1,2:T(8,128)(2,1)} %get-tuple-element.41), channel_id=1, source_target_pairs={{0,3},{1,0},{2,1},{3,2},{4,7},{5,4},{6,5},{7,6},{8,11},{9,8},{10,9... | collective-permute-start | bytes 393224 | tf_op jit(solution)/shard_map/ppermute | solution.py:107
  103.1 16.5 %collective-permute-start.4 = (bf16[256,1,2,128]{3,0,1,2:T(8,128)(2,1)}, bf16[256,1,2,128]{3,0,1,2:T(8,128)(2,1)}, u32[]{:S(2)}, u32[]{:S(2)}) collective-permute-start(bf16[256,1,2,128]{3,0,1,2:T(8,128)(2,1)} %get-tuple-element.40), channel_id=1, source_target_pairs={{0,2},{1,3},{2,0},{3,1},{4,6},{5,7},{6,4},{7,5},{8,10},{9,11},{10,... | collective-permute-start | bytes 393224 | tf_op jit(solution)/shard_map/ppermute | solution.py:107
  104.0 16.8 %collective-permute-start.5 = (bf16[256,1,2,128]{3,0,1,2:T(8,128)(2,1)}, bf16[256,1,2,128]{3,0,1,2:T(8,128)(2,1)S(1)}, u32[]{:S(2)}, u32[]{:S(2)}) collective-permute-start(bf16[256,1,2,128]{3,0,1,2:T(8,128)(2,1)} %get-tuple-element.39), channel_id=1, source_target_pairs={{0,1},{1,2},{2,3},{3,0},{4,5},{5,6},{6,7},{7,4},{8,9},{9,10},{10,1... | collective-permute-start | bytes 393224 | tf_op jit(solution)/shard_map/ppermute | solution.py:107
  110.2 21.2 %all-to-all-start.3 = ((f32[32,40,128]{2,1,0:T(8,128)}), f32[32,40,128]{2,1,0:T(8,128)S(1)}, u32[]{:S(2)}, u32[]{:S(2)}) async-start(f32[32,40,128]{2,1,0:T(8,128)} %copy.105), calls=%async_computation.3 | async-start | bytes 1310720 | tf_op jit(solution)/shard_map/all_to_all | solution.py:80
  121.0 13.4 %copy-start.19 = (bf16[256,1,8,128]{3,2,1,0:T(8,128)(2,1)}, bf16[256,1,8,128]{3,2,1,0:T(8,128)(2,1)S(1)}, u32[]{:S(2)}) copy-start(bf16[256,1,8,128]{3,2,1,0:T(8,128)(2,1)S(1)} %copy_dynamic-update-slice_fusion) | copy-start | bytes 1572868
  131.5 3.1 %copy-start.5 = (f32[2,256,1056]{1,2,0:T(8,128)S(1)}, f32[2,256,1056]{1,2,0:T(8,128)}, u32[]{:S(2)}) copy-start(f32[2,256,1056]{1,2,0:T(8,128)} %copy-done.4) | copy-start | bytes 6488068
  131.5 3.1 %copy-start.18 = (bf16[256,2,128]{2,0,1:T(8,128)(2,1)S(1)}, bf16[256,2,128]{2,0,1:T(8,128)(2,1)}, u32[]{:S(2)}) copy-start(bf16[256,2,128]{2,0,1:T(8,128)(2,1)} %copy.218) | copy-start | bytes 393220
  134.5 1.7 %copy-start.25 = (bf16[1056,32,1]{0,1,2:T(8,128)(2,1)S(1)}, bf16[1056,32,1]{0,1,2:T(8,128)(2,1)}, u32[]{:S(2)}) copy-start(bf16[1056,32,1]{0,1,2:T(8,128)(2,1)} %constant.97) | copy-start | bytes 202756
  136.3 0.8 copy-start.17
  136.3 1.2 copy-start.23
  136.3 2.4 %copy-start.1 = (bf16[256,8,128]{2,1,0:T(8,128)(2,1)S(1)}, bf16[256,8,128]{2,1,0:T(8,128)(2,1)}, u32[]{:S(2)}) copy-start(bf16[256,8,128]{2,1,0:T(8,128)(2,1)} %param.10) | copy-start | bytes 1572868

commit v10 on v8

--- a/solution.py
+++ b/solution.py
@@ -90,11 +90,6 @@
     state_out = back[: heads * feat].reshape(heads, feat, width)
     total_out = back[heads * feat : heads * (feat + total_rows)].reshape(heads, total_rows * width)
     return state_out, total_out[:, :feat]
-
-
-def ctx_scan(state, total, reverse):
-    summed = scan_sum(scan_send(state, total), reverse)
-    return scan_return(summed, state.shape[0], state.shape[1])
 
 
 def head_exchange(stacked, owned):
@@ -171,7 +166,12 @@
     value_heads = value_part.transpose(1, 0, 2)
     block_state = jnp.einsum("htf,htd->hfd", key_feat, value_heads, preferred_element_type=f32)
     block_total = jnp.sum(key_feat, 1, dtype=f32)
-    state_in, total_in = ctx_scan(block_state, block_total, False)
+    block_state, block_total, query_part, grad_part = lax.optimization_barrier(
+        (block_state, block_total, query_part, grad_part)
+    )
+    state_in, total_in = scan_return(
+        scan_sum(scan_send(block_state, block_total), False), block_state.shape[0], block_state.shape[1]
+    )
 
     query_one, query_two = sketch_parts(query_part, projector, "tmhd,df->hmtf")
     query_feat = tri_features(query_one, query_two, take_a, take_b)

time: 135 us -> 135 us (level)
  waiting for transfers between devices: 29.6 us -> 34.3 us
  matrix products: 39.3 us -> 34.8 us
  starting transfers between devices: 33.9 us -> 31.1 us
  local copies, waits for them, and re-layouts: 12.4 us -> 14.1 us
    all_to_all x2, waiting for transfers between devices: 4.75 us -> 14.6 us  [scan_send(): return lax.all_to_all(flat.reshape(n, per, width), 'ctx', 0, 0, tiled=True)]
    ppermute x3, waiting for transfers between devices: 10.4 us -> 5.18 us  [head_exchange(): lax.ppermute(piece, 'head', [(j, (j + k) % count) for j in range(count)])]
    mul x1 -> x0, other arithmetic: 4.22 us -> none  [body(): query_wfeat = query_feat * weight]
    convert_element_type x0 -> x1, other arithmetic: none -> 4.2 us  [tri_features(): return (first * second * (1.0 / width)).astype(bf16)]
    all_to_all x2, starting transfers between devices: 12.4 us -> 8.86 us  [scan_return(): lax.all_to_all(summed, 'ctx', 0, 0, tiled=True).reshape(n * per, width)]
    dot_general x12, matrix products: 10.9 us -> 8.31 us  [dot_parts(): term = jnp.einsum(pattern, *args, preferred_element_type=f32)]
    unnamed x65 -> x49, local copies, waits for them, and re-layouts: 4.92 us -> 5.33 us
  transfers between devices with their start and end apart: 10 -> 10, of which waited for: 7 -> 7; matrix products, arithmetic and copies ran while one was open for 25% -> 26% of each run, Pallas kernels for 0% -> 0%
where the time goes in v10:
time: 135 us; the launch traced here: 134 us
  matrix products  34.8 us (26%)
  waiting for transfers between devices  34.3 us (25%)
  starting transfers between devices  31.1 us (23%)
  other arithmetic  18.4 us (14%)
  local copies, waits for them, and re-layouts  14.1 us (10%)
    all_to_all x2, waiting for transfers between devices, scan_send(): return lax.all_to_all(flat.reshape(n, per, width), 'ctx', 0, 0, tiled=True)  14.6 us
    all_to_all x2, starting transfers between devices, scan_send(): return lax.all_to_all(flat.reshape(n, per, width), 'ctx', 0, 0, tiled=True)  12.7 us
    all_to_all x2, starting transfers between devices, scan_return(): lax.all_to_all(summed, 'ctx', 0, 0, tiled=True).reshape(n * per, width)  8.86 us
    dot_general x12, matrix products, dot_parts(): term = jnp.einsum(pattern, *args, preferred_element_type=f32)  8.31 us
    ppermute x3, waiting for transfers between devices, head_return(): lax.ppermute(piece, 'head', [(j, (j - k) % count) for j in range(count)])  7.79 us
    all_to_all x2, waiting for transfers between devices, scan_return(): lax.all_to_all(summed, 'ctx', 0, 0, tiled=True).reshape(n * per, width)  6.7 us
    ppermute x3, starting transfers between devices, head_exchange(): lax.ppermute(piece, 'head', [(j, (j + k) % count) for j in range(count)])  6.57 us
    dot_general x2, matrix products, take_pair(): out = jnp.einsum('...k,kn->...n', lhs, rhs, preferred_element_type=f32)  6.13 us
  transfers between devices with their start and end apart: 10, of which 7 were waited for; matrix products, arithmetic and copies ran while one was open for 26% of the time, Pallas kernels for 0%

profile of v10, /device:TPU:1, one launch (start us, length us, event | category | flops | bytes accessed | tf_op | source)
XLA Modules:
  0.0 134.0 jit_solution(11466960662535457655)
XLA Ops:
  0.7 1.4 %copy.66 = bf16[256,1,8,128]{0,3,2,1:T(8,128)(2,1)S(1)} copy(bf16[256,1,8,128]{3,2,1,0:T(8,128)(2,1)} %param.9) | data formatting | bytes 1048576 | tf_op args[0]
  2.1 1.3 copy.67
  3.5 2.5 %collective-permute-start = (bf16[2,256,1,2,128]{1,4,2,3,0:T(8,128)(2,1)S(1)}, bf16[2,256,1,2,128]{1,4,2,3,0:T(8,128)(2,1)S(1)}, u32[]{:S(2)}, u32[]{:S(2)}) collective-permute-start(bf16[2,256,1,2,128]{1,4,2,3,0:T(8,128)(2,1)S(1)} %get-tuple-element.39), channel_id=1, source_target_pairs={{0,1},{1,2},{2,3},{3,0},{4,5},{5,6},{6,7},{7,4},{8,9},{9,10},{10,1... | collective-permute-start | bytes 786440 | tf_op jit(solution)/shard_map/ppermute | solution.py:103
  6.1 3.3 %collective-permute-start.1 = (bf16[2,256,1,2,128]{1,4,2,3,0:T(8,128)(2,1)S(1)}, bf16[2,256,1,2,128]{1,4,2,3,0:T(8,128)(2,1)S(1)}, u32[]{:S(2)}, u32[]{:S(2)}) collective-permute-start(bf16[2,256,1,2,128]{1,4,2,3,0:T(8,128)(2,1)S(1)} %get-tuple-element.40), channel_id=1, source_target_pairs={{0,2},{1,3},{2,0},{3,1},{4,6},{5,7},{6,4},{7,5},{8,10},{9,11},{10,... | collective-permute-start | bytes 786440 | tf_op jit(solution)/shard_map/ppermute | solution.py:103
  9.4 0.7 collective-permute-start.2
  10.1 0.6 iota_compare_fusion.1
  11.1 0.8 reduce-precision_convert_fusion.16
  11.9 1.4 %fusion.119 = f32[2,256,1056]{1,2,0:T(8,128)S(1)} fusion(bf16[96,1056,1]{1,0,2:T(8,128)(2,1)} %constant.94, bf16[2,256,32]{1,2,0:T(8,128)(2,1)S(1)} %get-tuple-element.65, bf16[2,256,32]{1,2,0:T(8,128)(2,1)S(1)} %get-tuple-element.64, bf16[2,256,32]{1,2,0:T(8,128)(2,1)S(1)} %get-tuple-element.63), kind=kOutput, calls=%fused_computation.183 | convolution fusion | flops 104103936 | bytes 2463744 | tf_op jit(solution)/shard_map/...k,kn->...n/dot_general | solution.py:49
  13.6 1.6 %constant_dynamic-slice_fusion = bf16[256,2,128]{2,1,0:T(2,128)(2,1)S(1)} fusion(bf16[256,8,128]{2,1,0:T(8,128)(2,1)} %param.11, s32[]{:T(128)S(6)} %select_n.54), kind=kLoop, calls=%fused_computation.243 | loop fusion | bytes 262148 | tf_op jit(solution)/shard_map/dynamic_slice | solution.py:160
  15.5 5.2 %collective-permute-done.1 = bf16[2,256,1,2,128]{1,4,2,3,0:T(8,128)(2,1)S(1)} collective-permute-done((bf16[2,256,1,2,128]{1,4,2,3,0:T(8,128)(2,1)S(1)}, bf16[2,256,1,2,128]{1,4,2,3,0:T(8,128)(2,1)S(1)}, u32[]{:S(2)}, u32[]{:S(2)}) %collective-permute-start.1) | collective-permute-done | bytes 262176 | tf_op jit(solution)/shard_map/ppermute | solution.py:103
  20.7 1.1 pad_maximum_fusion.2
  21.8 0.9 slice_bitcast_fusion
  22.7 0.9 fusion.79
  23.6 8.6 %all-to-all-start = ((f32[32,40,128]{2,1,0:T(8,128)}), f32[32,40,128]{2,1,0:T(8,128)S(1)}, u32[]{:S(2)}, u32[]{:S(2)}) async-start(f32[32,40,128]{2,1,0:T(8,128)} %bitcast.26), calls=%async_computation | async-start | bytes 1310720 | tf_op jit(solution)/shard_map/all_to_all | solution.py:70
  32.4 0.9 reduce-precision_convert_fusion.13
  33.3 4.7 %fusion.93 = f32[2,4,256,1056]{2,3,1,0:T(8,128)} fusion(bf16[96,1056,1,1]{1,0,3,2:T(8,128)(2,1)S(1)} %copy-done.15, bf16[2,4,256,32]{2,3,0,1:T(8,128)(2,1)S(1)} %get-tuple-element.60, bf16[2,4,256,32]{2,3,0,1:T(8,128)(2,1)S(1)} %get-tuple-element.59, bf16[2,4,256,32]{2,3,0,1:T(8,128)(2,1)S(1)} %get-tuple-element.58), kind=kOutput, calls=%fused_computation.150 | convolution fusion | flops 416415744 | bytes 9246720 | tf_op jit(solution)/shard_map/...k,kn->...n/dot_general | solution.py:49
  38.1 7.1 %all-to-all-done = f32[32,40,128]{2,1,0:T(8,128)S(1)} async-done(((f32[32,40,128]{2,1,0:T(8,128)}), f32[32,40,128]{2,1,0:T(8,128)S(1)}, u32[]{:S(2)}, u32[]{:S(2)}) %all-to-all-start) | async-done | bytes 655392 | tf_op jit(solution)/shard_map/all_to_all | solution.py:70
  45.3 0.3 fusion.63
  45.6 1.2 copy.73
  46.9 4.8 %all-to-all-start.1 = ((f32[32,40,128]{2,1,0:T(8,128)}), f32[32,40,128]{2,1,0:T(8,128)}, u32[]{:S(2)}, u32[]{:S(2)}) async-start(f32[32,40,128]{2,1,0:T(8,128)} %copy.73), calls=%async_computation.1 | async-start | bytes 1310720 | tf_op jit(solution)/shard_map/all_to_all | solution.py:89
  51.7 4.2 %multiply_convert_fusion = bf16[2,4,256,528]{2,3,1,0:T(8,128)(2,1)S(1)} fusion(f32[2,4,256,1056]{2,3,1,0:T(8,128)} %fusion.93), kind=kLoop, calls=%fused_computation.10 | loop fusion | flops 3244032 | bytes 10813440 | tf_op jit(solution)/shard_map/convert_element_type | solution.py:132
  55.9 2.1 %select_reduce_fusion = (f32[2,4,256]{2,1,0:T(4,128)S(1)}, bf16[2,4,256,256]{2,3,1,0:T(8,128)(2,1)}) fusion(pred[256,256]{0,1:T(8,128)(4,1)S(1)} %copy-done.18, bf16[2,256,528]{1,2,0:T(8,128)(2,1)S(1)} %get-tuple-element.29, bf16[2,4,256,528]{2,3,1,0:T(8,128)(2,1)S(1)} %multiply_convert_fusion, bf16[528]{0:T(1024)(128)(2,1)S(1)} %copy-done.17), kind=kOutput, calls=%fused_computation.26 | convolution fusion | flops 556300288 | bytes 3826720 | tf_op jit(solution)/shard_map/hmif,hjf->hmij/dot_general | solution.py:186
  58.0 6.7 %all-to-all-done.1 = f32[32,40,128]{2,1,0:T(8,128)} async-done(((f32[32,40,128]{2,1,0:T(8,128)}), f32[32,40,128]{2,1,0:T(8,128)}, u32[]{:S(2)}, u32[]{:S(2)}) %all-to-all-start.1) | async-done | bytes 655392 | tf_op jit(solution)/shard_map/all_to_all | solution.py:89
  64.7 0.7 slice.90
  65.4 1.9 %slice.92 = f32[1056,128]{1,0:T(8,128)} slice(f32[1280,128]{1,0:T(8,128)} %bitcast.27), slice={[0:1056], [0:128]} | slice | bytes 1081344 | tf_op jit(solution)/shard_map/slice | solution.py:90
  67.3 0.5 fusion.48
  67.8 0.5 fusion.46
  68.4 1.2 reduce-precision_convert_fusion.2
  69.6 1.6 %fusion.177 = f32[2,528,128,1]{2,1,3,0:T(8,128)} fusion(bf16[2,4,256,528]{2,3,1,0:T(8,128)(2,1)S(1)} %multiply_convert_fusion, bf16[256,4,2,128]{0,3,1,2:T(8,128)(2,1)S(1)} %copy-done.6, f32[2,4,256]{2,1,0:T(4,128)S(1)} %fusion.142), kind=kOutput, calls=%fused_computation.258 | convolution fusion | flops 277610496 | bytes 3235840 | tf_op jit(solution)/shard_map/hmif,hmid->hfd/dot_general | solution.py:198
  71.1 1.1 convolution_bitcast_fusion.1
  72.3 0.7 fusion.44
  73.0 0.8 convolution_add_fusion.3
  73.9 0.5 fusion.27
  74.4 0.5 select_convert_fusion
  74.9 1.8 %convolution_bitcast_fusion = f32[2,256,528]{1,2,0:T(8,128)} fusion(bf16[2,4,256,256]{2,3,1,0:T(8,128)(2,1)S(1)} %select_convert_fusion, bf16[2,4,256,528]{2,3,1,0:T(8,128)(2,1)S(1)} %multiply_convert_fusion), kind=kOutput, calls=%fused_computation.39 | convolution fusion | flops 553648128 | bytes 4292608 | tf_op jit(solution)/shard_map/hmij,hmif->hjf/dot_general | solution.py:219
  76.6 0.7 fusion.149
  77.3 0.7 fusion.147
  78.0 2.1 %select_maximum_fusion = f32[1280,128]{1,0:T(8,128)} fusion(f32[10,128]{1,0:T(8,128)S(1)} %reshape.59, f32[1056,128]{1,0:T(8,128)} %bitcast.181), kind=kLoop, calls=%fused_computation.129 | loop fusion | flops 655360 | bytes 1201152 | tf_op jit(solution)/shard_map/concatenate | solution.py:58
  80.1 4.1 %all-to-all-start.2 = ((f32[32,40,128]{2,1,0:T(8,128)}), f32[32,40,128]{2,1,0:T(8,128)S(1)}, u32[]{:S(2)}, u32[]{:S(2)}) async-start(f32[32,40,128]{2,1,0:T(8,128)} %bitcast.45), calls=%async_computation.2 | async-start | bytes 1310720 | tf_op jit(solution)/shard_map/all_to_all | solution.py:70
  84.3 5.3 %multiply_add_fusion = f32[2,4,256,528]{2,3,1,0:T(8,128)} fusion(f32[2,528]{1,0:T(2,128)S(1)} %get-tuple-element.69, f32[2,4,256]{2,1,0:T(4,128)S(1)} %get-tuple-element.66, bf16[2,4,256,128]{2,3,1,0:T(8,128)(2,1)} %get-tuple-element.53, bf16[2,4,256,128]{2,3,1,0:T(8,128)(2,1)} %get-tuple-element.52, bf16[2,4,256,256]{2,3,1,0:T(8,128)(2,1)S(1)} %copy-done.11, ...), kind=kOutput, calls=%fused_computation.9 | convolution fusion | flops 1402175488 | bytes 7516288 | tf_op jit(solution)/shard_map/hmik,hkf->hmif/dot_general | solution.py:211
  89.6 7.6 %all-to-all-done.2 = f32[32,40,128]{2,1,0:T(8,128)S(1)} async-done(((f32[32,40,128]{2,1,0:T(8,128)}), f32[32,40,128]{2,1,0:T(8,128)S(1)}, u32[]{:S(2)}, u32[]{:S(2)}) %all-to-all-start.2) | async-done | bytes 655392 | tf_op jit(solution)/shard_map/all_to_all | solution.py:70
  97.4 0.3 fusion.69
  97.7 1.2 copy.91
  99.0 4.1 %all-to-all-start.3 = ((f32[32,40,128]{2,1,0:T(8,128)}), f32[32,40,128]{2,1,0:T(8,128)S(1)}, u32[]{:S(2)}, u32[]{:S(2)}) async-start(f32[32,40,128]{2,1,0:T(8,128)} %copy.91), calls=%async_computation.3 | async-start | bytes 1310720 | tf_op jit(solution)/shard_map/all_to_all | solution.py:89
  103.1 5.9 %slice_multiply_fusion = (f32[2,4,256,528]{2,3,1,0:T(8,128)S(1)}, f32[2,4,256,528]{2,3,1,0:T(8,128)S(1)}) fusion(f32[2,4,256,528]{2,3,1,0:T(8,128)} %multiply_add_fusion, f32[2,4,256,1056]{2,3,1,0:T(8,128)} %fusion.93, f32[528]{0:T(1024)S(1)} %copy-done.20), kind=kLoop, calls=%fused_computation.11 | loop fusion | flops 3244032 | bytes 21628992 | tf_op jit(solution)/shard_map/mul | solution.py:139
  109.1 1.4 %reduce-precision_convert_fusion = (bf16[2,4,256,1056]{2,3,1,0:T(8,128)(2,1)S(1)}, bf16[2,4,256,1056]{2,3,1,0:T(8,128)(2,1)S(1)}) fusion(f32[2,4,256,528]{2,3,1,0:T(8,128)S(1)} %get-tuple-element.31, f32[2,4,256,528]{2,3,1,0:T(8,128)S(1)} %get-tuple-element.30), kind=kLoop, calls=%fused_computation.1 | loop fusion | flops 10813440 | bytes 17301504 | tf_op jit(solution)/shard_map/convert_element_type | solution.py:26
  110.5 0.9 fusion.1
  111.4 0.9 fusion.183
  112.3 1.0 fusion.111
  113.3 1.0 fusion.28
  114.4 2.1 %collective-permute-start.3 = (bf16[256,1,2,128]{3,0,1,2:T(8,128)(2,1)S(1)}, bf16[256,1,2,128]{3,0,1,2:T(8,128)(2,1)S(1)}, u32[]{:S(2)}, u32[]{:S(2)}) collective-permute-start(bf16[256,1,2,128]{3,0,1,2:T(8,128)(2,1)S(1)} %get-tuple-element.56), channel_id=1, source_target_pairs={{0,3},{1,0},{2,1},{3,2},{4,7},{5,4},{6,5},{7,6},{8,11},{9,8},{10,9... | collective-permute-start | bytes 393224 | tf_op jit(solution)/shard_map/ppermute | solution.py:116
  116.4 0.9 collective-permute-start.4
  117.7 1.4 %collective-permute-done.3 = bf16[256,1,2,128]{3,0,1,2:T(8,128)(2,1)S(1)} collective-permute-done((bf16[256,1,2,128]{3,0,1,2:T(8,128)(2,1)S(1)}, bf16[256,1,2,128]{3,0,1,2:T(8,128)(2,1)S(1)}, u32[]{:S(2)}, u32[]{:S(2)}) %collective-permute-start.3) | collective-permute-done | bytes 131104 | tf_op jit(solution)/shard_map/ppermute | solution.py:116
  119.3 2.8 %collective-permute-done.4 = bf16[256,1,2,128]{3,0,1,2:T(8,128)(2,1)S(1)} collective-permute-done((bf16[256,1,2,128]{3,0,1,2:T(8,128)(2,1)S(1)}, bf16[256,1,2,128]{3,0,1,2:T(8,128)(2,1)S(1)}, u32[]{:S(2)}, u32[]{:S(2)}) %collective-permute-start.4) | collective-permute-done | bytes 131104 | tf_op jit(solution)/shard_map/ppermute | solution.py:116
  122.3 3.6 %collective-permute-done.5 = bf16[256,1,2,128]{3,0,1,2:T(8,128)(2,1)S(1)} collective-permute-done((bf16[256,1,2,128]{3,0,1,2:T(8,128)(2,1)S(1)}, bf16[256,1,2,128]{3,0,1,2:T(8,128)(2,1)S(1)}, u32[]{:S(2)}, u32[]{:S(2)}) %collective-permute-start.5) | collective-permute-done | bytes 131104 | tf_op jit(solution)/shard_map/ppermute | solution.py:116
  126.2 0.7 copy-done.12
  127.0 0.5 fusion.89
  127.5 1.6 %fusion.42 = bf16[256,2,128]{2,0,1:T(8,128)(2,1)S(1)} fusion(f32[2,256,128]{2,1,0:T(8,128)} %convolution_bitcast_fusion.1, f32[2,256,128]{2,1,0:T(8,128)S(1)} %fusion.89, bf16[2,256,528]{1,2,0:T(8,128)(2,1)S(1)} %get-tuple-element.29, f32[2,528,128]{2,1,0:T(8,128)S(1)} %bitcast.171, bf16[528]{0:T(1024)(128)(2,1)S(1)} %copy-done.17), kind=kOutput, calls=%fused_computation.70 | convolution fusion | flops 70078464 | bytes 1737760 | tf_op jit(solution)/shard_map/htf,hfd->htd/dot_general | solution.py:36
  129.1 0.8 copy.93
  130.0 1.7 %slice_multiply_fusion.1 = (f32[2,256,528]{1,2,0:T(8,128)S(1)}, f32[2,256,528]{1,2,0:T(8,128)S(1)}) fusion(f32[2,256,1056]{1,2,0:T(8,128)S(1)} %copy-done.3, f32[528]{0:T(1024)S(1)} %copy-done.20, f32[2,528]{1,0:T(2,128)S(1)} %bitcast.183, f32[2,256,528]{1,2,0:T(8,128)} %convolution_bitcast_fusion, bf16[2,128,528]{1,2,0:T(8,128)(2,1)S(1)} %get-tuple-element.49, ...), kind=kOutput, calls=%fused_computation.98 | convolution fusion | flops 141369344 | bytes 6084800 | tf_op jit(solution)/shard_map/htk,hkf->htf/dot_general | solution.py:235
  132.0 0.3 fusion.52
  132.4 0.4 fusion.127
  132.8 0.4 fusion.41
  133.2 0.8 copy.92
  (80 shorter events, 3.6 us)
Async XLA Ops:
  0.6 10.1 %copy-start = (bf16[256,8,128]{2,1,0:T(8,128)(2,1)S(1)}, bf16[256,8,128]{2,1,0:T(8,128)(2,1)}, u32[]{:S(2)}) copy-start(bf16[256,8,128]{2,1,0:T(8,128)(2,1)} %param.10) | copy-start | bytes 1572868
  0.7 10.1 %copy-start.19 = (s32[2,128,32]{1,2,0:T(8,128)S(1)}, s32[2,128,32]{1,2,0:T(8,128)}, u32[]{:S(2)}) copy-start(s32[2,128,32]{1,2,0:T(8,128)} %param.13) | copy-start | bytes 98308
  3.5 12.0 %collective-permute-start = (bf16[2,256,1,2,128]{1,4,2,3,0:T(8,128)(2,1)S(1)}, bf16[2,256,1,2,128]{1,4,2,3,0:T(8,128)(2,1)S(1)}, u32[]{:S(2)}, u32[]{:S(2)}) collective-permute-start(bf16[2,256,1,2,128]{1,4,2,3,0:T(8,128)(2,1)S(1)} %get-tuple-element.39), channel_id=1, source_target_pairs={{0,1},{1,2},{2,3},{3,0},{4,5},{5,6},{6,7},{7,4},{8,9},{9,10},{10,1... | collective-permute-start | bytes 786440 | tf_op jit(solution)/shard_map/ppermute | solution.py:103
  6.1 14.6 %collective-permute-start.1 = (bf16[2,256,1,2,128]{1,4,2,3,0:T(8,128)(2,1)S(1)}, bf16[2,256,1,2,128]{1,4,2,3,0:T(8,128)(2,1)S(1)}, u32[]{:S(2)}, u32[]{:S(2)}) collective-permute-start(bf16[2,256,1,2,128]{1,4,2,3,0:T(8,128)(2,1)S(1)} %get-tuple-element.40), channel_id=1, source_target_pairs={{0,2},{1,3},{2,0},{3,1},{4,6},{5,7},{6,4},{7,5},{8,10},{9,11},{10,... | collective-permute-start | bytes 786440 | tf_op jit(solution)/shard_map/ppermute | solution.py:103
  9.4 11.3 %collective-permute-start.2 = (bf16[2,256,1,2,128]{1,4,2,3,0:T(8,128)(2,1)S(1)}, bf16[2,256,1,2,128]{1,4,2,3,0:T(8,128)(2,1)}, u32[]{:S(2)}, u32[]{:S(2)}) collective-permute-start(bf16[2,256,1,2,128]{1,4,2,3,0:T(8,128)(2,1)S(1)} %get-tuple-element.41), channel_id=1, source_target_pairs={{0,3},{1,0},{2,1},{3,2},{4,7},{5,4},{6,5},{7,6},{8,11},{9,8},{10,9... | collective-permute-start | bytes 786440 | tf_op jit(solution)/shard_map/ppermute | solution.py:103
  13.3 2.2 %copy-start.2 = (f32[2,256,1056]{1,2,0:T(8,128)}, f32[2,256,1056]{1,2,0:T(8,128)S(1)}, u32[]{:S(2)}) copy-start(f32[2,256,1056]{1,2,0:T(8,128)S(1)} %fusion.119) | copy-start | bytes 6488068
  15.2 5.6 %copy-start.7 = (bf16[256,2,128]{2,1,0:T(2,128)(2,1)}, bf16[256,2,128]{2,1,0:T(2,128)(2,1)S(1)}, u32[]{:S(2)}) copy-start(bf16[256,2,128]{2,1,0:T(2,128)(2,1)S(1)} %constant_dynamic-slice_fusion) | copy-start | bytes 393220
  22.7 10.7 %copy-start.15 = (bf16[96,1056,1,1]{1,0,3,2:T(8,128)(2,1)S(1)}, bf16[96,1056,1,1]{1,0,3,2:T(8,128)(2,1)}, u32[]{:S(2)}) copy-start(bf16[96,1056,1,1]{1,0,3,2:T(8,128)(2,1)} %constant.95) | copy-start | bytes 608260
  23.6 21.5 %all-to-all-start = ((f32[32,40,128]{2,1,0:T(8,128)}), f32[32,40,128]{2,1,0:T(8,128)S(1)}, u32[]{:S(2)}, u32[]{:S(2)}) async-start(f32[32,40,128]{2,1,0:T(8,128)} %bitcast.26), calls=%async_computation | async-start | bytes 1310720 | tf_op jit(solution)/shard_map/all_to_all | solution.py:70
  46.9 17.8 %all-to-all-start.1 = ((f32[32,40,128]{2,1,0:T(8,128)}), f32[32,40,128]{2,1,0:T(8,128)}, u32[]{:S(2)}, u32[]{:S(2)}) async-start(f32[32,40,128]{2,1,0:T(8,128)} %copy.73), calls=%async_computation.1 | async-start | bytes 1310720 | tf_op jit(solution)/shard_map/all_to_all | solution.py:89
  51.6 4.2 %copy-start.17 = (bf16[528]{0:T(1024)(128)(2,1)S(1)}, bf16[528]{0:T(1024)(128)(2,1)}, u32[]{:S(2)}) copy-start(bf16[528]{0:T(1024)(128)(2,1)} %constant.77.clone) | copy-start | bytes 3172
  51.7 4.2 %copy-start.18 = (pred[256,256]{0,1:T(8,128)(4,1)S(1)}, pred[256,256]{0,1:T(8,128)(4,1)}, u32[]{:S(2)}) copy-start(pred[256,256]{0,1:T(8,128)(4,1)} %iota_compare_fusion.1) | copy-start | bytes 196612
  67.3 1.0 copy-start.6
  69.6 1.6 %copy-start.21 = (bf16[2,4,256,256]{2,3,1,0:T(8,128)(2,1)S(1)}, bf16[2,4,256,256]{2,3,1,0:T(8,128)(2,1)}, u32[]{:S(2)}) copy-start(bf16[2,4,256,256]{2,3,1,0:T(8,128)(2,1)} %get-tuple-element.75) | copy-start | bytes 3145732
  71.1 1.1 copy-start.4
  73.0 0.9 copy-start.8
  74.8 2.4 %copy-start.10 = (bf16[2,4,256,256]{2,3,1,0:T(8,128)(2,1)}, bf16[2,4,256,256]{2,3,1,0:T(8,128)(2,1)S(1)}, u32[]{:S(2)}) copy-start(bf16[2,4,256,256]{2,3,1,0:T(8,128)(2,1)S(1)} %select_convert_fusion) | copy-start | bytes 3145732
  77.9 6.2 %copy-start.5 = (f32[1056,128]{1,0:T(8,128)S(1)}, f32[1056,128]{1,0:T(8,128)}, u32[]{:S(2)}) copy-start(f32[1056,128]{1,0:T(8,128)} %slice.92) | copy-start | bytes 1622020
  77.9 6.3 %copy-start.11 = (bf16[2,4,256,256]{2,3,1,0:T(8,128)(2,1)S(1)}, bf16[2,4,256,256]{2,3,1,0:T(8,128)(2,1)}, u32[]{:S(2)}) copy-start(bf16[2,4,256,256]{2,3,1,0:T(8,128)(2,1)} %copy-done.10) | copy-start | bytes 3145732
  80.1 17.1 %all-to-all-start.2 = ((f32[32,40,128]{2,1,0:T(8,128)}), f32[32,40,128]{2,1,0:T(8,128)S(1)}, u32[]{:S(2)}, u32[]{:S(2)}) async-start(f32[32,40,128]{2,1,0:T(8,128)} %bitcast.45), calls=%async_computation.2 | async-start | bytes 1310720 | tf_op jit(solution)/shard_map/all_to_all | solution.py:70
  97.4 5.7 %copy-start.20 = (f32[528]{0:T(1024)S(1)}, f32[528]{0:T(1024)}, u32[]{:S(2)}) copy-start(f32[528]{0:T(1024)} %constant.78.clone) | copy-start | bytes 6340
  99.0 27.2 %all-to-all-start.3 = ((f32[32,40,128]{2,1,0:T(8,128)}), f32[32,40,128]{2,1,0:T(8,128)S(1)}, u32[]{:S(2)}, u32[]{:S(2)}) async-start(f32[32,40,128]{2,1,0:T(8,128)} %copy.91), calls=%async_computation.3 | async-start | bytes 1310720 | tf_op jit(solution)/shard_map/all_to_all | solution.py:89
  109.0 1.4 %copy-start.13 = (bf16[1056,32,1,1]{0,1,2,3:T(8,128)(2,1)S(1)}, bf16[1056,32,1,1]{0,1,2,3:T(8,128)(2,1)}, u32[]{:S(2)}) copy-start(bf16[1056,32,1,1]{0,1,2,3:T(8,128)(2,1)} %constant.96) | copy-start | bytes 202756
  110.5 1.0 copy-start.9
  114.4 4.7 %collective-permute-start.3 = (bf16[256,1,2,128]{3,0,1,2:T(8,128)(2,1)S(1)}, bf16[256,1,2,128]{3,0,1,2:T(8,128)(2,1)S(1)}, u32[]{:S(2)}, u32[]{:S(2)}) collective-permute-start(bf16[256,1,2,128]{3,0,1,2:T(8,128)(2,1)S(1)} %get-tuple-element.56), channel_id=1, source_target_pairs={{0,3},{1,0},{2,1},{3,2},{4,7},{5,4},{6,5},{7,6},{8,11},{9,8},{10,9... | collective-permute-start | bytes 393224 | tf_op jit(solution)/shard_map/ppermute | solution.py:116
  116.4 5.7 %collective-permute-start.4 = (bf16[256,1,2,128]{3,0,1,2:T(8,128)(2,1)S(1)}, bf16[256,1,2,128]{3,0,1,2:T(8,128)(2,1)S(1)}, u32[]{:S(2)}, u32[]{:S(2)}) collective-permute-start(bf16[256,1,2,128]{3,0,1,2:T(8,128)(2,1)S(1)} %get-tuple-element.55), channel_id=1, source_target_pairs={{0,2},{1,3},{2,0},{3,1},{4,6},{5,7},{6,4},{7,5},{8,10},{9,11},{10,... | collective-permute-start | bytes 393224 | tf_op jit(solution)/shard_map/ppermute | solution.py:116
  117.3 8.6 %collective-permute-start.5 = (bf16[256,1,2,128]{3,0,1,2:T(8,128)(2,1)S(1)}, bf16[256,1,2,128]{3,0,1,2:T(8,128)(2,1)S(1)}, u32[]{:S(2)}, u32[]{:S(2)}) collective-permute-start(bf16[256,1,2,128]{3,0,1,2:T(8,128)(2,1)S(1)} %get-tuple-element.54), channel_id=1, source_target_pairs={{0,1},{1,2},{2,3},{3,0},{4,5},{5,6},{6,7},{7,4},{8,9},{9,10},{10,1... | collective-permute-start | bytes 393224 | tf_op jit(solution)/shard_map/ppermute | solution.py:116
  126.2 0.8 copy-start.12
  127.0 3.0 %copy-start.3 = (f32[2,256,1056]{1,2,0:T(8,128)S(1)}, f32[2,256,1056]{1,2,0:T(8,128)}, u32[]{:S(2)}) copy-start(f32[2,256,1056]{1,2,0:T(8,128)} %copy-done.2) | copy-start | bytes 6488068
  130.0 1.7 %copy-start.16 = (bf16[1056,32,1]{0,1,2:T(8,128)(2,1)S(1)}, bf16[1056,32,1]{0,1,2:T(8,128)(2,1)}, u32[]{:S(2)}) copy-start(bf16[1056,32,1]{0,1,2:T(8,128)(2,1)} %constant.97) | copy-start | bytes 202756
  131.7 1.1 copy-start.14
  131.7 2.3 %copy-start.1 = (bf16[256,8,128]{2,1,0:T(8,128)(2,1)S(1)}, bf16[256,8,128]{2,1,0:T(8,128)(2,1)}, u32[]{:S(2)}) copy-start(bf16[256,8,128]{2,1,0:T(8,128)(2,1)} %param.10) | copy-start | bytes 1572868

commit v11 on v8

--- a/solution.py
+++ b/solution.py
@@ -74,13 +74,8 @@
     n = got.shape[0]
     src = lax.broadcasted_iota(jnp.int32, (n, n), 1)
     dst = lax.broadcasted_iota(jnp.int32, (n, n), 0)
-    mask = (src > dst if reverse else src < dst).astype(bf16)
-    return jnp.einsum(
-        "ij,jrc->irc",
-        jnp.concatenate([mask, mask, mask], axis=1),
-        jnp.concatenate(split_parts(got, 3), axis=0),
-        preferred_element_type=f32,
-    )
+    mask = (src > dst if reverse else src < dst).astype(f32)
+    return jnp.einsum("ij,jrc->irc", mask, got, precision=highest)
 
 
 def scan_return(summed, heads, feat):
@@ -113,14 +108,15 @@
 def head_return(grads, heads_all):
     count = lax.axis_size("head")
     me = lax.axis_index("head")
-    owned = grads.shape[2]
-    out = jnp.zeros((grads.shape[0], 1, heads_all, grads.shape[3]), grads.dtype)
+    pieces = []
     for k in range(count):
-        piece = grads[:, k : k + 1]
+        piece = grads[:, k]
         if k:
             piece = lax.ppermute(piece, "head", [(j, (j - k) % count) for j in range(count)])
-        out = lax.dynamic_update_slice_in_dim(out, piece, ((me + k) % count) * owned, axis=2)
-    return out
+        pieces.append(piece)
+    ordered = jnp.roll(jnp.stack(pieces), me, axis=0)
+    tokens, owned, width = grads.shape[0], grads.shape[2], grads.shape[3]
+    return ordered.transpose(1, 0, 2, 3).reshape(tokens, 1, heads_all, width)
 
 
 def sketch_parts(tokens, projector, pattern):
@@ -187,16 +183,28 @@
         0.0,
     )
     weights = scores.astype(bf16)
-    numerator = jnp.einsum(
-        "hmij,hjd->hmid", weights, value_heads, preferred_element_type=f32
-    ) + dot_split("hmif,hfd->hmid", query_wfeat, state_in)
-    denominator = 1.0 + jnp.sum(scores, -1) + dot_split("hmif,hf->hmi", query_wfeat, total_in)
+    width_v = value_heads.shape[-1]
+    carried = dot_split(
+        "hmif,hfd->hmid", query_wfeat, jnp.concatenate([state_in, total_in[..., None]], axis=-1)
+    )
+    numerator = (
+        jnp.einsum("hmij,hjd->hmid", weights, value_heads, preferred_element_type=f32)
+        + carried[..., :width_v]
+    )
+    denominator = 1.0 + jnp.sum(scores, -1) + carried[..., width_v]
     output_rows = numerator / denominator[..., None]
     grad_rows = grad_heads / denominator[..., None]
     grad_low = grad_rows.astype(bf16)
     correction = -jnp.sum(grad_rows * output_rows, -1)
-    suffix_part = jnp.einsum("hmif,hmid->hfd", query_feat, grad_low, preferred_element_type=f32)
-    suffix_sum = dot_split("hmif,hmi->hf", query_feat, correction)
+    corr_hi, corr_lo = split_parts(correction[..., None], 2)
+    suffix_both = jnp.einsum(
+        "hmif,hmid->hfd",
+        query_feat,
+        jnp.concatenate([grad_low, corr_hi, corr_lo], axis=-1),
+        preferred_element_type=f32,
+    )
+    suffix_part = suffix_both[..., :width_v]
+    suffix_sum = suffix_both[..., width_v] + suffix_both[..., width_v + 1]
     suffix_got = scan_send(suffix_part, suffix_sum)
 
     dscores = jnp.where(
@@ -227,6 +235,9 @@
         grad_qfeat, query_one, query_two, proj_wide, take_a, take_b, off
     )
     query_low = query_grad.transpose(2, 1, 0, 3).astype(bf16)
+    query_low, merged_state, merged_total = lax.optimization_barrier(
+        (query_low, merged_state, merged_total)
+    )
     query_out = head_return(query_low, heads_all)
 
     merged_hi, merged_lo = split_parts(merged_state.transpose(0, 2, 1), 2)

time: 135 us -> 145 us (1.074)
  local copies, waits for them, and re-layouts: 12.4 us -> 27.9 us
  matrix products: 39.3 us -> 27.5 us
  other arithmetic: 17.6 us -> 25.4 us
  waiting for transfers between devices: 29.6 us -> 26.1 us
    unnamed x65 -> x92, local copies, waits for them, and re-layouts: 4.92 us -> 13.4 us
    dot_general x12 -> x8, matrix products: 10.9 us -> 6.07 us  [dot_parts(): term = jnp.einsum(pattern, *args, preferred_element_type=f32)]
    dot_general x2, matrix products: 6.15 us -> 1.81 us  [take_pair(): out = jnp.einsum('...k,kn->...n', lhs, rhs, preferred_element_type=f32)]
    another operation x1, other arithmetic: 0.1 us -> 4.38 us  [body(): both = head_exchange(jnp.stack([queries, dout]), owned)]
    another operation x1 -> x2, local copies, waits for them, and re-layouts: 0.19 us -> 4.46 us  [body(): both = head_exchange(jnp.stack([queries, dout]), owned)]
    mul x1 -> x0, other arithmetic: 4.22 us -> none  [body(): query_wfeat = query_feat * weight]
    ppermute x3, waiting for transfers between devices: 10.4 us -> 6.33 us  [head_exchange(): lax.ppermute(piece, 'head', [(j, (j + k) % count) for j in range(count)])]
    concatenate x1, other arithmetic: 0.13 us -> 3.8 us  [head_exchange(): return jnp.concatenate(pieces, axis=2)]
  transfers between devices with their start and end apart: 10 -> 10, of which waited for: 7 -> 5; matrix products, arithmetic and copies ran while one was open for 25% -> 28% of each run, Pallas kernels for 0% -> 0%
where the time goes in v11:
time: 145 us; the launch traced here: 144 us
  starting transfers between devices  35.2 us (24%)
  local copies, waits for them, and re-layouts  27.9 us (19%)
  matrix products  27.5 us (19%)
  waiting for transfers between devices  26.1 us (18%)
  other arithmetic  25.4 us (18%)
  between operations  1.48 us (1%)
    unnamed x92, local copies, waits for them, and re-layouts  13.4 us
    all_to_all x2, starting transfers between devices, scan_return(): lax.all_to_all(summed, 'ctx', 0, 0, tiled=True).reshape(n * per, width)  12.7 us
    all_to_all x2, starting transfers between devices, scan_send(): return lax.all_to_all(flat.reshape(n, per, width), 'ctx', 0, 0, tiled=True)  12.7 us
    all_to_all x2, waiting for transfers between devices, scan_return(): lax.all_to_all(summed, 'ctx', 0, 0, tiled=True).reshape(n * per, width)  9.57 us
    ppermute x3, starting transfers between devices, head_exchange(): lax.ppermute(piece, 'head', [(j, (j + k) % count) for j in range(count)])  6.5 us
    ppermute x3, waiting for transfers between devices, head_exchange(): lax.ppermute(piece, 'head', [(j, (j + k) % count) for j in range(count)])  6.33 us
    dot_general x8, matrix products, dot_parts(): term = jnp.einsum(pattern, *args, preferred_element_type=f32)  6.07 us
    mul x1, other arithmetic, tri_feature_back(): cotangent * second  5.95 us
  transfers between devices with their start and end apart: 10, of which 5 were waited for; matrix products, arithmetic and copies ran while one was open for 28% of the time, Pallas kernels for 0%

profile of v11, /device:TPU:1, one launch (start us, length us, event | category | flops | bytes accessed | tf_op | source)
XLA Modules:
  0.0 143.6 jit_solution(10880655094491842684)
XLA Ops:
  0.7 2.2 %copy.172 = bf16[1,256,1,8,128]{1,2,4,3,0:T(2,128)(2,1)S(1)} copy(bf16[1,256,1,8,128]{4,3,1,2,0:T(8,128)(2,1)} %bitcast.216) | data formatting | bytes 1048576 | tf_op jit(solution)/shard_map/stack | solution.py:162
  2.9 2.2 %copy.173 = bf16[1,256,1,8,128]{1,2,4,3,0:T(2,128)(2,1)S(1)} copy(bf16[1,256,1,8,128]{4,3,1,2,0:T(8,128)(2,1)} %bitcast.217) | data formatting | bytes 1048576 | tf_op jit(solution)/shard_map/stack | solution.py:162
  5.2 4.4 %fusion.78 = (bf16[2,256,1,2,128]{1,2,4,3,0:T(2,128)(2,1)S(1)}, bf16[2,256,1,2,128]{1,2,4,3,0:T(2,128)(2,1)}, bf16[2,256,1,2,128]{1,2,4,3,0:T(2,128)(2,1)}, bf16[2,256,1,2,128]{1,2,4,3,0:T(2,128)(2,1)}) fusion(s32[]{:T(128)S(6)} %select_n.53, bf16[1,256,1,8,128]{1,2,4,3,0:T(2,128)(2,1)S(1)} %copy.172, bf16[1,256,1,8,128]{1,2,4,3,0:T(2,128)(2,1)S(1)} %copy.173, ...), kind=kLoop, calls=%fused_computation.126 | loop fusion | flops 524288 | bytes 2097168 | tf_op jit(solution)/shard_map/stack | solution.py:162
  9.6 2.5 %collective-permute-start = (bf16[2,256,1,2,128]{1,2,4,3,0:T(2,128)(2,1)}, bf16[2,256,1,2,128]{1,2,4,3,0:T(2,128)(2,1)S(1)}, u32[]{:S(2)}, u32[]{:S(2)}) collective-permute-start(bf16[2,256,1,2,128]{1,2,4,3,0:T(2,128)(2,1)} %get-tuple-element.41), channel_id=1, source_target_pairs={{0,1},{1,2},{2,3},{3,0},{4,5},{5,6},{6,7},{7,4},{8,9},{9,10},{10,1... | collective-permute-start | bytes 786440 | tf_op jit(solution)/shard_map/ppermute | solution.py:103
  12.1 3.3 %collective-permute-start.1 = (bf16[2,256,1,2,128]{1,2,4,3,0:T(2,128)(2,1)}, bf16[2,256,1,2,128]{1,2,4,3,0:T(2,128)(2,1)S(1)}, u32[]{:S(2)}, u32[]{:S(2)}) collective-permute-start(bf16[2,256,1,2,128]{1,2,4,3,0:T(2,128)(2,1)} %get-tuple-element.42), channel_id=1, source_target_pairs={{0,2},{1,3},{2,0},{3,1},{4,6},{5,7},{6,4},{7,5},{8,10},{9,11},{10,... | collective-permute-start | bytes 786440 | tf_op jit(solution)/shard_map/ppermute | solution.py:103
  15.4 0.7 collective-permute-start.2
  16.1 1.5 %constant_dynamic-slice_fusion.1 = (bf16[256,2,128]{2,1,0:T(2,128)(2,1)S(1)}, bf16[256,2,128]{2,1,0:T(2,128)(2,1)S(1)}) fusion(bf16[256,8,128]{2,1,0:T(8,128)(2,1)} %param.11, s32[]{:T(128)S(6)} %select_n.60, bf16[256,8,128]{2,1,0:T(8,128)(2,1)} %param.10), kind=kLoop, calls=%fused_computation.214 | loop fusion | bytes 524292 | tf_op jit(solution)/shard_map/dynamic_slice | solution.py:161
  17.7 0.8 reduce-precision_convert_fusion.12
  19.0 1.3 copy-done.1
  21.0 0.9 fusion.60
  21.9 8.6 %all-to-all-start = ((f32[32,40,128]{2,1,0:T(8,128)}), f32[32,40,128]{2,1,0:T(8,128)S(1)}, u32[]{:S(2)}, u32[]{:S(2)}) async-start(f32[32,40,128]{2,1,0:T(8,128)} %bitcast.28), calls=%async_computation | async-start | bytes 1310720 | tf_op jit(solution)/shard_map/all_to_all | solution.py:70
  30.5 0.7 copy.294
  31.1 0.7 iota_compare_fusion.1
  31.8 6.3 %collective-permute-done.1 = bf16[2,256,1,2,128]{1,2,4,3,0:T(2,128)(2,1)S(1)} collective-permute-done((bf16[2,256,1,2,128]{1,2,4,3,0:T(2,128)(2,1)}, bf16[2,256,1,2,128]{1,2,4,3,0:T(2,128)(2,1)S(1)}, u32[]{:S(2)}, u32[]{:S(2)}) %collective-permute-start.1) | collective-permute-done | bytes 262176 | tf_op jit(solution)/shard_map/ppermute | solution.py:103
  38.1 0.8 copy-done.19
  38.9 3.8 %pad_maximum_fusion.3 = bf16[2,256,4,2,128]{1,2,4,3,0:T(4,128)(2,1)S(1)} fusion(bf16[2,256,1,2,128]{1,2,4,3,0:T(2,128)(2,1)} %collective-permute-done.2, bf16[2,256,1,2,128]{1,2,4,3,0:T(2,128)(2,1)} %copy-done.19, bf16[2,256,1,2,128]{1,2,4,3,0:T(2,128)(2,1)} %copy-done.18, bf16[2,256,1,2,128]{1,2,4,3,0:T(2,128)(2,1)S(1)} %get-tuple-element.40), kind=kLoop, calls=%fused_computation.86 | loop fusion | flops 4194304 | bytes 2097152 | tf_op jit(solution)/shard_map/concatenate | solution.py:105
  42.7 1.0 copy-done.4
  44.6 1.0 reduce-precision_convert_fusion.9
  45.6 1.3 fusion.84
  46.9 3.4 %copy-done = f32[2,4,256,1056]{2,3,1,0:T(8,128)} copy-done((f32[2,4,256,1056]{2,3,1,0:T(8,128)}, f32[2,4,256,1056]{2,3,1,0:T(8,128)S(1)}, u32[]{:S(2)}) %copy-start) | copy-done | bytes 8650776
  50.3 0.7 multiply_convert_fusion
  51.6 1.3 copy.180
  52.8 8.6 %all-to-all-start.1 = ((f32[32,40,128]{2,1,0:T(8,128)}), f32[32,40,128]{2,1,0:T(8,128)S(1)}, u32[]{:S(2)}, u32[]{:S(2)}) async-start(f32[32,40,128]{2,1,0:T(8,128)} %copy.180), calls=%async_computation.1 | async-start | bytes 1310720 | tf_op jit(solution)/shard_map/all_to_all | solution.py:84
  61.5 2.6 %select_reduce_fusion = (f32[2,4,256]{2,1,0:T(4,128)}, bf16[2,4,256,256]{2,3,1,0:T(8,128)(2,1)S(1)}) fusion(pred[256,256]{0,1:T(8,128)(4,1)} %iota_compare_fusion.1, bf16[2,256,528]{1,2,0:T(8,128)(2,1)S(1)} %get-tuple-element.33, bf16[2,4,256,528]{2,3,1,0:T(8,128)(2,1)S(1)} %multiply_convert_fusion, bf16[528]{0:T(1024)(128)(2,1)} %constant.81.clone), kind=kOutput, calls=%fused_computation.26 | convolution fusion | flops 556300288 | bytes 3826720 | tf_op jit(solution)/shard_map/hmif,hjf->hmij/dot_general | solution.py:182
  64.1 1.0 copy-done.13
  65.1 1.4 fusion.86
  66.5 7.9 %all-to-all-done.1 = f32[32,40,128]{2,1,0:T(8,128)S(1)} async-done(((f32[32,40,128]{2,1,0:T(8,128)}), f32[32,40,128]{2,1,0:T(8,128)S(1)}, u32[]{:S(2)}, u32[]{:S(2)}) %all-to-all-start.1) | async-done | bytes 655392 | tf_op jit(solution)/shard_map/all_to_all | solution.py:84
  74.4 0.6 slice.111
  75.0 0.9 slice.110
  75.8 0.7 reshape.98
  76.5 0.6 fusion.149
  77.4 1.9 %fusion.18 = f32[2,4,256,129]{2,3,1,0:T(8,128)S(1)} fusion(bf16[2,4,256,528]{2,3,1,0:T(8,128)(2,1)S(1)} %multiply_convert_fusion, bf16[528]{0:T(1024)(128)(2,1)} %constant.81.clone, f32[2,528,1]{2,1,0:T(8,128)S(1)} %copy.181, f32[2,528,128]{2,1,0:T(8,128)} %bitcast.212), kind=kOutput, calls=%fused_computation.29 | convolution fusion | flops 280476768 | bytes 3765408 | tf_op jit(solution)/shard_map/hmif,hfd->hmid/dot_general | solution.py:36
  79.3 0.8 fusion.16
  80.1 0.7 copy_add_fusion
  81.6 2.1 %reduce-precision_convert_fusion.3 = (bf16[2,4,256,128]{2,1,3,0:T(4,128)(2,1)}, bf16[2,4,256,128]{2,1,3,0:T(4,128)(2,1)}, f32[2,4,256]{2,1,0:T(4,128)S(1)}, bf16[2,4,256,128]{2,1,3,0:T(4,128)(2,1)S(1)}) fusion(f32[2,4,256]{2,1,0:T(4,128)S(1)} %fusion.120, bf16[2,256,4,2,128]{1,2,4,3,0:T(4,128)(2,1)S(1)} %copy-done.5, ...), kind=kLoop, calls=%fused_computation.36 | loop fusion | flops 2881536 | bytes 4210688 | tf_op jit(solution)/shard_map/convert_element_type | solution.py:26
  83.8 0.6 neg.20
  84.4 1.1 copy.197
  85.9 0.9 convolution_bitcast_fusion.1
  86.9 0.6 slice_add_fusion.2
  87.5 0.9 fusion.66
  88.4 1.1 copy.195
  89.5 0.7 copy.295
  90.2 1.9 %select_maximum_fusion = f32[1280,128]{1,0:T(8,128)} fusion(f32[10,128]{1,0:T(8,128)S(1)} %reshape.100, f32[1056,128]{1,0:T(8,128)} %bitcast.211), kind=kLoop, calls=%fused_computation.105 | loop fusion | flops 655360 | bytes 1201152 | tf_op jit(solution)/shard_map/concatenate | solution.py:58
  92.1 4.1 %all-to-all-start.2 = ((f32[32,40,128]{2,1,0:T(8,128)}), f32[32,40,128]{2,1,0:T(8,128)S(1)}, u32[]{:S(2)}, u32[]{:S(2)}) async-start(f32[32,40,128]{2,1,0:T(8,128)} %bitcast.205), calls=%async_computation.2 | async-start | bytes 1310720 | tf_op jit(solution)/shard_map/all_to_all | solution.py:70
  96.2 1.5 %select_convert_fusion = bf16[2,4,256,256]{2,3,1,0:T(8,128)(2,1)S(1)} fusion(bf16[2,4,256,128]{3,2,1,0:T(8,128)(2,1)} %copy.197, f32[2,4,256]{2,1,0:T(4,128)} %neg.20, pred[256,256]{0,1:T(8,128)(4,1)} %iota_compare_fusion.1, bf16[256,2,128]{2,1,0:T(2,128)(2,1)S(1)} %get-tuple-element.71), kind=kOutput, calls=%fused_computation.24 | convolution fusion | flops 135790592 | bytes 1777664 | tf_op jit(solution)/shard_map/hmid,hjd->hmij/dot_general | solution.py:212
  97.8 1.7 %convolution_bitcast_fusion = f32[2,256,528]{1,2,0:T(8,128)} fusion(bf16[2,4,256,256]{2,3,1,0:T(8,128)(2,1)S(1)} %select_convert_fusion, bf16[2,4,256,528]{2,3,1,0:T(8,128)(2,1)S(1)} %multiply_convert_fusion), kind=kOutput, calls=%fused_computation.39 | convolution fusion | flops 553648128 | bytes 4292608 | tf_op jit(solution)/shard_map/hmij,hmif->hjf/dot_general | solution.py:227
  99.6 1.1 convolution_bitcast_fusion.2
  100.9 3.5 %multiply_add_fusion = f32[2,4,256,528]{2,3,1,0:T(8,128)} fusion(f32[2,528]{1,0:T(2,128)S(1)} %copy-done.39, f32[2,4,256]{2,1,0:T(4,128)S(1)} %copy-done.38, bf16[2,4,256,128]{2,3,1,0:T(8,128)(2,1)S(1)} %copy.200, bf16[2,4,256,128]{2,3,1,0:T(8,128)(2,1)S(1)} %copy.198, bf16[2,4,256,256]{2,3,1,0:T(8,128)(2,1)S(1)} %select_convert_fusion, ...), kind=kOutput, calls=%fused_computation.9 | convolution fusion | flops 1402175488 | bytes 7516288 | tf_op jit(solution)/shard_map/hmik,hkf->hmif/dot_general | solution.py:219
  104.5 4.8 %all-to-all-done.2 = f32[32,40,128]{2,1,0:T(8,128)S(1)} async-done(((f32[32,40,128]{2,1,0:T(8,128)}), f32[32,40,128]{2,1,0:T(8,128)S(1)}, u32[]{:S(2)}, u32[]{:S(2)}) %all-to-all-start.2) | async-done | bytes 655392 | tf_op jit(solution)/shard_map/all_to_all | solution.py:70
  109.7 1.2 copy.208
  110.9 4.1 %all-to-all-start.3 = ((f32[32,40,128]{2,1,0:T(8,128)}), f32[32,40,128]{2,1,0:T(8,128)S(1)}, u32[]{:S(2)}, u32[]{:S(2)}) async-start(f32[32,40,128]{2,1,0:T(8,128)} %copy.208), calls=%async_computation.3 | async-start | bytes 1310720 | tf_op jit(solution)/shard_map/all_to_all | solution.py:84
  115.1 5.9 %slice_multiply_fusion = (f32[2,4,256,528]{2,3,1,0:T(8,128)S(1)}, f32[2,4,256,528]{2,3,1,0:T(8,128)S(1)}) fusion(f32[2,4,256,528]{2,3,1,0:T(8,128)} %multiply_add_fusion, f32[2,4,256,1056]{2,3,1,0:T(8,128)} %copy-done, f32[528]{0:T(1024)S(1)} %copy-done.34), kind=kLoop, calls=%fused_computation.11 | loop fusion | flops 3244032 | bytes 21628992 | tf_op jit(solution)/shard_map/mul | solution.py:140
  121.0 1.4 reduce-precision_convert_fusion
  122.4 0.9 fusion.1
  123.5 0.9 fusion.148
  124.4 1.0 fusion.95
  125.4 1.0 fusion.31
  126.4 1.7 %all-to-all-done.3 = f32[32,40,128]{2,1,0:T(8,128)S(1)} async-done(((f32[32,40,128]{2,1,0:T(8,128)}), f32[32,40,128]{2,1,0:T(8,128)S(1)}, u32[]{:S(2)}, u32[]{:S(2)}) %all-to-all-start.3) | async-done | bytes 655392 | tf_op jit(solution)/shard_map/all_to_all | solution.py:84
  129.6 0.8 copy.214
  132.9 0.8 copy.213
  133.7 2.0 %collective-permute-start.4 = (bf16[256,2,128]{2,0,1:T(8,128)(2,1)S(1)}, bf16[256,2,128]{2,0,1:T(8,128)(2,1)S(1)}, u32[]{:S(2)}, u32[]{:S(2)}) collective-permute-start(bf16[256,2,128]{2,0,1:T(8,128)(2,1)S(1)} %get-tuple-element.52), channel_id=1, source_target_pairs={{0,2},{1,3},{2,0},{3,1},{4,6},{5,7},{6,4},{7,5},{8,10},{9,11},{10,... | collective-permute-start | bytes 393224 | tf_op jit(solution)/shard_map/ppermute | solution.py:115
  135.7 1.1 collective-permute-start.3
  136.7 5.4 %collective-permute-done.3 = bf16[256,2,128]{2,0,1:T(8,128)(2,1)S(1)} collective-permute-done((bf16[256,2,128]{2,0,1:T(8,128)(2,1)S(1)}, bf16[256,2,128]{2,0,1:T(8,128)(2,1)S(1)}, u32[]{:S(2)}, u32[]{:S(2)}) %collective-permute-start.3) | collective-permute-done | bytes 131104 | tf_op jit(solution)/shard_map/ppermute | solution.py:115
  142.4 1.1 copy.212
  (124 shorter events, 9.1 us)
Async XLA Ops:
  5.2 10.9 %copy-start.33 = (s32[2,128,32]{1,2,0:T(8,128)S(1)}, s32[2,128,32]{1,2,0:T(8,128)}, u32[]{:S(2)}) copy-start(s32[2,128,32]{1,2,0:T(8,128)} %param.13) | copy-start | bytes 98308
  5.2 13.3 %copy-start.30 = (bf16[96,1056,1]{1,0,2:T(8,128)(2,1)S(1)}, bf16[96,1056,1]{1,0,2:T(8,128)(2,1)}, u32[]{:S(2)}) copy-start(bf16[96,1056,1]{1,0,2:T(8,128)(2,1)} %constant.99) | copy-start | bytes 608260
  9.6 22.2 %collective-permute-start = (bf16[2,256,1,2,128]{1,2,4,3,0:T(2,128)(2,1)}, bf16[2,256,1,2,128]{1,2,4,3,0:T(2,128)(2,1)S(1)}, u32[]{:S(2)}, u32[]{:S(2)}) collective-permute-start(bf16[2,256,1,2,128]{1,2,4,3,0:T(2,128)(2,1)} %get-tuple-element.41), channel_id=1, source_target_pairs={{0,1},{1,2},{2,3},{3,0},{4,5},{5,6},{6,7},{7,4},{8,9},{9,10},{10,1... | collective-permute-start | bytes 786440 | tf_op jit(solution)/shard_map/ppermute | solution.py:103
  12.1 26.1 %collective-permute-start.1 = (bf16[2,256,1,2,128]{1,2,4,3,0:T(2,128)(2,1)}, bf16[2,256,1,2,128]{1,2,4,3,0:T(2,128)(2,1)S(1)}, u32[]{:S(2)}, u32[]{:S(2)}) collective-permute-start(bf16[2,256,1,2,128]{1,2,4,3,0:T(2,128)(2,1)} %get-tuple-element.42), channel_id=1, source_target_pairs={{0,2},{1,3},{2,0},{3,1},{4,6},{5,7},{6,4},{7,5},{8,10},{9,11},{10,... | collective-permute-start | bytes 786440 | tf_op jit(solution)/shard_map/ppermute | solution.py:103
  15.4 22.8 %collective-permute-start.2 = (bf16[2,256,1,2,128]{1,2,4,3,0:T(2,128)(2,1)}, bf16[2,256,1,2,128]{1,2,4,3,0:T(2,128)(2,1)}, u32[]{:S(2)}, u32[]{:S(2)}) collective-permute-start(bf16[2,256,1,2,128]{1,2,4,3,0:T(2,128)(2,1)} %get-tuple-element.43), channel_id=1, source_target_pairs={{0,3},{1,0},{2,1},{3,2},{4,7},{5,4},{6,5},{7,6},{8,11},{9,8},{10,9... | collective-permute-start | bytes 786440 | tf_op jit(solution)/shard_map/ppermute | solution.py:103
  16.1 4.5 %copy-start.20 = (bf16[2,128,32]{1,2,0:T(8,128)(2,1)}, bf16[2,128,32]{1,2,0:T(8,128)(2,1)S(1)}, u32[]{:S(2)}) copy-start(bf16[2,128,32]{1,2,0:T(8,128)(2,1)S(1)} %add_convert_fusion) | copy-start | bytes 49156
  19.0 1.3 copy-start.1
  21.9 29.2 %all-to-all-start = ((f32[32,40,128]{2,1,0:T(8,128)}), f32[32,40,128]{2,1,0:T(8,128)S(1)}, u32[]{:S(2)}, u32[]{:S(2)}) async-start(f32[32,40,128]{2,1,0:T(8,128)} %bitcast.28), calls=%async_computation | async-start | bytes 1310720 | tf_op jit(solution)/shard_map/all_to_all | solution.py:70
  31.8 6.3 %copy-start.18 = (bf16[2,256,1,2,128]{1,2,4,3,0:T(2,128)(2,1)}, bf16[2,256,1,2,128]{1,2,4,3,0:T(2,128)(2,1)S(1)}, u32[]{:S(2)}) copy-start(bf16[2,256,1,2,128]{1,2,4,3,0:T(2,128)(2,1)S(1)} %collective-permute-done) | copy-start | bytes 786436
  38.1 0.8 copy-start.19
  38.9 5.4 %copy-start.21 = (bf16[2,128,32]{1,2,0:T(8,128)(2,1)S(1)}, bf16[2,128,32]{1,2,0:T(8,128)(2,1)}, u32[]{:S(2)}) copy-start(bf16[2,128,32]{1,2,0:T(8,128)(2,1)} %copy-done.20) | copy-start | bytes 49156
  42.7 1.0 copy-start.4
  43.7 1.9 %copy-start.31 = (bf16[96,1056,1,1]{1,0,3,2:T(8,128)(2,1)S(1)}, bf16[96,1056,1,1]{1,0,3,2:T(8,128)(2,1)}, u32[]{:S(2)}) copy-start(bf16[96,1056,1,1]{1,0,3,2:T(8,128)(2,1)} %constant.98) | copy-start | bytes 608260
  44.6 1.0 copy-start.7
  46.9 3.4 %copy-start = (f32[2,4,256,1056]{2,3,1,0:T(8,128)}, f32[2,4,256,1056]{2,3,1,0:T(8,128)S(1)}, u32[]{:S(2)}) copy-start(f32[2,4,256,1056]{2,3,1,0:T(8,128)S(1)} %fusion.84) | copy-start | bytes 25952260
  52.8 21.5 %all-to-all-start.1 = ((f32[32,40,128]{2,1,0:T(8,128)}), f32[32,40,128]{2,1,0:T(8,128)S(1)}, u32[]{:S(2)}, u32[]{:S(2)}) async-start(f32[32,40,128]{2,1,0:T(8,128)} %copy.180), calls=%async_computation.1 | async-start | bytes 1310720 | tf_op jit(solution)/shard_map/all_to_all | solution.py:84
  61.5 3.6 %copy-start.26 = (pred[256,256]{0,1:T(8,128)(4,1)S(1)}, pred[256,256]{0,1:T(8,128)(4,1)}, u32[]{:S(2)}) copy-start(pred[256,256]{0,1:T(8,128)(4,1)} %iota_compare_fusion.1) | copy-start | bytes 196612
  64.1 1.0 copy-start.13
  77.4 1.9 %copy-start.9 = (f32[1056,128]{1,0:T(8,128)S(1)}, f32[1056,128]{1,0:T(8,128)}, u32[]{:S(2)}) copy-start(f32[1056,128]{1,0:T(8,128)} %slice.110) | copy-start | bytes 1622020
  77.4 1.9 %copy-start.35 = (bf16[528]{0:T(1024)(128)(2,1)S(1)}, bf16[528]{0:T(1024)(128)(2,1)}, u32[]{:S(2)}) copy-start(bf16[528]{0:T(1024)(128)(2,1)} %constant.81.clone) | copy-start | bytes 3172
  80.1 0.7 copy-start.37
  80.1 1.2 copy-start.5
  80.1 1.5 %copy-start.6 = (f32[2,4,256,128]{2,3,1,0:T(8,128)S(1)}, f32[2,4,256,128]{2,3,1,0:T(8,128)}, u32[]{:S(2)}) copy-start(f32[2,4,256,128]{2,3,1,0:T(8,128)} %fusion.86) | copy-start | bytes 3145732
  85.9 1.6 %copy-start.10 = (f32[1056,128]{1,0:T(8,128)S(1)}, f32[1056,128]{1,0:T(8,128)}, u32[]{:S(2)}) copy-start(f32[1056,128]{1,0:T(8,128)} %slice.110) | copy-start | bytes 1622020
  92.1 17.1 %all-to-all-start.2 = ((f32[32,40,128]{2,1,0:T(8,128)}), f32[32,40,128]{2,1,0:T(8,128)S(1)}, u32[]{:S(2)}, u32[]{:S(2)}) async-start(f32[32,40,128]{2,1,0:T(8,128)} %bitcast.205), calls=%async_computation.2 | async-start | bytes 1310720 | tf_op jit(solution)/shard_map/all_to_all | solution.py:70
  97.7 1.8 %copy-start.14 = (bf16[2,4,256,256]{2,3,1,0:T(8,128)(2,1)S(1)}, bf16[2,4,256,256]{2,3,1,0:T(8,128)(2,1)}, u32[]{:S(2)}) copy-start(bf16[2,4,256,256]{2,3,1,0:T(8,128)(2,1)} %copy-done.13) | copy-start | bytes 3145732
  97.7 1.8 %copy-start.17 = (bf16[2,4,256,128]{3,2,1,0:T(8,128)(2,1)S(1)}, bf16[2,4,256,128]{3,2,1,0:T(8,128)(2,1)}, u32[]{:S(2)}) copy-start(bf16[2,4,256,128]{3,2,1,0:T(8,128)(2,1)} %copy.197) | copy-start | bytes 1572868
  97.7 1.8 %copy-start.27 = (pred[256,256]{0,1:T(8,128)(4,1)S(1)}, pred[256,256]{0,1:T(8,128)(4,1)}, u32[]{:S(2)}) copy-start(pred[256,256]{0,1:T(8,128)(4,1)} %iota_compare_fusion.1) | copy-start | bytes 196612
  99.5 1.2 copy-start.12
  99.5 1.3 copy-start.11
  99.5 1.3 copy-start.24
  99.5 1.3 copy-start.25
  99.6 1.3 copy-start.38
  99.6 1.3 copy-start.39
  104.5 10.6 %copy-start.34 = (f32[528]{0:T(1024)S(1)}, f32[528]{0:T(1024)}, u32[]{:S(2)}) copy-start(f32[528]{0:T(1024)} %constant.82.clone) | copy-start | bytes 6340
  110.9 17.1 %all-to-all-start.3 = ((f32[32,40,128]{2,1,0:T(8,128)}), f32[32,40,128]{2,1,0:T(8,128)S(1)}, u32[]{:S(2)}, u32[]{:S(2)}) async-start(f32[32,40,128]{2,1,0:T(8,128)} %copy.208), calls=%async_computation.3 | async-start | bytes 1310720 | tf_op jit(solution)/shard_map/all_to_all | solution.py:84
  121.0 1.4 copy-start.23
  122.4 1.0 copy-start.8
  122.4 1.0 copy-start.15
  123.5 0.9 copy-start.22
  124.4 3.8 %copy-start.36 = (bf16[528]{0:T(1024)(128)(2,1)S(1)}, bf16[528]{0:T(1024)(128)(2,1)}, u32[]{:S(2)}) copy-start(bf16[528]{0:T(1024)(128)(2,1)} %constant.81.clone) | copy-start | bytes 3172
  128.1 1.0 copy-start.28
  128.7 1.7 %copy-start.2 = (f32[2,256,1056]{1,2,0:T(8,128)S(1)}, f32[2,256,1056]{1,2,0:T(8,128)}, u32[]{:S(2)}) copy-start(f32[2,256,1056]{1,2,0:T(8,128)} %copy-done.1) | copy-start | bytes 6488068
  128.7 1.9 %copy-start.3 = (f32[2,256,528]{1,2,0:T(8,128)S(1)}, f32[2,256,528]{1,2,0:T(8,128)}, u32[]{:S(2)}) copy-start(f32[2,256,528]{1,2,0:T(8,128)} %convolution_bitcast_fusion) | copy-start | bytes 3244036
  128.7 1.9 %copy-start.16 = (bf16[256,2,128]{2,0,1:T(8,128)(2,1)S(1)}, bf16[256,2,128]{2,0,1:T(8,128)(2,1)}, u32[]{:S(2)}) copy-start(bf16[256,2,128]{2,0,1:T(8,128)(2,1)} %copy.294) | copy-start | bytes 393220
  128.8 13.4 %collective-permute-start.5 = (bf16[256,2,128]{2,0,1:T(8,128)(2,1)S(1)}, bf16[256,2,128]{2,0,1:T(8,128)(2,1)S(1)}, u32[]{:S(2)}, u32[]{:S(2)}) collective-permute-start(bf16[256,2,128]{2,0,1:T(8,128)(2,1)S(1)} %slice_bitcast_fusion.5), channel_id=1, source_target_pairs={{0,1},{1,2},{2,3},{3,0},{4,5},{5,6},{6,7},{7,4},{8,9},{9,10},{10,1... | collective-permute-start | bytes 393224 | tf_op jit(solution)/shard_map/ppermute | solution.py:115
  130.6 0.9 copy-start.32
  131.4 1.1 copy-start.29
  133.7 8.5 %collective-permute-start.4 = (bf16[256,2,128]{2,0,1:T(8,128)(2,1)S(1)}, bf16[256,2,128]{2,0,1:T(8,128)(2,1)S(1)}, u32[]{:S(2)}, u32[]{:S(2)}) collective-permute-start(bf16[256,2,128]{2,0,1:T(8,128)(2,1)S(1)} %get-tuple-element.52), channel_id=1, source_target_pairs={{0,2},{1,3},{2,0},{3,1},{4,6},{5,7},{6,4},{7,5},{8,10},{9,11},{10,... | collective-permute-start | bytes 393224 | tf_op jit(solution)/shard_map/ppermute | solution.py:115
  135.7 6.5 %collective-permute-start.3 = (bf16[256,2,128]{2,0,1:T(8,128)(2,1)S(1)}, bf16[256,2,128]{2,0,1:T(8,128)(2,1)S(1)}, u32[]{:S(2)}, u32[]{:S(2)}) collective-permute-start(bf16[256,2,128]{2,0,1:T(8,128)(2,1)S(1)} %get-tuple-element.53), channel_id=1, source_target_pairs={{0,3},{1,0},{2,1},{3,2},{4,7},{5,4},{6,5},{7,6},{8,11},{9,8},{10,9... | collective-permute-start | bytes 393224 | tf_op jit(solution)/shard_map/ppermute | solution.py:115

commit v12 on v8

--- a/solution.py
+++ b/solution.py
@@ -74,13 +74,8 @@
     n = got.shape[0]
     src = lax.broadcasted_iota(jnp.int32, (n, n), 1)
     dst = lax.broadcasted_iota(jnp.int32, (n, n), 0)
-    mask = (src > dst if reverse else src < dst).astype(bf16)
-    return jnp.einsum(
-        "ij,jrc->irc",
-        jnp.concatenate([mask, mask, mask], axis=1),
-        jnp.concatenate(split_parts(got, 3), axis=0),
-        preferred_element_type=f32,
-    )
+    mask = (src > dst if reverse else src < dst).astype(f32)
+    return jnp.einsum("ij,jrc->irc", mask, got, precision=highest)
 
 
 def scan_return(summed, heads, feat):
@@ -227,6 +222,9 @@
         grad_qfeat, query_one, query_two, proj_wide, take_a, take_b, off
     )
     query_low = query_grad.transpose(2, 1, 0, 3).astype(bf16)
+    query_low, merged_state, merged_total = lax.optimization_barrier(
+        (query_low, merged_state, merged_total)
+    )
     query_out = head_return(query_low, heads_all)
 
     merged_hi, merged_lo = split_parts(merged_state.transpose(0, 2, 1), 2)

time: 135 us -> 125 us (0.926)
  waiting for transfers between devices: 29.6 us -> 22.1 us
  local copies, waits for them, and re-layouts: 12.4 us -> 15.6 us
  matrix products: 39.3 us -> 36.3 us
  starting transfers between devices: 33.9 us -> 31.1 us
    ppermute x3, waiting for transfers between devices: 10.4 us -> 0.01 us  [head_exchange(): lax.ppermute(piece, 'head', [(j, (j + k) % count) for j in range(count)])]
    all_to_all x2, starting transfers between devices: 12.4 us -> 9.07 us  [scan_return(): lax.all_to_all(summed, 'ctx', 0, 0, tiled=True).reshape(n * per, width)]
    all_to_all x2, waiting for transfers between devices: 4.75 us -> 7.99 us  [scan_send(): return lax.all_to_all(flat.reshape(n, per, width), 'ctx', 0, 0, tiled=True)]
    ppermute x3, waiting for transfers between devices: 8.02 us -> 5.84 us  [head_return(): lax.ppermute(piece, 'head', [(j, (j - k) % count) for j in range(count)])]
    unnamed x65 -> x73, local copies, waits for them, and re-layouts: 4.92 us -> 6.89 us
    all_to_all x2, waiting for transfers between devices: 6.44 us -> 8.29 us  [scan_return(): lax.all_to_all(summed, 'ctx', 0, 0, tiled=True).reshape(n * per, width)]
    convert_element_type x5 -> x3, other arithmetic: 3.23 us -> 2.8 us  [split_parts(): parts.append(hi.astype(bf16))]
  transfers between devices with their start and end apart: 10 -> 10, of which waited for: 7 -> 7; matrix products, arithmetic and copies ran while one was open for 25% -> 31% of each run, Pallas kernels for 0% -> 0%
where the time goes in v12:
time: 125 us; the launch traced here: 124 us
  matrix products  36.3 us (29%)
  starting transfers between devices  31.1 us (25%)
  waiting for transfers between devices  22.1 us (18%)
  other arithmetic  17.6 us (14%)
  local copies, waits for them, and re-layouts  15.6 us (12%)
  between operations  1.4 us (1%)
    all_to_all x2, starting transfers between devices, scan_send(): return lax.all_to_all(flat.reshape(n, per, width), 'ctx', 0, 0, tiled=True)  12.8 us
    dot_general x12, matrix products, dot_parts(): term = jnp.einsum(pattern, *args, preferred_element_type=f32)  9.63 us
    all_to_all x2, starting transfers between devices, scan_return(): lax.all_to_all(summed, 'ctx', 0, 0, tiled=True).reshape(n * per, width)  9.07 us
    all_to_all x2, waiting for transfers between devices, scan_return(): lax.all_to_all(summed, 'ctx', 0, 0, tiled=True).reshape(n * per, width)  8.29 us
    all_to_all x2, waiting for transfers between devices, scan_send(): return lax.all_to_all(flat.reshape(n, per, width), 'ctx', 0, 0, tiled=True)  7.99 us
    unnamed x73, local copies, waits for them, and re-layouts  6.89 us
    ppermute x3, starting transfers between devices, head_exchange(): lax.ppermute(piece, 'head', [(j, (j + k) % count) for j in range(count)])  6.57 us
    mul x1, other arithmetic, tri_feature_back(): cotangent * second  5.95 us
  transfers between devices with their start and end apart: 10, of which 7 were waited for; matrix products, arithmetic and copies ran while one was open for 31% of the time, Pallas kernels for 0%

profile of v12, /device:TPU:1, one launch (start us, length us, event | category | flops | bytes accessed | tf_op | source)
XLA Modules:
  0.0 124.0 jit_solution(11976906083538529843)
XLA Ops:
  0.7 1.4 %copy_bitcast_fusion = (bf16[1,256,1,8,128]{4,1,3,2,0:T(8,128)(2,1)S(1)}, bf16[1,256,1,8,128]{4,1,3,2,0:T(8,128)(2,1)S(1)}) fusion(bf16[256,1,8,128]{3,2,1,0:T(8,128)(2,1)} %param.12, bf16[256,1,8,128]{3,2,1,0:T(8,128)(2,1)} %param.9), kind=kLoop, calls=%fused_computation.120 | loop fusion | bytes 2097152 | tf_op jit(solution)/shard_map/stack | solution.py:161
  2.3 2.5 %collective-permute-start = (bf16[2,256,1,2,128]{4,1,3,2,0:T(8,128)(2,1)S(1)}, bf16[2,256,1,2,128]{4,1,3,2,0:T(8,128)(2,1)S(1)}, u32[]{:S(2)}, u32[]{:S(2)}) collective-permute-start(bf16[2,256,1,2,128]{4,1,3,2,0:T(8,128)(2,1)S(1)} %get-tuple-element.40), channel_id=1, source_target_pairs={{0,1},{1,2},{2,3},{3,0},{4,5},{5,6},{6,7},{7,4},{8,9},{9,10},{10,1... | collective-permute-start | bytes 786440 | tf_op jit(solution)/shard_map/ppermute | solution.py:103
  4.8 3.3 %collective-permute-start.1 = (bf16[2,256,1,2,128]{4,1,3,2,0:T(8,128)(2,1)S(1)}, bf16[2,256,1,2,128]{4,1,3,2,0:T(8,128)(2,1)S(1)}, u32[]{:S(2)}, u32[]{:S(2)}) collective-permute-start(bf16[2,256,1,2,128]{4,1,3,2,0:T(8,128)(2,1)S(1)} %get-tuple-element.41), channel_id=1, source_target_pairs={{0,2},{1,3},{2,0},{3,1},{4,6},{5,7},{6,4},{7,5},{8,10},{9,11},{10,... | collective-permute-start | bytes 786440 | tf_op jit(solution)/shard_map/ppermute | solution.py:103
  8.1 0.7 collective-permute-start.2
  8.8 1.5 %constant_dynamic-slice_fusion = (bf16[256,2,128]{2,1,0:T(2,128)(2,1)S(1)}, bf16[256,2,128]{2,1,0:T(2,128)(2,1)S(1)}) fusion(bf16[256,8,128]{2,1,0:T(8,128)(2,1)} %param.11, s32[]{:T(128)S(6)} %select_n.62, bf16[256,8,128]{2,1,0:T(8,128)(2,1)} %param.10), kind=kLoop, calls=%fused_computation.217 | loop fusion | bytes 524292 | tf_op jit(solution)/shard_map/dynamic_slice | solution.py:160
  10.5 0.8 reduce-precision_convert_fusion.12
  11.3 0.5 fusion.107
  11.8 1.3 %copy-done.2 = f32[2,256,1056]{1,2,0:T(8,128)} copy-done((f32[2,256,1056]{1,2,0:T(8,128)}, f32[2,256,1056]{1,2,0:T(8,128)S(1)}, u32[]{:S(2)}) %copy-start.2) | copy-done | bytes 2162712
  13.7 0.9 fusion.60
  14.6 8.6 %all-to-all-start = ((f32[32,40,128]{2,1,0:T(8,128)}), f32[32,40,128]{2,1,0:T(8,128)S(1)}, u32[]{:S(2)}, u32[]{:S(2)}) async-start(f32[32,40,128]{2,1,0:T(8,128)} %bitcast.26), calls=%async_computation | async-start | bytes 1310720 | tf_op jit(solution)/shard_map/all_to_all | solution.py:70
  23.2 0.7 copy.208
  24.0 0.7 copy-done.27
  24.8 1.3 %pad_maximum_fusion.2 = bf16[2,256,4,2,128]{4,1,3,2,0:T(8,128)(2,1)S(1)} fusion(bf16[2,256,1,2,128]{4,1,3,2,0:T(8,128)(2,1)} %collective-permute-done.2, bf16[2,256,1,2,128]{4,1,3,2,0:T(8,128)(2,1)} %copy-done.28, bf16[2,256,1,2,128]{4,1,3,2,0:T(8,128)(2,1)} %copy-done.27, bf16[2,256,1,2,128]{4,1,3,2,0:T(8,128)(2,1)S(1)} %get-tuple-element.39), kind=kLoop, calls=%fused_computation.87 | loop fusion | flops 1572864 | bytes 2097152 | tf_op jit(solution)/shard_map/concatenate | solution.py:105
  26.3 0.8 copy-done.4
  27.1 1.0 reduce-precision_convert_fusion.9
  28.1 4.7 %fusion.81 = f32[2,4,256,1056]{2,3,1,0:T(8,128)} fusion(bf16[96,1056,1,1]{1,0,3,2:T(8,128)(2,1)S(1)} %copy-done.30, bf16[2,4,256,32]{2,3,0,1:T(8,128)(2,1)S(1)} %get-tuple-element.53, bf16[2,4,256,32]{2,3,0,1:T(8,128)(2,1)S(1)} %get-tuple-element.52, bf16[2,4,256,32]{2,3,0,1:T(8,128)(2,1)S(1)} %get-tuple-element.51), kind=kOutput, calls=%fused_computation.130 | convolution fusion | flops 416415744 | bytes 9246720 | tf_op jit(solution)/shard_map/...k,kn->...n/dot_general | solution.py:49
  32.8 3.3 %all-to-all-done = f32[32,40,128]{2,1,0:T(8,128)S(1)} async-done(((f32[32,40,128]{2,1,0:T(8,128)}), f32[32,40,128]{2,1,0:T(8,128)S(1)}, u32[]{:S(2)}, u32[]{:S(2)}) %all-to-all-start) | async-done | bytes 655392 | tf_op jit(solution)/shard_map/all_to_all | solution.py:70
  36.1 0.5 fusion.63
  36.6 1.2 copy.78
  37.8 4.8 %all-to-all-start.1 = ((f32[32,40,128]{2,1,0:T(8,128)}), f32[32,40,128]{2,1,0:T(8,128)}, u32[]{:S(2)}, u32[]{:S(2)}) async-start(f32[32,40,128]{2,1,0:T(8,128)} %copy.78), calls=%async_computation.1 | async-start | bytes 1310720 | tf_op jit(solution)/shard_map/all_to_all | solution.py:84
  42.6 4.2 %broadcast_multiply_fusion = (bf16[2,4,256,528]{2,3,1,0:T(8,128)(2,1)S(1)}, bf16[2,4,256,528]{2,3,1,0:T(8,128)(2,1)S(1)}) fusion(bf16[528]{0:T(1024)(128)(2,1)S(1)} %copy-done.33, f32[2,4,256,1056]{2,3,1,0:T(8,128)} %fusion.81), kind=kLoop, calls=%fused_computation.84 | loop fusion | flops 4325376 | bytes 12977184 | tf_op jit(solution)/shard_map/mul | solution.py:173
  46.8 2.1 %select_convert_fusion.1 = (bf16[2,4,256,256]{2,3,1,0:T(8,128)(2,1)}, f32[2,4,256,256]{2,3,1,0:T(8,128)S(1)}) fusion(pred[256,256]{0,1:T(8,128)(4,1)S(1)} %iota_compare_fusion.1, bf16[2,4,256,528]{2,3,1,0:T(8,128)(2,1)S(1)} %get-tuple-element.28, bf16[2,256,528]{1,2,0:T(8,128)(2,1)S(1)} %get-tuple-element.27), kind=kOutput, calls=%fused_computation.25 | convolution fusion | flops 554172416 | bytes 5914624 | tf_op jit(solution)/shard_map/hmif,hjf->hmij/dot_general | solution.py:181
  49.1 6.5 %all-to-all-done.1 = f32[32,40,128]{2,1,0:T(8,128)} async-done(((f32[32,40,128]{2,1,0:T(8,128)}), f32[32,40,128]{2,1,0:T(8,128)}, u32[]{:S(2)}, u32[]{:S(2)}) %all-to-all-start.1) | async-done | bytes 655392 | tf_op jit(solution)/shard_map/all_to_all | solution.py:84
  55.6 0.7 slice.90
  56.3 1.1 slice.92
  57.5 2.2 %fusion.146 = f32[2,1,4,256]{3,1,2,0:T(1,128)S(1)} fusion(bf16[2,4,256,528]{2,3,1,0:T(8,128)(2,1)} %copy-done, bf16[2,528,1,1]{1,0,2,3:T(2,128)(2,1)S(1)} %get-tuple-element.63), kind=kOutput, calls=%fused_computation.213 | convolution fusion | flops 2162688 | bytes 2172992 | tf_op jit(solution)/shard_map/hmif,hf->hmi/dot_general | solution.py:36
  60.1 1.3 %reduce-precision_convert_fusion.2 = (bf16[2,4,256,128]{3,2,0,1:T(8,128)(2,1)}, bf16[2,4,256,128]{3,2,0,1:T(8,128)(2,1)}, bf16[2,4,256,128]{3,2,0,1:T(8,128)(2,1)S(1)}) fusion(f32[2,4,256]{2,0,1:T(2,128)S(1)} %copy.79, bf16[2,256,4,2,128]{4,1,3,2,0:T(8,128)(2,1)S(1)} %copy-done.5), kind=kLoop, calls=%fused_computation.32 | loop fusion | flops 1835008 | bytes 2105344 | tf_op jit(solution)/shard_map/convert_element_type | solution.py:26
  61.5 1.2 fusion.16
  62.6 1.2 fusion.23
  63.9 1.1 fusion.34
  65.1 0.4 select_convert_fusion
  65.5 1.6 %fusion.79 = f32[2,528,128,1]{2,1,3,0:T(8,128)} fusion(bf16[2,4,256,528]{2,3,1,0:T(8,128)(2,1)S(1)} %get-tuple-element.29, bf16[2,4,256,128]{3,2,0,1:T(8,128)(2,1)S(1)} %get-tuple-element.38), kind=kOutput, calls=%fused_computation.127 | convolution fusion | flops 276824064 | bytes 3227648 | tf_op jit(solution)/shard_map/hmif,hmid->hfd/dot_general | solution.py:193
  67.1 1.8 %convolution_bitcast_fusion = f32[2,256,528]{1,2,0:T(8,128)} fusion(bf16[2,4,256,256]{2,3,1,0:T(8,128)(2,1)S(1)} %select_convert_fusion, bf16[2,4,256,528]{2,3,1,0:T(8,128)(2,1)S(1)} %get-tuple-element.29), kind=kOutput, calls=%fused_computation.43 | convolution fusion | flops 553648128 | bytes 4292608 | tf_op jit(solution)/shard_map/hmij,hmif->hjf/dot_general | solution.py:214
  68.9 0.9 fusion.66
  69.8 0.7 fusion.133
  70.4 0.7 fusion.131
  71.2 0.9 select_maximum_fusion
  72.1 4.2 %all-to-all-start.2 = ((f32[32,40,128]{2,1,0:T(8,128)}), f32[32,40,128]{2,1,0:T(8,128)S(1)}, u32[]{:S(2)}, u32[]{:S(2)}) async-start(f32[32,40,128]{2,1,0:T(8,128)} %bitcast.43), calls=%async_computation.2 | async-start | bytes 1310720 | tf_op jit(solution)/shard_map/all_to_all | solution.py:70
  76.3 2.4 %convolution_bitcast_fusion.1 = f32[2,256,128]{2,1,0:T(8,128)} fusion(bf16[2,4,256,256]{2,3,1,0:T(8,128)(2,1)} %get-tuple-element.67, bf16[2,4,256,128]{3,2,0,1:T(8,128)(2,1)S(1)} %copy-done.9), kind=kOutput, calls=%fused_computation.69 | convolution fusion | flops 134217728 | bytes 1835008 | tf_op jit(solution)/shard_map/hmij,hmid->hjd/dot_general | solution.py:215
  79.2 5.4 %multiply_add_fusion = f32[2,4,256,528]{2,3,1,0:T(8,128)} fusion(f32[2,528]{1,0:T(2,128)S(1)} %get-tuple-element.62, f32[2,4,256]{2,1,0:T(4,128)S(1)} %copy.88, bf16[2,4,256,128]{2,3,1,0:T(8,128)(2,1)S(1)} %copy.91, bf16[2,4,256,128]{2,3,1,0:T(8,128)(2,1)S(1)} %copy.89, bf16[2,4,256,256]{2,3,1,0:T(8,128)(2,1)} %copy-done.18, ...), kind=kOutput, calls=%fused_computation.9 | convolution fusion | flops 1402175488 | bytes 7516288 | tf_op jit(solution)/shard_map/hmik,hkf->hmif/dot_general | solution.py:206
  84.6 4.7 %all-to-all-done.2 = f32[32,40,128]{2,1,0:T(8,128)S(1)} async-done(((f32[32,40,128]{2,1,0:T(8,128)}), f32[32,40,128]{2,1,0:T(8,128)S(1)}, u32[]{:S(2)}, u32[]{:S(2)}) %all-to-all-start.2) | async-done | bytes 655392 | tf_op jit(solution)/shard_map/all_to_all | solution.py:70
  89.3 0.5 fusion.61
  89.8 1.3 %copy.100 = f32[32,40,128]{2,1,0:T(8,128)} copy(f32[32,40,128]{2,0,1:T(8,128)S(1)} %fusion.61) | data formatting | bytes 1310720 | tf_op jit(solution)/shard_map/optimization_barrier | solution.py:217
  91.1 4.3 %all-to-all-start.3 = ((f32[32,40,128]{2,1,0:T(8,128)}), f32[32,40,128]{2,1,0:T(8,128)S(1)}, u32[]{:S(2)}, u32[]{:S(2)}) async-start(f32[32,40,128]{2,1,0:T(8,128)} %copy.100), calls=%async_computation.3 | async-start | bytes 1310720 | tf_op jit(solution)/shard_map/all_to_all | solution.py:84
  95.4 5.9 %slice_multiply_fusion = (f32[2,4,256,528]{2,3,1,0:T(8,128)S(1)}, f32[2,4,256,528]{2,3,1,0:T(8,128)S(1)}) fusion(f32[2,4,256,528]{2,3,1,0:T(8,128)} %multiply_add_fusion, f32[2,4,256,1056]{2,3,1,0:T(8,128)} %fusion.81, f32[528]{0:T(1024)S(1)} %copy-done.34), kind=kLoop, calls=%fused_computation.11 | loop fusion | flops 3244032 | bytes 21628992 | tf_op jit(solution)/shard_map/mul | solution.py:139
  101.4 1.4 %reduce-precision_convert_fusion = (bf16[2,4,256,1056]{2,3,1,0:T(8,128)(2,1)S(1)}, bf16[2,4,256,1056]{2,3,1,0:T(8,128)(2,1)S(1)}) fusion(f32[2,4,256,528]{2,3,1,0:T(8,128)S(1)} %get-tuple-element.31, f32[2,4,256,528]{2,3,1,0:T(8,128)S(1)} %get-tuple-element.30), kind=kLoop, calls=%fused_computation.1 | loop fusion | flops 10813440 | bytes 17301504 | tf_op jit(solution)/shard_map/convert_element_type | solution.py:26
  102.8 0.9 fusion.1
  103.7 0.9 fusion.160
  104.6 1.0 fusion.99
  105.6 1.0 fusion.35
  106.7 1.8 %all-to-all-done.3 = f32[32,40,128]{2,1,0:T(8,128)S(1)} async-done(((f32[32,40,128]{2,1,0:T(8,128)}), f32[32,40,128]{2,1,0:T(8,128)S(1)}, u32[]{:S(2)}, u32[]{:S(2)}) %all-to-all-start.3) | async-done | bytes 655392 | tf_op jit(solution)/shard_map/all_to_all | solution.py:84
  108.5 0.5 fusion.75
  109.1 0.5 fusion.49
  109.6 0.8 copy.106
  110.4 0.5 slice_multiply_fusion.1
  110.9 0.4 copy-done.31
  112.2 0.4 fusion.115
  112.6 0.4 fusion.48
  113.0 0.8 copy.105
  113.9 2.5 %collective-permute-start.4 = (bf16[256,1,2,128]{3,0,1,2:T(8,128)(2,1)S(1)}, bf16[256,1,2,128]{3,0,1,2:T(8,128)(2,1)S(1)}, u32[]{:S(2)}, u32[]{:S(2)}) collective-permute-start(bf16[256,1,2,128]{3,0,1,2:T(8,128)(2,1)S(1)} %get-tuple-element.48), channel_id=1, source_target_pairs={{0,2},{1,3},{2,0},{3,1},{4,6},{5,7},{6,4},{7,5},{8,10},{9,11},{10,... | collective-permute-start | bytes 393224 | tf_op jit(solution)/shard_map/ppermute | solution.py:116
  116.7 1.7 %collective-permute-done.3 = bf16[256,1,2,128]{3,0,1,2:T(8,128)(2,1)S(1)} collective-permute-done((bf16[256,1,2,128]{3,0,1,2:T(8,128)(2,1)S(1)}, bf16[256,1,2,128]{3,0,1,2:T(8,128)(2,1)S(1)}, u32[]{:S(2)}, u32[]{:S(2)}) %collective-permute-start.3) | collective-permute-done | bytes 131104 | tf_op jit(solution)/shard_map/ppermute | solution.py:116
  118.6 1.4 %collective-permute-done.4 = bf16[256,1,2,128]{3,0,1,2:T(8,128)(2,1)S(1)} collective-permute-done((bf16[256,1,2,128]{3,0,1,2:T(8,128)(2,1)S(1)}, bf16[256,1,2,128]{3,0,1,2:T(8,128)(2,1)S(1)}, u32[]{:S(2)}, u32[]{:S(2)}) %collective-permute-start.4) | collective-permute-done | bytes 131104 | tf_op jit(solution)/shard_map/ppermute | solution.py:116
  120.2 2.8 %collective-permute-done.5 = bf16[256,1,2,128]{3,0,1,2:T(8,128)(2,1)S(1)} collective-permute-done((bf16[256,1,2,128]{3,0,1,2:T(8,128)(2,1)S(1)}, bf16[256,1,2,128]{3,0,1,2:T(8,128)(2,1)S(1)}, u32[]{:S(2)}, u32[]{:S(2)}) %collective-permute-start.5) | collective-permute-done | bytes 131104 | tf_op jit(solution)/shard_map/ppermute | solution.py:116
  123.3 0.8 copy-done.22
  (104 shorter events, 4.7 us)
Async XLA Ops:
  0.6 8.2 %copy-start.32 = (s32[2,128,32]{1,2,0:T(8,128)S(1)}, s32[2,128,32]{1,2,0:T(8,128)}, u32[]{:S(2)}) copy-start(s32[2,128,32]{1,2,0:T(8,128)} %param.13) | copy-start | bytes 98308
  0.7 10.6 %copy-start.29 = (bf16[96,1056,1]{1,0,2:T(8,128)(2,1)S(1)}, bf16[96,1056,1]{1,0,2:T(8,128)(2,1)}, u32[]{:S(2)}) copy-start(bf16[96,1056,1]{1,0,2:T(8,128)(2,1)} %constant.95) | copy-start | bytes 608260
  2.3 21.7 %collective-permute-start = (bf16[2,256,1,2,128]{4,1,3,2,0:T(8,128)(2,1)S(1)}, bf16[2,256,1,2,128]{4,1,3,2,0:T(8,128)(2,1)S(1)}, u32[]{:S(2)}, u32[]{:S(2)}) collective-permute-start(bf16[2,256,1,2,128]{4,1,3,2,0:T(8,128)(2,1)S(1)} %get-tuple-element.40), channel_id=1, source_target_pairs={{0,1},{1,2},{2,3},{3,0},{4,5},{5,6},{6,7},{7,4},{8,9},{9,10},{10,1... | collective-permute-start | bytes 786440 | tf_op jit(solution)/shard_map/ppermute | solution.py:103
  4.8 19.2 %collective-permute-start.1 = (bf16[2,256,1,2,128]{4,1,3,2,0:T(8,128)(2,1)S(1)}, bf16[2,256,1,2,128]{4,1,3,2,0:T(8,128)(2,1)S(1)}, u32[]{:S(2)}, u32[]{:S(2)}) collective-permute-start(bf16[2,256,1,2,128]{4,1,3,2,0:T(8,128)(2,1)S(1)} %get-tuple-element.41), channel_id=1, source_target_pairs={{0,2},{1,3},{2,0},{3,1},{4,6},{5,7},{6,4},{7,5},{8,10},{9,11},{10,... | collective-permute-start | bytes 786440 | tf_op jit(solution)/shard_map/ppermute | solution.py:103
  8.1 15.9 %collective-permute-start.2 = (bf16[2,256,1,2,128]{4,1,3,2,0:T(8,128)(2,1)S(1)}, bf16[2,256,1,2,128]{4,1,3,2,0:T(8,128)(2,1)}, u32[]{:S(2)}, u32[]{:S(2)}) collective-permute-start(bf16[2,256,1,2,128]{4,1,3,2,0:T(8,128)(2,1)S(1)} %get-tuple-element.42), channel_id=1, source_target_pairs={{0,3},{1,0},{2,1},{3,2},{4,7},{5,4},{6,5},{7,6},{8,11},{9,8},{10,9... | collective-permute-start | bytes 786440 | tf_op jit(solution)/shard_map/ppermute | solution.py:103
  10.3 12.9 %copy-start.12 = (bf16[256,2,128]{2,1,0:T(2,128)(2,1)}, bf16[256,2,128]{2,1,0:T(2,128)(2,1)S(1)}, u32[]{:S(2)}) copy-start(bf16[256,2,128]{2,1,0:T(2,128)(2,1)S(1)} %get-tuple-element.72) | copy-start | bytes 393220
  10.5 2.9 %copy-start.19 = (f32[2,256,32]{1,2,0:T(8,128)}, f32[2,256,32]{1,2,0:T(8,128)S(1)}, u32[]{:S(2)}) copy-start(f32[2,256,32]{1,2,0:T(8,128)S(1)} %fusion.51) | copy-start | bytes 196612
  11.8 1.3 %copy-start.2 = (f32[2,256,1056]{1,2,0:T(8,128)}, f32[2,256,1056]{1,2,0:T(8,128)S(1)}, u32[]{:S(2)}) copy-start(f32[2,256,1056]{1,2,0:T(8,128)S(1)} %fusion.107) | copy-start | bytes 6488068
  14.6 21.5 %all-to-all-start = ((f32[32,40,128]{2,1,0:T(8,128)}), f32[32,40,128]{2,1,0:T(8,128)S(1)}, u32[]{:S(2)}, u32[]{:S(2)}) async-start(f32[32,40,128]{2,1,0:T(8,128)} %bitcast.26), calls=%async_computation | async-start | bytes 1310720 | tf_op jit(solution)/shard_map/all_to_all | solution.py:70
  23.9 25.0 %copy-start.14 = (pred[256,256]{0,1:T(8,128)(4,1)}, pred[256,256]{0,1:T(8,128)(4,1)S(1)}, u32[]{:S(2)}) copy-start(pred[256,256]{0,1:T(8,128)(4,1)S(1)} %iota_compare_fusion.1) | copy-start | bytes 196612
  23.9 0.7 copy-start.27
  24.0 0.8 copy-start.28
  24.8 3.3 %copy-start.30 = (bf16[96,1056,1,1]{1,0,3,2:T(8,128)(2,1)S(1)}, bf16[96,1056,1,1]{1,0,3,2:T(8,128)(2,1)}, u32[]{:S(2)}) copy-start(bf16[96,1056,1,1]{1,0,3,2:T(8,128)(2,1)} %constant.94) | copy-start | bytes 608260
  26.1 1.1 copy-start.4
  32.8 9.7 %copy-start.33 = (bf16[528]{0:T(1024)(128)(2,1)S(1)}, bf16[528]{0:T(1024)(128)(2,1)}, u32[]{:S(2)}) copy-start(bf16[528]{0:T(1024)(128)(2,1)} %constant.77.clone) | copy-start | bytes 3172
  37.8 17.8 %all-to-all-start.1 = ((f32[32,40,128]{2,1,0:T(8,128)}), f32[32,40,128]{2,1,0:T(8,128)}, u32[]{:S(2)}, u32[]{:S(2)}) async-start(f32[32,40,128]{2,1,0:T(8,128)} %copy.78), calls=%async_computation.1 | async-start | bytes 1310720 | tf_op jit(solution)/shard_map/all_to_all | solution.py:84
  46.8 2.1 %copy-start = (bf16[2,4,256,528]{2,3,1,0:T(8,128)(2,1)}, bf16[2,4,256,528]{2,3,1,0:T(8,128)(2,1)S(1)}, u32[]{:S(2)}) copy-start(bf16[2,4,256,528]{2,3,1,0:T(8,128)(2,1)S(1)} %get-tuple-element.28) | copy-start | bytes 6488068
  57.4 2.3 %copy-start.1 = (bf16[2,4,256,528]{2,3,1,0:T(8,128)(2,1)S(1)}, bf16[2,4,256,528]{2,3,1,0:T(8,128)(2,1)}, u32[]{:S(2)}) copy-start(bf16[2,4,256,528]{2,3,1,0:T(8,128)(2,1)} %copy-done) | copy-start | bytes 6488068
  57.5 2.7 %copy-start.5 = (bf16[2,256,4,2,128]{4,1,3,2,0:T(8,128)(2,1)S(1)}, bf16[2,256,4,2,128]{4,1,3,2,0:T(8,128)(2,1)}, u32[]{:S(2)}) copy-start(bf16[2,256,4,2,128]{4,1,3,2,0:T(8,128)(2,1)} %copy-done.4) | copy-start | bytes 3145732
  61.5 4.1 %copy-start.8 = (bf16[2,4,256,128]{3,2,0,1:T(8,128)(2,1)}, bf16[2,4,256,128]{3,2,0,1:T(8,128)(2,1)S(1)}, u32[]{:S(2)}) copy-start(bf16[2,4,256,128]{3,2,0,1:T(8,128)(2,1)S(1)} %get-tuple-element.38) | copy-start | bytes 1572868
  62.6 1.2 copy-start.13
  62.6 1.3 %copy-start.17 = (bf16[2,4,256,256]{2,3,1,0:T(8,128)(2,1)S(1)}, bf16[2,4,256,256]{2,3,1,0:T(8,128)(2,1)}, u32[]{:S(2)}) copy-start(bf16[2,4,256,256]{2,3,1,0:T(8,128)(2,1)} %get-tuple-element.67) | copy-start | bytes 3145732
  63.9 1.1 copy-start.15
  65.5 3.3 %copy-start.18 = (bf16[2,4,256,256]{2,3,1,0:T(8,128)(2,1)}, bf16[2,4,256,256]{2,3,1,0:T(8,128)(2,1)S(1)}, u32[]{:S(2)}) copy-start(bf16[2,4,256,256]{2,3,1,0:T(8,128)(2,1)S(1)} %select_convert_fusion) | copy-start | bytes 3145732
  69.8 1.4 %copy-start.7 = (f32[2,528,128,1]{2,1,3,0:T(8,128)S(1)}, f32[2,528,128,1]{2,1,3,0:T(8,128)}, u32[]{:S(2)}) copy-start(f32[2,528,128,1]{2,1,3,0:T(8,128)} %fusion.79) | copy-start | bytes 1622020
  71.1 5.2 %copy-start.9 = (bf16[2,4,256,128]{3,2,0,1:T(8,128)(2,1)S(1)}, bf16[2,4,256,128]{3,2,0,1:T(8,128)(2,1)}, u32[]{:S(2)}) copy-start(bf16[2,4,256,128]{3,2,0,1:T(8,128)(2,1)} %copy-done.8) | copy-start | bytes 1572868
  72.1 6.7 %copy-start.11 = (bf16[2,4,256,128]{3,2,0,1:T(8,128)(2,1)S(1)}, bf16[2,4,256,128]{3,2,0,1:T(8,128)(2,1)}, u32[]{:S(2)}) copy-start(bf16[2,4,256,128]{3,2,0,1:T(8,128)(2,1)} %get-tuple-element.36) | copy-start | bytes 1572868
  72.1 6.9 %copy-start.10 = (bf16[2,4,256,128]{3,2,0,1:T(8,128)(2,1)S(1)}, bf16[2,4,256,128]{3,2,0,1:T(8,128)(2,1)}, u32[]{:S(2)}) copy-start(bf16[2,4,256,128]{3,2,0,1:T(8,128)(2,1)} %get-tuple-element.37) | copy-start | bytes 1572868
  72.1 17.3 %all-to-all-start.2 = ((f32[32,40,128]{2,1,0:T(8,128)}), f32[32,40,128]{2,1,0:T(8,128)S(1)}, u32[]{:S(2)}, u32[]{:S(2)}) async-start(f32[32,40,128]{2,1,0:T(8,128)} %bitcast.43), calls=%async_computation.2 | async-start | bytes 1310720 | tf_op jit(solution)/shard_map/all_to_all | solution.py:70
  76.3 2.9 %copy-start.24 = (bf16[2,128,528]{1,2,0:T(8,128)(2,1)S(1)}, bf16[2,128,528]{1,2,0:T(8,128)(2,1)}, u32[]{:S(2)}) copy-start(bf16[2,128,528]{1,2,0:T(8,128)(2,1)} %get-tuple-element.45) | copy-start | bytes 811012
  84.6 10.8 %copy-start.34 = (f32[528]{0:T(1024)S(1)}, f32[528]{0:T(1024)}, u32[]{:S(2)}) copy-start(f32[528]{0:T(1024)} %constant.78.clone) | copy-start | bytes 6340
  91.1 17.3 %all-to-all-start.3 = ((f32[32,40,128]{2,1,0:T(8,128)}), f32[32,40,128]{2,1,0:T(8,128)S(1)}, u32[]{:S(2)}, u32[]{:S(2)}) async-start(f32[32,40,128]{2,1,0:T(8,128)} %copy.100), calls=%async_computation.3 | async-start | bytes 1310720 | tf_op jit(solution)/shard_map/all_to_all | solution.py:84
  101.3 1.4 %copy-start.23 = (bf16[1056,32,1,1]{0,1,2,3:T(8,128)(2,1)S(1)}, bf16[1056,32,1,1]{0,1,2,3:T(8,128)(2,1)}, u32[]{:S(2)}) copy-start(bf16[1056,32,1,1]{0,1,2,3:T(8,128)(2,1)} %constant.96) | copy-start | bytes 202756
  102.7 1.0 copy-start.16
  106.6 2.5 %copy-start.25 = (f32[2,256,128]{2,1,0:T(8,128)S(1)}, f32[2,256,128]{2,1,0:T(8,128)}, u32[]{:S(2)}) copy-start(f32[2,256,128]{2,1,0:T(8,128)} %convolution_bitcast_fusion.1) | copy-start | bytes 786436
  108.5 2.0 %copy-start.3 = (f32[2,256,1056]{1,2,0:T(8,128)S(1)}, f32[2,256,1056]{1,2,0:T(8,128)}, u32[]{:S(2)}) copy-start(f32[2,256,1056]{1,2,0:T(8,128)} %copy-done.2) | copy-start | bytes 6488068
  108.5 2.0 %copy-start.6 = (f32[2,256,528]{1,2,0:T(8,128)S(1)}, f32[2,256,528]{1,2,0:T(8,128)}, u32[]{:S(2)}) copy-start(f32[2,256,528]{1,2,0:T(8,128)} %convolution_bitcast_fusion) | copy-start | bytes 3244036
  108.5 2.0 %copy-start.21 = (bf16[256,2,128]{2,0,1:T(8,128)(2,1)S(1)}, bf16[256,2,128]{2,0,1:T(8,128)(2,1)}, u32[]{:S(2)}) copy-start(bf16[256,2,128]{2,0,1:T(8,128)(2,1)} %copy.208) | copy-start | bytes 393220
  110.4 0.9 copy-start.31
  111.3 0.8 copy-start.20
  111.3 1.2 copy-start.26
  113.8 4.6 %collective-permute-start.3 = (bf16[256,1,2,128]{3,0,1,2:T(8,128)(2,1)S(1)}, bf16[256,1,2,128]{3,0,1,2:T(8,128)(2,1)S(1)}, u32[]{:S(2)}, u32[]{:S(2)}) collective-permute-start(bf16[256,1,2,128]{3,0,1,2:T(8,128)(2,1)S(1)} %get-tuple-element.49), channel_id=1, source_target_pairs={{0,3},{1,0},{2,1},{3,2},{4,7},{5,4},{6,5},{7,6},{8,11},{9,8},{10,9... | collective-permute-start | bytes 393224 | tf_op jit(solution)/shard_map/ppermute | solution.py:116
  113.9 6.1 %collective-permute-start.4 = (bf16[256,1,2,128]{3,0,1,2:T(8,128)(2,1)S(1)}, bf16[256,1,2,128]{3,0,1,2:T(8,128)(2,1)S(1)}, u32[]{:S(2)}, u32[]{:S(2)}) collective-permute-start(bf16[256,1,2,128]{3,0,1,2:T(8,128)(2,1)S(1)} %get-tuple-element.48), channel_id=1, source_target_pairs={{0,2},{1,3},{2,0},{3,1},{4,6},{5,7},{6,4},{7,5},{8,10},{9,11},{10,... | collective-permute-start | bytes 393224 | tf_op jit(solution)/shard_map/ppermute | solution.py:116
  116.4 6.6 %collective-permute-start.5 = (bf16[256,1,2,128]{3,0,1,2:T(8,128)(2,1)S(1)}, bf16[256,1,2,128]{3,0,1,2:T(8,128)(2,1)S(1)}, u32[]{:S(2)}, u32[]{:S(2)}) collective-permute-start(bf16[256,1,2,128]{3,0,1,2:T(8,128)(2,1)S(1)} %get-tuple-element.47), channel_id=1, source_target_pairs={{0,1},{1,2},{2,3},{3,0},{4,5},{5,6},{6,7},{7,4},{8,9},{9,10},{10,1... | collective-permute-start | bytes 393224 | tf_op jit(solution)/shard_map/ppermute | solution.py:116
  123.2 0.8 copy-start.22

commit v13 on v12

--- a/solution.py
+++ b/solution.py
@@ -211,21 +211,16 @@
         )
         + correction[..., None] * total_in[:, None, None, :]
     )
+    query_grad = tri_feature_back(
+        grad_qfeat, query_one, query_two, proj_wide, take_a, take_b, off
+    )
+    query_low = query_grad.transpose(2, 1, 0, 3).astype(bf16)
+    query_out = head_return(query_low, heads_all)
+    suffix_summed = scan_sum(suffix_got, True)
+    suffix_summed, query_out = lax.optimization_barrier((suffix_summed, query_out))
+    merged_state, merged_total = scan_return(suffix_summed, suffix_part.shape[0], suffix_part.shape[1])
     grad_kfeat = jnp.einsum("hmij,hmif->hjf", dscores, query_feat, preferred_element_type=f32)
     grad_value = jnp.einsum("hmij,hmid->hjd", weights, grad_low, preferred_element_type=f32)
-    suffix_summed = scan_sum(suffix_got, True)
-    suffix_summed, grad_qfeat, grad_kfeat, grad_value = lax.optimization_barrier(
-        (suffix_summed, grad_qfeat, grad_kfeat, grad_value)
-    )
-    merged_state, merged_total = scan_return(suffix_summed, suffix_part.shape[0], suffix_part.shape[1])
-    query_grad = tri_feature_back(
-        grad_qfeat, query_one, query_two, proj_wide, take_a, take_b, off
-    )
-    query_low = query_grad.transpose(2, 1, 0, 3).astype(bf16)
-    query_low, merged_state, merged_total = lax.optimization_barrier(
-        (query_low, merged_state, merged_total)
-    )
-    query_out = head_return(query_low, heads_all)
 
     merged_hi, merged_lo = split_parts(merged_state.transpose(0, 2, 1), 2)
     kfeat_total = (

time: 125 us -> 143 us (1.14)
  local copies, waits for them, and re-layouts: 15.6 us -> 28 us
  starting transfers between devices: 31.1 us -> 36.8 us
  matrix products: 36.3 us -> 39.2 us
  other arithmetic: 17.6 us -> 14.8 us
    mul x1 -> x0, other arithmetic: 5.95 us -> none  [tri_feature_back(): cotangent * second]
    all_to_all x2, waiting for transfers between devices: 8.29 us -> 13.2 us  [scan_return(): lax.all_to_all(summed, 'ctx', 0, 0, tiled=True).reshape(n * per, width)]
    all_to_all x2, starting transfers between devices: 9.07 us -> 13.6 us  [scan_return(): lax.all_to_all(summed, 'ctx', 0, 0, tiled=True).reshape(n * per, width)]
    all_to_all x2, waiting for transfers between devices: 7.99 us -> 4.36 us  [scan_send(): return lax.all_to_all(flat.reshape(n, per, width), 'ctx', 0, 0, tiled=True)]
    dynamic_update_slice x4, local copies, waits for them, and re-layouts: 0.9 us -> 3.16 us  [head_return(): lax.dynamic_update_slice_in_dim(out, piece, (me + k) % count * owned, axi...]
    ppermute x3, waiting for transfers between devices: 5.84 us -> 3.96 us  [head_return(): lax.ppermute(piece, 'head', [(j, (j - k) % count) for j in range(count)])]
    slice x2, local copies, waits for them, and re-layouts: 1.12 us -> 2.96 us  [scan_return(): state_out = back[:heads * feat].reshape(heads, feat, width)]
    convert_element_type x1, local copies, waits for them, and re-layouts: 0.21 us -> 2.06 us  [split_parts(): parts.append(hi.astype(bf16))]
  transfers between devices with their start and end apart: 10 -> 10, of which waited for: 7 -> 4; matrix products, arithmetic and copies ran while one was open for 31% -> 28% of each run, Pallas kernels for 0% -> 0%
where the time goes in v13:
time: 143 us; the launch traced here: 142 us
  matrix products  39.2 us (27%)
  starting transfers between devices  36.8 us (26%)
  local copies, waits for them, and re-layouts  28 us (20%)
  waiting for transfers between devices  21.5 us (15%)
  other arithmetic  14.8 us (10%)
  between operations  1.43 us (1%)
    all_to_all x2, starting transfers between devices, scan_return(): lax.all_to_all(summed, 'ctx', 0, 0, tiled=True).reshape(n * per, width)  13.6 us
    all_to_all x2, starting transfers between devices, scan_send(): return lax.all_to_all(flat.reshape(n, per, width), 'ctx', 0, 0, tiled=True)  13.4 us
    all_to_all x2, waiting for transfers between devices, scan_return(): lax.all_to_all(summed, 'ctx', 0, 0, tiled=True).reshape(n * per, width)  13.2 us
    dot_general x12, matrix products, dot_parts(): term = jnp.einsum(pattern, *args, preferred_element_type=f32)  9.53 us
    ppermute x3, starting transfers between devices, head_exchange(): lax.ppermute(piece, 'head', [(j, (j + k) % count) for j in range(count)])  6.57 us
    unnamed x81, local copies, waits for them, and re-layouts  5.83 us
    dot_general x2, matrix products, take_pair(): out = jnp.einsum('...k,kn->...n', lhs, rhs, preferred_element_type=f32)  5.23 us
    dot_general x1, matrix products, body(): jnp.einsum('hmik,hkf->hmif', jnp.concatenate([dscores, grad_hi, grad_hi,...  5.05 us
  transfers between devices with their start and end apart: 10, of which 4 were waited for; matrix products, arithmetic and copies ran while one was open for 28% of the time, Pallas kernels for 0%

profile of v13, /device:TPU:1, one launch (start us, length us, event | category | flops | bytes accessed | tf_op | source)
XLA Modules:
  0.0 141.8 jit_solution(15893473689812433052)
XLA Ops:
  0.7 1.4 %copy_bitcast_fusion = (bf16[1,256,1,8,128]{4,1,3,2,0:T(8,128)(2,1)S(1)}, bf16[1,256,1,8,128]{4,1,3,2,0:T(8,128)(2,1)S(1)}) fusion(bf16[256,1,8,128]{3,2,1,0:T(8,128)(2,1)} %param.12, bf16[256,1,8,128]{3,2,1,0:T(8,128)(2,1)} %param.9), kind=kLoop, calls=%fused_computation.120 | loop fusion | bytes 2097152 | tf_op jit(solution)/shard_map/stack | solution.py:161
  2.3 2.5 %collective-permute-start = (bf16[2,256,1,2,128]{4,1,3,2,0:T(8,128)(2,1)S(1)}, bf16[2,256,1,2,128]{4,1,3,2,0:T(8,128)(2,1)S(1)}, u32[]{:S(2)}, u32[]{:S(2)}) collective-permute-start(bf16[2,256,1,2,128]{4,1,3,2,0:T(8,128)(2,1)S(1)} %get-tuple-element.30), channel_id=1, source_target_pairs={{0,1},{1,2},{2,3},{3,0},{4,5},{5,6},{6,7},{7,4},{8,9},{9,10},{10,1... | collective-permute-start | bytes 786440 | tf_op jit(solution)/shard_map/ppermute | solution.py:103
  4.8 3.3 %collective-permute-start.1 = (bf16[2,256,1,2,128]{4,1,3,2,0:T(8,128)(2,1)S(1)}, bf16[2,256,1,2,128]{4,1,3,2,0:T(8,128)(2,1)S(1)}, u32[]{:S(2)}, u32[]{:S(2)}) collective-permute-start(bf16[2,256,1,2,128]{4,1,3,2,0:T(8,128)(2,1)S(1)} %get-tuple-element.31), channel_id=1, source_target_pairs={{0,2},{1,3},{2,0},{3,1},{4,6},{5,7},{6,4},{7,5},{8,10},{9,11},{10,... | collective-permute-start | bytes 786440 | tf_op jit(solution)/shard_map/ppermute | solution.py:103
  8.1 0.7 collective-permute-start.2
  9.1 1.2 constant_dynamic-slice_fusion.1
  10.4 0.8 reduce-precision_convert_fusion.12
  11.7 1.3 copy-done.3
  13.7 0.9 fusion.58
  14.6 8.6 %all-to-all-start = ((f32[32,40,128]{2,1,0:T(8,128)}), f32[32,40,128]{2,1,0:T(8,128)S(1)}, u32[]{:S(2)}, u32[]{:S(2)}) async-start(f32[32,40,128]{2,1,0:T(8,128)} %bitcast.26), calls=%async_computation | async-start | bytes 1310720 | tf_op jit(solution)/shard_map/all_to_all | solution.py:70
  23.2 0.7 iota_compare_fusion.1
  23.9 1.1 pad_maximum_fusion.2
  25.3 0.7 copy-done.5
  26.0 1.0 reduce-precision_convert_fusion.9
  27.0 4.7 %fusion.79 = f32[2,4,256,1056]{2,3,1,0:T(8,128)} fusion(bf16[96,1056,1,1]{1,0,3,2:T(8,128)(2,1)S(1)} %copy-done.26, bf16[2,4,256,32]{2,3,0,1:T(8,128)(2,1)S(1)} %get-tuple-element.43, bf16[2,4,256,32]{2,3,0,1:T(8,128)(2,1)S(1)} %get-tuple-element.42, bf16[2,4,256,32]{2,3,0,1:T(8,128)(2,1)S(1)} %get-tuple-element.41), kind=kOutput, calls=%fused_computation.130 | convolution fusion | flops 416415744 | bytes 9246720 | tf_op jit(solution)/shard_map/...k,kn->...n/dot_general | solution.py:49
  31.7 4.4 %all-to-all-done = f32[32,40,128]{2,1,0:T(8,128)S(1)} async-done(((f32[32,40,128]{2,1,0:T(8,128)}), f32[32,40,128]{2,1,0:T(8,128)S(1)}, u32[]{:S(2)}, u32[]{:S(2)}) %all-to-all-start) | async-done | bytes 655392 | tf_op jit(solution)/shard_map/all_to_all | solution.py:70
  36.6 1.2 copy.78
  37.8 4.8 %all-to-all-start.1 = ((f32[32,40,128]{2,1,0:T(8,128)}), f32[32,40,128]{2,1,0:T(8,128)}, u32[]{:S(2)}, u32[]{:S(2)}) async-start(f32[32,40,128]{2,1,0:T(8,128)} %copy.78), calls=%async_computation.1 | async-start | bytes 1310720 | tf_op jit(solution)/shard_map/all_to_all | solution.py:84
  42.6 4.3 %broadcast_multiply_fusion = (bf16[2,4,256,528]{2,3,1,0:T(8,128)(2,1)S(1)}, bf16[2,4,256,528]{2,3,1,0:T(8,128)(2,1)S(1)}) fusion(bf16[528]{0:T(1024)(128)(2,1)} %constant.77.clone, f32[2,4,256,1056]{2,3,1,0:T(8,128)} %fusion.79), kind=kLoop, calls=%fused_computation.84 | loop fusion | flops 4325376 | bytes 12977184 | tf_op jit(solution)/shard_map/mul | solution.py:173
  46.8 1.5 %copy-done.1 = bf16[2,4,256,528]{2,3,1,0:T(8,128)(2,1)} copy-done((bf16[2,4,256,528]{2,3,1,0:T(8,128)(2,1)}, bf16[2,4,256,528]{2,3,1,0:T(8,128)(2,1)S(1)}, u32[]{:S(2)}) %copy-start.1) | copy-done | bytes 2162712
  48.3 2.6 %select_reduce_fusion = (f32[2,4,256]{2,1,0:T(4,128)}, bf16[2,4,256,256]{2,3,1,0:T(8,128)(2,1)}) fusion(pred[256,256]{0,1:T(8,128)(4,1)S(1)} %copy-done.28, bf16[2,4,256,528]{2,3,1,0:T(8,128)(2,1)S(1)} %get-tuple-element.18, bf16[2,256,528]{1,2,0:T(8,128)(2,1)S(1)} %get-tuple-element.17), kind=kOutput, calls=%fused_computation.26 | convolution fusion | flops 555218944 | bytes 3825664 | tf_op jit(solution)/shard_map/hmif,hjf->hmij/dot_general | solution.py:181
  50.9 4.7 %all-to-all-done.1 = f32[32,40,128]{2,1,0:T(8,128)} async-done(((f32[32,40,128]{2,1,0:T(8,128)}), f32[32,40,128]{2,1,0:T(8,128)}, u32[]{:S(2)}, u32[]{:S(2)}) %all-to-all-start.1) | async-done | bytes 655392 | tf_op jit(solution)/shard_map/all_to_all | solution.py:84
  55.6 1.3 slice.90
  56.9 1.9 %slice.92 = f32[1056,128]{1,0:T(8,128)} slice(f32[1280,128]{1,0:T(8,128)} %bitcast.27), slice={[0:1056], [0:128]} | slice | bytes 1081344 | tf_op jit(solution)/shard_map/slice | solution.py:85
  58.8 1.3 reshape.58
  60.1 1.4 %fusion.160 = (f32[2,528]{1,0:T(2,128)}, bf16[2,528,1,1]{1,0,2,3:T(2,128)(2,1)S(1)}, bf16[2,528,1,1]{1,0,2,3:T(2,128)(2,1)S(1)}) fusion(f32[2,640]{1,0:T(2,128)} %reshape.58), kind=kLoop, calls=%fused_computation.231 | loop fusion | flops 4224 | bytes 12672 | tf_op jit(solution)/shard_map/slice | solution.py:87
  61.5 2.0 %fusion.64 = (bf16[2,128,528]{1,2,0:T(8,128)(2,1)}, bf16[2,128,528]{1,2,0:T(8,128)(2,1)}) fusion(f32[2,128,528]{1,2,0:T(8,128)} %bitcast.185), kind=kLoop, calls=%fused_computation.110 | loop fusion | flops 540672 | bytes 1081344 | tf_op jit(solution)/shard_map/convert_element_type | solution.py:28
  63.5 2.1 %fusion.142 = f32[2,1,4,256]{3,1,2,0:T(1,128)S(1)} fusion(bf16[2,4,256,528]{2,3,1,0:T(8,128)(2,1)} %copy-done.1, bf16[2,528,1,1]{1,0,2,3:T(2,128)(2,1)S(1)} %get-tuple-element.54), kind=kOutput, calls=%fused_computation.211 | convolution fusion | flops 2162688 | bytes 2172992 | tf_op jit(solution)/shard_map/hmif,hf->hmi/dot_general | solution.py:36
  65.9 1.2 fusion.14
  67.2 1.2 fusion.21
  68.4 1.6 %reduce-precision_convert_fusion.2 = (bf16[2,4,256,128]{3,2,0,1:T(8,128)(2,1)}, bf16[2,4,256,128]{3,2,0,1:T(8,128)(2,1)}, bf16[2,4,256,128]{3,2,0,1:T(8,128)(2,1)}) fusion(f32[2,4,256]{2,0,1:T(2,128)S(1)} %copy.79, bf16[2,256,4,2,128]{4,1,3,2,0:T(8,128)(2,1)S(1)} %copy-done.6), kind=kLoop, calls=%fused_computation.32 | loop fusion | flops 1835008 | bytes 2105344 | tf_op jit(solution)/shard_map/convert_element_type | solution.py:26
  70.0 1.1 fusion.32
  71.7 0.7 fusion.131
  72.4 0.7 fusion.129
  73.7 1.3 reshape.61
  75.0 2.1 %copy.89 = bf16[2,4,256,128]{2,3,1,0:T(8,128)(2,1)} copy(bf16[2,4,256,128]{3,2,0,1:T(8,128)(2,1)} %get-tuple-element.26) | data formatting | bytes 1048576 | tf_op jit(solution)/shard_map/convert_element_type | solution.py:26
  77.0 2.0 %copy.91 = bf16[2,4,256,128]{2,3,1,0:T(8,128)(2,1)} copy(bf16[2,4,256,128]{3,2,0,1:T(8,128)(2,1)} %get-tuple-element.27) | data formatting | bytes 1048576 | tf_op jit(solution)/shard_map/convert_element_type | solution.py:28
  79.1 1.8 %fusion.77 = f32[2,528,128,1]{2,1,3,0:T(8,128)S(1)} fusion(bf16[2,4,256,528]{2,3,1,0:T(8,128)(2,1)S(1)} %get-tuple-element.19, bf16[2,4,256,128]{3,2,0,1:T(8,128)(2,1)} %get-tuple-element.28), kind=kOutput, calls=%fused_computation.127 | convolution fusion | flops 276824064 | bytes 3227648 | tf_op jit(solution)/shard_map/hmif,hmid->hfd/dot_general | solution.py:193
  80.9 0.9 select_maximum_fusion
  81.8 4.8 %all-to-all-start.2 = ((f32[32,40,128]{2,1,0:T(8,128)}), f32[32,40,128]{2,1,0:T(8,128)}, u32[]{:S(2)}, u32[]{:S(2)}) async-start(f32[32,40,128]{2,1,0:T(8,128)} %bitcast.188), calls=%async_computation.2 | async-start | bytes 1310720 | tf_op jit(solution)/shard_map/all_to_all | solution.py:70
  86.6 1.7 %select_convert_fusion = bf16[2,4,256,256]{2,3,1,0:T(8,128)(2,1)S(1)} fusion(f32[2,4,256]{2,1,0:T(4,128)} %copy.88, pred[256,256]{0,1:T(8,128)(4,1)} %iota_compare_fusion.1, bf16[2,4,256,128]{3,2,0,1:T(8,128)(2,1)} %get-tuple-element.28, bf16[256,2,128]{2,1,0:T(2,128)(2,1)} %copy-done.9), kind=kOutput, calls=%fused_computation.24 | convolution fusion | flops 135790592 | bytes 1777664 | tf_op jit(solution)/shard_map/hmid,hjd->hmij/dot_general | solution.py:199
  88.3 5.0 %slice_multiply_fusion = (f32[2,4,256,528]{2,3,1,0:T(8,128)S(1)}, f32[2,4,256,528]{2,3,1,0:T(8,128)S(1)}) fusion(f32[2,4,256,1056]{2,3,1,0:T(8,128)} %fusion.79, f32[2,528]{1,0:T(2,128)S(1)} %copy-done.35, f32[2,4,256]{2,1,0:T(4,128)S(1)} %copy-done.33, f32[528]{0:T(1024)S(1)} %copy-done.36, bf16[2,4,256,128]{2,3,1,0:T(8,128)(2,1)S(1)} %copy-done.16, ...), kind=kOutput, calls=%fused_computation.11 | convolution fusion | flops 1405419520 | bytes 20494528 | tf_op jit(solution)/shard_map/hmik,hkf->hmif/dot_general | solution.py:206
  93.4 1.5 %reduce-precision_convert_fusion = (bf16[2,4,256,1056]{2,3,1,0:T(8,128)(2,1)S(1)}, bf16[2,4,256,1056]{2,3,1,0:T(8,128)(2,1)S(1)}) fusion(f32[2,4,256,528]{2,3,1,0:T(8,128)S(1)} %get-tuple-element.21, f32[2,4,256,528]{2,3,1,0:T(8,128)S(1)} %get-tuple-element.20), kind=kLoop, calls=%fused_computation.1 | loop fusion | flops 10813440 | bytes 17301504 | tf_op jit(solution)/shard_map/convert_element_type | solution.py:26
  95.0 0.9 fusion.1
  95.9 0.9 fusion.158
  96.8 1.0 fusion.97
  97.9 1.0 fusion.33
  98.9 0.8 collective-permute-start.5
  99.9 2.3 %collective-permute-start.3 = (bf16[256,1,2,128]{3,0,1,2:T(8,128)(2,1)S(1)}, bf16[256,1,2,128]{3,0,1,2:T(8,128)(2,1)S(1)}, u32[]{:S(2)}, u32[]{:S(2)}) collective-permute-start(bf16[256,1,2,128]{3,0,1,2:T(8,128)(2,1)S(1)} %get-tuple-element.39), channel_id=1, source_target_pairs={{0,3},{1,0},{2,1},{3,2},{4,7},{5,4},{6,5},{7,6},{8,11},{9,8},{10,9... | collective-permute-start | bytes 393224 | tf_op jit(solution)/shard_map/ppermute | solution.py:116
  102.2 0.9 broadcast_in_dim.27
  103.1 0.8 copy_dynamic-update-slice_fusion.3
  103.9 4.0 %collective-permute-done.3 = bf16[256,1,2,128]{3,0,1,2:T(8,128)(2,1)S(1)} collective-permute-done((bf16[256,1,2,128]{3,0,1,2:T(8,128)(2,1)S(1)}, bf16[256,1,2,128]{3,0,1,2:T(8,128)(2,1)S(1)}, u32[]{:S(2)}, u32[]{:S(2)}) %collective-permute-start.3) | collective-permute-done | bytes 131104 | tf_op jit(solution)/shard_map/ppermute | solution.py:116
  107.8 0.8 copy_dynamic-update-slice_fusion.2
  108.6 0.8 copy_dynamic-update-slice_fusion.1
  109.4 0.8 copy_dynamic-update-slice_fusion
  110.2 1.6 %fusion.59 = f32[32,40,128]{2,0,1:T(8,128)S(1)} fusion(f32[32,40,128]{2,1,0:T(8,128)} %all-to-all-done.2), kind=kOutput, calls=%fused_computation.105 | convolution fusion | flops 62915584 | bytes 1310720 | tf_op jit(solution)/shard_map/ij,jrc->irc/dot_general | solution.py:78
  111.8 1.2 copy.103
  113.0 8.9 %all-to-all-start.3 = ((f32[32,40,128]{2,1,0:T(8,128)}), f32[32,40,128]{2,1,0:T(8,128)}, u32[]{:S(2)}, u32[]{:S(2)}) async-start(f32[32,40,128]{2,1,0:T(8,128)} %copy.103), calls=%async_computation.3 | async-start | bytes 1310720 | tf_op jit(solution)/shard_map/all_to_all | solution.py:84
  121.9 2.6 %convolution_bitcast_fusion.1 = f32[2,256,128]{2,1,0:T(8,128)} fusion(bf16[2,4,256,128]{3,2,0,1:T(8,128)(2,1)} %get-tuple-element.28, bf16[2,4,256,256]{2,3,1,0:T(8,128)(2,1)} %get-tuple-element.58, pred[256,256]{0,1:T(8,128)(4,1)} %iota_compare_fusion.1), kind=kOutput, calls=%fused_computation.69 | convolution fusion | flops 134742016 | bytes 1900544 | tf_op jit(solution)/shard_map/hmij,hmid->hjd/dot_general | solution.py:223
  124.5 1.8 %convolution_bitcast_fusion = f32[2,256,528]{1,2,0:T(8,128)} fusion(bf16[2,4,256,256]{2,3,1,0:T(8,128)(2,1)S(1)} %copy-done.14, bf16[2,4,256,528]{2,3,1,0:T(8,128)(2,1)S(1)} %get-tuple-element.19), kind=kOutput, calls=%fused_computation.43 | convolution fusion | flops 553648128 | bytes 4292608 | tf_op jit(solution)/shard_map/hmij,hmif->hjf/dot_general | solution.py:222
  126.3 8.5 %all-to-all-done.3 = f32[32,40,128]{2,1,0:T(8,128)} async-done(((f32[32,40,128]{2,1,0:T(8,128)}), f32[32,40,128]{2,1,0:T(8,128)}, u32[]{:S(2)}, u32[]{:S(2)}) %all-to-all-start.3) | async-done | bytes 655392 | tf_op jit(solution)/shard_map/all_to_all | solution.py:84
  134.8 0.7 slice.98
  135.5 1.1 slice.97
  137.7 0.8 copy.106
  141.1 0.8 copy.105
  (111 shorter events, 7.8 us)
Async XLA Ops:
  0.6 8.3 %copy-start = (bf16[256,8,128]{2,1,0:T(8,128)(2,1)S(1)}, bf16[256,8,128]{2,1,0:T(8,128)(2,1)}, u32[]{:S(2)}) copy-start(bf16[256,8,128]{2,1,0:T(8,128)(2,1)} %param.11) | copy-start | bytes 1572868
  0.7 8.2 %copy-start.31 = (s32[2,128,32]{1,2,0:T(8,128)S(1)}, s32[2,128,32]{1,2,0:T(8,128)}, u32[]{:S(2)}) copy-start(s32[2,128,32]{1,2,0:T(8,128)} %param.13) | copy-start | bytes 98308
  0.7 10.5 %copy-start.25 = (bf16[96,1056,1]{1,0,2:T(8,128)(2,1)S(1)}, bf16[96,1056,1]{1,0,2:T(8,128)(2,1)}, u32[]{:S(2)}) copy-start(bf16[96,1056,1]{1,0,2:T(8,128)(2,1)} %constant.95) | copy-start | bytes 608260
  2.3 21.5 %collective-permute-start = (bf16[2,256,1,2,128]{4,1,3,2,0:T(8,128)(2,1)S(1)}, bf16[2,256,1,2,128]{4,1,3,2,0:T(8,128)(2,1)S(1)}, u32[]{:S(2)}, u32[]{:S(2)}) collective-permute-start(bf16[2,256,1,2,128]{4,1,3,2,0:T(8,128)(2,1)S(1)} %get-tuple-element.30), channel_id=1, source_target_pairs={{0,1},{1,2},{2,3},{3,0},{4,5},{5,6},{6,7},{7,4},{8,9},{9,10},{10,1... | collective-permute-start | bytes 786440 | tf_op jit(solution)/shard_map/ppermute | solution.py:103
  4.8 19.0 %collective-permute-start.1 = (bf16[2,256,1,2,128]{4,1,3,2,0:T(8,128)(2,1)S(1)}, bf16[2,256,1,2,128]{4,1,3,2,0:T(8,128)(2,1)S(1)}, u32[]{:S(2)}, u32[]{:S(2)}) collective-permute-start(bf16[2,256,1,2,128]{4,1,3,2,0:T(8,128)(2,1)S(1)} %get-tuple-element.31), channel_id=1, source_target_pairs={{0,2},{1,3},{2,0},{3,1},{4,6},{5,7},{6,4},{7,5},{8,10},{9,11},{10,... | collective-permute-start | bytes 786440 | tf_op jit(solution)/shard_map/ppermute | solution.py:103
  8.1 15.7 %collective-permute-start.2 = (bf16[2,256,1,2,128]{4,1,3,2,0:T(8,128)(2,1)S(1)}, bf16[2,256,1,2,128]{4,1,3,2,0:T(8,128)(2,1)}, u32[]{:S(2)}, u32[]{:S(2)}) collective-permute-start(bf16[2,256,1,2,128]{4,1,3,2,0:T(8,128)(2,1)S(1)} %get-tuple-element.32), channel_id=1, source_target_pairs={{0,3},{1,0},{2,1},{3,2},{4,7},{5,4},{6,5},{7,6},{8,11},{9,8},{10,9... | collective-permute-start | bytes 786440 | tf_op jit(solution)/shard_map/ppermute | solution.py:103
  8.9 16.4 %copy-start.17 = (bf16[2,128,32]{1,2,0:T(8,128)(2,1)}, bf16[2,128,32]{1,2,0:T(8,128)(2,1)S(1)}, u32[]{:S(2)}) copy-start(bf16[2,128,32]{1,2,0:T(8,128)(2,1)S(1)} %add_convert_fusion) | copy-start | bytes 49156
  9.0 4.3 %copy-start.9 = (bf16[256,2,128]{2,1,0:T(2,128)(2,1)}, bf16[256,2,128]{2,1,0:T(2,128)(2,1)S(1)}, u32[]{:S(2)}) copy-start(bf16[256,2,128]{2,1,0:T(2,128)(2,1)S(1)} %constant_dynamic-slice_fusion) | copy-start | bytes 393220
  11.7 1.3 copy-start.3
  14.6 21.5 %all-to-all-start = ((f32[32,40,128]{2,1,0:T(8,128)}), f32[32,40,128]{2,1,0:T(8,128)S(1)}, u32[]{:S(2)}, u32[]{:S(2)}) async-start(f32[32,40,128]{2,1,0:T(8,128)} %bitcast.26), calls=%async_computation | async-start | bytes 1310720 | tf_op jit(solution)/shard_map/all_to_all | solution.py:70
  23.8 3.1 %copy-start.26 = (bf16[96,1056,1,1]{1,0,3,2:T(8,128)(2,1)S(1)}, bf16[96,1056,1,1]{1,0,3,2:T(8,128)(2,1)}, u32[]{:S(2)}) copy-start(bf16[96,1056,1,1]{1,0,3,2:T(8,128)(2,1)} %constant.94) | copy-start | bytes 608260
  25.0 1.0 copy-start.5
  37.8 17.8 %all-to-all-start.1 = ((f32[32,40,128]{2,1,0:T(8,128)}), f32[32,40,128]{2,1,0:T(8,128)}, u32[]{:S(2)}, u32[]{:S(2)}) async-start(f32[32,40,128]{2,1,0:T(8,128)} %copy.78), calls=%async_computation.1 | async-start | bytes 1310720 | tf_op jit(solution)/shard_map/all_to_all | solution.py:84
  42.5 5.7 %copy-start.28 = (pred[256,256]{0,1:T(8,128)(4,1)S(1)}, pred[256,256]{0,1:T(8,128)(4,1)}, u32[]{:S(2)}) copy-start(pred[256,256]{0,1:T(8,128)(4,1)} %iota_compare_fusion.1) | copy-start | bytes 196612
  46.8 1.5 %copy-start.1 = (bf16[2,4,256,528]{2,3,1,0:T(8,128)(2,1)}, bf16[2,4,256,528]{2,3,1,0:T(8,128)(2,1)S(1)}, u32[]{:S(2)}) copy-start(bf16[2,4,256,528]{2,3,1,0:T(8,128)(2,1)S(1)} %get-tuple-element.18) | copy-start | bytes 6488068
  60.1 5.5 %copy-start.2 = (bf16[2,4,256,528]{2,3,1,0:T(8,128)(2,1)S(1)}, bf16[2,4,256,528]{2,3,1,0:T(8,128)(2,1)}, u32[]{:S(2)}) copy-start(bf16[2,4,256,528]{2,3,1,0:T(8,128)(2,1)} %copy-done.1) | copy-start | bytes 6488068
  63.5 2.5 %copy-start.7 = (f32[1056,128]{1,0:T(8,128)S(1)}, f32[1056,128]{1,0:T(8,128)}, u32[]{:S(2)}) copy-start(f32[1056,128]{1,0:T(8,128)} %slice.92) | copy-start | bytes 1622020
  67.1 1.2 copy-start.34
  67.1 1.3 copy-start.6
  67.1 2.9 %copy-start.10 = (bf16[256,2,128]{2,1,0:T(2,128)(2,1)S(1)}, bf16[256,2,128]{2,1,0:T(2,128)(2,1)}, u32[]{:S(2)}) copy-start(bf16[256,2,128]{2,1,0:T(2,128)(2,1)} %copy-done.9) | copy-start | bytes 393220
  67.2 2.9 %copy-start.29 = (pred[256,256]{0,1:T(8,128)(4,1)S(1)}, pred[256,256]{0,1:T(8,128)(4,1)}, u32[]{:S(2)}) copy-start(pred[256,256]{0,1:T(8,128)(4,1)} %iota_compare_fusion.1) | copy-start | bytes 196612
  67.2 2.9 %copy-start.38 = (bf16[2,4,256,256]{2,3,1,0:T(8,128)(2,1)S(1)}, bf16[2,4,256,256]{2,3,1,0:T(8,128)(2,1)}, u32[]{:S(2)}) copy-start(bf16[2,4,256,256]{2,3,1,0:T(8,128)(2,1)} %get-tuple-element.58) | copy-start | bytes 3145732
  79.1 1.8 %copy-start.30 = (f32[10,128]{1,0:T(8,128)S(1)}, f32[10,128]{1,0:T(8,128)}, u32[]{:S(2)}) copy-start(f32[10,128]{1,0:T(8,128)} %reshape.61) | copy-start | bytes 15364
  81.8 28.5 %all-to-all-start.2 = ((f32[32,40,128]{2,1,0:T(8,128)}), f32[32,40,128]{2,1,0:T(8,128)}, u32[]{:S(2)}, u32[]{:S(2)}) async-start(f32[32,40,128]{2,1,0:T(8,128)} %bitcast.188), calls=%async_computation.2 | async-start | bytes 1310720 | tf_op jit(solution)/shard_map/all_to_all | solution.py:70
  86.5 1.8 %copy-start.15 = (bf16[2,4,256,128]{2,3,1,0:T(8,128)(2,1)S(1)}, bf16[2,4,256,128]{2,3,1,0:T(8,128)(2,1)}, u32[]{:S(2)}) copy-start(bf16[2,4,256,128]{2,3,1,0:T(8,128)(2,1)} %copy.89) | copy-start | bytes 1572868
  86.5 1.8 %copy-start.16 = (bf16[2,4,256,128]{2,3,1,0:T(8,128)(2,1)S(1)}, bf16[2,4,256,128]{2,3,1,0:T(8,128)(2,1)}, u32[]{:S(2)}) copy-start(bf16[2,4,256,128]{2,3,1,0:T(8,128)(2,1)} %copy.91) | copy-start | bytes 1572868
  86.5 1.7 %copy-start.21 = (bf16[2,128,528]{1,2,0:T(8,128)(2,1)S(1)}, bf16[2,128,528]{1,2,0:T(8,128)(2,1)}, u32[]{:S(2)}) copy-start(bf16[2,128,528]{1,2,0:T(8,128)(2,1)} %get-tuple-element.35) | copy-start | bytes 811012
  86.6 1.7 %copy-start.22 = (bf16[2,128,528]{1,2,0:T(8,128)(2,1)S(1)}, bf16[2,128,528]{1,2,0:T(8,128)(2,1)}, u32[]{:S(2)}) copy-start(bf16[2,128,528]{1,2,0:T(8,128)(2,1)} %get-tuple-element.36) | copy-start | bytes 811012
  86.6 1.7 %copy-start.33 = (f32[2,4,256]{2,1,0:T(4,128)S(1)}, f32[2,4,256]{2,1,0:T(4,128)}, u32[]{:S(2)}) copy-start(f32[2,4,256]{2,1,0:T(4,128)} %copy.88) | copy-start | bytes 24580
  86.6 1.7 %copy-start.35 = (f32[2,528]{1,0:T(2,128)S(1)}, f32[2,528]{1,0:T(2,128)}, u32[]{:S(2)}) copy-start(f32[2,528]{1,0:T(2,128)} %get-tuple-element.52) | copy-start | bytes 12676
  86.6 1.7 %copy-start.36 = (f32[528]{0:T(1024)S(1)}, f32[528]{0:T(1024)}, u32[]{:S(2)}) copy-start(f32[528]{0:T(1024)} %constant.78.clone) | copy-start | bytes 6340
  88.3 5.1 %copy-start.13 = (bf16[2,4,256,256]{2,3,1,0:T(8,128)(2,1)}, bf16[2,4,256,256]{2,3,1,0:T(8,128)(2,1)S(1)}, u32[]{:S(2)}) copy-start(bf16[2,4,256,256]{2,3,1,0:T(8,128)(2,1)S(1)} %select_convert_fusion) | copy-start | bytes 3145732
  93.4 1.6 %copy-start.20 = (bf16[1056,32,1,1]{0,1,2,3:T(8,128)(2,1)S(1)}, bf16[1056,32,1,1]{0,1,2,3:T(8,128)(2,1)}, u32[]{:S(2)}) copy-start(bf16[1056,32,1,1]{0,1,2,3:T(8,128)(2,1)} %constant.96) | copy-start | bytes 202756
  95.0 1.0 copy-start.12
  95.9 0.9 copy-start.18
  98.9 10.5 %collective-permute-start.5 = (bf16[256,1,2,128]{3,0,1,2:T(8,128)(2,1)S(1)}, bf16[256,1,2,128]{3,0,1,2:T(8,128)(2,1)S(1)}, u32[]{:S(2)}, u32[]{:S(2)}) collective-permute-start(bf16[256,1,2,128]{3,0,1,2:T(8,128)(2,1)S(1)} %get-tuple-element.37), channel_id=1, source_target_pairs={{0,1},{1,2},{2,3},{3,0},{4,5},{5,6},{6,7},{7,4},{8,9},{9,10},{10,1... | collective-permute-start | bytes 393224 | tf_op jit(solution)/shard_map/ppermute | solution.py:116
  99.7 8.9 %collective-permute-start.4 = (bf16[256,1,2,128]{3,0,1,2:T(8,128)(2,1)S(1)}, bf16[256,1,2,128]{3,0,1,2:T(8,128)(2,1)S(1)}, u32[]{:S(2)}, u32[]{:S(2)}) collective-permute-start(bf16[256,1,2,128]{3,0,1,2:T(8,128)(2,1)S(1)} %get-tuple-element.38), channel_id=1, source_target_pairs={{0,2},{1,3},{2,0},{3,1},{4,6},{5,7},{6,4},{7,5},{8,10},{9,11},{10,... | collective-permute-start | bytes 393224 | tf_op jit(solution)/shard_map/ppermute | solution.py:116
  99.9 7.9 %collective-permute-start.3 = (bf16[256,1,2,128]{3,0,1,2:T(8,128)(2,1)S(1)}, bf16[256,1,2,128]{3,0,1,2:T(8,128)(2,1)S(1)}, u32[]{:S(2)}, u32[]{:S(2)}) collective-permute-start(bf16[256,1,2,128]{3,0,1,2:T(8,128)(2,1)S(1)} %get-tuple-element.39), channel_id=1, source_target_pairs={{0,3},{1,0},{2,1},{3,2},{4,7},{5,4},{6,5},{7,6},{8,11},{9,8},{10,9... | collective-permute-start | bytes 393224 | tf_op jit(solution)/shard_map/ppermute | solution.py:116
  109.4 12.5 %copy-start.11 = (bf16[256,2,128]{2,1,0:T(2,128)(2,1)S(1)}, bf16[256,2,128]{2,1,0:T(2,128)(2,1)}, u32[]{:S(2)}) copy-start(bf16[256,2,128]{2,1,0:T(2,128)(2,1)} %copy-done.9) | copy-start | bytes 393220
  113.0 21.8 %all-to-all-start.3 = ((f32[32,40,128]{2,1,0:T(8,128)}), f32[32,40,128]{2,1,0:T(8,128)}, u32[]{:S(2)}, u32[]{:S(2)}) async-start(f32[32,40,128]{2,1,0:T(8,128)} %copy.103), calls=%async_computation.3 | async-start | bytes 1310720 | tf_op jit(solution)/shard_map/all_to_all | solution.py:84
  121.9 2.6 %copy-start.14 = (bf16[2,4,256,256]{2,3,1,0:T(8,128)(2,1)S(1)}, bf16[2,4,256,256]{2,3,1,0:T(8,128)(2,1)}, u32[]{:S(2)}) copy-start(bf16[2,4,256,256]{2,3,1,0:T(8,128)(2,1)} %copy-done.13) | copy-start | bytes 3145732
  124.5 12.1 %copy-start.32 = (bf16[528]{0:T(1024)(128)(2,1)S(1)}, bf16[528]{0:T(1024)(128)(2,1)}, u32[]{:S(2)}) copy-start(bf16[528]{0:T(1024)(128)(2,1)} %constant.77.clone) | copy-start | bytes 3172
  126.3 10.9 %copy-start.23 = (f32[2,256,128]{2,1,0:T(8,128)S(1)}, f32[2,256,128]{2,1,0:T(8,128)}, u32[]{:S(2)}) copy-start(f32[2,256,128]{2,1,0:T(8,128)} %convolution_bitcast_fusion.1) | copy-start | bytes 786436
  136.6 2.0 %copy-start.4 = (f32[2,256,1056]{1,2,0:T(8,128)S(1)}, f32[2,256,1056]{1,2,0:T(8,128)}, u32[]{:S(2)}) copy-start(f32[2,256,1056]{1,2,0:T(8,128)} %copy-done.3) | copy-start | bytes 6488068
  136.7 2.0 %copy-start.8 = (f32[2,256,528]{1,2,0:T(8,128)S(1)}, f32[2,256,528]{1,2,0:T(8,128)}, u32[]{:S(2)}) copy-start(f32[2,256,528]{1,2,0:T(8,128)} %convolution_bitcast_fusion) | copy-start | bytes 3244036
  136.7 2.0 %copy-start.37 = (f32[528]{0:T(1024)S(1)}, f32[528]{0:T(1024)}, u32[]{:S(2)}) copy-start(f32[528]{0:T(1024)} %constant.78.clone) | copy-start | bytes 6340
  138.6 0.9 copy-start.27
  139.5 0.7 copy-start.19
  139.5 1.1 copy-start.24

commit v14 on v12

--- a/solution.py
+++ b/solution.py
@@ -139,9 +139,16 @@
     spread = jnp.concatenate([cotangent * second, cotangent * first * off], axis=-1)
     gather = jnp.concatenate([take_a.T, take_b.T], axis=0).astype(bf16)
     dsketch = dot_parts("...k,ka->...a", spread, gather, 2) * (2.0 / width)
-    back_one = jnp.einsum("...f,df->...d", dsketch * sketch_two, proj_wide[0], precision=highest)
-    back_two = jnp.einsum("...f,df->...d", dsketch * sketch_one, proj_wide[1], precision=highest)
-    return (back_one + back_two) * proj_wide.shape[1] ** (-0.5)
+    one_hi, one_lo = split_parts(dsketch * sketch_two, 2)
+    two_hi, two_lo = split_parts(dsketch * sketch_one, 2)
+    proj = proj_wide.astype(bf16)
+    back = jnp.einsum(
+        "...k,dk->...d",
+        jnp.concatenate([one_hi, one_lo, two_hi, two_lo], axis=-1),
+        jnp.concatenate([proj[0], proj[0], proj[1], proj[1]], axis=-1),
+        preferred_element_type=f32,
+    )
+    return back * proj_wide.shape[1] ** (-0.5)
 
 
 def body(queries, keys, values, dout, signs):

time: 125 us -> 124 us (level)
  matrix products: 36.3 us -> 34.1 us
  waiting for transfers between devices: 22.1 us -> 23.5 us
    dot_general x4 -> x2, matrix products: 2.81 us -> 0.55 us  [tri_feature_back(): jnp.einsum('...k,dk->...d', jnp.concatenate([one_hi, one_lo, two_hi, two_...]
    all_to_all x2, waiting for transfers between devices: 8.29 us -> 9.93 us  [scan_return(): lax.all_to_all(summed, 'ctx', 0, 0, tiled=True).reshape(n * per, width)]
    unnamed x73 -> x75, local copies, waits for them, and re-layouts: 6.89 us -> 6.78 us
where the time goes in v14:
time: 124 us; the launch traced here: 123 us
  matrix products  34.1 us (28%)
  starting transfers between devices  31.1 us (25%)
  waiting for transfers between devices  23.5 us (19%)
  other arithmetic  17.4 us (14%)
  local copies, waits for them, and re-layouts  16.1 us (13%)
  between operations  1.39 us (1%)
    all_to_all x2, starting transfers between devices, scan_send(): return lax.all_to_all(flat.reshape(n, per, width), 'ctx', 0, 0, tiled=True)  12.8 us
    all_to_all x2, waiting for transfers between devices, scan_return(): lax.all_to_all(summed, 'ctx', 0, 0, tiled=True).reshape(n * per, width)  9.93 us
    dot_general x12, matrix products, dot_parts(): term = jnp.einsum(pattern, *args, preferred_element_type=f32)  9.67 us
    all_to_all x2, starting transfers between devices, scan_return(): lax.all_to_all(summed, 'ctx', 0, 0, tiled=True).reshape(n * per, width)  9.07 us
    all_to_all x2, waiting for transfers between devices, scan_send(): return lax.all_to_all(flat.reshape(n, per, width), 'ctx', 0, 0, tiled=True)  7.68 us
    unnamed x75, local copies, waits for them, and re-layouts  6.78 us
    ppermute x3, starting transfers between devices, head_exchange(): lax.ppermute(piece, 'head', [(j, (j + k) % count) for j in range(count)])  6.57 us
    mul x1, other arithmetic, tri_feature_back(): cotangent * second  5.95 us
  transfers between devices with their start and end apart: 10, of which 7 were waited for; matrix products, arithmetic and copies ran while one was open for 31% of the time, Pallas kernels for 0%

profile of v14, /device:TPU:1, one launch (start us, length us, event | category | flops | bytes accessed | tf_op | source)
XLA Modules:
  0.0 123.4 jit_solution(1300685670878565092)
XLA Ops:
  0.7 1.4 %copy_bitcast_fusion = (bf16[1,256,1,8,128]{4,1,3,2,0:T(8,128)(2,1)S(1)}, bf16[1,256,1,8,128]{4,1,3,2,0:T(8,128)(2,1)S(1)}) fusion(bf16[256,1,8,128]{3,2,1,0:T(8,128)(2,1)} %param.12, bf16[256,1,8,128]{3,2,1,0:T(8,128)(2,1)} %param.9), kind=kLoop, calls=%fused_computation.120 | loop fusion | bytes 2097152 | tf_op jit(solution)/shard_map/stack | solution.py:168
  2.3 2.5 %collective-permute-start = (bf16[2,256,1,2,128]{4,1,3,2,0:T(8,128)(2,1)S(1)}, bf16[2,256,1,2,128]{4,1,3,2,0:T(8,128)(2,1)S(1)}, u32[]{:S(2)}, u32[]{:S(2)}) collective-permute-start(bf16[2,256,1,2,128]{4,1,3,2,0:T(8,128)(2,1)S(1)} %get-tuple-element.40), channel_id=1, source_target_pairs={{0,1},{1,2},{2,3},{3,0},{4,5},{5,6},{6,7},{7,4},{8,9},{9,10},{10,1... | collective-permute-start | bytes 786440 | tf_op jit(solution)/shard_map/ppermute | solution.py:103
  4.8 3.3 %collective-permute-start.1 = (bf16[2,256,1,2,128]{4,1,3,2,0:T(8,128)(2,1)S(1)}, bf16[2,256,1,2,128]{4,1,3,2,0:T(8,128)(2,1)S(1)}, u32[]{:S(2)}, u32[]{:S(2)}) collective-permute-start(bf16[2,256,1,2,128]{4,1,3,2,0:T(8,128)(2,1)S(1)} %get-tuple-element.41), channel_id=1, source_target_pairs={{0,2},{1,3},{2,0},{3,1},{4,6},{5,7},{6,4},{7,5},{8,10},{9,11},{10,... | collective-permute-start | bytes 786440 | tf_op jit(solution)/shard_map/ppermute | solution.py:103
  8.1 0.7 collective-permute-start.2
  8.8 1.5 %constant_dynamic-slice_fusion = (bf16[256,2,128]{2,1,0:T(2,128)(2,1)S(1)}, bf16[256,2,128]{2,1,0:T(2,128)(2,1)S(1)}) fusion(bf16[256,8,128]{2,1,0:T(8,128)(2,1)} %param.11, s32[]{:T(128)S(6)} %select_n.62, bf16[256,8,128]{2,1,0:T(8,128)(2,1)} %param.10), kind=kLoop, calls=%fused_computation.227 | loop fusion | bytes 524292 | tf_op jit(solution)/shard_map/dynamic_slice | solution.py:167
  10.5 0.8 reduce-precision_convert_fusion.16
  11.3 0.5 fusion.112
  11.8 1.3 %copy-done.2 = f32[2,256,1056]{1,2,0:T(8,128)} copy-done((f32[2,256,1056]{1,2,0:T(8,128)}, f32[2,256,1056]{1,2,0:T(8,128)S(1)}, u32[]{:S(2)}) %copy-start.2) | copy-done | bytes 2162712
  13.7 0.9 fusion.58
  14.6 8.6 %all-to-all-start = ((f32[32,40,128]{2,1,0:T(8,128)}), f32[32,40,128]{2,1,0:T(8,128)S(1)}, u32[]{:S(2)}, u32[]{:S(2)}) async-start(f32[32,40,128]{2,1,0:T(8,128)} %bitcast.26), calls=%async_computation | async-start | bytes 1310720 | tf_op jit(solution)/shard_map/all_to_all | solution.py:70
  23.2 0.7 copy.219
  23.9 0.6 slice_bitcast_fusion.5
  24.6 0.7 copy-done.26
  25.3 1.1 pad_maximum_fusion.2
  26.7 0.8 copy-done.4
  27.4 1.0 reduce-precision_convert_fusion.11
  28.4 4.7 %fusion.80 = f32[2,4,256,1056]{2,3,1,0:T(8,128)} fusion(bf16[96,1056,1,1]{1,0,3,2:T(8,128)(2,1)S(1)} %copy-done.28, bf16[2,4,256,32]{2,3,0,1:T(8,128)(2,1)S(1)} %get-tuple-element.57, bf16[2,4,256,32]{2,3,0,1:T(8,128)(2,1)S(1)} %get-tuple-element.56, bf16[2,4,256,32]{2,3,0,1:T(8,128)(2,1)S(1)} %get-tuple-element.55), kind=kOutput, calls=%fused_computation.130 | convolution fusion | flops 416415744 | bytes 9246720 | tf_op jit(solution)/shard_map/...k,kn->...n/dot_general | solution.py:49
  33.2 2.9 %all-to-all-done = f32[32,40,128]{2,1,0:T(8,128)S(1)} async-done(((f32[32,40,128]{2,1,0:T(8,128)}), f32[32,40,128]{2,1,0:T(8,128)S(1)}, u32[]{:S(2)}, u32[]{:S(2)}) %all-to-all-start) | async-done | bytes 655392 | tf_op jit(solution)/shard_map/all_to_all | solution.py:70
  36.1 0.5 fusion.61
  36.6 1.2 %copy.82 = f32[32,40,128]{2,1,0:T(8,128)} copy(f32[32,40,128]{2,0,1:T(8,128)S(1)} %fusion.61) | data formatting | bytes 1310720 | tf_op jit(solution)/shard_map/ij,jrc->irc/dot_general | solution.py:78
  37.8 4.8 %all-to-all-start.1 = ((f32[32,40,128]{2,1,0:T(8,128)}), f32[32,40,128]{2,1,0:T(8,128)}, u32[]{:S(2)}, u32[]{:S(2)}) async-start(f32[32,40,128]{2,1,0:T(8,128)} %copy.82), calls=%async_computation.1 | async-start | bytes 1310720 | tf_op jit(solution)/shard_map/all_to_all | solution.py:84
  42.6 4.2 %broadcast_multiply_fusion = (bf16[2,4,256,528]{2,3,1,0:T(8,128)(2,1)S(1)}, bf16[2,4,256,528]{2,3,1,0:T(8,128)(2,1)S(1)}) fusion(bf16[528]{0:T(1024)(128)(2,1)S(1)} %copy-done.32, f32[2,4,256,1056]{2,3,1,0:T(8,128)} %fusion.80), kind=kLoop, calls=%fused_computation.82 | loop fusion | flops 4325376 | bytes 12977184 | tf_op jit(solution)/shard_map/mul | solution.py:180
  46.8 2.1 %select_convert_fusion.1 = (bf16[2,4,256,256]{2,3,1,0:T(8,128)(2,1)}, f32[2,4,256,256]{2,3,1,0:T(8,128)S(1)}) fusion(pred[256,256]{0,1:T(8,128)(4,1)S(1)} %iota_compare_fusion.1, bf16[2,4,256,528]{2,3,1,0:T(8,128)(2,1)S(1)} %get-tuple-element.28, bf16[2,256,528]{1,2,0:T(8,128)(2,1)S(1)} %get-tuple-element.27), kind=kOutput, calls=%fused_computation.25 | convolution fusion | flops 554172416 | bytes 5914624 | tf_op jit(solution)/shard_map/hmif,hjf->hmij/dot_general | solution.py:188
  49.1 6.5 %all-to-all-done.1 = f32[32,40,128]{2,1,0:T(8,128)} async-done(((f32[32,40,128]{2,1,0:T(8,128)}), f32[32,40,128]{2,1,0:T(8,128)}, u32[]{:S(2)}, u32[]{:S(2)}) %all-to-all-start.1) | async-done | bytes 655392 | tf_op jit(solution)/shard_map/all_to_all | solution.py:84
  55.6 0.7 slice.94
  56.3 1.1 slice.96
  57.5 2.2 %fusion.144 = f32[2,1,4,256]{3,1,2,0:T(1,128)S(1)} fusion(bf16[2,4,256,528]{2,3,1,0:T(8,128)(2,1)} %copy-done, bf16[2,528,1,1]{1,0,2,3:T(2,128)(2,1)S(1)} %get-tuple-element.75), kind=kOutput, calls=%fused_computation.223 | convolution fusion | flops 2162688 | bytes 2172992 | tf_op jit(solution)/shard_map/hmif,hf->hmi/dot_general | solution.py:36
  59.7 0.4 fusion.142
  60.1 1.3 %reduce-precision_convert_fusion.2 = (bf16[2,4,256,128]{3,2,0,1:T(8,128)(2,1)}, bf16[2,4,256,128]{3,2,0,1:T(8,128)(2,1)}, bf16[2,4,256,128]{3,2,0,1:T(8,128)(2,1)S(1)}) fusion(f32[2,4,256]{2,0,1:T(2,128)S(1)} %copy.83, bf16[2,256,4,2,128]{4,1,3,2,0:T(8,128)(2,1)S(1)} %copy-done.5), kind=kLoop, calls=%fused_computation.32 | loop fusion | flops 1835008 | bytes 2105344 | tf_op jit(solution)/shard_map/convert_element_type | solution.py:26
  61.5 1.2 fusion.16
  62.7 1.2 fusion.23
  63.9 1.1 fusion.33
  65.1 0.4 select_convert_fusion
  65.5 1.6 %fusion.78 = f32[2,528,128,1]{2,1,3,0:T(8,128)} fusion(bf16[2,4,256,528]{2,3,1,0:T(8,128)(2,1)S(1)} %get-tuple-element.29, bf16[2,4,256,128]{3,2,0,1:T(8,128)(2,1)S(1)} %get-tuple-element.38), kind=kOutput, calls=%fused_computation.127 | convolution fusion | flops 276824064 | bytes 3227648 | tf_op jit(solution)/shard_map/hmif,hmid->hfd/dot_general | solution.py:200
  67.1 1.8 %convolution_bitcast_fusion = f32[2,256,528]{1,2,0:T(8,128)} fusion(bf16[2,4,256,256]{2,3,1,0:T(8,128)(2,1)S(1)} %select_convert_fusion, bf16[2,4,256,528]{2,3,1,0:T(8,128)(2,1)S(1)} %get-tuple-element.29), kind=kOutput, calls=%fused_computation.43 | convolution fusion | flops 553648128 | bytes 4292608 | tf_op jit(solution)/shard_map/hmij,hmif->hjf/dot_general | solution.py:221
  68.9 0.9 fusion.64
  69.8 0.7 fusion.135
  70.4 0.7 fusion.133
  71.2 0.9 select_maximum_fusion
  72.1 4.2 %all-to-all-start.2 = ((f32[32,40,128]{2,1,0:T(8,128)}), f32[32,40,128]{2,1,0:T(8,128)S(1)}, u32[]{:S(2)}, u32[]{:S(2)}) async-start(f32[32,40,128]{2,1,0:T(8,128)} %bitcast.43), calls=%async_computation.2 | async-start | bytes 1310720 | tf_op jit(solution)/shard_map/all_to_all | solution.py:70
  76.3 2.4 %convolution_bitcast_fusion.1 = f32[2,256,128]{2,1,0:T(8,128)} fusion(bf16[2,4,256,256]{2,3,1,0:T(8,128)(2,1)} %get-tuple-element.79, bf16[2,4,256,128]{3,2,0,1:T(8,128)(2,1)S(1)} %copy-done.9), kind=kOutput, calls=%fused_computation.67 | convolution fusion | flops 134217728 | bytes 1835008 | tf_op jit(solution)/shard_map/hmij,hmid->hjd/dot_general | solution.py:222
  79.2 5.4 %multiply_add_fusion = f32[2,4,256,528]{2,3,1,0:T(8,128)} fusion(f32[2,528]{1,0:T(2,128)S(1)} %get-tuple-element.74, f32[2,4,256]{2,1,0:T(4,128)S(1)} %copy.92, bf16[2,4,256,128]{2,3,1,0:T(8,128)(2,1)S(1)} %copy.95, bf16[2,4,256,128]{2,3,1,0:T(8,128)(2,1)S(1)} %copy.93, bf16[2,4,256,256]{2,3,1,0:T(8,128)(2,1)} %copy-done.18, ...), kind=kOutput, calls=%fused_computation.9 | convolution fusion | flops 1402175488 | bytes 7516288 | tf_op jit(solution)/shard_map/hmik,hkf->hmif/dot_general | solution.py:213
  84.6 4.7 %all-to-all-done.2 = f32[32,40,128]{2,1,0:T(8,128)S(1)} async-done(((f32[32,40,128]{2,1,0:T(8,128)}), f32[32,40,128]{2,1,0:T(8,128)S(1)}, u32[]{:S(2)}, u32[]{:S(2)}) %all-to-all-start.2) | async-done | bytes 655392 | tf_op jit(solution)/shard_map/all_to_all | solution.py:70
  89.3 0.5 fusion.59
  89.8 1.2 copy.104
  91.0 4.3 %all-to-all-start.3 = ((f32[32,40,128]{2,1,0:T(8,128)}), f32[32,40,128]{2,1,0:T(8,128)S(1)}, u32[]{:S(2)}, u32[]{:S(2)}) async-start(f32[32,40,128]{2,1,0:T(8,128)} %copy.104), calls=%async_computation.3 | async-start | bytes 1310720 | tf_op jit(solution)/shard_map/all_to_all | solution.py:84
  95.3 5.9 %slice_multiply_fusion = (f32[2,4,256,528]{2,3,1,0:T(8,128)S(1)}, f32[2,4,256,528]{2,3,1,0:T(8,128)S(1)}) fusion(f32[2,4,256,528]{2,3,1,0:T(8,128)} %multiply_add_fusion, f32[2,4,256,1056]{2,3,1,0:T(8,128)} %fusion.80, f32[528]{0:T(1024)S(1)} %copy-done.33), kind=kLoop, calls=%fused_computation.11 | loop fusion | flops 3244032 | bytes 21628992 | tf_op jit(solution)/shard_map/mul | solution.py:139
  101.3 1.4 %reduce-precision_convert_fusion = (bf16[2,4,256,1056]{2,3,1,0:T(8,128)(2,1)S(1)}, bf16[2,4,256,1056]{2,3,1,0:T(8,128)(2,1)S(1)}) fusion(f32[2,4,256,528]{2,3,1,0:T(8,128)S(1)} %get-tuple-element.31, f32[2,4,256,528]{2,3,1,0:T(8,128)S(1)} %get-tuple-element.30), kind=kLoop, calls=%fused_computation.1 | loop fusion | flops 10813440 | bytes 17301504 | tf_op jit(solution)/shard_map/convert_element_type | solution.py:26
  102.7 0.9 fusion.1
  103.7 0.9 reduce-precision_convert_fusion.9
  104.6 0.3 fusion.34
  105.0 3.4 %all-to-all-done.3 = f32[32,40,128]{2,1,0:T(8,128)S(1)} async-done(((f32[32,40,128]{2,1,0:T(8,128)}), f32[32,40,128]{2,1,0:T(8,128)S(1)}, u32[]{:S(2)}, u32[]{:S(2)}) %all-to-all-start.3) | async-done | bytes 655392 | tf_op jit(solution)/shard_map/all_to_all | solution.py:84
  108.5 0.5 fusion.74
  109.1 0.5 fusion.47
  109.6 0.8 copy.112
  110.4 0.5 slice_multiply_fusion.1
  110.9 0.4 copy-done.29
  111.8 0.4 reduce-precision_convert_fusion.14
  112.3 0.8 copy.111
  113.3 2.5 %collective-permute-start.4 = (bf16[256,1,2,128]{3,0,1,2:T(8,128)(2,1)S(1)}, bf16[256,1,2,128]{3,0,1,2:T(8,128)(2,1)S(1)}, u32[]{:S(2)}, u32[]{:S(2)}) collective-permute-start(bf16[256,1,2,128]{3,0,1,2:T(8,128)(2,1)S(1)} %get-tuple-element.48), channel_id=1, source_target_pairs={{0,2},{1,3},{2,0},{3,1},{4,6},{5,7},{6,4},{7,5},{8,10},{9,11},{10,... | collective-permute-start | bytes 393224 | tf_op jit(solution)/shard_map/ppermute | solution.py:116
  116.1 1.7 %collective-permute-done.3 = bf16[256,1,2,128]{3,0,1,2:T(8,128)(2,1)S(1)} collective-permute-done((bf16[256,1,2,128]{3,0,1,2:T(8,128)(2,1)S(1)}, bf16[256,1,2,128]{3,0,1,2:T(8,128)(2,1)S(1)}, u32[]{:S(2)}, u32[]{:S(2)}) %collective-permute-start.3) | collective-permute-done | bytes 131104 | tf_op jit(solution)/shard_map/ppermute | solution.py:116
  118.0 1.4 %collective-permute-done.4 = bf16[256,1,2,128]{3,0,1,2:T(8,128)(2,1)S(1)} collective-permute-done((bf16[256,1,2,128]{3,0,1,2:T(8,128)(2,1)S(1)}, bf16[256,1,2,128]{3,0,1,2:T(8,128)(2,1)S(1)}, u32[]{:S(2)}, u32[]{:S(2)}) %collective-permute-start.4) | collective-permute-done | bytes 131104 | tf_op jit(solution)/shard_map/ppermute | solution.py:116
  119.6 2.8 %collective-permute-done.5 = bf16[256,1,2,128]{3,0,1,2:T(8,128)(2,1)S(1)} collective-permute-done((bf16[256,1,2,128]{3,0,1,2:T(8,128)(2,1)S(1)}, bf16[256,1,2,128]{3,0,1,2:T(8,128)(2,1)S(1)}, u32[]{:S(2)}, u32[]{:S(2)}) %collective-permute-start.5) | collective-permute-done | bytes 131104 | tf_op jit(solution)/shard_map/ppermute | solution.py:116
  122.6 0.8 copy-done.20
  (105 shorter events, 4.1 us)
Async XLA Ops:
  0.6 8.2 %copy-start.31 = (s32[2,128,32]{1,2,0:T(8,128)S(1)}, s32[2,128,32]{1,2,0:T(8,128)}, u32[]{:S(2)}) copy-start(s32[2,128,32]{1,2,0:T(8,128)} %param.13) | copy-start | bytes 98308
  0.7 10.6 %copy-start.27 = (bf16[96,1056,1]{1,0,2:T(8,128)(2,1)S(1)}, bf16[96,1056,1]{1,0,2:T(8,128)(2,1)}, u32[]{:S(2)}) copy-start(bf16[96,1056,1]{1,0,2:T(8,128)(2,1)} %constant.95) | copy-start | bytes 608260
  2.3 22.3 %collective-permute-start = (bf16[2,256,1,2,128]{4,1,3,2,0:T(8,128)(2,1)S(1)}, bf16[2,256,1,2,128]{4,1,3,2,0:T(8,128)(2,1)S(1)}, u32[]{:S(2)}, u32[]{:S(2)}) collective-permute-start(bf16[2,256,1,2,128]{4,1,3,2,0:T(8,128)(2,1)S(1)} %get-tuple-element.40), channel_id=1, source_target_pairs={{0,1},{1,2},{2,3},{3,0},{4,5},{5,6},{6,7},{7,4},{8,9},{9,10},{10,1... | collective-permute-start | bytes 786440 | tf_op jit(solution)/shard_map/ppermute | solution.py:103
  4.8 19.7 %collective-permute-start.1 = (bf16[2,256,1,2,128]{4,1,3,2,0:T(8,128)(2,1)S(1)}, bf16[2,256,1,2,128]{4,1,3,2,0:T(8,128)(2,1)S(1)}, u32[]{:S(2)}, u32[]{:S(2)}) collective-permute-start(bf16[2,256,1,2,128]{4,1,3,2,0:T(8,128)(2,1)S(1)} %get-tuple-element.41), channel_id=1, source_target_pairs={{0,2},{1,3},{2,0},{3,1},{4,6},{5,7},{6,4},{7,5},{8,10},{9,11},{10,... | collective-permute-start | bytes 786440 | tf_op jit(solution)/shard_map/ppermute | solution.py:103
  8.1 16.4 %collective-permute-start.2 = (bf16[2,256,1,2,128]{4,1,3,2,0:T(8,128)(2,1)S(1)}, bf16[2,256,1,2,128]{4,1,3,2,0:T(8,128)(2,1)S(1)}, u32[]{:S(2)}, u32[]{:S(2)}) collective-permute-start(bf16[2,256,1,2,128]{4,1,3,2,0:T(8,128)(2,1)S(1)} %get-tuple-element.42), channel_id=1, source_target_pairs={{0,3},{1,0},{2,1},{3,2},{4,7},{5,4},{6,5},{7,6},{8,11},{9,8},{10,9... | collective-permute-start | bytes 786440 | tf_op jit(solution)/shard_map/ppermute | solution.py:103
  10.3 12.9 %copy-start.12 = (bf16[256,2,128]{2,1,0:T(2,128)(2,1)}, bf16[256,2,128]{2,1,0:T(2,128)(2,1)S(1)}, u32[]{:S(2)}) copy-start(bf16[256,2,128]{2,1,0:T(2,128)(2,1)S(1)} %get-tuple-element.83) | copy-start | bytes 393220
  10.5 2.9 %copy-start.23 = (f32[2,256,32]{1,2,0:T(8,128)}, f32[2,256,32]{1,2,0:T(8,128)S(1)}, u32[]{:S(2)}) copy-start(f32[2,256,32]{1,2,0:T(8,128)S(1)} %fusion.49) | copy-start | bytes 196612
  11.8 1.3 %copy-start.2 = (f32[2,256,1056]{1,2,0:T(8,128)}, f32[2,256,1056]{1,2,0:T(8,128)S(1)}, u32[]{:S(2)}) copy-start(f32[2,256,1056]{1,2,0:T(8,128)S(1)} %fusion.112) | copy-start | bytes 6488068
  14.6 21.5 %all-to-all-start = ((f32[32,40,128]{2,1,0:T(8,128)}), f32[32,40,128]{2,1,0:T(8,128)S(1)}, u32[]{:S(2)}, u32[]{:S(2)}) async-start(f32[32,40,128]{2,1,0:T(8,128)} %bitcast.26), calls=%async_computation | async-start | bytes 1310720 | tf_op jit(solution)/shard_map/all_to_all | solution.py:70
  23.2 25.7 %copy-start.14 = (pred[256,256]{0,1:T(8,128)(4,1)}, pred[256,256]{0,1:T(8,128)(4,1)S(1)}, u32[]{:S(2)}) copy-start(pred[256,256]{0,1:T(8,128)(4,1)S(1)} %iota_compare_fusion.1) | copy-start | bytes 196612
  24.5 0.7 copy-start.26
  25.2 3.2 %copy-start.28 = (bf16[96,1056,1,1]{1,0,3,2:T(8,128)(2,1)S(1)}, bf16[96,1056,1,1]{1,0,3,2:T(8,128)(2,1)}, u32[]{:S(2)}) copy-start(bf16[96,1056,1,1]{1,0,3,2:T(8,128)(2,1)} %constant.94) | copy-start | bytes 608260
  26.4 1.0 copy-start.4
  33.2 9.4 %copy-start.32 = (bf16[528]{0:T(1024)(128)(2,1)S(1)}, bf16[528]{0:T(1024)(128)(2,1)}, u32[]{:S(2)}) copy-start(bf16[528]{0:T(1024)(128)(2,1)} %constant.77.clone) | copy-start | bytes 3172
  37.8 17.8 %all-to-all-start.1 = ((f32[32,40,128]{2,1,0:T(8,128)}), f32[32,40,128]{2,1,0:T(8,128)}, u32[]{:S(2)}, u32[]{:S(2)}) async-start(f32[32,40,128]{2,1,0:T(8,128)} %copy.82), calls=%async_computation.1 | async-start | bytes 1310720 | tf_op jit(solution)/shard_map/all_to_all | solution.py:84
  46.8 2.1 %copy-start = (bf16[2,4,256,528]{2,3,1,0:T(8,128)(2,1)}, bf16[2,4,256,528]{2,3,1,0:T(8,128)(2,1)S(1)}, u32[]{:S(2)}) copy-start(bf16[2,4,256,528]{2,3,1,0:T(8,128)(2,1)S(1)} %get-tuple-element.28) | copy-start | bytes 6488068
  57.4 2.3 %copy-start.1 = (bf16[2,4,256,528]{2,3,1,0:T(8,128)(2,1)S(1)}, bf16[2,4,256,528]{2,3,1,0:T(8,128)(2,1)}, u32[]{:S(2)}) copy-start(bf16[2,4,256,528]{2,3,1,0:T(8,128)(2,1)} %copy-done) | copy-start | bytes 6488068
  57.5 2.7 %copy-start.5 = (bf16[2,256,4,2,128]{4,1,3,2,0:T(8,128)(2,1)S(1)}, bf16[2,256,4,2,128]{4,1,3,2,0:T(8,128)(2,1)}, u32[]{:S(2)}) copy-start(bf16[2,256,4,2,128]{4,1,3,2,0:T(8,128)(2,1)} %copy-done.4) | copy-start | bytes 3145732
  61.5 4.1 %copy-start.8 = (bf16[2,4,256,128]{3,2,0,1:T(8,128)(2,1)}, bf16[2,4,256,128]{3,2,0,1:T(8,128)(2,1)S(1)}, u32[]{:S(2)}) copy-start(bf16[2,4,256,128]{3,2,0,1:T(8,128)(2,1)S(1)} %get-tuple-element.38) | copy-start | bytes 1572868
  62.6 1.2 copy-start.13
  62.7 1.3 %copy-start.17 = (bf16[2,4,256,256]{2,3,1,0:T(8,128)(2,1)S(1)}, bf16[2,4,256,256]{2,3,1,0:T(8,128)(2,1)}, u32[]{:S(2)}) copy-start(bf16[2,4,256,256]{2,3,1,0:T(8,128)(2,1)} %get-tuple-element.79) | copy-start | bytes 3145732
  63.9 1.1 copy-start.15
  65.5 3.4 %copy-start.18 = (bf16[2,4,256,256]{2,3,1,0:T(8,128)(2,1)}, bf16[2,4,256,256]{2,3,1,0:T(8,128)(2,1)S(1)}, u32[]{:S(2)}) copy-start(bf16[2,4,256,256]{2,3,1,0:T(8,128)(2,1)S(1)} %select_convert_fusion) | copy-start | bytes 3145732
  69.8 1.4 %copy-start.7 = (f32[2,528,128,1]{2,1,3,0:T(8,128)S(1)}, f32[2,528,128,1]{2,1,3,0:T(8,128)}, u32[]{:S(2)}) copy-start(f32[2,528,128,1]{2,1,3,0:T(8,128)} %fusion.78) | copy-start | bytes 1622020
  71.1 5.2 %copy-start.9 = (bf16[2,4,256,128]{3,2,0,1:T(8,128)(2,1)S(1)}, bf16[2,4,256,128]{3,2,0,1:T(8,128)(2,1)}, u32[]{:S(2)}) copy-start(bf16[2,4,256,128]{3,2,0,1:T(8,128)(2,1)} %copy-done.8) | copy-start | bytes 1572868
  72.1 6.7 %copy-start.11 = (bf16[2,4,256,128]{3,2,0,1:T(8,128)(2,1)S(1)}, bf16[2,4,256,128]{3,2,0,1:T(8,128)(2,1)}, u32[]{:S(2)}) copy-start(bf16[2,4,256,128]{3,2,0,1:T(8,128)(2,1)} %get-tuple-element.36) | copy-start | bytes 1572868
  72.1 6.9 %copy-start.10 = (bf16[2,4,256,128]{3,2,0,1:T(8,128)(2,1)S(1)}, bf16[2,4,256,128]{3,2,0,1:T(8,128)(2,1)}, u32[]{:S(2)}) copy-start(bf16[2,4,256,128]{3,2,0,1:T(8,128)(2,1)} %get-tuple-element.37) | copy-start | bytes 1572868
  72.1 17.2 %all-to-all-start.2 = ((f32[32,40,128]{2,1,0:T(8,128)}), f32[32,40,128]{2,1,0:T(8,128)S(1)}, u32[]{:S(2)}, u32[]{:S(2)}) async-start(f32[32,40,128]{2,1,0:T(8,128)} %bitcast.43), calls=%async_computation.2 | async-start | bytes 1310720 | tf_op jit(solution)/shard_map/all_to_all | solution.py:70
  76.3 2.9 %copy-start.22 = (bf16[2,128,528]{1,2,0:T(8,128)(2,1)S(1)}, bf16[2,128,528]{1,2,0:T(8,128)(2,1)}, u32[]{:S(2)}) copy-start(bf16[2,128,528]{1,2,0:T(8,128)(2,1)} %get-tuple-element.45) | copy-start | bytes 811012
  84.6 10.8 %copy-start.33 = (f32[528]{0:T(1024)S(1)}, f32[528]{0:T(1024)}, u32[]{:S(2)}) copy-start(f32[528]{0:T(1024)} %constant.78.clone) | copy-start | bytes 6340
  91.0 17.3 %all-to-all-start.3 = ((f32[32,40,128]{2,1,0:T(8,128)}), f32[32,40,128]{2,1,0:T(8,128)S(1)}, u32[]{:S(2)}, u32[]{:S(2)}) async-start(f32[32,40,128]{2,1,0:T(8,128)} %copy.104), calls=%async_computation.3 | async-start | bytes 1310720 | tf_op jit(solution)/shard_map/all_to_all | solution.py:84
  101.3 1.4 %copy-start.21 = (bf16[1056,32,1,1]{0,1,2,3:T(8,128)(2,1)S(1)}, bf16[1056,32,1,1]{0,1,2,3:T(8,128)(2,1)}, u32[]{:S(2)}) copy-start(bf16[1056,32,1,1]{0,1,2,3:T(8,128)(2,1)} %constant.96) | copy-start | bytes 202756
  102.7 1.0 copy-start.16
  103.7 0.9 copy-start.34
  103.7 0.9 copy-start.35
  105.0 4.1 %copy-start.25 = (f32[2,256,128]{2,1,0:T(8,128)S(1)}, f32[2,256,128]{2,1,0:T(8,128)}, u32[]{:S(2)}) copy-start(f32[2,256,128]{2,1,0:T(8,128)} %convolution_bitcast_fusion.1) | copy-start | bytes 786436
  108.4 2.0 %copy-start.3 = (f32[2,256,1056]{1,2,0:T(8,128)S(1)}, f32[2,256,1056]{1,2,0:T(8,128)}, u32[]{:S(2)}) copy-start(f32[2,256,1056]{1,2,0:T(8,128)} %copy-done.2) | copy-start | bytes 6488068
  108.4 2.0 %copy-start.6 = (f32[2,256,528]{1,2,0:T(8,128)S(1)}, f32[2,256,528]{1,2,0:T(8,128)}, u32[]{:S(2)}) copy-start(f32[2,256,528]{1,2,0:T(8,128)} %convolution_bitcast_fusion) | copy-start | bytes 3244036
  108.4 2.0 %copy-start.19 = (bf16[256,2,128]{2,0,1:T(8,128)(2,1)S(1)}, bf16[256,2,128]{2,0,1:T(8,128)(2,1)}, u32[]{:S(2)}) copy-start(bf16[256,2,128]{2,0,1:T(8,128)(2,1)} %copy.219) | copy-start | bytes 393220
  110.4 0.9 copy-start.29
  110.9 0.8 copy-start.24
  110.9 0.9 copy-start.30
  113.2 4.6 %collective-permute-start.3 = (bf16[256,1,2,128]{3,0,1,2:T(8,128)(2,1)S(1)}, bf16[256,1,2,128]{3,0,1,2:T(8,128)(2,1)S(1)}, u32[]{:S(2)}, u32[]{:S(2)}) collective-permute-start(bf16[256,1,2,128]{3,0,1,2:T(8,128)(2,1)S(1)} %get-tuple-element.49), channel_id=1, source_target_pairs={{0,3},{1,0},{2,1},{3,2},{4,7},{5,4},{6,5},{7,6},{8,11},{9,8},{10,9... | collective-permute-start | bytes 393224 | tf_op jit(solution)/shard_map/ppermute | solution.py:116
  113.3 6.1 %collective-permute-start.4 = (bf16[256,1,2,128]{3,0,1,2:T(8,128)(2,1)S(1)}, bf16[256,1,2,128]{3,0,1,2:T(8,128)(2,1)S(1)}, u32[]{:S(2)}, u32[]{:S(2)}) collective-permute-start(bf16[256,1,2,128]{3,0,1,2:T(8,128)(2,1)S(1)} %get-tuple-element.48), channel_id=1, source_target_pairs={{0,2},{1,3},{2,0},{3,1},{4,6},{5,7},{6,4},{7,5},{8,10},{9,11},{10,... | collective-permute-start | bytes 393224 | tf_op jit(solution)/shard_map/ppermute | solution.py:116
  115.8 6.6 %collective-permute-start.5 = (bf16[256,1,2,128]{3,0,1,2:T(8,128)(2,1)S(1)}, bf16[256,1,2,128]{3,0,1,2:T(8,128)(2,1)S(1)}, u32[]{:S(2)}, u32[]{:S(2)}) collective-permute-start(bf16[256,1,2,128]{3,0,1,2:T(8,128)(2,1)S(1)} %get-tuple-element.47), channel_id=1, source_target_pairs={{0,1},{1,2},{2,3},{3,0},{4,5},{5,6},{6,7},{7,4},{8,9},{9,10},{10,1... | collective-permute-start | bytes 393224 | tf_op jit(solution)/shard_map/ppermute | solution.py:116
  122.6 0.8 copy-start.20

commit v15 on v14

--- a/solution.py
+++ b/solution.py
@@ -197,8 +197,16 @@
     grad_rows = grad_heads / denominator[..., None]
     grad_low = grad_rows.astype(bf16)
     correction = -jnp.sum(grad_rows * output_rows, -1)
-    suffix_part = jnp.einsum("hmif,hmid->hfd", query_feat, grad_low, preferred_element_type=f32)
-    suffix_sum = dot_split("hmif,hmi->hf", query_feat, correction)
+    width_v = value_heads.shape[-1]
+    corr_hi, corr_lo = split_parts(correction[..., None], 2)
+    suffix_both = jnp.einsum(
+        "hmif,hmid->hfd",
+        query_feat,
+        jnp.concatenate([grad_low, corr_hi, corr_lo], axis=-1),
+        preferred_element_type=f32,
+    )
+    suffix_part = suffix_both[..., :width_v]
+    suffix_sum = suffix_both[..., width_v] + suffix_both[..., width_v + 1]
     suffix_got = scan_send(suffix_part, suffix_sum)
 
     dscores = jnp.where(

time: 124 us -> 134 us (1.081)
  local copies, waits for them, and re-layouts: 16.1 us -> 23.3 us
  other arithmetic: 17.4 us -> 22.8 us
  matrix products: 34.1 us -> 31.3 us
    dot_general x12 -> x10, matrix products: 9.67 us -> 6.54 us  [dot_parts(): term = jnp.einsum(pattern, *args, preferred_element_type=f32)]
    slice x0 -> x2, local copies, waits for them, and re-layouts: none -> 2.26 us  [body(): suffix_part = suffix_both[..., :width_v]]
    all_to_all x2, waiting for transfers between devices: 7.68 us -> 9.57 us  [scan_send(): return lax.all_to_all(flat.reshape(n, per, width), 'ctx', 0, 0, tiled=True)]
    all_to_all x2, waiting for transfers between devices: 9.93 us -> 8.08 us  [scan_return(): lax.all_to_all(summed, 'ctx', 0, 0, tiled=True).reshape(n * per, width)]
    convert_element_type x1 -> x2, local copies, waits for them, and re-layouts: 0.21 us -> 1.98 us  [split_parts(): parts.append(hi.astype(bf16))]
    convert_element_type x1 -> x2, local copies, waits for them, and re-layouts: 0.21 us -> 1.96 us  [split_parts(): parts.append(rest.astype(bf16))]
    mul x1, other arithmetic: 4.22 us -> 5.56 us  [body(): query_wfeat = query_feat * weight]
    unnamed x75 -> x74, local copies, waits for them, and re-layouts: 6.78 us -> 5.68 us
  transfers between devices with their start and end apart: 10 -> 10, of which waited for: 7 -> 7; matrix products, arithmetic and copies ran while one was open for 31% -> 29% of each run, Pallas kernels for 0% -> 0%
where the time goes in v15:
time: 134 us; the launch traced here: 133 us
  matrix products  31.3 us (23%)
  starting transfers between devices  30.8 us (23%)
  waiting for transfers between devices  23.5 us (18%)
  local copies, waits for them, and re-layouts  23.3 us (17%)
  other arithmetic  22.8 us (17%)
  between operations  1.37 us (1%)
    all_to_all x2, starting transfers between devices, scan_send(): return lax.all_to_all(flat.reshape(n, per, width), 'ctx', 0, 0, tiled=True)  12.8 us
    all_to_all x2, waiting for transfers between devices, scan_send(): return lax.all_to_all(flat.reshape(n, per, width), 'ctx', 0, 0, tiled=True)  9.57 us
    all_to_all x2, starting transfers between devices, scan_return(): lax.all_to_all(summed, 'ctx', 0, 0, tiled=True).reshape(n * per, width)  8.85 us
    all_to_all x2, waiting for transfers between devices, scan_return(): lax.all_to_all(summed, 'ctx', 0, 0, tiled=True).reshape(n * per, width)  8.08 us
    ppermute x3, starting transfers between devices, head_exchange(): lax.ppermute(piece, 'head', [(j, (j + k) % count) for j in range(count)])  6.57 us
    dot_general x10, matrix products, dot_parts(): term = jnp.einsum(pattern, *args, preferred_element_type=f32)  6.54 us
    mul x1, other arithmetic, tri_feature_back(): cotangent * second  5.95 us
    ppermute x3, waiting for transfers between devices, head_return(): lax.ppermute(piece, 'head', [(j, (j - k) % count) for j in range(count)])  5.84 us
  transfers between devices with their start and end apart: 10, of which 7 were waited for; matrix products, arithmetic and copies ran while one was open for 29% of the time, Pallas kernels for 0%

profile of v15, /device:TPU:1, one launch (start us, length us, event | category | flops | bytes accessed | tf_op | source)
XLA Modules:
  0.0 133.0 jit_solution(15044322874412192685)
XLA Ops:
  0.7 1.4 %copy_bitcast_fusion = (bf16[1,256,1,8,128]{4,1,3,2,0:T(8,128)(2,1)S(1)}, bf16[1,256,1,8,128]{4,1,3,2,0:T(8,128)(2,1)S(1)}) fusion(bf16[256,1,8,128]{3,2,1,0:T(8,128)(2,1)} %param.12, bf16[256,1,8,128]{3,2,1,0:T(8,128)(2,1)} %param.9), kind=kLoop, calls=%fused_computation.123 | loop fusion | bytes 2097152 | tf_op jit(solution)/shard_map/stack | solution.py:168
  2.3 2.5 %collective-permute-start = (bf16[2,256,1,2,128]{4,1,3,2,0:T(8,128)(2,1)S(1)}, bf16[2,256,1,2,128]{4,1,3,2,0:T(8,128)(2,1)S(1)}, u32[]{:S(2)}, u32[]{:S(2)}) collective-permute-start(bf16[2,256,1,2,128]{4,1,3,2,0:T(8,128)(2,1)S(1)} %get-tuple-element.43), channel_id=1, source_target_pairs={{0,1},{1,2},{2,3},{3,0},{4,5},{5,6},{6,7},{7,4},{8,9},{9,10},{10,1... | collective-permute-start | bytes 786440 | tf_op jit(solution)/shard_map/ppermute | solution.py:103
  4.8 3.3 %collective-permute-start.1 = (bf16[2,256,1,2,128]{4,1,3,2,0:T(8,128)(2,1)S(1)}, bf16[2,256,1,2,128]{4,1,3,2,0:T(8,128)(2,1)}, u32[]{:S(2)}, u32[]{:S(2)}) collective-permute-start(bf16[2,256,1,2,128]{4,1,3,2,0:T(8,128)(2,1)S(1)} %get-tuple-element.44), channel_id=1, source_target_pairs={{0,2},{1,3},{2,0},{3,1},{4,6},{5,7},{6,4},{7,5},{8,10},{9,11},{10,... | collective-permute-start | bytes 786440 | tf_op jit(solution)/shard_map/ppermute | solution.py:103
  8.1 0.7 collective-permute-start.2
  9.2 0.8 reduce-precision_convert_fusion.16
  10.0 0.5 fusion.111
  10.5 1.3 copy-done.2
  12.1 1.2 constant_dynamic-slice_fusion
  13.6 0.9 fusion.59
  14.5 8.6 %all-to-all-start = ((f32[32,40,128]{2,1,0:T(8,128)}), f32[32,40,128]{2,1,0:T(8,128)S(1)}, u32[]{:S(2)}, u32[]{:S(2)}) async-start(f32[32,40,128]{2,1,0:T(8,128)} %bitcast.26), calls=%async_computation | async-start | bytes 1310720 | tf_op jit(solution)/shard_map/all_to_all | solution.py:70
  23.2 0.6 slice_bitcast_fusion.5
  23.8 1.2 pad_maximum_fusion.2
  25.3 0.8 copy-done.5
  26.4 4.7 %fusion.79 = f32[2,4,256,1056]{2,3,1,0:T(8,128)} fusion(bf16[96,1056,1,1]{1,0,3,2:T(8,128)(2,1)S(1)} %copy-done.22, bf16[2,4,256,32]{2,3,0,1:T(8,128)(2,1)S(1)} %get-tuple-element.60, bf16[2,4,256,32]{2,3,0,1:T(8,128)(2,1)S(1)} %get-tuple-element.59, bf16[2,4,256,32]{2,3,0,1:T(8,128)(2,1)S(1)} %get-tuple-element.58), kind=kOutput, calls=%fused_computation.131 | convolution fusion | flops 416415744 | bytes 9246720 | tf_op jit(solution)/shard_map/...k,kn->...n/dot_general | solution.py:49
  31.1 4.9 %all-to-all-done = f32[32,40,128]{2,1,0:T(8,128)S(1)} async-done(((f32[32,40,128]{2,1,0:T(8,128)}), f32[32,40,128]{2,1,0:T(8,128)S(1)}, u32[]{:S(2)}, u32[]{:S(2)}) %all-to-all-start) | async-done | bytes 655392 | tf_op jit(solution)/shard_map/all_to_all | solution.py:70
  36.0 0.5 fusion.62
  36.5 1.2 copy.128
  37.7 4.8 %all-to-all-start.1 = ((f32[32,40,128]{2,1,0:T(8,128)}), f32[32,40,128]{2,1,0:T(8,128)}, u32[]{:S(2)}, u32[]{:S(2)}) async-start(f32[32,40,128]{2,1,0:T(8,128)} %copy.128), calls=%async_computation.1 | async-start | bytes 1310720 | tf_op jit(solution)/shard_map/all_to_all | solution.py:84
  42.5 5.6 %broadcast_multiply_fusion = (bf16[2,4,256,528]{2,3,1,0:T(8,128)(2,1)S(1)}, bf16[2,4,256,528]{2,3,1,0:T(8,128)(2,1)}) fusion(bf16[528]{0:T(1024)(128)(2,1)} %constant.77.clone, f32[2,4,256,1056]{2,3,1,0:T(8,128)} %fusion.79), kind=kLoop, calls=%fused_computation.83 | loop fusion | flops 4325376 | bytes 12977184 | tf_op jit(solution)/shard_map/mul | solution.py:180
  48.0 2.1 %select_convert_fusion.1 = (bf16[2,4,256,256]{2,3,1,0:T(8,128)(2,1)}, f32[2,4,256,256]{2,3,1,0:T(8,128)S(1)}) fusion(pred[256,256]{0,1:T(8,128)(4,1)S(1)} %iota_compare_fusion.1, bf16[2,4,256,528]{2,3,1,0:T(8,128)(2,1)S(1)} %get-tuple-element.31, bf16[2,256,528]{1,2,0:T(8,128)(2,1)S(1)} %get-tuple-element.30), kind=kOutput, calls=%fused_computation.25 | convolution fusion | flops 554172416 | bytes 5914624 | tf_op jit(solution)/shard_map/hmif,hjf->hmij/dot_general | solution.py:188
  50.1 0.8 select_reduce_fusion
  50.9 4.6 %all-to-all-done.1 = f32[32,40,128]{2,1,0:T(8,128)} async-done(((f32[32,40,128]{2,1,0:T(8,128)}), f32[32,40,128]{2,1,0:T(8,128)}, u32[]{:S(2)}, u32[]{:S(2)}) %all-to-all-start.1) | async-done | bytes 655392 | tf_op jit(solution)/shard_map/all_to_all | solution.py:84
  55.5 1.3 slice.106
  56.8 1.9 %slice.108 = f32[1056,128]{1,0:T(8,128)} slice(f32[1280,128]{1,0:T(8,128)} %bitcast.27), slice={[0:1056], [0:128]} | slice | bytes 1081344 | tf_op jit(solution)/shard_map/slice | solution.py:85
  58.8 1.3 reshape.86
  60.1 1.3 fusion.153
  62.6 1.6 %reduce-precision_convert_fusion.2 = (bf16[2,4,256,128]{3,2,0,1:T(8,128)(2,1)}, bf16[2,4,256,128]{3,2,0,1:T(8,128)(2,1)}, bf16[2,4,256,128]{3,2,0,1:T(8,128)(2,1)}) fusion(f32[2,4,256]{2,0,1:T(2,128)S(1)} %copy.129, bf16[2,256,4,2,128]{4,1,3,2,0:T(8,128)(2,1)S(1)} %copy-done.6), kind=kLoop, calls=%fused_computation.32 | loop fusion | flops 1835008 | bytes 2105344 | tf_op jit(solution)/shard_map/convert_element_type | solution.py:26
  64.2 1.1 fusion.16
  65.4 1.1 fusion.23
  66.6 1.1 fusion.33
  67.7 0.6 copy_negate_fusion
  68.3 0.6 reduce-precision_convert_fusion.17
  68.9 1.8 %copy.138 = bf16[2,4,256,1]{3,2,0,1:T(8,128)(2,1)} copy(bf16[2,4,256,1]{2,1,3,0:T(4,128)(2,1)} %get-tuple-element.74) | data formatting | bytes 8192 | tf_op jit(solution)/shard_map/convert_element_type | solution.py:26
  70.6 1.8 %copy.139 = bf16[2,4,256,1]{3,2,0,1:T(8,128)(2,1)} copy(bf16[2,4,256,1]{2,1,3,0:T(4,128)(2,1)} %get-tuple-element.75) | data formatting | bytes 8192 | tf_op jit(solution)/shard_map/convert_element_type | solution.py:28
  72.4 2.5 %convolution_bitcast_fusion.1 = f32[2,528,130]{1,2,0:T(8,128)S(1)} fusion(bf16[2,4,256,528]{2,3,1,0:T(8,128)(2,1)S(1)} %copy-done.4, bf16[2,4,256,1]{3,2,0,1:T(8,128)(2,1)} %copy.139, bf16[2,4,256,1]{3,2,0,1:T(8,128)(2,1)} %copy.138, bf16[2,4,256,128]{3,2,0,1:T(8,128)(2,1)} %get-tuple-element.41), kind=kOutput, calls=%fused_computation.57 | convolution fusion | flops 282746880 | bytes 3244288 | tf_op jit(solution)/shard_map/hmif,hmid->hfd/dot_general | solution.py:202
  74.9 0.9 slice.109
  75.9 0.6 slice_add_fusion
  76.5 0.4 select_convert_fusion
  77.0 1.8 %convolution_bitcast_fusion = f32[2,256,528]{1,2,0:T(8,128)} fusion(bf16[2,4,256,256]{2,3,1,0:T(8,128)(2,1)S(1)} %select_convert_fusion, bf16[2,4,256,528]{2,3,1,0:T(8,128)(2,1)S(1)} %copy-done.4), kind=kOutput, calls=%fused_computation.43 | convolution fusion | flops 553648128 | bytes 4292608 | tf_op jit(solution)/shard_map/hmij,hmif->hjf/dot_general | solution.py:229
  78.7 0.9 fusion.65
  79.6 1.3 copy.141
  81.0 0.9 select_maximum_fusion
  81.9 4.2 %all-to-all-start.2 = ((f32[32,40,128]{2,1,0:T(8,128)}), f32[32,40,128]{2,1,0:T(8,128)S(1)}, u32[]{:S(2)}, u32[]{:S(2)}) async-start(f32[32,40,128]{2,1,0:T(8,128)} %bitcast.42), calls=%async_computation.2 | async-start | bytes 1310720 | tf_op jit(solution)/shard_map/all_to_all | solution.py:70
  86.2 2.4 %convolution_bitcast_fusion.2 = f32[2,256,128]{2,1,0:T(8,128)} fusion(bf16[2,4,256,256]{2,3,1,0:T(8,128)(2,1)} %get-tuple-element.81, bf16[2,4,256,128]{3,2,0,1:T(8,128)(2,1)S(1)} %copy-done.16), kind=kOutput, calls=%fused_computation.68 | convolution fusion | flops 134217728 | bytes 1835008 | tf_op jit(solution)/shard_map/hmij,hmid->hjd/dot_general | solution.py:230
  89.0 5.5 %multiply_add_fusion = f32[2,4,256,528]{2,3,1,0:T(8,128)} fusion(f32[2,528]{1,0:T(2,128)S(1)} %copy-done.34, f32[2,4,256]{2,1,0:T(4,128)S(1)} %copy-done.31, bf16[2,4,256,128]{2,3,1,0:T(8,128)(2,1)S(1)} %copy.146, bf16[2,4,256,128]{2,3,1,0:T(8,128)(2,1)S(1)} %copy.144, bf16[2,4,256,256]{2,3,1,0:T(8,128)(2,1)} %copy-done.13, ...), kind=kOutput, calls=%fused_computation.9 | convolution fusion | flops 1402175488 | bytes 7516288 | tf_op jit(solution)/shard_map/hmik,hkf->hmif/dot_general | solution.py:221
  94.5 4.7 %all-to-all-done.2 = f32[32,40,128]{2,1,0:T(8,128)S(1)} async-done(((f32[32,40,128]{2,1,0:T(8,128)}), f32[32,40,128]{2,1,0:T(8,128)S(1)}, u32[]{:S(2)}, u32[]{:S(2)}) %all-to-all-start.2) | async-done | bytes 655392 | tf_op jit(solution)/shard_map/all_to_all | solution.py:70
  99.2 0.5 fusion.60
  99.6 1.2 copy.154
  100.9 4.1 %all-to-all-start.3 = ((f32[32,40,128]{2,1,0:T(8,128)}), f32[32,40,128]{2,1,0:T(8,128)S(1)}, u32[]{:S(2)}, u32[]{:S(2)}) async-start(f32[32,40,128]{2,1,0:T(8,128)} %copy.154), calls=%async_computation.3 | async-start | bytes 1310720 | tf_op jit(solution)/shard_map/all_to_all | solution.py:84
  105.0 5.9 %slice_multiply_fusion = (f32[2,4,256,528]{2,3,1,0:T(8,128)S(1)}, f32[2,4,256,528]{2,3,1,0:T(8,128)S(1)}) fusion(f32[2,4,256,528]{2,3,1,0:T(8,128)} %multiply_add_fusion, f32[2,4,256,1056]{2,3,1,0:T(8,128)} %fusion.79, f32[528]{0:T(1024)S(1)} %copy-done.29), kind=kLoop, calls=%fused_computation.11 | loop fusion | flops 3244032 | bytes 21628992 | tf_op jit(solution)/shard_map/mul | solution.py:139
  111.0 1.4 %reduce-precision_convert_fusion = (bf16[2,4,256,1056]{2,3,1,0:T(8,128)(2,1)S(1)}, bf16[2,4,256,1056]{2,3,1,0:T(8,128)(2,1)S(1)}) fusion(f32[2,4,256,528]{2,3,1,0:T(8,128)S(1)} %get-tuple-element.34, f32[2,4,256,528]{2,3,1,0:T(8,128)S(1)} %get-tuple-element.33), kind=kLoop, calls=%fused_computation.1 | loop fusion | flops 10813440 | bytes 17301504 | tf_op jit(solution)/shard_map/convert_element_type | solution.py:26
  112.3 0.9 fusion.1
  113.2 0.9 reduce-precision_convert_fusion.9
  114.6 3.4 %all-to-all-done.3 = f32[32,40,128]{2,1,0:T(8,128)S(1)} async-done(((f32[32,40,128]{2,1,0:T(8,128)}), f32[32,40,128]{2,1,0:T(8,128)S(1)}, u32[]{:S(2)}, u32[]{:S(2)}) %all-to-all-start.3) | async-done | bytes 655392 | tf_op jit(solution)/shard_map/all_to_all | solution.py:84
  118.1 0.5 fusion.75
  118.7 0.5 fusion.47
  119.2 0.8 copy.162
  120.0 0.5 slice_multiply_fusion.1
  122.0 0.8 copy.161
  122.9 2.5 %collective-permute-start.4 = (bf16[256,1,2,128]{3,0,1,2:T(8,128)(2,1)S(1)}, bf16[256,1,2,128]{3,0,1,2:T(8,128)(2,1)S(1)}, u32[]{:S(2)}, u32[]{:S(2)}) collective-permute-start(bf16[256,1,2,128]{3,0,1,2:T(8,128)(2,1)S(1)} %get-tuple-element.51), channel_id=1, source_target_pairs={{0,2},{1,3},{2,0},{3,1},{4,6},{5,7},{6,4},{7,5},{8,10},{9,11},{10,... | collective-permute-start | bytes 393224 | tf_op jit(solution)/shard_map/ppermute | solution.py:116
  125.7 1.7 %collective-permute-done.3 = bf16[256,1,2,128]{3,0,1,2:T(8,128)(2,1)S(1)} collective-permute-done((bf16[256,1,2,128]{3,0,1,2:T(8,128)(2,1)S(1)}, bf16[256,1,2,128]{3,0,1,2:T(8,128)(2,1)S(1)}, u32[]{:S(2)}, u32[]{:S(2)}) %collective-permute-start.3) | collective-permute-done | bytes 131104 | tf_op jit(solution)/shard_map/ppermute | solution.py:116
  127.6 1.4 %collective-permute-done.4 = bf16[256,1,2,128]{3,0,1,2:T(8,128)(2,1)S(1)} collective-permute-done((bf16[256,1,2,128]{3,0,1,2:T(8,128)(2,1)S(1)}, bf16[256,1,2,128]{3,0,1,2:T(8,128)(2,1)S(1)}, u32[]{:S(2)}, u32[]{:S(2)}) %collective-permute-start.4) | collective-permute-done | bytes 131104 | tf_op jit(solution)/shard_map/ppermute | solution.py:116
  129.2 2.8 %collective-permute-done.5 = bf16[256,1,2,128]{3,0,1,2:T(8,128)(2,1)S(1)} collective-permute-done((bf16[256,1,2,128]{3,0,1,2:T(8,128)(2,1)S(1)}, bf16[256,1,2,128]{3,0,1,2:T(8,128)(2,1)S(1)}, u32[]{:S(2)}, u32[]{:S(2)}) %collective-permute-start.5) | collective-permute-done | bytes 131104 | tf_op jit(solution)/shard_map/ppermute | solution.py:116
  132.2 0.8 copy-done.14
  (107 shorter events, 6.4 us)
Async XLA Ops:
  0.6 8.2 %copy-start = (bf16[256,8,128]{2,1,0:T(8,128)(2,1)S(1)}, bf16[256,8,128]{2,1,0:T(8,128)(2,1)}, u32[]{:S(2)}) copy-start(bf16[256,8,128]{2,1,0:T(8,128)(2,1)} %param.10) | copy-start | bytes 1572868
  0.7 8.2 %copy-start.26 = (s32[2,128,32]{1,2,0:T(8,128)S(1)}, s32[2,128,32]{1,2,0:T(8,128)}, u32[]{:S(2)}) copy-start(s32[2,128,32]{1,2,0:T(8,128)} %param.13) | copy-start | bytes 98308
  0.7 9.3 %copy-start.21 = (bf16[96,1056,1]{1,0,2:T(8,128)(2,1)S(1)}, bf16[96,1056,1]{1,0,2:T(8,128)(2,1)}, u32[]{:S(2)}) copy-start(bf16[96,1056,1]{1,0,2:T(8,128)(2,1)} %constant.95) | copy-start | bytes 608260
  2.3 21.5 %collective-permute-start = (bf16[2,256,1,2,128]{4,1,3,2,0:T(8,128)(2,1)S(1)}, bf16[2,256,1,2,128]{4,1,3,2,0:T(8,128)(2,1)S(1)}, u32[]{:S(2)}, u32[]{:S(2)}) collective-permute-start(bf16[2,256,1,2,128]{4,1,3,2,0:T(8,128)(2,1)S(1)} %get-tuple-element.43), channel_id=1, source_target_pairs={{0,1},{1,2},{2,3},{3,0},{4,5},{5,6},{6,7},{7,4},{8,9},{9,10},{10,1... | collective-permute-start | bytes 786440 | tf_op jit(solution)/shard_map/ppermute | solution.py:103
  4.8 18.9 %collective-permute-start.1 = (bf16[2,256,1,2,128]{4,1,3,2,0:T(8,128)(2,1)S(1)}, bf16[2,256,1,2,128]{4,1,3,2,0:T(8,128)(2,1)}, u32[]{:S(2)}, u32[]{:S(2)}) collective-permute-start(bf16[2,256,1,2,128]{4,1,3,2,0:T(8,128)(2,1)S(1)} %get-tuple-element.44), channel_id=1, source_target_pairs={{0,2},{1,3},{2,0},{3,1},{4,6},{5,7},{6,4},{7,5},{8,10},{9,11},{10,... | collective-permute-start | bytes 786440 | tf_op jit(solution)/shard_map/ppermute | solution.py:103
  8.1 15.6 %collective-permute-start.2 = (bf16[2,256,1,2,128]{4,1,3,2,0:T(8,128)(2,1)S(1)}, bf16[2,256,1,2,128]{4,1,3,2,0:T(8,128)(2,1)}, u32[]{:S(2)}, u32[]{:S(2)}) collective-permute-start(bf16[2,256,1,2,128]{4,1,3,2,0:T(8,128)(2,1)S(1)} %get-tuple-element.45), channel_id=1, source_target_pairs={{0,3},{1,0},{2,1},{3,2},{4,7},{5,4},{6,5},{7,6},{8,11},{9,8},{10,9... | collective-permute-start | bytes 786440 | tf_op jit(solution)/shard_map/ppermute | solution.py:103
  9.2 2.9 %copy-start.18 = (f32[2,256,32]{1,2,0:T(8,128)}, f32[2,256,32]{1,2,0:T(8,128)S(1)}, u32[]{:S(2)}) copy-start(f32[2,256,32]{1,2,0:T(8,128)S(1)} %fusion.49) | copy-start | bytes 196612
  10.5 1.3 %copy-start.2 = (f32[2,256,1056]{1,2,0:T(8,128)}, f32[2,256,1056]{1,2,0:T(8,128)S(1)}, u32[]{:S(2)}) copy-start(f32[2,256,1056]{1,2,0:T(8,128)S(1)} %fusion.111) | copy-start | bytes 6488068
  14.5 21.5 %all-to-all-start = ((f32[32,40,128]{2,1,0:T(8,128)}), f32[32,40,128]{2,1,0:T(8,128)S(1)}, u32[]{:S(2)}, u32[]{:S(2)}) async-start(f32[32,40,128]{2,1,0:T(8,128)} %bitcast.26), calls=%async_computation | async-start | bytes 1310720 | tf_op jit(solution)/shard_map/all_to_all | solution.py:70
  23.8 2.6 %copy-start.22 = (bf16[96,1056,1,1]{1,0,3,2:T(8,128)(2,1)S(1)}, bf16[96,1056,1,1]{1,0,3,2:T(8,128)(2,1)}, u32[]{:S(2)}) copy-start(bf16[96,1056,1,1]{1,0,3,2:T(8,128)(2,1)} %constant.94) | copy-start | bytes 608260
  25.0 1.0 copy-start.5
  37.7 17.8 %all-to-all-start.1 = ((f32[32,40,128]{2,1,0:T(8,128)}), f32[32,40,128]{2,1,0:T(8,128)}, u32[]{:S(2)}, u32[]{:S(2)}) async-start(f32[32,40,128]{2,1,0:T(8,128)} %copy.128), calls=%async_computation.1 | async-start | bytes 1310720 | tf_op jit(solution)/shard_map/all_to_all | solution.py:84
  61.3 0.8 copy-start.25
  61.3 1.2 copy-start.6
  61.7 2.5 %copy-start.7 = (f32[1056,128]{1,0:T(8,128)S(1)}, f32[1056,128]{1,0:T(8,128)}, u32[]{:S(2)}) copy-start(f32[1056,128]{1,0:T(8,128)} %slice.108) | copy-start | bytes 1622020
  65.4 1.2 copy-start.12
  66.6 5.8 %copy-start.4 = (bf16[2,4,256,528]{2,3,1,0:T(8,128)(2,1)S(1)}, bf16[2,4,256,528]{2,3,1,0:T(8,128)(2,1)}, u32[]{:S(2)}) copy-start(bf16[2,4,256,528]{2,3,1,0:T(8,128)(2,1)} %get-tuple-element.32) | copy-start | bytes 6488068
  72.4 4.1 %copy-start.15 = (bf16[2,4,256,128]{3,2,0,1:T(8,128)(2,1)S(1)}, bf16[2,4,256,128]{3,2,0,1:T(8,128)(2,1)}, u32[]{:S(2)}) copy-start(bf16[2,4,256,128]{3,2,0,1:T(8,128)(2,1)} %get-tuple-element.41) | copy-start | bytes 1572868
  72.4 4.1 %copy-start.30 = (f32[2,4,256]{2,1,0:T(4,128)S(1)}, f32[2,4,256]{2,1,0:T(4,128)}, u32[]{:S(2)}) copy-start(f32[2,4,256]{2,1,0:T(4,128)} %copy_negate_fusion) | copy-start | bytes 24580
  76.9 1.8 %copy-start.13 = (bf16[2,4,256,256]{2,3,1,0:T(8,128)(2,1)}, bf16[2,4,256,256]{2,3,1,0:T(8,128)(2,1)S(1)}, u32[]{:S(2)}) copy-start(bf16[2,4,256,256]{2,3,1,0:T(8,128)(2,1)S(1)} %select_convert_fusion) | copy-start | bytes 3145732
  77.0 1.8 %copy-start.8 = (f32[1056,128]{1,0:T(8,128)S(1)}, f32[1056,128]{1,0:T(8,128)}, u32[]{:S(2)}) copy-start(f32[1056,128]{1,0:T(8,128)} %slice.108) | copy-start | bytes 1622020
  78.7 2.2 %copy-start.27 = (f32[2,528,1]{1,2,0:T(1,128)S(1)}, f32[2,528,1]{1,2,0:T(1,128)}, u32[]{:S(2)}) copy-start(f32[2,528,1]{1,2,0:T(1,128)} %slice_add_fusion) | copy-start | bytes 12676
  78.7 7.4 %copy-start.16 = (bf16[2,4,256,128]{3,2,0,1:T(8,128)(2,1)S(1)}, bf16[2,4,256,128]{3,2,0,1:T(8,128)(2,1)}, u32[]{:S(2)}) copy-start(bf16[2,4,256,128]{3,2,0,1:T(8,128)(2,1)} %get-tuple-element.41) | copy-start | bytes 1572868
  81.0 7.6 %copy-start.11 = (bf16[2,4,256,128]{3,2,0,1:T(8,128)(2,1)S(1)}, bf16[2,4,256,128]{3,2,0,1:T(8,128)(2,1)}, u32[]{:S(2)}) copy-start(bf16[2,4,256,128]{3,2,0,1:T(8,128)(2,1)} %get-tuple-element.39) | copy-start | bytes 1572868
  81.9 6.9 %copy-start.10 = (bf16[2,4,256,128]{3,2,0,1:T(8,128)(2,1)S(1)}, bf16[2,4,256,128]{3,2,0,1:T(8,128)(2,1)}, u32[]{:S(2)}) copy-start(bf16[2,4,256,128]{3,2,0,1:T(8,128)(2,1)} %get-tuple-element.40) | copy-start | bytes 1572868
  81.9 17.3 %all-to-all-start.2 = ((f32[32,40,128]{2,1,0:T(8,128)}), f32[32,40,128]{2,1,0:T(8,128)S(1)}, u32[]{:S(2)}, u32[]{:S(2)}) async-start(f32[32,40,128]{2,1,0:T(8,128)} %bitcast.42), calls=%async_computation.2 | async-start | bytes 1310720 | tf_op jit(solution)/shard_map/all_to_all | solution.py:70
  86.2 2.9 %copy-start.31 = (f32[2,4,256]{2,1,0:T(4,128)S(1)}, f32[2,4,256]{2,1,0:T(4,128)}, u32[]{:S(2)}) copy-start(f32[2,4,256]{2,1,0:T(4,128)} %copy_negate_fusion) | copy-start | bytes 24580
  86.2 2.9 %copy-start.34 = (f32[2,528]{1,0:T(2,128)S(1)}, f32[2,528]{1,0:T(2,128)}, u32[]{:S(2)}) copy-start(f32[2,528]{1,0:T(2,128)} %get-tuple-element.76) | copy-start | bytes 12676
  94.5 10.5 %copy-start.29 = (f32[528]{0:T(1024)S(1)}, f32[528]{0:T(1024)}, u32[]{:S(2)}) copy-start(f32[528]{0:T(1024)} %constant.78.clone) | copy-start | bytes 6340
  100.9 17.1 %all-to-all-start.3 = ((f32[32,40,128]{2,1,0:T(8,128)}), f32[32,40,128]{2,1,0:T(8,128)S(1)}, u32[]{:S(2)}, u32[]{:S(2)}) async-start(f32[32,40,128]{2,1,0:T(8,128)} %copy.154), calls=%async_computation.3 | async-start | bytes 1310720 | tf_op jit(solution)/shard_map/all_to_all | solution.py:84
  110.9 1.4 %copy-start.17 = (bf16[1056,32,1,1]{0,1,2,3:T(8,128)(2,1)S(1)}, bf16[1056,32,1,1]{0,1,2,3:T(8,128)(2,1)}, u32[]{:S(2)}) copy-start(bf16[1056,32,1,1]{0,1,2,3:T(8,128)(2,1)} %constant.96) | copy-start | bytes 202756
  113.2 1.0 copy-start.32
  113.2 1.0 copy-start.33
  114.2 3.9 %copy-start.28 = (bf16[528]{0:T(1024)(128)(2,1)S(1)}, bf16[528]{0:T(1024)(128)(2,1)}, u32[]{:S(2)}) copy-start(bf16[528]{0:T(1024)(128)(2,1)} %constant.77.clone) | copy-start | bytes 3172
  114.5 4.2 %copy-start.20 = (f32[2,256,128]{2,1,0:T(8,128)S(1)}, f32[2,256,128]{2,1,0:T(8,128)}, u32[]{:S(2)}) copy-start(f32[2,256,128]{2,1,0:T(8,128)} %convolution_bitcast_fusion.2) | copy-start | bytes 786436
  118.1 2.0 %copy-start.3 = (f32[2,256,1056]{1,2,0:T(8,128)S(1)}, f32[2,256,1056]{1,2,0:T(8,128)}, u32[]{:S(2)}) copy-start(f32[2,256,1056]{1,2,0:T(8,128)} %copy-done.2) | copy-start | bytes 6488068
  118.1 1.9 %copy-start.9 = (f32[2,256,528]{1,2,0:T(8,128)S(1)}, f32[2,256,528]{1,2,0:T(8,128)}, u32[]{:S(2)}) copy-start(f32[2,256,528]{1,2,0:T(8,128)} %convolution_bitcast_fusion) | copy-start | bytes 3244036
  120.0 0.9 copy-start.23
  120.5 0.8 copy-start.19
  120.5 0.9 copy-start.24
  121.4 11.6 %copy-start.1 = (bf16[256,8,128]{2,1,0:T(8,128)(2,1)S(1)}, bf16[256,8,128]{2,1,0:T(8,128)(2,1)}, u32[]{:S(2)}) copy-start(bf16[256,8,128]{2,1,0:T(8,128)(2,1)} %param.10) | copy-start | bytes 1572868
  122.8 4.6 %collective-permute-start.3 = (bf16[256,1,2,128]{3,0,1,2:T(8,128)(2,1)S(1)}, bf16[256,1,2,128]{3,0,1,2:T(8,128)(2,1)S(1)}, u32[]{:S(2)}, u32[]{:S(2)}) collective-permute-start(bf16[256,1,2,128]{3,0,1,2:T(8,128)(2,1)S(1)} %get-tuple-element.52), channel_id=1, source_target_pairs={{0,3},{1,0},{2,1},{3,2},{4,7},{5,4},{6,5},{7,6},{8,11},{9,8},{10,9... | collective-permute-start | bytes 393224 | tf_op jit(solution)/shard_map/ppermute | solution.py:116
  122.9 6.1 %collective-permute-start.4 = (bf16[256,1,2,128]{3,0,1,2:T(8,128)(2,1)S(1)}, bf16[256,1,2,128]{3,0,1,2:T(8,128)(2,1)S(1)}, u32[]{:S(2)}, u32[]{:S(2)}) collective-permute-start(bf16[256,1,2,128]{3,0,1,2:T(8,128)(2,1)S(1)} %get-tuple-element.51), channel_id=1, source_target_pairs={{0,2},{1,3},{2,0},{3,1},{4,6},{5,7},{6,4},{7,5},{8,10},{9,11},{10,... | collective-permute-start | bytes 393224 | tf_op jit(solution)/shard_map/ppermute | solution.py:116
  125.4 6.6 %collective-permute-start.5 = (bf16[256,1,2,128]{3,0,1,2:T(8,128)(2,1)S(1)}, bf16[256,1,2,128]{3,0,1,2:T(8,128)(2,1)S(1)}, u32[]{:S(2)}, u32[]{:S(2)}) collective-permute-start(bf16[256,1,2,128]{3,0,1,2:T(8,128)(2,1)S(1)} %get-tuple-element.50), channel_id=1, source_target_pairs={{0,1},{1,2},{2,3},{3,0},{4,5},{5,6},{6,7},{7,4},{8,9},{9,10},{10,1... | collective-permute-start | bytes 393224 | tf_op jit(solution)/shard_map/ppermute | solution.py:116
  132.2 0.8 copy-start.14

commit v16 on v14

--- a/solution.py
+++ b/solution.py
@@ -108,14 +108,14 @@
 def head_return(grads, heads_all):
     count = lax.axis_size("head")
     me = lax.axis_index("head")
-    owned = grads.shape[2]
-    out = jnp.zeros((grads.shape[0], 1, heads_all, grads.shape[3]), grads.dtype)
+    pieces = []
     for k in range(count):
         piece = grads[:, k : k + 1]
         if k:
             piece = lax.ppermute(piece, "head", [(j, (j - k) % count) for j in range(count)])
-        out = lax.dynamic_update_slice_in_dim(out, piece, ((me + k) % count) * owned, axis=2)
-    return out
+        pieces.append(piece)
+    blocks = [lax.select_n((b - me) % count, *pieces) for b in range(count)]
+    return jnp.concatenate(blocks, axis=2)
 
 
 def sketch_parts(tokens, projector, pattern):

time: 124 us -> 124 us (level)
  waiting for transfers between devices: 23.5 us -> 17.7 us
  matrix products: 34.1 us -> 38.4 us
  starting transfers between devices: 31.1 us -> 33.9 us
  local copies, waits for them, and re-layouts: 16.1 us -> 14.1 us
    ppermute x3, waiting for transfers between devices: 5.84 us -> 0.9 us  [head_return(): lax.ppermute(piece, 'head', [(j, (j - k) % count) for j in range(count)])]
    dot_general x12, matrix products: 9.67 us -> 12.1 us  [dot_parts(): term = jnp.einsum(pattern, *args, preferred_element_type=f32)]
    ppermute x3, starting transfers between devices: 2.59 us -> 4.74 us  [head_return(): lax.ppermute(piece, 'head', [(j, (j - k) % count) for j in range(count)])]
    all_to_all x2, starting transfers between devices: 9.07 us -> 10.4 us  [scan_return(): lax.all_to_all(summed, 'ctx', 0, 0, tiled=True).reshape(n * per, width)]
    dot_general x1, matrix products: 2.4 us -> 1.15 us  [body(): jnp.einsum('hmij,hmid->hjd', weights, grad_low, preferred_element_type=f32)]
    unnamed x75 -> x70, local copies, waits for them, and re-layouts: 6.78 us -> 6.27 us
  transfers between devices with their start and end apart: 10 -> 10, of which waited for: 7 -> 5; matrix products, arithmetic and copies ran while one was open for 31% -> 35% of each run, Pallas kernels for 0% -> 0%
where the time goes in v16:
time: 124 us; the launch traced here: 123 us
  matrix products  38.4 us (31%)
  starting transfers between devices  33.9 us (27%)
  waiting for transfers between devices  17.7 us (14%)
  other arithmetic  17.5 us (14%)
  local copies, waits for them, and re-layouts  14.1 us (11%)
  between operations  1.46 us (1%)
    all_to_all x2, starting transfers between devices, scan_send(): return lax.all_to_all(flat.reshape(n, per, width), 'ctx', 0, 0, tiled=True)  13.3 us
    dot_general x12, matrix products, dot_parts(): term = jnp.einsum(pattern, *args, preferred_element_type=f32)  12.1 us
    all_to_all x2, starting transfers between devices, scan_return(): lax.all_to_all(summed, 'ctx', 0, 0, tiled=True).reshape(n * per, width)  10.4 us
    all_to_all x2, waiting for transfers between devices, scan_return(): lax.all_to_all(summed, 'ctx', 0, 0, tiled=True).reshape(n * per, width)  9.86 us
    all_to_all x2, waiting for transfers between devices, scan_send(): return lax.all_to_all(flat.reshape(n, per, width), 'ctx', 0, 0, tiled=True)  6.97 us
    unnamed x70, local copies, waits for them, and re-layouts  6.27 us
    dot_general x2, matrix products, take_pair(): out = jnp.einsum('...k,kn->...n', lhs, rhs, preferred_element_type=f32)  6.15 us
    mul x1, other arithmetic, tri_feature_back(): cotangent * second  5.95 us
  transfers between devices with their start and end apart: 10, of which 5 were waited for; matrix products, arithmetic and copies ran while one was open for 35% of the time, Pallas kernels for 0%

profile of v16, /device:TPU:1, one launch (start us, length us, event | category | flops | bytes accessed | tf_op | source)
XLA Modules:
  0.0 123.1 jit_solution(1807188039319278591)
XLA Ops:
  0.7 1.4 %copy_bitcast_fusion = (bf16[1,256,1,8,128]{4,1,3,2,0:T(8,128)(2,1)S(1)}, bf16[1,256,1,8,128]{4,1,3,2,0:T(8,128)(2,1)S(1)}) fusion(bf16[256,1,8,128]{3,2,1,0:T(8,128)(2,1)} %param.12, bf16[256,1,8,128]{3,2,1,0:T(8,128)(2,1)} %param.9), kind=kLoop, calls=%fused_computation.121 | loop fusion | bytes 2097152 | tf_op jit(solution)/shard_map/stack | solution.py:168
  2.2 4.7 %collective-permute-start.2 = (bf16[2,256,1,2,128]{4,1,3,2,0:T(8,128)(2,1)S(1)}, bf16[2,256,1,2,128]{4,1,3,2,0:T(8,128)(2,1)S(1)}, u32[]{:S(2)}, u32[]{:S(2)}) collective-permute-start(bf16[2,256,1,2,128]{4,1,3,2,0:T(8,128)(2,1)S(1)} %get-tuple-element.42), channel_id=1, source_target_pairs={{0,3},{1,0},{2,1},{3,2},{4,7},{5,4},{6,5},{7,6},{8,11},{9,8},{10,9... | collective-permute-start | bytes 786440 | tf_op jit(solution)/shard_map/ppermute | solution.py:103
  6.9 0.7 collective-permute-start
  7.6 1.5 %constant_dynamic-slice_fusion = (bf16[256,2,128]{2,1,0:T(2,128)(2,1)S(1)}, bf16[256,2,128]{2,1,0:T(2,128)(2,1)S(1)}) fusion(bf16[256,8,128]{2,1,0:T(8,128)(2,1)} %param.11, s32[]{:T(128)S(6)} %select_n.179, bf16[256,8,128]{2,1,0:T(8,128)(2,1)} %param.10), kind=kLoop, calls=%fused_computation.230 | loop fusion | bytes 524292 | tf_op jit(solution)/shard_map/dynamic_slice | solution.py:167
  9.2 0.8 reduce-precision_convert_fusion.16
  10.0 1.4 %fusion.112 = f32[2,256,1056]{1,2,0:T(8,128)S(1)} fusion(bf16[96,1056,1]{1,0,2:T(8,128)(2,1)} %constant.101, bf16[2,256,32]{1,2,0:T(8,128)(2,1)S(1)} %get-tuple-element.69, bf16[2,256,32]{1,2,0:T(8,128)(2,1)S(1)} %get-tuple-element.68, bf16[2,256,32]{1,2,0:T(8,128)(2,1)S(1)} %get-tuple-element.67), kind=kOutput, calls=%fused_computation.174 | convolution fusion | flops 104103936 | bytes 2463744 | tf_op jit(solution)/shard_map/...k,kn->...n/dot_general | solution.py:49
  11.5 1.3 %copy-done.3 = f32[2,256,1056]{1,2,0:T(8,128)} copy-done((f32[2,256,1056]{1,2,0:T(8,128)}, f32[2,256,1056]{1,2,0:T(8,128)S(1)}, u32[]{:S(2)}) %copy-start.3) | copy-done | bytes 2162712
  13.1 0.3 fusion.157
  13.4 0.9 fusion.58
  14.3 8.6 %all-to-all-start = ((f32[32,40,128]{2,1,0:T(8,128)}), f32[32,40,128]{2,1,0:T(8,128)S(1)}, u32[]{:S(2)}, u32[]{:S(2)}) async-start(f32[32,40,128]{2,1,0:T(8,128)} %bitcast.26), calls=%async_computation | async-start | bytes 1310720 | tf_op jit(solution)/shard_map/all_to_all | solution.py:70
  23.0 0.7 copy.206
  23.9 0.3 fusion.35
  24.2 0.8 copy-done.5
  24.9 1.0 reduce-precision_convert_fusion.11
  25.9 4.7 %fusion.80 = f32[2,4,256,1056]{2,3,1,0:T(8,128)} fusion(bf16[96,1056,1,1]{1,0,3,2:T(8,128)(2,1)S(1)} %copy-done.26, bf16[2,4,256,32]{2,3,0,1:T(8,128)(2,1)S(1)} %get-tuple-element.60, bf16[2,4,256,32]{2,3,0,1:T(8,128)(2,1)S(1)} %get-tuple-element.59, bf16[2,4,256,32]{2,3,0,1:T(8,128)(2,1)S(1)} %get-tuple-element.58), kind=kOutput, calls=%fused_computation.131 | convolution fusion | flops 416415744 | bytes 9246720 | tf_op jit(solution)/shard_map/...k,kn->...n/dot_general | solution.py:49
  30.7 5.1 %all-to-all-done = f32[32,40,128]{2,1,0:T(8,128)S(1)} async-done(((f32[32,40,128]{2,1,0:T(8,128)}), f32[32,40,128]{2,1,0:T(8,128)S(1)}, u32[]{:S(2)}, u32[]{:S(2)}) %all-to-all-start) | async-done | bytes 655392 | tf_op jit(solution)/shard_map/all_to_all | solution.py:70
  35.8 0.5 fusion.61
  36.3 1.2 copy.76
  37.5 4.8 %all-to-all-start.1 = ((f32[32,40,128]{2,1,0:T(8,128)}), f32[32,40,128]{2,1,0:T(8,128)}, u32[]{:S(2)}, u32[]{:S(2)}) async-start(f32[32,40,128]{2,1,0:T(8,128)} %copy.76), calls=%async_computation.1 | async-start | bytes 1310720 | tf_op jit(solution)/shard_map/all_to_all | solution.py:84
  42.3 4.2 %broadcast_multiply_fusion = (bf16[2,4,256,528]{2,3,1,0:T(8,128)(2,1)S(1)}, bf16[2,4,256,528]{2,3,1,0:T(8,128)(2,1)S(1)}) fusion(bf16[528]{0:T(1024)(128)(2,1)S(1)} %copy-done.30, f32[2,4,256,1056]{2,3,1,0:T(8,128)} %fusion.80), kind=kLoop, calls=%fused_computation.82 | loop fusion | flops 4325376 | bytes 12977184 | tf_op jit(solution)/shard_map/mul | solution.py:180
  46.5 2.1 %select_convert_fusion.1 = (bf16[2,4,256,256]{2,3,1,0:T(8,128)(2,1)}, f32[2,4,256,256]{2,3,1,0:T(8,128)S(1)}) fusion(pred[256,256]{0,1:T(8,128)(4,1)S(1)} %iota_compare_fusion.1, bf16[2,4,256,528]{2,3,1,0:T(8,128)(2,1)S(1)} %get-tuple-element.28, bf16[2,256,528]{1,2,0:T(8,128)(2,1)S(1)} %get-tuple-element.27), kind=kOutput, calls=%fused_computation.25 | convolution fusion | flops 554172416 | bytes 5914624 | tf_op jit(solution)/shard_map/hmif,hjf->hmij/dot_general | solution.py:188
  48.8 6.5 %all-to-all-done.1 = f32[32,40,128]{2,1,0:T(8,128)} async-done(((f32[32,40,128]{2,1,0:T(8,128)}), f32[32,40,128]{2,1,0:T(8,128)}, u32[]{:S(2)}, u32[]{:S(2)}) %all-to-all-start.1) | async-done | bytes 655392 | tf_op jit(solution)/shard_map/all_to_all | solution.py:84
  55.3 1.1 slice.96
  56.4 0.8 slice.94
  57.3 2.7 %fusion.16 = f32[2,4,256,128]{3,2,0,1:T(8,128)S(1)} fusion(bf16[2,4,256,528]{2,3,1,0:T(8,128)(2,1)} %copy-done, f32[2,528,128]{2,1,0:T(8,128)S(1)} %bitcast.184), kind=kOutput, calls=%fused_computation.27 | convolution fusion | flops 277229568 | bytes 3751936 | tf_op jit(solution)/shard_map/hmif,hfd->hmid/dot_general | solution.py:36
  60.0 2.1 %fusion.23 = f32[2,4,256,128]{3,2,0,1:T(8,128)} fusion(f32[2,4,256,128]{3,2,0,1:T(8,128)S(1)} %fusion.16, bf16[2,4,256,528]{2,3,1,0:T(8,128)(2,1)S(1)} %copy-done.1, f32[2,528,128]{2,1,0:T(8,128)S(1)} %bitcast.185), kind=kOutput, calls=%fused_computation.47 | convolution fusion | flops 277356544 | bytes 4800512 | tf_op jit(solution)/shard_map/hmif,hfd->hmid/dot_general | solution.py:36
  62.2 0.6 fusion.161
  62.8 2.1 %fusion.142 = f32[2,1,4,256]{3,1,2,0:T(1,128)S(1)} fusion(bf16[2,4,256,528]{2,3,1,0:T(8,128)(2,1)} %copy-done, bf16[2,528,1,1]{1,0,2,3:T(2,128)(2,1)S(1)} %get-tuple-element.79), kind=kOutput, calls=%fused_computation.222 | convolution fusion | flops 2162688 | bytes 2172992 | tf_op jit(solution)/shard_map/hmif,hf->hmi/dot_general | solution.py:36
  64.9 0.4 fusion.144
  65.3 1.6 %reduce-precision_convert_fusion.2 = (bf16[2,4,256,128]{3,2,0,1:T(8,128)(2,1)}, bf16[2,4,256,128]{3,2,0,1:T(8,128)(2,1)}, bf16[2,4,256,128]{3,2,0,1:T(8,128)(2,1)}) fusion(f32[2,4,256]{2,0,1:T(2,128)S(1)} %copy.77, bf16[2,256,4,2,128]{4,1,3,2,0:T(8,128)(2,1)S(1)} %copy-done.6), kind=kLoop, calls=%fused_computation.32 | loop fusion | flops 1835008 | bytes 2105344 | tf_op jit(solution)/shard_map/convert_element_type | solution.py:26
  67.0 1.1 fusion.33
  68.1 0.7 fusion.133
  68.7 0.7 fusion.135
  69.4 1.8 %fusion.78 = f32[2,528,128,1]{2,1,3,0:T(8,128)S(1)} fusion(bf16[2,4,256,528]{2,3,1,0:T(8,128)(2,1)S(1)} %get-tuple-element.29, bf16[2,4,256,128]{3,2,0,1:T(8,128)(2,1)} %get-tuple-element.38), kind=kOutput, calls=%fused_computation.128 | convolution fusion | flops 276824064 | bytes 3227648 | tf_op jit(solution)/shard_map/hmif,hmid->hfd/dot_general | solution.py:200
  71.2 0.9 select_maximum_fusion
  72.1 4.7 %all-to-all-start.2 = ((f32[32,40,128]{2,1,0:T(8,128)}), f32[32,40,128]{2,1,0:T(8,128)}, u32[]{:S(2)}, u32[]{:S(2)}) async-start(f32[32,40,128]{2,1,0:T(8,128)} %bitcast.187), calls=%async_computation.2 | async-start | bytes 1310720 | tf_op jit(solution)/shard_map/all_to_all | solution.py:70
  76.9 1.6 %select_convert_fusion = bf16[2,4,256,256]{2,3,1,0:T(8,128)(2,1)S(1)} fusion(f32[2,4,256]{2,1,0:T(4,128)S(1)} %copy.86, pred[256,256]{0,1:T(8,128)(4,1)} %copy-done.13, bf16[2,4,256,128]{3,2,0,1:T(8,128)(2,1)} %get-tuple-element.38, bf16[256,2,128]{2,1,0:T(2,128)(2,1)} %copy-done.11), kind=kOutput, calls=%fused_computation.24 | convolution fusion | flops 135790592 | bytes 1777664 | tf_op jit(solution)/shard_map/hmid,hjd->hmij/dot_general | solution.py:206
  78.4 1.0 fusion.64
  79.4 1.7 %convolution_bitcast_fusion = f32[2,256,528]{1,2,0:T(8,128)} fusion(bf16[2,4,256,256]{2,3,1,0:T(8,128)(2,1)S(1)} %select_convert_fusion, bf16[2,4,256,528]{2,3,1,0:T(8,128)(2,1)S(1)} %get-tuple-element.29), kind=kOutput, calls=%fused_computation.43 | convolution fusion | flops 553648128 | bytes 4292608 | tf_op jit(solution)/shard_map/hmij,hmif->hjf/dot_general | solution.py:221
  81.2 1.2 convolution_bitcast_fusion.1
  82.9 5.2 %multiply_add_fusion = f32[2,4,256,528]{2,3,1,0:T(8,128)} fusion(f32[2,528]{1,0:T(2,128)S(1)} %copy-done.32, f32[2,4,256]{2,1,0:T(4,128)S(1)} %copy.86, bf16[2,4,256,128]{2,3,1,0:T(8,128)(2,1)S(1)} %copy.89, bf16[2,4,256,128]{2,3,1,0:T(8,128)(2,1)S(1)} %copy.87, bf16[2,4,256,256]{2,3,1,0:T(8,128)(2,1)} %copy-done.18, ...), kind=kOutput, calls=%fused_computation.9 | convolution fusion | flops 1402175488 | bytes 7516288 | tf_op jit(solution)/shard_map/hmik,hkf->hmif/dot_general | solution.py:213
  88.1 1.8 %all-to-all-done.2 = f32[32,40,128]{2,1,0:T(8,128)} async-done(((f32[32,40,128]{2,1,0:T(8,128)}), f32[32,40,128]{2,1,0:T(8,128)}, u32[]{:S(2)}, u32[]{:S(2)}) %all-to-all-start.2) | async-done | bytes 655392 | tf_op jit(solution)/shard_map/all_to_all | solution.py:70
  89.9 1.6 %fusion.59 = f32[32,40,128]{2,0,1:T(8,128)S(1)} fusion(f32[32,40,128]{2,1,0:T(8,128)} %all-to-all-done.2), kind=kOutput, calls=%fused_computation.103 | convolution fusion | flops 62915584 | bytes 1310720 | tf_op jit(solution)/shard_map/ij,jrc->irc/dot_general | solution.py:78
  91.5 1.2 %copy.98 = f32[32,40,128]{2,1,0:T(8,128)} copy(f32[32,40,128]{2,0,1:T(8,128)S(1)} %fusion.59) | data formatting | bytes 1310720 | tf_op jit(solution)/shard_map/optimization_barrier | solution.py:224
  92.7 5.7 %all-to-all-start.3 = ((f32[32,40,128]{2,1,0:T(8,128)}), f32[32,40,128]{2,1,0:T(8,128)S(1)}, u32[]{:S(2)}, u32[]{:S(2)}) async-start(f32[32,40,128]{2,1,0:T(8,128)} %copy.98), calls=%async_computation.3 | async-start | bytes 1310720 | tf_op jit(solution)/shard_map/all_to_all | solution.py:84
  98.4 5.9 %slice_multiply_fusion = (f32[2,4,256,528]{2,3,1,0:T(8,128)S(1)}, f32[2,4,256,528]{2,3,1,0:T(8,128)S(1)}) fusion(f32[2,4,256,528]{2,3,1,0:T(8,128)} %multiply_add_fusion, f32[2,4,256,1056]{2,3,1,0:T(8,128)} %fusion.80, f32[528]{0:T(1024)S(1)} %copy-done.31), kind=kLoop, calls=%fused_computation.11 | loop fusion | flops 3244032 | bytes 21628992 | tf_op jit(solution)/shard_map/mul | solution.py:139
  104.4 1.4 %reduce-precision_convert_fusion = (bf16[2,4,256,1056]{2,3,1,0:T(8,128)(2,1)S(1)}, bf16[2,4,256,1056]{2,3,1,0:T(8,128)(2,1)S(1)}) fusion(f32[2,4,256,528]{2,3,1,0:T(8,128)S(1)} %get-tuple-element.31, f32[2,4,256,528]{2,3,1,0:T(8,128)S(1)} %get-tuple-element.30), kind=kLoop, calls=%fused_computation.1 | loop fusion | flops 10813440 | bytes 17301504 | tf_op jit(solution)/shard_map/convert_element_type | solution.py:26
  105.8 0.9 fusion.1
  106.7 0.9 reduce-precision_convert_fusion.9
  107.7 0.3 fusion.34
  108.0 3.3 %all-to-all-done.3 = f32[32,40,128]{2,1,0:T(8,128)S(1)} async-done(((f32[32,40,128]{2,1,0:T(8,128)}), f32[32,40,128]{2,1,0:T(8,128)S(1)}, u32[]{:S(2)}, u32[]{:S(2)}) %all-to-all-start.3) | async-done | bytes 655392 | tf_op jit(solution)/shard_map/all_to_all | solution.py:84
  111.5 0.5 fusion.74
  112.1 2.1 %collective-permute-start.4 = (bf16[256,1,2,128]{3,0,1,2:T(8,128)(2,1)S(1)}, bf16[256,1,2,128]{3,0,1,2:T(8,128)(2,1)S(1)}, u32[]{:S(2)}, u32[]{:S(2)}) collective-permute-start(bf16[256,1,2,128]{3,0,1,2:T(8,128)(2,1)S(1)} %get-tuple-element.53), channel_id=1, source_target_pairs={{0,2},{1,3},{2,0},{3,1},{4,6},{5,7},{6,4},{7,5},{8,10},{9,11},{10,... | collective-permute-start | bytes 393224 | tf_op jit(solution)/shard_map/ppermute | solution.py:115
  114.1 0.3 collective-permute-start.5
  114.4 2.4 %collective-permute-start.3 = (bf16[256,1,2,128]{3,0,1,2:T(8,128)(2,1)S(1)}, bf16[256,1,2,128]{3,0,1,2:T(8,128)(2,1)S(1)}, u32[]{:S(2)}, u32[]{:S(2)}) collective-permute-start(bf16[256,1,2,128]{3,0,1,2:T(8,128)(2,1)S(1)} %get-tuple-element.51), channel_id=1, source_target_pairs={{0,3},{1,0},{2,1},{3,2},{4,7},{5,4},{6,5},{7,6},{8,11},{9,8},{10,9... | collective-permute-start | bytes 393224 | tf_op jit(solution)/shard_map/ppermute | solution.py:115
  116.8 0.5 fusion.47
  117.4 0.5 slice_multiply_fusion.1
  117.9 0.4 copy-done.27
  118.2 0.3 fusion.51
  118.7 0.4 reduce-precision_convert_fusion.14
  119.3 0.8 copy.102
  120.1 0.8 copy.103
  120.9 0.9 collective-permute-done.5
  121.9 1.1 copy.101
  (97 shorter events, 2.3 us)
Async XLA Ops:
  0.6 6.9 %copy-start.29 = (s32[2,128,32]{1,2,0:T(8,128)S(1)}, s32[2,128,32]{1,2,0:T(8,128)}, u32[]{:S(2)}) copy-start(s32[2,128,32]{1,2,0:T(8,128)} %param.13) | copy-start | bytes 98308
  2.2 21.5 %collective-permute-start.2 = (bf16[2,256,1,2,128]{4,1,3,2,0:T(8,128)(2,1)S(1)}, bf16[2,256,1,2,128]{4,1,3,2,0:T(8,128)(2,1)S(1)}, u32[]{:S(2)}, u32[]{:S(2)}) collective-permute-start(bf16[2,256,1,2,128]{4,1,3,2,0:T(8,128)(2,1)S(1)} %get-tuple-element.42), channel_id=1, source_target_pairs={{0,3},{1,0},{2,1},{3,2},{4,7},{5,4},{6,5},{7,6},{8,11},{9,8},{10,9... | collective-permute-start | bytes 786440 | tf_op jit(solution)/shard_map/ppermute | solution.py:103
  6.9 16.8 %collective-permute-start.1 = (bf16[2,256,1,2,128]{4,1,3,2,0:T(8,128)(2,1)S(1)}, bf16[2,256,1,2,128]{4,1,3,2,0:T(8,128)(2,1)S(1)}, u32[]{:S(2)}, u32[]{:S(2)}) collective-permute-start(bf16[2,256,1,2,128]{4,1,3,2,0:T(8,128)(2,1)S(1)} %get-tuple-element.41), channel_id=1, source_target_pairs={{0,2},{1,3},{2,0},{3,1},{4,6},{5,7},{6,4},{7,5},{8,10},{9,11},{10,... | collective-permute-start | bytes 786440 | tf_op jit(solution)/shard_map/ppermute | solution.py:103
  6.9 16.8 %collective-permute-start = (bf16[2,256,1,2,128]{4,1,3,2,0:T(8,128)(2,1)S(1)}, bf16[2,256,1,2,128]{4,1,3,2,0:T(8,128)(2,1)S(1)}, u32[]{:S(2)}, u32[]{:S(2)}) collective-permute-start(bf16[2,256,1,2,128]{4,1,3,2,0:T(8,128)(2,1)S(1)} %get-tuple-element.40), channel_id=1, source_target_pairs={{0,1},{1,2},{2,3},{3,0},{4,5},{5,6},{6,7},{7,4},{8,9},{9,10},{10,1... | collective-permute-start | bytes 786440 | tf_op jit(solution)/shard_map/ppermute | solution.py:103
  9.1 13.9 %copy-start.11 = (bf16[256,2,128]{2,1,0:T(2,128)(2,1)}, bf16[256,2,128]{2,1,0:T(2,128)(2,1)S(1)}, u32[]{:S(2)}) copy-start(bf16[256,2,128]{2,1,0:T(2,128)(2,1)S(1)} %get-tuple-element.86) | copy-start | bytes 393220
  9.2 3.8 %copy-start.23 = (f32[2,256,32]{1,2,0:T(8,128)}, f32[2,256,32]{1,2,0:T(8,128)S(1)}, u32[]{:S(2)}) copy-start(f32[2,256,32]{1,2,0:T(8,128)S(1)} %fusion.49) | copy-start | bytes 196612
  11.5 1.3 %copy-start.3 = (f32[2,256,1056]{1,2,0:T(8,128)}, f32[2,256,1056]{1,2,0:T(8,128)S(1)}, u32[]{:S(2)}) copy-start(f32[2,256,1056]{1,2,0:T(8,128)S(1)} %fusion.112) | copy-start | bytes 6488068
  14.3 21.5 %all-to-all-start = ((f32[32,40,128]{2,1,0:T(8,128)}), f32[32,40,128]{2,1,0:T(8,128)S(1)}, u32[]{:S(2)}, u32[]{:S(2)}) async-start(f32[32,40,128]{2,1,0:T(8,128)} %bitcast.26), calls=%async_computation | async-start | bytes 1310720 | tf_op jit(solution)/shard_map/all_to_all | solution.py:70
  22.9 25.7 %copy-start.13 = (pred[256,256]{0,1:T(8,128)(4,1)}, pred[256,256]{0,1:T(8,128)(4,1)S(1)}, u32[]{:S(2)}) copy-start(pred[256,256]{0,1:T(8,128)(4,1)S(1)} %iota_compare_fusion.1) | copy-start | bytes 196612
  23.7 2.2 %copy-start.26 = (bf16[96,1056,1,1]{1,0,3,2:T(8,128)(2,1)S(1)}, bf16[96,1056,1,1]{1,0,3,2:T(8,128)(2,1)}, u32[]{:S(2)}) copy-start(bf16[96,1056,1,1]{1,0,3,2:T(8,128)(2,1)} %constant.100) | copy-start | bytes 608260
  23.9 1.0 copy-start.5
  30.7 11.6 %copy-start.30 = (bf16[528]{0:T(1024)(128)(2,1)S(1)}, bf16[528]{0:T(1024)(128)(2,1)}, u32[]{:S(2)}) copy-start(bf16[528]{0:T(1024)(128)(2,1)} %constant.83.clone) | copy-start | bytes 3172
  37.5 17.8 %all-to-all-start.1 = ((f32[32,40,128]{2,1,0:T(8,128)}), f32[32,40,128]{2,1,0:T(8,128)}, u32[]{:S(2)}, u32[]{:S(2)}) async-start(f32[32,40,128]{2,1,0:T(8,128)} %copy.76), calls=%async_computation.1 | async-start | bytes 1310720 | tf_op jit(solution)/shard_map/all_to_all | solution.py:84
  46.5 2.1 %copy-start = (bf16[2,4,256,528]{2,3,1,0:T(8,128)(2,1)}, bf16[2,4,256,528]{2,3,1,0:T(8,128)(2,1)S(1)}, u32[]{:S(2)}) copy-start(bf16[2,4,256,528]{2,3,1,0:T(8,128)(2,1)S(1)} %get-tuple-element.28) | copy-start | bytes 6488068
  56.4 3.6 %copy-start.1 = (bf16[2,4,256,528]{2,3,1,0:T(8,128)(2,1)S(1)}, bf16[2,4,256,528]{2,3,1,0:T(8,128)(2,1)}, u32[]{:S(2)}) copy-start(bf16[2,4,256,528]{2,3,1,0:T(8,128)(2,1)} %copy-done) | copy-start | bytes 6488068
  62.2 2.7 %copy-start.2 = (bf16[2,4,256,528]{2,3,1,0:T(8,128)(2,1)S(1)}, bf16[2,4,256,528]{2,3,1,0:T(8,128)(2,1)}, u32[]{:S(2)}) copy-start(bf16[2,4,256,528]{2,3,1,0:T(8,128)(2,1)} %copy-done) | copy-start | bytes 6488068
  62.8 2.6 %copy-start.6 = (bf16[2,256,4,2,128]{4,1,3,2,0:T(8,128)(2,1)S(1)}, bf16[2,256,4,2,128]{4,1,3,2,0:T(8,128)(2,1)}, u32[]{:S(2)}) copy-start(bf16[2,256,4,2,128]{4,1,3,2,0:T(8,128)(2,1)} %copy-done.5) | copy-start | bytes 3145732
  64.9 2.1 %copy-start.12 = (bf16[256,2,128]{2,1,0:T(2,128)(2,1)S(1)}, bf16[256,2,128]{2,1,0:T(2,128)(2,1)}, u32[]{:S(2)}) copy-start(bf16[256,2,128]{2,1,0:T(2,128)(2,1)} %copy-done.11) | copy-start | bytes 393220
  64.9 2.1 %copy-start.15 = (bf16[2,4,256,256]{2,3,1,0:T(8,128)(2,1)S(1)}, bf16[2,4,256,256]{2,3,1,0:T(8,128)(2,1)}, u32[]{:S(2)}) copy-start(bf16[2,4,256,256]{2,3,1,0:T(8,128)(2,1)} %get-tuple-element.82) | copy-start | bytes 3145732
  64.9 2.1 %copy-start.17 = (f32[2,4,256,128]{3,2,0,1:T(8,128)S(1)}, f32[2,4,256,128]{3,2,0,1:T(8,128)}, u32[]{:S(2)}) copy-start(f32[2,4,256,128]{3,2,0,1:T(8,128)} %fusion.23) | copy-start | bytes 3145732
  72.1 17.8 %all-to-all-start.2 = ((f32[32,40,128]{2,1,0:T(8,128)}), f32[32,40,128]{2,1,0:T(8,128)}, u32[]{:S(2)}, u32[]{:S(2)}) async-start(f32[32,40,128]{2,1,0:T(8,128)} %bitcast.187), calls=%async_computation.2 | async-start | bytes 1310720 | tf_op jit(solution)/shard_map/all_to_all | solution.py:70
  78.4 2.7 %copy-start.18 = (bf16[2,4,256,256]{2,3,1,0:T(8,128)(2,1)}, bf16[2,4,256,256]{2,3,1,0:T(8,128)(2,1)S(1)}, u32[]{:S(2)}) copy-start(bf16[2,4,256,256]{2,3,1,0:T(8,128)(2,1)S(1)} %select_convert_fusion) | copy-start | bytes 3145732
  79.4 1.8 %copy-start.8 = (bf16[2,4,256,128]{3,2,0,1:T(8,128)(2,1)S(1)}, bf16[2,4,256,128]{3,2,0,1:T(8,128)(2,1)}, u32[]{:S(2)}) copy-start(bf16[2,4,256,128]{3,2,0,1:T(8,128)(2,1)} %get-tuple-element.38) | copy-start | bytes 1572868
  79.4 1.8 %copy-start.16 = (bf16[2,4,256,256]{2,3,1,0:T(8,128)(2,1)S(1)}, bf16[2,4,256,256]{2,3,1,0:T(8,128)(2,1)}, u32[]{:S(2)}) copy-start(bf16[2,4,256,256]{2,3,1,0:T(8,128)(2,1)} %get-tuple-element.82) | copy-start | bytes 3145732
  81.2 1.2 copy-start.10
  81.2 1.4 %copy-start.9 = (bf16[2,4,256,128]{3,2,0,1:T(8,128)(2,1)S(1)}, bf16[2,4,256,128]{3,2,0,1:T(8,128)(2,1)}, u32[]{:S(2)}) copy-start(bf16[2,4,256,128]{3,2,0,1:T(8,128)(2,1)} %get-tuple-element.36) | copy-start | bytes 1572868
  81.2 1.6 %copy-start.21 = (bf16[2,128,528]{1,2,0:T(8,128)(2,1)S(1)}, bf16[2,128,528]{1,2,0:T(8,128)(2,1)}, u32[]{:S(2)}) copy-start(bf16[2,128,528]{1,2,0:T(8,128)(2,1)} %get-tuple-element.49) | copy-start | bytes 811012
  81.2 1.6 %copy-start.22 = (bf16[2,128,528]{1,2,0:T(8,128)(2,1)S(1)}, bf16[2,128,528]{1,2,0:T(8,128)(2,1)}, u32[]{:S(2)}) copy-start(bf16[2,128,528]{1,2,0:T(8,128)(2,1)} %get-tuple-element.50) | copy-start | bytes 811012
  81.2 1.6 %copy-start.32 = (f32[2,528]{1,0:T(2,128)S(1)}, f32[2,528]{1,0:T(2,128)}, u32[]{:S(2)}) copy-start(f32[2,528]{1,0:T(2,128)} %get-tuple-element.77) | copy-start | bytes 12676
  88.1 10.3 %copy-start.31 = (f32[528]{0:T(1024)S(1)}, f32[528]{0:T(1024)}, u32[]{:S(2)}) copy-start(f32[528]{0:T(1024)} %constant.84.clone) | copy-start | bytes 6340
  92.7 18.6 %all-to-all-start.3 = ((f32[32,40,128]{2,1,0:T(8,128)}), f32[32,40,128]{2,1,0:T(8,128)S(1)}, u32[]{:S(2)}, u32[]{:S(2)}) async-start(f32[32,40,128]{2,1,0:T(8,128)} %copy.98), calls=%async_computation.3 | async-start | bytes 1310720 | tf_op jit(solution)/shard_map/all_to_all | solution.py:84
  104.4 1.4 %copy-start.20 = (bf16[1056,32,1,1]{0,1,2,3:T(8,128)(2,1)S(1)}, bf16[1056,32,1,1]{0,1,2,3:T(8,128)(2,1)}, u32[]{:S(2)}) copy-start(bf16[1056,32,1,1]{0,1,2,3:T(8,128)(2,1)} %constant.102) | copy-start | bytes 202756
  105.8 1.0 copy-start.14
  111.3 5.5 %copy-start.25 = (f32[2,256,128]{2,1,0:T(8,128)S(1)}, f32[2,256,128]{2,1,0:T(8,128)}, u32[]{:S(2)}) copy-start(f32[2,256,128]{2,1,0:T(8,128)} %convolution_bitcast_fusion.1) | copy-start | bytes 786436
  111.5 5.8 %copy-start.4 = (f32[2,256,1056]{1,2,0:T(8,128)S(1)}, f32[2,256,1056]{1,2,0:T(8,128)}, u32[]{:S(2)}) copy-start(f32[2,256,1056]{1,2,0:T(8,128)} %copy-done.3) | copy-start | bytes 6488068
  111.5 5.8 %copy-start.7 = (f32[2,256,528]{1,2,0:T(8,128)S(1)}, f32[2,256,528]{1,2,0:T(8,128)}, u32[]{:S(2)}) copy-start(f32[2,256,528]{1,2,0:T(8,128)} %convolution_bitcast_fusion) | copy-start | bytes 3244036
  111.5 5.8 %copy-start.19 = (bf16[256,2,128]{2,0,1:T(8,128)(2,1)S(1)}, bf16[256,2,128]{2,0,1:T(8,128)(2,1)}, u32[]{:S(2)}) copy-start(bf16[256,2,128]{2,0,1:T(8,128)(2,1)} %copy.206) | copy-start | bytes 393220
  112.1 8.8 %collective-permute-start.4 = (bf16[256,1,2,128]{3,0,1,2:T(8,128)(2,1)S(1)}, bf16[256,1,2,128]{3,0,1,2:T(8,128)(2,1)S(1)}, u32[]{:S(2)}, u32[]{:S(2)}) collective-permute-start(bf16[256,1,2,128]{3,0,1,2:T(8,128)(2,1)S(1)} %get-tuple-element.53), channel_id=1, source_target_pairs={{0,2},{1,3},{2,0},{3,1},{4,6},{5,7},{6,4},{7,5},{8,10},{9,11},{10,... | collective-permute-start | bytes 393224 | tf_op jit(solution)/shard_map/ppermute | solution.py:115
  114.1 7.7 %collective-permute-start.5 = (bf16[256,1,2,128]{3,0,1,2:T(8,128)(2,1)S(1)}, bf16[256,1,2,128]{3,0,1,2:T(8,128)(2,1)S(1)}, u32[]{:S(2)}, u32[]{:S(2)}) collective-permute-start(bf16[256,1,2,128]{3,0,1,2:T(8,128)(2,1)S(1)} %get-tuple-element.52), channel_id=1, source_target_pairs={{0,1},{1,2},{2,3},{3,0},{4,5},{5,6},{6,7},{7,4},{8,9},{9,10},{10,1... | collective-permute-start | bytes 393224 | tf_op jit(solution)/shard_map/ppermute | solution.py:115
  114.4 7.4 %collective-permute-start.3 = (bf16[256,1,2,128]{3,0,1,2:T(8,128)(2,1)S(1)}, bf16[256,1,2,128]{3,0,1,2:T(8,128)(2,1)S(1)}, u32[]{:S(2)}, u32[]{:S(2)}) collective-permute-start(bf16[256,1,2,128]{3,0,1,2:T(8,128)(2,1)S(1)} %get-tuple-element.51), channel_id=1, source_target_pairs={{0,3},{1,0},{2,1},{3,2},{4,7},{5,4},{6,5},{7,6},{8,11},{9,8},{10,9... | collective-permute-start | bytes 393224 | tf_op jit(solution)/shard_map/ppermute | solution.py:115
  117.4 0.9 copy-start.27
  117.8 0.8 copy-start.24
  117.9 0.9 copy-start.28

commit v17 on v16

--- a/solution.py
+++ b/solution.py
@@ -97,8 +97,8 @@
     me = lax.axis_index("head")
     pieces = []
     for k in range(count):
-        target = (me + k) % count
-        piece = lax.dynamic_slice_in_dim(stacked, target * owned, owned, axis=3)
+        blocks = [stacked[:, :, :, b * owned : (b + 1) * owned] for b in range(count)]
+        piece = lax.select_n((me + k) % count, *blocks)
         if k:
             piece = lax.ppermute(piece, "head", [(j, (j + k) % count) for j in range(count)])
         pieces.append(piece)

time: 124 us -> 123 us (level)
    unnamed x70 -> x72, local copies, waits for them, and re-layouts: 6.27 us -> 6.28 us
  transfers between devices with their start and end apart: 10 -> 10, of which waited for: 5 -> 5; matrix products, arithmetic and copies ran while one was open for 35% -> 34% of each run, Pallas kernels for 0% -> 0%
where the time goes in v17:
time: 123 us; the launch traced here: 122 us
  matrix products  37.5 us (30%)
  starting transfers between devices  33.9 us (28%)
  waiting for transfers between devices  17.7 us (14%)
  other arithmetic  17.6 us (14%)
  local copies, waits for them, and re-layouts  14.1 us (11%)
  between operations  1.46 us (1%)
    all_to_all x2, starting transfers between devices, scan_send(): return lax.all_to_all(flat.reshape(n, per, width), 'ctx', 0, 0, tiled=True)  13.3 us
    dot_general x12, matrix products, dot_parts(): term = jnp.einsum(pattern, *args, preferred_element_type=f32)  12.1 us
    all_to_all x2, starting transfers between devices, scan_return(): lax.all_to_all(summed, 'ctx', 0, 0, tiled=True).reshape(n * per, width)  10.5 us
    all_to_all x2, waiting for transfers between devices, scan_return(): lax.all_to_all(summed, 'ctx', 0, 0, tiled=True).reshape(n * per, width)  9.85 us
    all_to_all x2, waiting for transfers between devices, scan_send(): return lax.all_to_all(flat.reshape(n, per, width), 'ctx', 0, 0, tiled=True)  6.94 us
    unnamed x72, local copies, waits for them, and re-layouts  6.28 us
    mul x1, other arithmetic, tri_feature_back(): cotangent * second  5.95 us
    ppermute x3, starting transfers between devices, head_exchange(): lax.ppermute(piece, 'head', [(j, (j + k) % count) for j in range(count)])  5.36 us
  transfers between devices with their start and end apart: 10, of which 5 were waited for; matrix products, arithmetic and copies ran while one was open for 34% of the time, Pallas kernels for 0%

profile of v17, /device:TPU:1, one launch (start us, length us, event | category | flops | bytes accessed | tf_op | source)
XLA Modules:
  0.0 122.3 jit_solution(2749668420366479627)
XLA Ops:
  0.7 1.4 %copy_bitcast_fusion = (bf16[1,256,1,8,128]{4,1,3,2,0:T(8,128)(2,1)S(1)}, bf16[1,256,1,8,128]{4,1,3,2,0:T(8,128)(2,1)S(1)}) fusion(bf16[256,1,8,128]{3,2,1,0:T(8,128)(2,1)} %param.12, bf16[256,1,8,128]{3,2,1,0:T(8,128)(2,1)} %param.9), kind=kLoop, calls=%fused_computation.119 | loop fusion | bytes 2097152 | tf_op jit(solution)/shard_map/stack | solution.py:168
  2.3 4.7 %collective-permute-start.2 = (bf16[2,256,1,2,128]{4,1,3,2,0:T(8,128)(2,1)S(1)}, bf16[2,256,1,2,128]{4,1,3,2,0:T(8,128)(2,1)S(1)}, u32[]{:S(2)}, u32[]{:S(2)}) collective-permute-start(bf16[2,256,1,2,128]{4,1,3,2,0:T(8,128)(2,1)S(1)} %get-tuple-element.46), channel_id=1, source_target_pairs={{0,3},{1,0},{2,1},{3,2},{4,7},{5,4},{6,5},{7,6},{8,11},{9,8},{10,9... | collective-permute-start | bytes 786440 | tf_op jit(solution)/shard_map/ppermute | solution.py:103
  7.0 0.7 collective-permute-start
  7.7 1.5 %constant_dynamic-slice_fusion = (bf16[256,2,128]{2,1,0:T(2,128)(2,1)S(1)}, bf16[256,2,128]{2,1,0:T(2,128)(2,1)S(1)}) fusion(bf16[256,8,128]{2,1,0:T(8,128)(2,1)} %param.11, s32[]{:T(128)S(6)} %select_n.307, bf16[256,8,128]{2,1,0:T(8,128)(2,1)} %param.10), kind=kLoop, calls=%fused_computation.232 | loop fusion | bytes 524292 | tf_op jit(solution)/shard_map/dynamic_slice | solution.py:167
  9.3 0.8 reduce-precision_convert_fusion.16
  10.1 0.5 fusion.111
  10.6 1.3 %copy-done.3 = f32[2,256,1056]{1,2,0:T(8,128)} copy-done((f32[2,256,1056]{1,2,0:T(8,128)}, f32[2,256,1056]{1,2,0:T(8,128)S(1)}, u32[]{:S(2)}) %copy-start.3) | copy-done | bytes 2162712
  12.3 0.3 fusion.156
  12.6 0.9 fusion.58
  13.4 8.6 %all-to-all-start = ((f32[32,40,128]{2,1,0:T(8,128)}), f32[32,40,128]{2,1,0:T(8,128)S(1)}, u32[]{:S(2)}, u32[]{:S(2)}) async-start(f32[32,40,128]{2,1,0:T(8,128)} %bitcast.26), calls=%async_computation | async-start | bytes 1310720 | tf_op jit(solution)/shard_map/all_to_all | solution.py:70
  22.2 0.7 copy.206
  23.0 0.3 fusion.35
  23.3 0.8 copy-done.5
  24.1 1.0 reduce-precision_convert_fusion.11
  25.1 4.7 %fusion.80 = f32[2,4,256,1056]{2,3,1,0:T(8,128)} fusion(bf16[96,1056,1,1]{1,0,3,2:T(8,128)(2,1)S(1)} %copy-done.27, bf16[2,4,256,32]{2,3,0,1:T(8,128)(2,1)S(1)} %get-tuple-element.64, bf16[2,4,256,32]{2,3,0,1:T(8,128)(2,1)S(1)} %get-tuple-element.63, bf16[2,4,256,32]{2,3,0,1:T(8,128)(2,1)S(1)} %get-tuple-element.62), kind=kOutput, calls=%fused_computation.129 | convolution fusion | flops 416415744 | bytes 9246720 | tf_op jit(solution)/shard_map/...k,kn->...n/dot_general | solution.py:49
  29.8 5.1 %all-to-all-done = f32[32,40,128]{2,1,0:T(8,128)S(1)} async-done(((f32[32,40,128]{2,1,0:T(8,128)}), f32[32,40,128]{2,1,0:T(8,128)S(1)}, u32[]{:S(2)}, u32[]{:S(2)}) %all-to-all-start) | async-done | bytes 655392 | tf_op jit(solution)/shard_map/all_to_all | solution.py:70
  35.0 0.5 fusion.61
  35.4 1.2 %copy.76 = f32[32,40,128]{2,1,0:T(8,128)} copy(f32[32,40,128]{2,0,1:T(8,128)S(1)} %fusion.61) | data formatting | bytes 1310720 | tf_op jit(solution)/shard_map/ij,jrc->irc/dot_general | solution.py:78
  36.7 4.8 %all-to-all-start.1 = ((f32[32,40,128]{2,1,0:T(8,128)}), f32[32,40,128]{2,1,0:T(8,128)}, u32[]{:S(2)}, u32[]{:S(2)}) async-start(f32[32,40,128]{2,1,0:T(8,128)} %copy.76), calls=%async_computation.1 | async-start | bytes 1310720 | tf_op jit(solution)/shard_map/all_to_all | solution.py:84
  41.4 4.2 %broadcast_multiply_fusion = (bf16[2,4,256,528]{2,3,1,0:T(8,128)(2,1)S(1)}, bf16[2,4,256,528]{2,3,1,0:T(8,128)(2,1)S(1)}) fusion(bf16[528]{0:T(1024)(128)(2,1)S(1)} %copy-done.31, f32[2,4,256,1056]{2,3,1,0:T(8,128)} %fusion.80), kind=kLoop, calls=%fused_computation.80 | loop fusion | flops 4325376 | bytes 12977184 | tf_op jit(solution)/shard_map/mul | solution.py:180
  45.7 2.1 %select_convert_fusion.1 = (bf16[2,4,256,256]{2,3,1,0:T(8,128)(2,1)}, f32[2,4,256,256]{2,3,1,0:T(8,128)S(1)}) fusion(pred[256,256]{0,1:T(8,128)(4,1)S(1)} %iota_compare_fusion.1, bf16[2,4,256,528]{2,3,1,0:T(8,128)(2,1)S(1)} %get-tuple-element.28, bf16[2,256,528]{1,2,0:T(8,128)(2,1)S(1)} %get-tuple-element.27), kind=kOutput, calls=%fused_computation.25 | convolution fusion | flops 554172416 | bytes 5914624 | tf_op jit(solution)/shard_map/hmif,hjf->hmij/dot_general | solution.py:188
  48.0 6.5 %all-to-all-done.1 = f32[32,40,128]{2,1,0:T(8,128)} async-done(((f32[32,40,128]{2,1,0:T(8,128)}), f32[32,40,128]{2,1,0:T(8,128)}, u32[]{:S(2)}, u32[]{:S(2)}) %all-to-all-start.1) | async-done | bytes 655392 | tf_op jit(solution)/shard_map/all_to_all | solution.py:84
  54.5 1.1 slice.130
  55.6 0.8 slice.128
  56.4 2.7 %fusion.16 = f32[2,4,256,128]{3,2,0,1:T(8,128)S(1)} fusion(bf16[2,4,256,528]{2,3,1,0:T(8,128)(2,1)} %copy-done, f32[2,528,128]{2,1,0:T(8,128)S(1)} %bitcast.184), kind=kOutput, calls=%fused_computation.27 | convolution fusion | flops 277229568 | bytes 3751936 | tf_op jit(solution)/shard_map/hmif,hfd->hmid/dot_general | solution.py:36
  59.2 2.1 %fusion.23 = f32[2,4,256,128]{3,2,0,1:T(8,128)} fusion(f32[2,4,256,128]{3,2,0,1:T(8,128)S(1)} %fusion.16, bf16[2,4,256,528]{2,3,1,0:T(8,128)(2,1)S(1)} %copy-done.1, f32[2,528,128]{2,1,0:T(8,128)S(1)} %bitcast.185), kind=kOutput, calls=%fused_computation.39 | convolution fusion | flops 277356544 | bytes 4800512 | tf_op jit(solution)/shard_map/hmif,hfd->hmid/dot_general | solution.py:36
  61.3 0.6 fusion.163
  61.9 2.1 %fusion.141 = f32[2,1,4,256]{3,1,2,0:T(1,128)S(1)} fusion(bf16[2,4,256,528]{2,3,1,0:T(8,128)(2,1)} %copy-done, bf16[2,528,1,1]{1,0,2,3:T(2,128)(2,1)S(1)} %get-tuple-element.83), kind=kOutput, calls=%fused_computation.224 | convolution fusion | flops 2162688 | bytes 2172992 | tf_op jit(solution)/shard_map/hmif,hf->hmi/dot_general | solution.py:36
  64.1 0.4 fusion.143
  64.5 1.6 %reduce-precision_convert_fusion.2 = (bf16[2,4,256,128]{3,2,0,1:T(8,128)(2,1)}, bf16[2,4,256,128]{3,2,0,1:T(8,128)(2,1)}, bf16[2,4,256,128]{3,2,0,1:T(8,128)(2,1)}) fusion(f32[2,4,256]{2,0,1:T(2,128)S(1)} %copy.77, bf16[2,256,4,2,128]{4,1,3,2,0:T(8,128)(2,1)S(1)} %copy-done.6), kind=kLoop, calls=%fused_computation.32 | loop fusion | flops 1835008 | bytes 2105344 | tf_op jit(solution)/shard_map/convert_element_type | solution.py:26
  66.1 1.1 fusion.33
  67.2 0.7 fusion.132
  67.9 0.7 fusion.134
  68.6 1.8 %fusion.78 = f32[2,528,128,1]{2,1,3,0:T(8,128)S(1)} fusion(bf16[2,4,256,528]{2,3,1,0:T(8,128)(2,1)S(1)} %get-tuple-element.29, bf16[2,4,256,128]{3,2,0,1:T(8,128)(2,1)} %get-tuple-element.43), kind=kOutput, calls=%fused_computation.126 | convolution fusion | flops 276824064 | bytes 3227648 | tf_op jit(solution)/shard_map/hmif,hmid->hfd/dot_general | solution.py:200
  70.4 0.9 select_maximum_fusion
  71.3 4.7 %all-to-all-start.2 = ((f32[32,40,128]{2,1,0:T(8,128)}), f32[32,40,128]{2,1,0:T(8,128)}, u32[]{:S(2)}, u32[]{:S(2)}) async-start(f32[32,40,128]{2,1,0:T(8,128)} %bitcast.187), calls=%async_computation.2 | async-start | bytes 1310720 | tf_op jit(solution)/shard_map/all_to_all | solution.py:70
  76.0 1.6 %select_convert_fusion = bf16[2,4,256,256]{2,3,1,0:T(8,128)(2,1)S(1)} fusion(f32[2,4,256]{2,1,0:T(4,128)S(1)} %copy.86, pred[256,256]{0,1:T(8,128)(4,1)} %copy-done.13, bf16[2,4,256,128]{3,2,0,1:T(8,128)(2,1)} %get-tuple-element.43, bf16[256,2,128]{2,1,0:T(2,128)(2,1)} %copy-done.11), kind=kOutput, calls=%fused_computation.24 | convolution fusion | flops 135790592 | bytes 1777664 | tf_op jit(solution)/shard_map/hmid,hjd->hmij/dot_general | solution.py:206
  77.6 1.0 fusion.64
  78.6 1.8 %convolution_bitcast_fusion = f32[2,256,528]{1,2,0:T(8,128)} fusion(bf16[2,4,256,256]{2,3,1,0:T(8,128)(2,1)S(1)} %select_convert_fusion, bf16[2,4,256,528]{2,3,1,0:T(8,128)(2,1)S(1)} %get-tuple-element.29), kind=kOutput, calls=%fused_computation.35 | convolution fusion | flops 553648128 | bytes 4292608 | tf_op jit(solution)/shard_map/hmij,hmif->hjf/dot_general | solution.py:221
  80.4 1.2 convolution_bitcast_fusion.1
  82.1 5.2 %multiply_add_fusion = f32[2,4,256,528]{2,3,1,0:T(8,128)} fusion(f32[2,528]{1,0:T(2,128)S(1)} %copy-done.33, f32[2,4,256]{2,1,0:T(4,128)S(1)} %copy.86, bf16[2,4,256,128]{2,3,1,0:T(8,128)(2,1)S(1)} %copy.89, bf16[2,4,256,128]{2,3,1,0:T(8,128)(2,1)S(1)} %copy.87, bf16[2,4,256,256]{2,3,1,0:T(8,128)(2,1)} %copy-done.18, ...), kind=kOutput, calls=%fused_computation.9 | convolution fusion | flops 1402175488 | bytes 7516288 | tf_op jit(solution)/shard_map/hmik,hkf->hmif/dot_general | solution.py:213
  87.3 1.8 %all-to-all-done.2 = f32[32,40,128]{2,1,0:T(8,128)} async-done(((f32[32,40,128]{2,1,0:T(8,128)}), f32[32,40,128]{2,1,0:T(8,128)}, u32[]{:S(2)}, u32[]{:S(2)}) %all-to-all-start.2) | async-done | bytes 655392 | tf_op jit(solution)/shard_map/all_to_all | solution.py:70
  89.1 1.6 %fusion.59 = f32[32,40,128]{2,0,1:T(8,128)S(1)} fusion(f32[32,40,128]{2,1,0:T(8,128)} %all-to-all-done.2), kind=kOutput, calls=%fused_computation.101 | convolution fusion | flops 62915584 | bytes 1310720 | tf_op jit(solution)/shard_map/ij,jrc->irc/dot_general | solution.py:78
  90.7 1.2 %copy.98 = f32[32,40,128]{2,1,0:T(8,128)} copy(f32[32,40,128]{2,0,1:T(8,128)S(1)} %fusion.59) | data formatting | bytes 1310720 | tf_op jit(solution)/shard_map/optimization_barrier | solution.py:224
  91.9 5.7 %all-to-all-start.3 = ((f32[32,40,128]{2,1,0:T(8,128)}), f32[32,40,128]{2,1,0:T(8,128)S(1)}, u32[]{:S(2)}, u32[]{:S(2)}) async-start(f32[32,40,128]{2,1,0:T(8,128)} %copy.98), calls=%async_computation.3 | async-start | bytes 1310720 | tf_op jit(solution)/shard_map/all_to_all | solution.py:84
  97.6 5.9 %slice_multiply_fusion = (f32[2,4,256,528]{2,3,1,0:T(8,128)S(1)}, f32[2,4,256,528]{2,3,1,0:T(8,128)S(1)}) fusion(f32[2,4,256,528]{2,3,1,0:T(8,128)} %multiply_add_fusion, f32[2,4,256,1056]{2,3,1,0:T(8,128)} %fusion.80, f32[528]{0:T(1024)S(1)} %copy-done.32), kind=kLoop, calls=%fused_computation.11 | loop fusion | flops 3244032 | bytes 21628992 | tf_op jit(solution)/shard_map/mul | solution.py:139
  103.6 1.4 %reduce-precision_convert_fusion = (bf16[2,4,256,1056]{2,3,1,0:T(8,128)(2,1)S(1)}, bf16[2,4,256,1056]{2,3,1,0:T(8,128)(2,1)S(1)}) fusion(f32[2,4,256,528]{2,3,1,0:T(8,128)S(1)} %get-tuple-element.36, f32[2,4,256,528]{2,3,1,0:T(8,128)S(1)} %get-tuple-element.35), kind=kLoop, calls=%fused_computation.1 | loop fusion | flops 10813440 | bytes 17301504 | tf_op jit(solution)/shard_map/convert_element_type | solution.py:26
  105.0 0.9 fusion.1
  105.9 0.9 reduce-precision_convert_fusion.9
  106.9 0.3 fusion.34
  107.2 3.3 %all-to-all-done.3 = f32[32,40,128]{2,1,0:T(8,128)S(1)} async-done(((f32[32,40,128]{2,1,0:T(8,128)}), f32[32,40,128]{2,1,0:T(8,128)S(1)}, u32[]{:S(2)}, u32[]{:S(2)}) %all-to-all-start.3) | async-done | bytes 655392 | tf_op jit(solution)/shard_map/all_to_all | solution.py:84
  110.7 0.5 fusion.74
  111.3 2.1 %collective-permute-start.4 = (bf16[256,1,2,128]{3,0,1,2:T(8,128)(2,1)S(1)}, bf16[256,1,2,128]{3,0,1,2:T(8,128)(2,1)S(1)}, u32[]{:S(2)}, u32[]{:S(2)}) collective-permute-start(bf16[256,1,2,128]{3,0,1,2:T(8,128)(2,1)S(1)} %get-tuple-element.57), channel_id=1, source_target_pairs={{0,2},{1,3},{2,0},{3,1},{4,6},{5,7},{6,4},{7,5},{8,10},{9,11},{10,... | collective-permute-start | bytes 393224 | tf_op jit(solution)/shard_map/ppermute | solution.py:115
  113.3 0.3 collective-permute-start.5
  113.6 2.4 %collective-permute-start.3 = (bf16[256,1,2,128]{3,0,1,2:T(8,128)(2,1)S(1)}, bf16[256,1,2,128]{3,0,1,2:T(8,128)(2,1)S(1)}, u32[]{:S(2)}, u32[]{:S(2)}) collective-permute-start(bf16[256,1,2,128]{3,0,1,2:T(8,128)(2,1)S(1)} %get-tuple-element.55), channel_id=1, source_target_pairs={{0,3},{1,0},{2,1},{3,2},{4,7},{5,4},{6,5},{7,6},{8,11},{9,8},{10,9... | collective-permute-start | bytes 393224 | tf_op jit(solution)/shard_map/ppermute | solution.py:115
  116.0 0.5 fusion.47
  116.6 0.5 slice_multiply_fusion.1
  117.1 0.4 copy-done.28
  117.5 0.3 fusion.51
  117.9 0.4 reduce-precision_convert_fusion.14
  118.5 0.8 copy.102
  119.3 0.8 copy.103
  120.1 0.9 collective-permute-done.5
  121.1 1.1 copy.101
  (100 shorter events, 2.4 us)
Async XLA Ops:
  2.1 5.6 %copy-start.30 = (s32[2,128,32]{1,2,0:T(8,128)S(1)}, s32[2,128,32]{1,2,0:T(8,128)}, u32[]{:S(2)}) copy-start(s32[2,128,32]{1,2,0:T(8,128)} %param.13) | copy-start | bytes 98308
  2.1 8.0 %copy-start.26 = (bf16[96,1056,1]{1,0,2:T(8,128)(2,1)S(1)}, bf16[96,1056,1]{1,0,2:T(8,128)(2,1)}, u32[]{:S(2)}) copy-start(bf16[96,1056,1]{1,0,2:T(8,128)(2,1)} %constant.101) | copy-start | bytes 608260
  2.3 20.5 %collective-permute-start.2 = (bf16[2,256,1,2,128]{4,1,3,2,0:T(8,128)(2,1)S(1)}, bf16[2,256,1,2,128]{4,1,3,2,0:T(8,128)(2,1)S(1)}, u32[]{:S(2)}, u32[]{:S(2)}) collective-permute-start(bf16[2,256,1,2,128]{4,1,3,2,0:T(8,128)(2,1)S(1)} %get-tuple-element.46), channel_id=1, source_target_pairs={{0,3},{1,0},{2,1},{3,2},{4,7},{5,4},{6,5},{7,6},{8,11},{9,8},{10,9... | collective-permute-start | bytes 786440 | tf_op jit(solution)/shard_map/ppermute | solution.py:103
  7.0 15.9 %collective-permute-start.1 = (bf16[2,256,1,2,128]{4,1,3,2,0:T(8,128)(2,1)S(1)}, bf16[2,256,1,2,128]{4,1,3,2,0:T(8,128)(2,1)S(1)}, u32[]{:S(2)}, u32[]{:S(2)}) collective-permute-start(bf16[2,256,1,2,128]{4,1,3,2,0:T(8,128)(2,1)S(1)} %get-tuple-element.45), channel_id=1, source_target_pairs={{0,2},{1,3},{2,0},{3,1},{4,6},{5,7},{6,4},{7,5},{8,10},{9,11},{10,... | collective-permute-start | bytes 786440 | tf_op jit(solution)/shard_map/ppermute | solution.py:103
  7.0 15.9 %collective-permute-start = (bf16[2,256,1,2,128]{4,1,3,2,0:T(8,128)(2,1)S(1)}, bf16[2,256,1,2,128]{4,1,3,2,0:T(8,128)(2,1)S(1)}, u32[]{:S(2)}, u32[]{:S(2)}) collective-permute-start(bf16[2,256,1,2,128]{4,1,3,2,0:T(8,128)(2,1)S(1)} %get-tuple-element.44), channel_id=1, source_target_pairs={{0,1},{1,2},{2,3},{3,0},{4,5},{5,6},{6,7},{7,4},{8,9},{9,10},{10,1... | collective-permute-start | bytes 786440 | tf_op jit(solution)/shard_map/ppermute | solution.py:103
  9.2 13.0 %copy-start.11 = (bf16[256,2,128]{2,1,0:T(2,128)(2,1)}, bf16[256,2,128]{2,1,0:T(2,128)(2,1)S(1)}, u32[]{:S(2)}) copy-start(bf16[256,2,128]{2,1,0:T(2,128)(2,1)S(1)} %get-tuple-element.90) | copy-start | bytes 393220
  9.3 0.8 copy-start.23
  10.6 1.3 %copy-start.3 = (f32[2,256,1056]{1,2,0:T(8,128)}, f32[2,256,1056]{1,2,0:T(8,128)S(1)}, u32[]{:S(2)}) copy-start(f32[2,256,1056]{1,2,0:T(8,128)S(1)} %fusion.111) | copy-start | bytes 6488068
  13.4 21.5 %all-to-all-start = ((f32[32,40,128]{2,1,0:T(8,128)}), f32[32,40,128]{2,1,0:T(8,128)S(1)}, u32[]{:S(2)}, u32[]{:S(2)}) async-start(f32[32,40,128]{2,1,0:T(8,128)} %bitcast.26), calls=%async_computation | async-start | bytes 1310720 | tf_op jit(solution)/shard_map/all_to_all | solution.py:70
  22.1 25.7 %copy-start.13 = (pred[256,256]{0,1:T(8,128)(4,1)}, pred[256,256]{0,1:T(8,128)(4,1)S(1)}, u32[]{:S(2)}) copy-start(pred[256,256]{0,1:T(8,128)(4,1)S(1)} %iota_compare_fusion.1) | copy-start | bytes 196612
  22.9 2.2 %copy-start.27 = (bf16[96,1056,1,1]{1,0,3,2:T(8,128)(2,1)S(1)}, bf16[96,1056,1,1]{1,0,3,2:T(8,128)(2,1)}, u32[]{:S(2)}) copy-start(bf16[96,1056,1,1]{1,0,3,2:T(8,128)(2,1)} %constant.100) | copy-start | bytes 608260
  23.0 1.0 copy-start.5
  29.8 11.6 %copy-start.31 = (bf16[528]{0:T(1024)(128)(2,1)S(1)}, bf16[528]{0:T(1024)(128)(2,1)}, u32[]{:S(2)}) copy-start(bf16[528]{0:T(1024)(128)(2,1)} %constant.83.clone) | copy-start | bytes 3172
  36.7 17.8 %all-to-all-start.1 = ((f32[32,40,128]{2,1,0:T(8,128)}), f32[32,40,128]{2,1,0:T(8,128)}, u32[]{:S(2)}, u32[]{:S(2)}) async-start(f32[32,40,128]{2,1,0:T(8,128)} %copy.76), calls=%async_computation.1 | async-start | bytes 1310720 | tf_op jit(solution)/shard_map/all_to_all | solution.py:84
  45.7 2.1 %copy-start = (bf16[2,4,256,528]{2,3,1,0:T(8,128)(2,1)}, bf16[2,4,256,528]{2,3,1,0:T(8,128)(2,1)S(1)}, u32[]{:S(2)}) copy-start(bf16[2,4,256,528]{2,3,1,0:T(8,128)(2,1)S(1)} %get-tuple-element.28) | copy-start | bytes 6488068
  55.6 3.6 %copy-start.1 = (bf16[2,4,256,528]{2,3,1,0:T(8,128)(2,1)S(1)}, bf16[2,4,256,528]{2,3,1,0:T(8,128)(2,1)}, u32[]{:S(2)}) copy-start(bf16[2,4,256,528]{2,3,1,0:T(8,128)(2,1)} %copy-done) | copy-start | bytes 6488068
  61.3 2.7 %copy-start.2 = (bf16[2,4,256,528]{2,3,1,0:T(8,128)(2,1)S(1)}, bf16[2,4,256,528]{2,3,1,0:T(8,128)(2,1)}, u32[]{:S(2)}) copy-start(bf16[2,4,256,528]{2,3,1,0:T(8,128)(2,1)} %copy-done) | copy-start | bytes 6488068
  61.9 2.6 %copy-start.6 = (bf16[2,256,4,2,128]{4,1,3,2,0:T(8,128)(2,1)S(1)}, bf16[2,256,4,2,128]{4,1,3,2,0:T(8,128)(2,1)}, u32[]{:S(2)}) copy-start(bf16[2,256,4,2,128]{4,1,3,2,0:T(8,128)(2,1)} %copy-done.5) | copy-start | bytes 3145732
  64.0 2.1 %copy-start.12 = (bf16[256,2,128]{2,1,0:T(2,128)(2,1)S(1)}, bf16[256,2,128]{2,1,0:T(2,128)(2,1)}, u32[]{:S(2)}) copy-start(bf16[256,2,128]{2,1,0:T(2,128)(2,1)} %copy-done.11) | copy-start | bytes 393220
  64.1 2.1 %copy-start.15 = (bf16[2,4,256,256]{2,3,1,0:T(8,128)(2,1)S(1)}, bf16[2,4,256,256]{2,3,1,0:T(8,128)(2,1)}, u32[]{:S(2)}) copy-start(bf16[2,4,256,256]{2,3,1,0:T(8,128)(2,1)} %get-tuple-element.86) | copy-start | bytes 3145732
  64.1 2.1 %copy-start.17 = (f32[2,4,256,128]{3,2,0,1:T(8,128)S(1)}, f32[2,4,256,128]{3,2,0,1:T(8,128)}, u32[]{:S(2)}) copy-start(f32[2,4,256,128]{3,2,0,1:T(8,128)} %fusion.23) | copy-start | bytes 3145732
  71.3 17.8 %all-to-all-start.2 = ((f32[32,40,128]{2,1,0:T(8,128)}), f32[32,40,128]{2,1,0:T(8,128)}, u32[]{:S(2)}, u32[]{:S(2)}) async-start(f32[32,40,128]{2,1,0:T(8,128)} %bitcast.187), calls=%async_computation.2 | async-start | bytes 1310720 | tf_op jit(solution)/shard_map/all_to_all | solution.py:70
  77.6 2.8 %copy-start.18 = (bf16[2,4,256,256]{2,3,1,0:T(8,128)(2,1)}, bf16[2,4,256,256]{2,3,1,0:T(8,128)(2,1)S(1)}, u32[]{:S(2)}) copy-start(bf16[2,4,256,256]{2,3,1,0:T(8,128)(2,1)S(1)} %select_convert_fusion) | copy-start | bytes 3145732
  78.6 1.8 %copy-start.8 = (bf16[2,4,256,128]{3,2,0,1:T(8,128)(2,1)S(1)}, bf16[2,4,256,128]{3,2,0,1:T(8,128)(2,1)}, u32[]{:S(2)}) copy-start(bf16[2,4,256,128]{3,2,0,1:T(8,128)(2,1)} %get-tuple-element.43) | copy-start | bytes 1572868
  78.6 1.8 %copy-start.16 = (bf16[2,4,256,256]{2,3,1,0:T(8,128)(2,1)S(1)}, bf16[2,4,256,256]{2,3,1,0:T(8,128)(2,1)}, u32[]{:S(2)}) copy-start(bf16[2,4,256,256]{2,3,1,0:T(8,128)(2,1)} %get-tuple-element.86) | copy-start | bytes 3145732
  80.4 1.2 copy-start.10
  80.4 1.4 %copy-start.9 = (bf16[2,4,256,128]{3,2,0,1:T(8,128)(2,1)S(1)}, bf16[2,4,256,128]{3,2,0,1:T(8,128)(2,1)}, u32[]{:S(2)}) copy-start(bf16[2,4,256,128]{3,2,0,1:T(8,128)(2,1)} %get-tuple-element.41) | copy-start | bytes 1572868
  80.4 1.6 %copy-start.21 = (bf16[2,128,528]{1,2,0:T(8,128)(2,1)S(1)}, bf16[2,128,528]{1,2,0:T(8,128)(2,1)}, u32[]{:S(2)}) copy-start(bf16[2,128,528]{1,2,0:T(8,128)(2,1)} %get-tuple-element.53) | copy-start | bytes 811012
  80.4 1.6 %copy-start.22 = (bf16[2,128,528]{1,2,0:T(8,128)(2,1)S(1)}, bf16[2,128,528]{1,2,0:T(8,128)(2,1)}, u32[]{:S(2)}) copy-start(bf16[2,128,528]{1,2,0:T(8,128)(2,1)} %get-tuple-element.54) | copy-start | bytes 811012
  80.4 1.6 %copy-start.33 = (f32[2,528]{1,0:T(2,128)S(1)}, f32[2,528]{1,0:T(2,128)}, u32[]{:S(2)}) copy-start(f32[2,528]{1,0:T(2,128)} %get-tuple-element.81) | copy-start | bytes 12676
  87.3 10.3 %copy-start.32 = (f32[528]{0:T(1024)S(1)}, f32[528]{0:T(1024)}, u32[]{:S(2)}) copy-start(f32[528]{0:T(1024)} %constant.84.clone) | copy-start | bytes 6340
  91.9 18.6 %all-to-all-start.3 = ((f32[32,40,128]{2,1,0:T(8,128)}), f32[32,40,128]{2,1,0:T(8,128)S(1)}, u32[]{:S(2)}, u32[]{:S(2)}) async-start(f32[32,40,128]{2,1,0:T(8,128)} %copy.98), calls=%async_computation.3 | async-start | bytes 1310720 | tf_op jit(solution)/shard_map/all_to_all | solution.py:84
  103.6 1.4 %copy-start.20 = (bf16[1056,32,1,1]{0,1,2,3:T(8,128)(2,1)S(1)}, bf16[1056,32,1,1]{0,1,2,3:T(8,128)(2,1)}, u32[]{:S(2)}) copy-start(bf16[1056,32,1,1]{0,1,2,3:T(8,128)(2,1)} %constant.102) | copy-start | bytes 202756
  105.0 1.0 copy-start.14
  110.5 5.5 %copy-start.25 = (f32[2,256,128]{2,1,0:T(8,128)S(1)}, f32[2,256,128]{2,1,0:T(8,128)}, u32[]{:S(2)}) copy-start(f32[2,256,128]{2,1,0:T(8,128)} %convolution_bitcast_fusion.1) | copy-start | bytes 786436
  110.7 5.9 %copy-start.4 = (f32[2,256,1056]{1,2,0:T(8,128)S(1)}, f32[2,256,1056]{1,2,0:T(8,128)}, u32[]{:S(2)}) copy-start(f32[2,256,1056]{1,2,0:T(8,128)} %copy-done.3) | copy-start | bytes 6488068
  110.7 5.9 %copy-start.7 = (f32[2,256,528]{1,2,0:T(8,128)S(1)}, f32[2,256,528]{1,2,0:T(8,128)}, u32[]{:S(2)}) copy-start(f32[2,256,528]{1,2,0:T(8,128)} %convolution_bitcast_fusion) | copy-start | bytes 3244036
  110.7 5.9 %copy-start.19 = (bf16[256,2,128]{2,0,1:T(8,128)(2,1)S(1)}, bf16[256,2,128]{2,0,1:T(8,128)(2,1)}, u32[]{:S(2)}) copy-start(bf16[256,2,128]{2,0,1:T(8,128)(2,1)} %copy.206) | copy-start | bytes 393220
  111.3 8.8 %collective-permute-start.4 = (bf16[256,1,2,128]{3,0,1,2:T(8,128)(2,1)S(1)}, bf16[256,1,2,128]{3,0,1,2:T(8,128)(2,1)S(1)}, u32[]{:S(2)}, u32[]{:S(2)}) collective-permute-start(bf16[256,1,2,128]{3,0,1,2:T(8,128)(2,1)S(1)} %get-tuple-element.57), channel_id=1, source_target_pairs={{0,2},{1,3},{2,0},{3,1},{4,6},{5,7},{6,4},{7,5},{8,10},{9,11},{10,... | collective-permute-start | bytes 393224 | tf_op jit(solution)/shard_map/ppermute | solution.py:115
  113.3 7.7 %collective-permute-start.5 = (bf16[256,1,2,128]{3,0,1,2:T(8,128)(2,1)S(1)}, bf16[256,1,2,128]{3,0,1,2:T(8,128)(2,1)S(1)}, u32[]{:S(2)}, u32[]{:S(2)}) collective-permute-start(bf16[256,1,2,128]{3,0,1,2:T(8,128)(2,1)S(1)} %get-tuple-element.56), channel_id=1, source_target_pairs={{0,1},{1,2},{2,3},{3,0},{4,5},{5,6},{6,7},{7,4},{8,9},{9,10},{10,1... | collective-permute-start | bytes 393224 | tf_op jit(solution)/shard_map/ppermute | solution.py:115
  113.6 7.4 %collective-permute-start.3 = (bf16[256,1,2,128]{3,0,1,2:T(8,128)(2,1)S(1)}, bf16[256,1,2,128]{3,0,1,2:T(8,128)(2,1)S(1)}, u32[]{:S(2)}, u32[]{:S(2)}) collective-permute-start(bf16[256,1,2,128]{3,0,1,2:T(8,128)(2,1)S(1)} %get-tuple-element.55), channel_id=1, source_target_pairs={{0,3},{1,0},{2,1},{3,2},{4,7},{5,4},{6,5},{7,6},{8,11},{9,8},{10,9... | collective-permute-start | bytes 393224 | tf_op jit(solution)/shard_map/ppermute | solution.py:115
  116.6 0.9 copy-start.28
  117.1 0.8 copy-start.24
  117.1 0.9 copy-start.29

commit v18 on v17

--- a/solution.py
+++ b/solution.py
@@ -74,8 +74,13 @@
     n = got.shape[0]
     src = lax.broadcasted_iota(jnp.int32, (n, n), 1)
     dst = lax.broadcasted_iota(jnp.int32, (n, n), 0)
-    mask = (src > dst if reverse else src < dst).astype(f32)
-    return jnp.einsum("ij,jrc->irc", mask, got, precision=highest)
+    mask = (src > dst if reverse else src < dst).astype(bf16)
+    return jnp.einsum(
+        "ij,jrc->irc",
+        jnp.concatenate([mask, mask, mask], axis=1),
+        jnp.concatenate(split_parts(got, 3), axis=0),
+        preferred_element_type=f32,
+    )
 
 
 def scan_return(summed, heads, feat):

time: 123 us -> 123 us (level)
  other arithmetic: 17.6 us -> 19.1 us
  matrix products: 37.5 us -> 36.2 us
    convert_element_type x3 -> x5, other arithmetic: 3.08 us -> 4.6 us  [split_parts(): parts.append(hi.astype(bf16))]
    dot_general x2, matrix products: 2.03 us -> 0.64 us  [scan_sum(): jnp.einsum('ij,jrc->irc', jnp.concatenate([mask, mask, mask], axis=1), jn...]
where the time goes in v18:
time: 123 us; the launch traced here: 122 us
  matrix products  36.2 us (29%)
  starting transfers between devices  33.9 us (28%)
  other arithmetic  19.1 us (16%)
  waiting for transfers between devices  17.7 us (14%)
  local copies, waits for them, and re-layouts  14.1 us (11%)
  between operations  1.48 us (1%)
    all_to_all x2, starting transfers between devices, scan_send(): return lax.all_to_all(flat.reshape(n, per, width), 'ctx', 0, 0, tiled=True)  13.3 us
    dot_general x12, matrix products, dot_parts(): term = jnp.einsum(pattern, *args, preferred_element_type=f32)  12.2 us
    all_to_all x2, starting transfers between devices, scan_return(): lax.all_to_all(summed, 'ctx', 0, 0, tiled=True).reshape(n * per, width)  10.5 us
    all_to_all x2, waiting for transfers between devices, scan_return(): lax.all_to_all(summed, 'ctx', 0, 0, tiled=True).reshape(n * per, width)  9.84 us
    all_to_all x2, waiting for transfers between devices, scan_send(): return lax.all_to_all(flat.reshape(n, per, width), 'ctx', 0, 0, tiled=True)  6.92 us
    unnamed x72, local copies, waits for them, and re-layouts  6.28 us
    mul x1, other arithmetic, tri_feature_back(): cotangent * second  5.95 us
    ppermute x3, starting transfers between devices, head_exchange(): lax.ppermute(piece, 'head', [(j, (j + k) % count) for j in range(count)])  5.36 us
  transfers between devices with their start and end apart: 10, of which 5 were waited for; matrix products, arithmetic and copies ran while one was open for 34% of the time, Pallas kernels for 0%

profile of v18, /device:TPU:1, one launch (start us, length us, event | category | flops | bytes accessed | tf_op | source)
XLA Modules:
  0.0 122.5 jit_solution(12324077884427146424)
XLA Ops:
  0.7 1.4 %copy_bitcast_fusion = (bf16[1,256,1,8,128]{4,1,3,2,0:T(8,128)(2,1)S(1)}, bf16[1,256,1,8,128]{4,1,3,2,0:T(8,128)(2,1)S(1)}) fusion(bf16[256,1,8,128]{3,2,1,0:T(8,128)(2,1)} %param.12, bf16[256,1,8,128]{3,2,1,0:T(8,128)(2,1)} %param.9), kind=kLoop, calls=%fused_computation.137 | loop fusion | bytes 2097152 | tf_op jit(solution)/shard_map/stack | solution.py:173
  2.3 4.7 %collective-permute-start.2 = (bf16[2,256,1,2,128]{4,1,3,2,0:T(8,128)(2,1)S(1)}, bf16[2,256,1,2,128]{4,1,3,2,0:T(8,128)(2,1)S(1)}, u32[]{:S(2)}, u32[]{:S(2)}) collective-permute-start(bf16[2,256,1,2,128]{4,1,3,2,0:T(8,128)(2,1)S(1)} %get-tuple-element.46), channel_id=1, source_target_pairs={{0,3},{1,0},{2,1},{3,2},{4,7},{5,4},{6,5},{7,6},{8,11},{9,8},{10,9... | collective-permute-start | bytes 786440 | tf_op jit(solution)/shard_map/ppermute | solution.py:108
  7.0 0.7 collective-permute-start
  7.7 1.5 %constant_dynamic-slice_fusion = (bf16[256,2,128]{2,1,0:T(2,128)(2,1)S(1)}, bf16[256,2,128]{2,1,0:T(2,128)(2,1)S(1)}) fusion(bf16[256,8,128]{2,1,0:T(8,128)(2,1)} %param.11, s32[]{:T(128)S(6)} %select_n.307, bf16[256,8,128]{2,1,0:T(8,128)(2,1)} %param.10), kind=kLoop, calls=%fused_computation.258 | loop fusion | bytes 524292 | tf_op jit(solution)/shard_map/dynamic_slice | solution.py:172
  9.3 0.8 reduce-precision_convert_fusion.20
  10.1 0.5 fusion.121
  10.6 1.3 %copy-done.3 = f32[2,256,1056]{1,2,0:T(8,128)} copy-done((f32[2,256,1056]{1,2,0:T(8,128)}, f32[2,256,1056]{1,2,0:T(8,128)S(1)}, u32[]{:S(2)}) %copy-start.3) | copy-done | bytes 2162712
  12.3 0.3 fusion.174
  12.6 0.9 fusion.72
  13.5 8.6 %all-to-all-start = ((f32[32,40,128]{2,1,0:T(8,128)}), f32[32,40,128]{2,1,0:T(8,128)S(1)}, u32[]{:S(2)}, u32[]{:S(2)}) async-start(f32[32,40,128]{2,1,0:T(8,128)} %bitcast.26), calls=%async_computation | async-start | bytes 1310720 | tf_op jit(solution)/shard_map/all_to_all | solution.py:70
  22.2 0.7 copy.216
  23.4 0.7 copy-done.5
  24.1 1.0 reduce-precision_convert_fusion.15
  25.1 4.8 %fusion.90 = f32[2,4,256,1056]{2,3,1,0:T(8,128)} fusion(bf16[96,1056,1,1]{1,0,3,2:T(8,128)(2,1)S(1)} %copy-done.27, bf16[2,4,256,32]{2,3,0,1:T(8,128)(2,1)S(1)} %get-tuple-element.70, bf16[2,4,256,32]{2,3,0,1:T(8,128)(2,1)S(1)} %get-tuple-element.69, bf16[2,4,256,32]{2,3,0,1:T(8,128)(2,1)S(1)} %get-tuple-element.68), kind=kOutput, calls=%fused_computation.147 | convolution fusion | flops 416415744 | bytes 9246720 | tf_op jit(solution)/shard_map/...k,kn->...n/dot_general | solution.py:49
  29.9 5.1 %all-to-all-done = f32[32,40,128]{2,1,0:T(8,128)S(1)} async-done(((f32[32,40,128]{2,1,0:T(8,128)}), f32[32,40,128]{2,1,0:T(8,128)S(1)}, u32[]{:S(2)}, u32[]{:S(2)}) %all-to-all-start) | async-done | bytes 655392 | tf_op jit(solution)/shard_map/all_to_all | solution.py:70
  35.2 0.3 fusion.56
  35.5 1.2 %copy.77 = f32[32,40,128]{2,1,0:T(8,128)} copy(f32[32,40,128]{2,0,1:T(8,128)S(1)} %fusion.56) | data formatting | bytes 1310720 | tf_op jit(solution)/shard_map/ij,jrc->irc/dot_general | solution.py:78
  36.8 4.8 %all-to-all-start.1 = ((f32[32,40,128]{2,1,0:T(8,128)}), f32[32,40,128]{2,1,0:T(8,128)}, u32[]{:S(2)}, u32[]{:S(2)}) async-start(f32[32,40,128]{2,1,0:T(8,128)} %copy.77), calls=%async_computation.1 | async-start | bytes 1310720 | tf_op jit(solution)/shard_map/all_to_all | solution.py:89
  41.5 4.2 %broadcast_multiply_fusion = (bf16[2,4,256,528]{2,3,1,0:T(8,128)(2,1)S(1)}, bf16[2,4,256,528]{2,3,1,0:T(8,128)(2,1)S(1)}) fusion(bf16[528]{0:T(1024)(128)(2,1)S(1)} %copy-done.31, f32[2,4,256,1056]{2,3,1,0:T(8,128)} %fusion.90), kind=kLoop, calls=%fused_computation.80 | loop fusion | flops 4325376 | bytes 12977184 | tf_op jit(solution)/shard_map/mul | solution.py:185
  45.8 2.1 %select_convert_fusion.1 = (bf16[2,4,256,256]{2,3,1,0:T(8,128)(2,1)}, f32[2,4,256,256]{2,3,1,0:T(8,128)S(1)}) fusion(pred[256,256]{0,1:T(8,128)(4,1)S(1)} %iota_compare_fusion.1, bf16[2,4,256,528]{2,3,1,0:T(8,128)(2,1)S(1)} %get-tuple-element.28, bf16[2,256,528]{1,2,0:T(8,128)(2,1)S(1)} %get-tuple-element.27), kind=kOutput, calls=%fused_computation.25 | convolution fusion | flops 554172416 | bytes 5914624 | tf_op jit(solution)/shard_map/hmif,hjf->hmij/dot_general | solution.py:193
  48.1 6.5 %all-to-all-done.1 = f32[32,40,128]{2,1,0:T(8,128)} async-done(((f32[32,40,128]{2,1,0:T(8,128)}), f32[32,40,128]{2,1,0:T(8,128)}, u32[]{:S(2)}, u32[]{:S(2)}) %all-to-all-start.1) | async-done | bytes 655392 | tf_op jit(solution)/shard_map/all_to_all | solution.py:89
  54.6 1.1 slice.130
  55.7 0.8 slice.128
  56.5 2.7 %fusion.16 = f32[2,4,256,128]{3,2,0,1:T(8,128)S(1)} fusion(bf16[2,4,256,528]{2,3,1,0:T(8,128)(2,1)} %copy-done, f32[2,528,128]{2,1,0:T(8,128)S(1)} %bitcast.184), kind=kOutput, calls=%fused_computation.27 | convolution fusion | flops 277229568 | bytes 3751936 | tf_op jit(solution)/shard_map/hmif,hfd->hmid/dot_general | solution.py:36
  59.3 2.1 %fusion.23 = f32[2,4,256,128]{3,2,0,1:T(8,128)} fusion(f32[2,4,256,128]{3,2,0,1:T(8,128)S(1)} %fusion.16, bf16[2,4,256,528]{2,3,1,0:T(8,128)(2,1)S(1)} %copy-done.1, f32[2,528,128]{2,1,0:T(8,128)S(1)} %bitcast.185), kind=kOutput, calls=%fused_computation.39 | convolution fusion | flops 277356544 | bytes 4800512 | tf_op jit(solution)/shard_map/hmif,hfd->hmid/dot_general | solution.py:36
  61.4 0.6 fusion.181
  62.0 2.1 %fusion.155 = f32[2,1,4,256]{3,1,2,0:T(1,128)S(1)} fusion(bf16[2,4,256,528]{2,3,1,0:T(8,128)(2,1)} %copy-done, bf16[2,528,1,1]{1,0,2,3:T(2,128)(2,1)S(1)} %get-tuple-element.89), kind=kOutput, calls=%fused_computation.250 | convolution fusion | flops 2162688 | bytes 2172992 | tf_op jit(solution)/shard_map/hmif,hf->hmi/dot_general | solution.py:36
  64.2 0.4 fusion.157
  64.6 1.6 %reduce-precision_convert_fusion.2 = (bf16[2,4,256,128]{3,2,0,1:T(8,128)(2,1)}, bf16[2,4,256,128]{3,2,0,1:T(8,128)(2,1)}, bf16[2,4,256,128]{3,2,0,1:T(8,128)(2,1)}) fusion(f32[2,4,256]{2,0,1:T(2,128)S(1)} %copy.78, bf16[2,256,4,2,128]{4,1,3,2,0:T(8,128)(2,1)S(1)} %copy-done.6), kind=kLoop, calls=%fused_computation.32 | loop fusion | flops 1835008 | bytes 2105344 | tf_op jit(solution)/shard_map/convert_element_type | solution.py:26
  66.2 1.1 fusion.33
  67.3 0.7 fusion.146
  68.0 0.7 fusion.148
  68.7 1.8 %fusion.88 = f32[2,528,128,1]{2,1,3,0:T(8,128)S(1)} fusion(bf16[2,4,256,528]{2,3,1,0:T(8,128)(2,1)S(1)} %get-tuple-element.29, bf16[2,4,256,128]{3,2,0,1:T(8,128)(2,1)} %get-tuple-element.43), kind=kOutput, calls=%fused_computation.144 | convolution fusion | flops 276824064 | bytes 3227648 | tf_op jit(solution)/shard_map/hmif,hmid->hfd/dot_general | solution.py:205
  70.5 0.9 select_maximum_fusion
  71.4 4.7 %all-to-all-start.2 = ((f32[32,40,128]{2,1,0:T(8,128)}), f32[32,40,128]{2,1,0:T(8,128)}, u32[]{:S(2)}, u32[]{:S(2)}) async-start(f32[32,40,128]{2,1,0:T(8,128)} %bitcast.187), calls=%async_computation.2 | async-start | bytes 1310720 | tf_op jit(solution)/shard_map/all_to_all | solution.py:70
  76.2 1.6 %select_convert_fusion = bf16[2,4,256,256]{2,3,1,0:T(8,128)(2,1)S(1)} fusion(f32[2,4,256]{2,1,0:T(4,128)S(1)} %copy.88, pred[256,256]{0,1:T(8,128)(4,1)} %copy-done.13, bf16[2,4,256,128]{3,2,0,1:T(8,128)(2,1)} %get-tuple-element.43, bf16[256,2,128]{2,1,0:T(2,128)(2,1)} %copy-done.11), kind=kOutput, calls=%fused_computation.24 | convolution fusion | flops 135790592 | bytes 1777664 | tf_op jit(solution)/shard_map/hmid,hjd->hmij/dot_general | solution.py:211
  77.7 1.0 fusion.74
  78.7 1.8 %convolution_bitcast_fusion = f32[2,256,528]{1,2,0:T(8,128)} fusion(bf16[2,4,256,256]{2,3,1,0:T(8,128)(2,1)S(1)} %select_convert_fusion, bf16[2,4,256,528]{2,3,1,0:T(8,128)(2,1)S(1)} %get-tuple-element.29), kind=kOutput, calls=%fused_computation.35 | convolution fusion | flops 553648128 | bytes 4292608 | tf_op jit(solution)/shard_map/hmij,hmif->hjf/dot_general | solution.py:226
  80.6 1.1 convolution_bitcast_fusion.1
  82.2 5.2 %multiply_add_fusion = f32[2,4,256,528]{2,3,1,0:T(8,128)} fusion(f32[2,528]{1,0:T(2,128)S(1)} %copy-done.33, f32[2,4,256]{2,1,0:T(4,128)S(1)} %copy.88, bf16[2,4,256,128]{2,3,1,0:T(8,128)(2,1)S(1)} %copy.91, bf16[2,4,256,128]{2,3,1,0:T(8,128)(2,1)S(1)} %copy.89, bf16[2,4,256,256]{2,3,1,0:T(8,128)(2,1)} %copy-done.18, ...), kind=kOutput, calls=%fused_computation.9 | convolution fusion | flops 1402175488 | bytes 7516288 | tf_op jit(solution)/shard_map/hmik,hkf->hmif/dot_general | solution.py:218
  87.4 1.8 %all-to-all-done.2 = f32[32,40,128]{2,1,0:T(8,128)} async-done(((f32[32,40,128]{2,1,0:T(8,128)}), f32[32,40,128]{2,1,0:T(8,128)}, u32[]{:S(2)}, u32[]{:S(2)}) %all-to-all-start.2) | async-done | bytes 655392 | tf_op jit(solution)/shard_map/all_to_all | solution.py:70
  89.2 1.3 %reduce-precision_convert_fusion.5 = (bf16[32,40,128]{2,0,1:T(8,128)(2,1)S(1)}, bf16[32,40,128]{2,0,1:T(8,128)(2,1)S(1)}, bf16[32,40,128]{2,0,1:T(8,128)(2,1)S(1)}) fusion(f32[32,40,128]{2,1,0:T(8,128)} %all-to-all-done.2), kind=kLoop, calls=%fused_computation.103 | loop fusion | flops 1146880 | bytes 1638400 | tf_op jit(solution)/shard_map/convert_element_type | solution.py:26
  90.5 0.3 fusion.62
  90.9 1.2 %copy.100 = f32[32,40,128]{2,1,0:T(8,128)} copy(f32[32,40,128]{2,0,1:T(8,128)S(1)} %fusion.62) | data formatting | bytes 1310720 | tf_op jit(solution)/shard_map/optimization_barrier | solution.py:229
  92.1 5.7 %all-to-all-start.3 = ((f32[32,40,128]{2,1,0:T(8,128)}), f32[32,40,128]{2,1,0:T(8,128)S(1)}, u32[]{:S(2)}, u32[]{:S(2)}) async-start(f32[32,40,128]{2,1,0:T(8,128)} %copy.100), calls=%async_computation.3 | async-start | bytes 1310720 | tf_op jit(solution)/shard_map/all_to_all | solution.py:89
  97.8 5.9 %slice_multiply_fusion = (f32[2,4,256,528]{2,3,1,0:T(8,128)S(1)}, f32[2,4,256,528]{2,3,1,0:T(8,128)S(1)}) fusion(f32[2,4,256,528]{2,3,1,0:T(8,128)} %multiply_add_fusion, f32[2,4,256,1056]{2,3,1,0:T(8,128)} %fusion.90, f32[528]{0:T(1024)S(1)} %copy-done.32), kind=kLoop, calls=%fused_computation.11 | loop fusion | flops 3244032 | bytes 21628992 | tf_op jit(solution)/shard_map/mul | solution.py:144
  103.8 1.4 %reduce-precision_convert_fusion = (bf16[2,4,256,1056]{2,3,1,0:T(8,128)(2,1)S(1)}, bf16[2,4,256,1056]{2,3,1,0:T(8,128)(2,1)S(1)}) fusion(f32[2,4,256,528]{2,3,1,0:T(8,128)S(1)} %get-tuple-element.36, f32[2,4,256,528]{2,3,1,0:T(8,128)S(1)} %get-tuple-element.35), kind=kLoop, calls=%fused_computation.1 | loop fusion | flops 10813440 | bytes 17301504 | tf_op jit(solution)/shard_map/convert_element_type | solution.py:26
  105.2 0.9 fusion.1
  106.1 0.9 reduce-precision_convert_fusion.13
  107.0 0.3 fusion.34
  107.4 3.3 %all-to-all-done.3 = f32[32,40,128]{2,1,0:T(8,128)S(1)} async-done(((f32[32,40,128]{2,1,0:T(8,128)}), f32[32,40,128]{2,1,0:T(8,128)S(1)}, u32[]{:S(2)}, u32[]{:S(2)}) %all-to-all-start.3) | async-done | bytes 655392 | tf_op jit(solution)/shard_map/all_to_all | solution.py:89
  110.9 0.5 fusion.84
  111.4 2.1 %collective-permute-start.4 = (bf16[256,1,2,128]{3,0,1,2:T(8,128)(2,1)S(1)}, bf16[256,1,2,128]{3,0,1,2:T(8,128)(2,1)S(1)}, u32[]{:S(2)}, u32[]{:S(2)}) collective-permute-start(bf16[256,1,2,128]{3,0,1,2:T(8,128)(2,1)S(1)} %get-tuple-element.63), channel_id=1, source_target_pairs={{0,2},{1,3},{2,0},{3,1},{4,6},{5,7},{6,4},{7,5},{8,10},{9,11},{10,... | collective-permute-start | bytes 393224 | tf_op jit(solution)/shard_map/ppermute | solution.py:120
  113.5 0.3 collective-permute-start.5
  113.8 2.4 %collective-permute-start.3 = (bf16[256,1,2,128]{3,0,1,2:T(8,128)(2,1)S(1)}, bf16[256,1,2,128]{3,0,1,2:T(8,128)(2,1)S(1)}, u32[]{:S(2)}, u32[]{:S(2)}) collective-permute-start(bf16[256,1,2,128]{3,0,1,2:T(8,128)(2,1)S(1)} %get-tuple-element.61), channel_id=1, source_target_pairs={{0,3},{1,0},{2,1},{3,2},{4,7},{5,4},{6,5},{7,6},{8,11},{9,8},{10,9... | collective-permute-start | bytes 393224 | tf_op jit(solution)/shard_map/ppermute | solution.py:120
  116.2 0.5 fusion.47
  116.8 0.5 slice_multiply_fusion.1
  117.3 0.4 copy-done.28
  117.6 0.3 fusion.51
  118.1 0.4 reduce-precision_convert_fusion.18
  118.7 0.8 copy.104
  119.5 0.8 copy.105
  120.3 0.9 collective-permute-done.5
  121.3 1.1 copy.103
  (104 shorter events, 2.9 us)
Async XLA Ops:
  2.1 5.6 %copy-start.30 = (s32[2,128,32]{1,2,0:T(8,128)S(1)}, s32[2,128,32]{1,2,0:T(8,128)}, u32[]{:S(2)}) copy-start(s32[2,128,32]{1,2,0:T(8,128)} %param.13) | copy-start | bytes 98308
  2.1 8.0 %copy-start.26 = (bf16[96,1056,1]{1,0,2:T(8,128)(2,1)S(1)}, bf16[96,1056,1]{1,0,2:T(8,128)(2,1)}, u32[]{:S(2)}) copy-start(bf16[96,1056,1]{1,0,2:T(8,128)(2,1)} %constant.101) | copy-start | bytes 608260
  2.3 20.6 %collective-permute-start.2 = (bf16[2,256,1,2,128]{4,1,3,2,0:T(8,128)(2,1)S(1)}, bf16[2,256,1,2,128]{4,1,3,2,0:T(8,128)(2,1)S(1)}, u32[]{:S(2)}, u32[]{:S(2)}) collective-permute-start(bf16[2,256,1,2,128]{4,1,3,2,0:T(8,128)(2,1)S(1)} %get-tuple-element.46), channel_id=1, source_target_pairs={{0,3},{1,0},{2,1},{3,2},{4,7},{5,4},{6,5},{7,6},{8,11},{9,8},{10,9... | collective-permute-start | bytes 786440 | tf_op jit(solution)/shard_map/ppermute | solution.py:108
  7.0 15.9 %collective-permute-start.1 = (bf16[2,256,1,2,128]{4,1,3,2,0:T(8,128)(2,1)S(1)}, bf16[2,256,1,2,128]{4,1,3,2,0:T(8,128)(2,1)S(1)}, u32[]{:S(2)}, u32[]{:S(2)}) collective-permute-start(bf16[2,256,1,2,128]{4,1,3,2,0:T(8,128)(2,1)S(1)} %get-tuple-element.45), channel_id=1, source_target_pairs={{0,2},{1,3},{2,0},{3,1},{4,6},{5,7},{6,4},{7,5},{8,10},{9,11},{10,... | collective-permute-start | bytes 786440 | tf_op jit(solution)/shard_map/ppermute | solution.py:108
  7.0 15.9 %collective-permute-start = (bf16[2,256,1,2,128]{4,1,3,2,0:T(8,128)(2,1)S(1)}, bf16[2,256,1,2,128]{4,1,3,2,0:T(8,128)(2,1)S(1)}, u32[]{:S(2)}, u32[]{:S(2)}) collective-permute-start(bf16[2,256,1,2,128]{4,1,3,2,0:T(8,128)(2,1)S(1)} %get-tuple-element.44), channel_id=1, source_target_pairs={{0,1},{1,2},{2,3},{3,0},{4,5},{5,6},{6,7},{7,4},{8,9},{9,10},{10,1... | collective-permute-start | bytes 786440 | tf_op jit(solution)/shard_map/ppermute | solution.py:108
  9.2 13.1 %copy-start.11 = (bf16[256,2,128]{2,1,0:T(2,128)(2,1)}, bf16[256,2,128]{2,1,0:T(2,128)(2,1)S(1)}, u32[]{:S(2)}) copy-start(bf16[256,2,128]{2,1,0:T(2,128)(2,1)S(1)} %get-tuple-element.96) | copy-start | bytes 393220
  9.3 0.8 copy-start.23
  10.6 1.4 %copy-start.3 = (f32[2,256,1056]{1,2,0:T(8,128)}, f32[2,256,1056]{1,2,0:T(8,128)S(1)}, u32[]{:S(2)}) copy-start(f32[2,256,1056]{1,2,0:T(8,128)S(1)} %fusion.121) | copy-start | bytes 6488068
  13.5 21.5 %all-to-all-start = ((f32[32,40,128]{2,1,0:T(8,128)}), f32[32,40,128]{2,1,0:T(8,128)S(1)}, u32[]{:S(2)}, u32[]{:S(2)}) async-start(f32[32,40,128]{2,1,0:T(8,128)} %bitcast.26), calls=%async_computation | async-start | bytes 1310720 | tf_op jit(solution)/shard_map/all_to_all | solution.py:70
  22.1 25.8 %copy-start.13 = (pred[256,256]{0,1:T(8,128)(4,1)}, pred[256,256]{0,1:T(8,128)(4,1)S(1)}, u32[]{:S(2)}) copy-start(pred[256,256]{0,1:T(8,128)(4,1)S(1)} %iota_compare_fusion.1) | copy-start | bytes 196612
  22.9 2.2 %copy-start.27 = (bf16[96,1056,1,1]{1,0,3,2:T(8,128)(2,1)S(1)}, bf16[96,1056,1,1]{1,0,3,2:T(8,128)(2,1)}, u32[]{:S(2)}) copy-start(bf16[96,1056,1,1]{1,0,3,2:T(8,128)(2,1)} %constant.100) | copy-start | bytes 608260
  23.1 1.0 copy-start.5
  35.2 6.3 %copy-start.31 = (bf16[528]{0:T(1024)(128)(2,1)S(1)}, bf16[528]{0:T(1024)(128)(2,1)}, u32[]{:S(2)}) copy-start(bf16[528]{0:T(1024)(128)(2,1)} %constant.83.clone) | copy-start | bytes 3172
  36.8 17.8 %all-to-all-start.1 = ((f32[32,40,128]{2,1,0:T(8,128)}), f32[32,40,128]{2,1,0:T(8,128)}, u32[]{:S(2)}, u32[]{:S(2)}) async-start(f32[32,40,128]{2,1,0:T(8,128)} %copy.77), calls=%async_computation.1 | async-start | bytes 1310720 | tf_op jit(solution)/shard_map/all_to_all | solution.py:89
  45.8 2.1 %copy-start = (bf16[2,4,256,528]{2,3,1,0:T(8,128)(2,1)}, bf16[2,4,256,528]{2,3,1,0:T(8,128)(2,1)S(1)}, u32[]{:S(2)}) copy-start(bf16[2,4,256,528]{2,3,1,0:T(8,128)(2,1)S(1)} %get-tuple-element.28) | copy-start | bytes 6488068
  55.7 3.6 %copy-start.1 = (bf16[2,4,256,528]{2,3,1,0:T(8,128)(2,1)S(1)}, bf16[2,4,256,528]{2,3,1,0:T(8,128)(2,1)}, u32[]{:S(2)}) copy-start(bf16[2,4,256,528]{2,3,1,0:T(8,128)(2,1)} %copy-done) | copy-start | bytes 6488068
  61.4 2.7 %copy-start.2 = (bf16[2,4,256,528]{2,3,1,0:T(8,128)(2,1)S(1)}, bf16[2,4,256,528]{2,3,1,0:T(8,128)(2,1)}, u32[]{:S(2)}) copy-start(bf16[2,4,256,528]{2,3,1,0:T(8,128)(2,1)} %copy-done) | copy-start | bytes 6488068
  62.0 2.6 %copy-start.6 = (bf16[2,256,4,2,128]{4,1,3,2,0:T(8,128)(2,1)S(1)}, bf16[2,256,4,2,128]{4,1,3,2,0:T(8,128)(2,1)}, u32[]{:S(2)}) copy-start(bf16[2,256,4,2,128]{4,1,3,2,0:T(8,128)(2,1)} %copy-done.5) | copy-start | bytes 3145732
  64.1 2.1 %copy-start.12 = (bf16[256,2,128]{2,1,0:T(2,128)(2,1)S(1)}, bf16[256,2,128]{2,1,0:T(2,128)(2,1)}, u32[]{:S(2)}) copy-start(bf16[256,2,128]{2,1,0:T(2,128)(2,1)} %copy-done.11) | copy-start | bytes 393220
  64.2 2.1 %copy-start.15 = (bf16[2,4,256,256]{2,3,1,0:T(8,128)(2,1)S(1)}, bf16[2,4,256,256]{2,3,1,0:T(8,128)(2,1)}, u32[]{:S(2)}) copy-start(bf16[2,4,256,256]{2,3,1,0:T(8,128)(2,1)} %get-tuple-element.92) | copy-start | bytes 3145732
  64.2 2.1 %copy-start.17 = (f32[2,4,256,128]{3,2,0,1:T(8,128)S(1)}, f32[2,4,256,128]{3,2,0,1:T(8,128)}, u32[]{:S(2)}) copy-start(f32[2,4,256,128]{3,2,0,1:T(8,128)} %fusion.23) | copy-start | bytes 3145732
  71.4 17.8 %all-to-all-start.2 = ((f32[32,40,128]{2,1,0:T(8,128)}), f32[32,40,128]{2,1,0:T(8,128)}, u32[]{:S(2)}, u32[]{:S(2)}) async-start(f32[32,40,128]{2,1,0:T(8,128)} %bitcast.187), calls=%async_computation.2 | async-start | bytes 1310720 | tf_op jit(solution)/shard_map/all_to_all | solution.py:70
  77.7 2.8 %copy-start.18 = (bf16[2,4,256,256]{2,3,1,0:T(8,128)(2,1)}, bf16[2,4,256,256]{2,3,1,0:T(8,128)(2,1)S(1)}, u32[]{:S(2)}) copy-start(bf16[2,4,256,256]{2,3,1,0:T(8,128)(2,1)S(1)} %select_convert_fusion) | copy-start | bytes 3145732
  78.7 1.8 %copy-start.8 = (bf16[2,4,256,128]{3,2,0,1:T(8,128)(2,1)S(1)}, bf16[2,4,256,128]{3,2,0,1:T(8,128)(2,1)}, u32[]{:S(2)}) copy-start(bf16[2,4,256,128]{3,2,0,1:T(8,128)(2,1)} %get-tuple-element.43) | copy-start | bytes 1572868
  78.7 1.8 %copy-start.16 = (bf16[2,4,256,256]{2,3,1,0:T(8,128)(2,1)S(1)}, bf16[2,4,256,256]{2,3,1,0:T(8,128)(2,1)}, u32[]{:S(2)}) copy-start(bf16[2,4,256,256]{2,3,1,0:T(8,128)(2,1)} %get-tuple-element.92) | copy-start | bytes 3145732
  80.5 1.2 copy-start.10
  80.5 1.4 %copy-start.9 = (bf16[2,4,256,128]{3,2,0,1:T(8,128)(2,1)S(1)}, bf16[2,4,256,128]{3,2,0,1:T(8,128)(2,1)}, u32[]{:S(2)}) copy-start(bf16[2,4,256,128]{3,2,0,1:T(8,128)(2,1)} %get-tuple-element.41) | copy-start | bytes 1572868
  80.5 1.6 %copy-start.21 = (bf16[2,128,528]{1,2,0:T(8,128)(2,1)S(1)}, bf16[2,128,528]{1,2,0:T(8,128)(2,1)}, u32[]{:S(2)}) copy-start(bf16[2,128,528]{1,2,0:T(8,128)(2,1)} %get-tuple-element.59) | copy-start | bytes 811012
  80.5 1.6 %copy-start.22 = (bf16[2,128,528]{1,2,0:T(8,128)(2,1)S(1)}, bf16[2,128,528]{1,2,0:T(8,128)(2,1)}, u32[]{:S(2)}) copy-start(bf16[2,128,528]{1,2,0:T(8,128)(2,1)} %get-tuple-element.60) | copy-start | bytes 811012
  80.5 1.6 %copy-start.33 = (f32[2,528]{1,0:T(2,128)S(1)}, f32[2,528]{1,0:T(2,128)}, u32[]{:S(2)}) copy-start(f32[2,528]{1,0:T(2,128)} %get-tuple-element.87) | copy-start | bytes 12676
  90.5 7.3 %copy-start.32 = (f32[528]{0:T(1024)S(1)}, f32[528]{0:T(1024)}, u32[]{:S(2)}) copy-start(f32[528]{0:T(1024)} %constant.84.clone) | copy-start | bytes 6340
  92.1 18.6 %all-to-all-start.3 = ((f32[32,40,128]{2,1,0:T(8,128)}), f32[32,40,128]{2,1,0:T(8,128)S(1)}, u32[]{:S(2)}, u32[]{:S(2)}) async-start(f32[32,40,128]{2,1,0:T(8,128)} %copy.100), calls=%async_computation.3 | async-start | bytes 1310720 | tf_op jit(solution)/shard_map/all_to_all | solution.py:89
  103.8 1.4 %copy-start.20 = (bf16[1056,32,1,1]{0,1,2,3:T(8,128)(2,1)S(1)}, bf16[1056,32,1,1]{0,1,2,3:T(8,128)(2,1)}, u32[]{:S(2)}) copy-start(bf16[1056,32,1,1]{0,1,2,3:T(8,128)(2,1)} %constant.102) | copy-start | bytes 202756
  105.2 1.0 copy-start.14
  110.7 5.5 %copy-start.25 = (f32[2,256,128]{2,1,0:T(8,128)S(1)}, f32[2,256,128]{2,1,0:T(8,128)}, u32[]{:S(2)}) copy-start(f32[2,256,128]{2,1,0:T(8,128)} %convolution_bitcast_fusion.1) | copy-start | bytes 786436
  110.9 5.9 %copy-start.4 = (f32[2,256,1056]{1,2,0:T(8,128)S(1)}, f32[2,256,1056]{1,2,0:T(8,128)}, u32[]{:S(2)}) copy-start(f32[2,256,1056]{1,2,0:T(8,128)} %copy-done.3) | copy-start | bytes 6488068
  110.9 5.9 %copy-start.7 = (f32[2,256,528]{1,2,0:T(8,128)S(1)}, f32[2,256,528]{1,2,0:T(8,128)}, u32[]{:S(2)}) copy-start(f32[2,256,528]{1,2,0:T(8,128)} %convolution_bitcast_fusion) | copy-start | bytes 3244036
  110.9 5.9 %copy-start.19 = (bf16[256,2,128]{2,0,1:T(8,128)(2,1)S(1)}, bf16[256,2,128]{2,0,1:T(8,128)(2,1)}, u32[]{:S(2)}) copy-start(bf16[256,2,128]{2,0,1:T(8,128)(2,1)} %copy.216) | copy-start | bytes 393220
  111.4 8.8 %collective-permute-start.4 = (bf16[256,1,2,128]{3,0,1,2:T(8,128)(2,1)S(1)}, bf16[256,1,2,128]{3,0,1,2:T(8,128)(2,1)S(1)}, u32[]{:S(2)}, u32[]{:S(2)}) collective-permute-start(bf16[256,1,2,128]{3,0,1,2:T(8,128)(2,1)S(1)} %get-tuple-element.63), channel_id=1, source_target_pairs={{0,2},{1,3},{2,0},{3,1},{4,6},{5,7},{6,4},{7,5},{8,10},{9,11},{10,... | collective-permute-start | bytes 393224 | tf_op jit(solution)/shard_map/ppermute | solution.py:120
  113.5 7.7 %collective-permute-start.5 = (bf16[256,1,2,128]{3,0,1,2:T(8,128)(2,1)S(1)}, bf16[256,1,2,128]{3,0,1,2:T(8,128)(2,1)S(1)}, u32[]{:S(2)}, u32[]{:S(2)}) collective-permute-start(bf16[256,1,2,128]{3,0,1,2:T(8,128)(2,1)S(1)} %get-tuple-element.62), channel_id=1, source_target_pairs={{0,1},{1,2},{2,3},{3,0},{4,5},{5,6},{6,7},{7,4},{8,9},{9,10},{10,1... | collective-permute-start | bytes 393224 | tf_op jit(solution)/shard_map/ppermute | solution.py:120
  113.8 7.4 %collective-permute-start.3 = (bf16[256,1,2,128]{3,0,1,2:T(8,128)(2,1)S(1)}, bf16[256,1,2,128]{3,0,1,2:T(8,128)(2,1)S(1)}, u32[]{:S(2)}, u32[]{:S(2)}) collective-permute-start(bf16[256,1,2,128]{3,0,1,2:T(8,128)(2,1)S(1)} %get-tuple-element.61), channel_id=1, source_target_pairs={{0,3},{1,0},{2,1},{3,2},{4,7},{5,4},{6,5},{7,6},{8,11},{9,8},{10,9... | collective-permute-start | bytes 393224 | tf_op jit(solution)/shard_map/ppermute | solution.py:120
  116.7 0.9 copy-start.28
  117.2 0.8 copy-start.24
  117.2 0.9 copy-start.29

commit v19 on v17

--- a/solution.py
+++ b/solution.py
@@ -163,8 +163,12 @@
     heads_all = keys.shape[1]
     owned = heads_all // lax.axis_size("head")
     offset = lax.axis_index("head") * owned
-    key_part = lax.dynamic_slice_in_dim(keys, offset, owned, 1)
-    value_part = lax.dynamic_slice_in_dim(values, offset, owned, 1)
+    groups = heads_all // owned
+    me_head = lax.axis_index("head")
+    key_part = lax.select_n(me_head, *[keys[:, b * owned : (b + 1) * owned] for b in range(groups)])
+    value_part = lax.select_n(
+        me_head, *[values[:, b * owned : (b + 1) * owned] for b in range(groups)]
+    )
     both = head_exchange(jnp.stack([queries, dout]), owned)
     query_part, grad_part = both[0], both[1]
     key_one, key_two = sketch_parts(key_part, projector, "thd,df->htf")

time: 123 us -> 123 us (level)
  local copies, waits for them, and re-layouts: 14.1 us -> 12.7 us
    dynamic_slice x1 -> x0, local copies, waits for them, and re-layouts: 1.48 us -> none  [body(): value_part = lax.dynamic_slice_in_dim(values, offset, owned, 1)]
    unnamed x72 -> x75, local copies, waits for them, and re-layouts: 6.28 us -> 5.62 us
  transfers between devices with their start and end apart: 10 -> 10, of which waited for: 5 -> 6; matrix products, arithmetic and copies ran while one was open for 34% -> 34% of each run, Pallas kernels for 0% -> 0%
where the time goes in v19:
time: 123 us; the launch traced here: 122 us
  matrix products  37.6 us (31%)
  starting transfers between devices  33.9 us (28%)
  other arithmetic  18.8 us (15%)
  waiting for transfers between devices  17.3 us (14%)
  local copies, waits for them, and re-layouts  12.7 us (10%)
  between operations  1.49 us (1%)
    all_to_all x2, starting transfers between devices, scan_send(): return lax.all_to_all(flat.reshape(n, per, width), 'ctx', 0, 0, tiled=True)  13.3 us
    dot_general x12, matrix products, dot_parts(): term = jnp.einsum(pattern, *args, preferred_element_type=f32)  12.2 us
    all_to_all x2, starting transfers between devices, scan_return(): lax.all_to_all(summed, 'ctx', 0, 0, tiled=True).reshape(n * per, width)  10.5 us
    all_to_all x2, waiting for transfers between devices, scan_return(): lax.all_to_all(summed, 'ctx', 0, 0, tiled=True).reshape(n * per, width)  9.86 us
    all_to_all x2, waiting for transfers between devices, scan_send(): return lax.all_to_all(flat.reshape(n, per, width), 'ctx', 0, 0, tiled=True)  6.46 us
    mul x1, other arithmetic, tri_feature_back(): cotangent * second  5.95 us
    unnamed x75, local copies, waits for them, and re-layouts  5.62 us
    ppermute x3, starting transfers between devices, head_exchange(): lax.ppermute(piece, 'head', [(j, (j + k) % count) for j in range(count)])  5.36 us
  transfers between devices with their start and end apart: 10, of which 6 were waited for; matrix products, arithmetic and copies ran while one was open for 34% of the time, Pallas kernels for 0%

profile of v19, /device:TPU:1, one launch (start us, length us, event | category | flops | bytes accessed | tf_op | source)
XLA Modules:
  0.0 121.8 jit_solution(4911563283928968677)
XLA Ops:
  0.7 1.4 %copy_bitcast_fusion = (bf16[1,256,1,8,128]{4,1,3,2,0:T(8,128)(2,1)S(1)}, bf16[1,256,1,8,128]{4,1,3,2,0:T(8,128)(2,1)S(1)}) fusion(bf16[256,1,8,128]{3,2,1,0:T(8,128)(2,1)} %param.12, bf16[256,1,8,128]{3,2,1,0:T(8,128)(2,1)} %param.9), kind=kLoop, calls=%fused_computation.119 | loop fusion | bytes 2097152 | tf_op jit(solution)/shard_map/stack | solution.py:172
  2.3 4.7 %collective-permute-start.2 = (bf16[2,256,1,2,128]{4,1,3,2,0:T(8,128)(2,1)S(1)}, bf16[2,256,1,2,128]{4,1,3,2,0:T(8,128)(2,1)S(1)}, u32[]{:S(2)}, u32[]{:S(2)}) collective-permute-start(bf16[2,256,1,2,128]{4,1,3,2,0:T(8,128)(2,1)S(1)} %get-tuple-element.46), channel_id=1, source_target_pairs={{0,3},{1,0},{2,1},{3,2},{4,7},{5,4},{6,5},{7,6},{8,11},{9,8},{10,9... | collective-permute-start | bytes 786440 | tf_op jit(solution)/shard_map/ppermute | solution.py:103
  7.0 0.7 collective-permute-start
  7.7 0.4 fusion.161
  8.1 0.4 fusion.162
  8.8 0.8 reduce-precision_convert_fusion.16
  9.6 0.5 fusion.109
  10.1 1.3 %copy-done.3 = f32[2,256,1056]{1,2,0:T(8,128)} copy-done((f32[2,256,1056]{1,2,0:T(8,128)}, f32[2,256,1056]{1,2,0:T(8,128)S(1)}, u32[]{:S(2)}) %copy-start.3) | copy-done | bytes 2162712
  11.8 0.3 fusion.154
  12.1 0.9 fusion.58
  12.9 8.6 %all-to-all-start = ((f32[32,40,128]{2,1,0:T(8,128)}), f32[32,40,128]{2,1,0:T(8,128)S(1)}, u32[]{:S(2)}, u32[]{:S(2)}) async-start(f32[32,40,128]{2,1,0:T(8,128)} %bitcast.26), calls=%async_computation | async-start | bytes 1310720 | tf_op jit(solution)/shard_map/all_to_all | solution.py:70
  21.8 1.2 pad_maximum_fusion.2
  23.3 0.8 copy-done.5
  24.1 1.0 reduce-precision_convert_fusion.11
  25.1 4.7 %fusion.80 = f32[2,4,256,1056]{2,3,1,0:T(8,128)} fusion(bf16[96,1056,1,1]{1,0,3,2:T(8,128)(2,1)S(1)} %copy-done.29, bf16[2,4,256,32]{2,3,0,1:T(8,128)(2,1)S(1)} %get-tuple-element.72, bf16[2,4,256,32]{2,3,0,1:T(8,128)(2,1)S(1)} %get-tuple-element.71, bf16[2,4,256,32]{2,3,0,1:T(8,128)(2,1)S(1)} %get-tuple-element.70), kind=kOutput, calls=%fused_computation.129 | convolution fusion | flops 416415744 | bytes 9246720 | tf_op jit(solution)/shard_map/...k,kn->...n/dot_general | solution.py:49
  29.8 4.6 %all-to-all-done = f32[32,40,128]{2,1,0:T(8,128)S(1)} async-done(((f32[32,40,128]{2,1,0:T(8,128)}), f32[32,40,128]{2,1,0:T(8,128)S(1)}, u32[]{:S(2)}, u32[]{:S(2)}) %all-to-all-start) | async-done | bytes 655392 | tf_op jit(solution)/shard_map/all_to_all | solution.py:70
  34.5 0.5 fusion.61
  34.9 1.2 %copy.94 = f32[32,40,128]{2,1,0:T(8,128)} copy(f32[32,40,128]{2,0,1:T(8,128)S(1)} %fusion.61) | data formatting | bytes 1310720 | tf_op jit(solution)/shard_map/ij,jrc->irc/dot_general | solution.py:78
  36.2 4.8 %all-to-all-start.1 = ((f32[32,40,128]{2,1,0:T(8,128)}), f32[32,40,128]{2,1,0:T(8,128)}, u32[]{:S(2)}, u32[]{:S(2)}) async-start(f32[32,40,128]{2,1,0:T(8,128)} %copy.94), calls=%async_computation.1 | async-start | bytes 1310720 | tf_op jit(solution)/shard_map/all_to_all | solution.py:84
  40.9 4.2 %broadcast_multiply_fusion = (bf16[2,4,256,528]{2,3,1,0:T(8,128)(2,1)S(1)}, bf16[2,4,256,528]{2,3,1,0:T(8,128)(2,1)S(1)}) fusion(bf16[528]{0:T(1024)(128)(2,1)S(1)} %copy-done.33, f32[2,4,256,1056]{2,3,1,0:T(8,128)} %fusion.80), kind=kLoop, calls=%fused_computation.80 | loop fusion | flops 4325376 | bytes 12977184 | tf_op jit(solution)/shard_map/mul | solution.py:184
  45.2 2.1 %select_convert_fusion.1 = (bf16[2,4,256,256]{2,3,1,0:T(8,128)(2,1)}, f32[2,4,256,256]{2,3,1,0:T(8,128)S(1)}) fusion(pred[256,256]{0,1:T(8,128)(4,1)S(1)} %iota_compare_fusion.1, bf16[2,4,256,528]{2,3,1,0:T(8,128)(2,1)S(1)} %get-tuple-element.28, bf16[2,256,528]{1,2,0:T(8,128)(2,1)S(1)} %get-tuple-element.27), kind=kOutput, calls=%fused_computation.25 | convolution fusion | flops 554172416 | bytes 5914624 | tf_op jit(solution)/shard_map/hmif,hjf->hmij/dot_general | solution.py:192
  47.5 6.5 %all-to-all-done.1 = f32[32,40,128]{2,1,0:T(8,128)} async-done(((f32[32,40,128]{2,1,0:T(8,128)}), f32[32,40,128]{2,1,0:T(8,128)}, u32[]{:S(2)}, u32[]{:S(2)}) %all-to-all-start.1) | async-done | bytes 655392 | tf_op jit(solution)/shard_map/all_to_all | solution.py:84
  54.0 1.1 slice.162
  55.1 0.8 slice.160
  56.0 2.7 %fusion.16 = f32[2,4,256,128]{3,2,0,1:T(8,128)S(1)} fusion(bf16[2,4,256,528]{2,3,1,0:T(8,128)(2,1)} %copy-done, f32[2,528,128]{2,1,0:T(8,128)S(1)} %bitcast.185), kind=kOutput, calls=%fused_computation.27 | convolution fusion | flops 277229568 | bytes 3751936 | tf_op jit(solution)/shard_map/hmif,hfd->hmid/dot_general | solution.py:36
  58.7 2.1 %fusion.23 = f32[2,4,256,128]{3,2,0,1:T(8,128)} fusion(f32[2,4,256,128]{3,2,0,1:T(8,128)S(1)} %fusion.16, bf16[2,4,256,528]{2,3,1,0:T(8,128)(2,1)S(1)} %copy-done.1, f32[2,528,128]{2,1,0:T(8,128)S(1)} %bitcast.186), kind=kOutput, calls=%fused_computation.39 | convolution fusion | flops 277356544 | bytes 4800512 | tf_op jit(solution)/shard_map/hmif,hfd->hmid/dot_general | solution.py:36
  60.9 0.6 fusion.164
  61.5 2.1 %fusion.139 = f32[2,1,4,256]{3,1,2,0:T(1,128)S(1)} fusion(bf16[2,4,256,528]{2,3,1,0:T(8,128)(2,1)} %copy-done, bf16[2,528,1,1]{1,0,2,3:T(2,128)(2,1)S(1)} %get-tuple-element.91), kind=kOutput, calls=%fused_computation.225 | convolution fusion | flops 2162688 | bytes 2172992 | tf_op jit(solution)/shard_map/hmif,hf->hmi/dot_general | solution.py:36
  63.6 0.4 fusion.141
  64.0 1.6 %reduce-precision_convert_fusion.2 = (bf16[2,4,256,128]{3,2,0,1:T(8,128)(2,1)}, bf16[2,4,256,128]{3,2,0,1:T(8,128)(2,1)}, bf16[2,4,256,128]{3,2,0,1:T(8,128)(2,1)}) fusion(f32[2,4,256]{2,0,1:T(2,128)S(1)} %copy.95, bf16[2,256,4,2,128]{4,1,3,2,0:T(8,128)(2,1)S(1)} %copy-done.6), kind=kLoop, calls=%fused_computation.32 | loop fusion | flops 1835008 | bytes 2105344 | tf_op jit(solution)/shard_map/convert_element_type | solution.py:26
  65.7 1.1 fusion.33
  66.8 0.7 fusion.130
  67.4 0.7 fusion.132
  68.1 1.8 %fusion.78 = f32[2,528,128,1]{2,1,3,0:T(8,128)S(1)} fusion(bf16[2,4,256,528]{2,3,1,0:T(8,128)(2,1)S(1)} %get-tuple-element.29, bf16[2,4,256,128]{3,2,0,1:T(8,128)(2,1)} %get-tuple-element.43), kind=kOutput, calls=%fused_computation.126 | convolution fusion | flops 276824064 | bytes 3227648 | tf_op jit(solution)/shard_map/hmif,hmid->hfd/dot_general | solution.py:204
  69.9 0.9 select_maximum_fusion
  70.8 4.7 %all-to-all-start.2 = ((f32[32,40,128]{2,1,0:T(8,128)}), f32[32,40,128]{2,1,0:T(8,128)}, u32[]{:S(2)}, u32[]{:S(2)}) async-start(f32[32,40,128]{2,1,0:T(8,128)} %bitcast.188), calls=%async_computation.2 | async-start | bytes 1310720 | tf_op jit(solution)/shard_map/all_to_all | solution.py:70
  75.6 1.6 %select_convert_fusion = bf16[2,4,256,256]{2,3,1,0:T(8,128)(2,1)S(1)} fusion(f32[2,4,256]{2,1,0:T(4,128)S(1)} %copy.104, pred[256,256]{0,1:T(8,128)(4,1)} %copy-done.14, bf16[2,4,256,128]{3,2,0,1:T(8,128)(2,1)} %get-tuple-element.43, bf16[256,2,128]{2,0,1:T(8,128)(2,1)} %copy-done.11), kind=kOutput, calls=%fused_computation.24 | convolution fusion | flops 135790592 | bytes 1777664 | tf_op jit(solution)/shard_map/hmid,hjd->hmij/dot_general | solution.py:210
  77.1 1.0 fusion.64
  78.1 1.8 %convolution_bitcast_fusion = f32[2,256,528]{1,2,0:T(8,128)} fusion(bf16[2,4,256,256]{2,3,1,0:T(8,128)(2,1)S(1)} %select_convert_fusion, bf16[2,4,256,528]{2,3,1,0:T(8,128)(2,1)S(1)} %get-tuple-element.29), kind=kOutput, calls=%fused_computation.35 | convolution fusion | flops 553648128 | bytes 4292608 | tf_op jit(solution)/shard_map/hmij,hmif->hjf/dot_general | solution.py:225
  80.0 1.2 convolution_bitcast_fusion.1
  81.6 5.2 %multiply_add_fusion = f32[2,4,256,528]{2,3,1,0:T(8,128)} fusion(f32[2,528]{1,0:T(2,128)S(1)} %copy-done.35, f32[2,4,256]{2,1,0:T(4,128)S(1)} %copy.104, bf16[2,4,256,128]{2,3,1,0:T(8,128)(2,1)S(1)} %copy.107, bf16[2,4,256,128]{2,3,1,0:T(8,128)(2,1)S(1)} %copy.105, bf16[2,4,256,256]{2,3,1,0:T(8,128)(2,1)} %copy-done.19, ...), kind=kOutput, calls=%fused_computation.9 | convolution fusion | flops 1402175488 | bytes 7516288 | tf_op jit(solution)/shard_map/hmik,hkf->hmif/dot_general | solution.py:217
  86.8 1.8 %all-to-all-done.2 = f32[32,40,128]{2,1,0:T(8,128)} async-done(((f32[32,40,128]{2,1,0:T(8,128)}), f32[32,40,128]{2,1,0:T(8,128)}, u32[]{:S(2)}, u32[]{:S(2)}) %all-to-all-start.2) | async-done | bytes 655392 | tf_op jit(solution)/shard_map/all_to_all | solution.py:70
  88.6 1.6 %fusion.59 = f32[32,40,128]{2,0,1:T(8,128)S(1)} fusion(f32[32,40,128]{2,1,0:T(8,128)} %all-to-all-done.2), kind=kOutput, calls=%fused_computation.101 | convolution fusion | flops 62915584 | bytes 1310720 | tf_op jit(solution)/shard_map/ij,jrc->irc/dot_general | solution.py:78
  90.2 1.2 copy.116
  91.4 5.7 %all-to-all-start.3 = ((f32[32,40,128]{2,1,0:T(8,128)}), f32[32,40,128]{2,1,0:T(8,128)S(1)}, u32[]{:S(2)}, u32[]{:S(2)}) async-start(f32[32,40,128]{2,1,0:T(8,128)} %copy.116), calls=%async_computation.3 | async-start | bytes 1310720 | tf_op jit(solution)/shard_map/all_to_all | solution.py:84
  97.1 5.9 %slice_multiply_fusion = (f32[2,4,256,528]{2,3,1,0:T(8,128)S(1)}, f32[2,4,256,528]{2,3,1,0:T(8,128)S(1)}) fusion(f32[2,4,256,528]{2,3,1,0:T(8,128)} %multiply_add_fusion, f32[2,4,256,1056]{2,3,1,0:T(8,128)} %fusion.80, f32[528]{0:T(1024)S(1)} %copy-done.34), kind=kLoop, calls=%fused_computation.11 | loop fusion | flops 3244032 | bytes 21628992 | tf_op jit(solution)/shard_map/mul | solution.py:139
  103.1 1.4 %reduce-precision_convert_fusion = (bf16[2,4,256,1056]{2,3,1,0:T(8,128)(2,1)S(1)}, bf16[2,4,256,1056]{2,3,1,0:T(8,128)(2,1)S(1)}) fusion(f32[2,4,256,528]{2,3,1,0:T(8,128)S(1)} %get-tuple-element.36, f32[2,4,256,528]{2,3,1,0:T(8,128)S(1)} %get-tuple-element.35), kind=kLoop, calls=%fused_computation.1 | loop fusion | flops 10813440 | bytes 17301504 | tf_op jit(solution)/shard_map/convert_element_type | solution.py:26
  104.5 0.9 fusion.1
  105.4 0.9 reduce-precision_convert_fusion.9
  106.4 0.3 fusion.34
  106.7 3.3 %all-to-all-done.3 = f32[32,40,128]{2,1,0:T(8,128)S(1)} async-done(((f32[32,40,128]{2,1,0:T(8,128)}), f32[32,40,128]{2,1,0:T(8,128)S(1)}, u32[]{:S(2)}, u32[]{:S(2)}) %all-to-all-start.3) | async-done | bytes 655392 | tf_op jit(solution)/shard_map/all_to_all | solution.py:84
  110.2 0.5 fusion.74
  110.8 2.1 %collective-permute-start.4 = (bf16[256,1,2,128]{3,0,1,2:T(8,128)(2,1)S(1)}, bf16[256,1,2,128]{3,0,1,2:T(8,128)(2,1)S(1)}, u32[]{:S(2)}, u32[]{:S(2)}) collective-permute-start(bf16[256,1,2,128]{3,0,1,2:T(8,128)(2,1)S(1)} %get-tuple-element.57), channel_id=1, source_target_pairs={{0,2},{1,3},{2,0},{3,1},{4,6},{5,7},{6,4},{7,5},{8,10},{9,11},{10,... | collective-permute-start | bytes 393224 | tf_op jit(solution)/shard_map/ppermute | solution.py:115
  112.8 0.3 collective-permute-start.5
  113.1 2.4 %collective-permute-start.3 = (bf16[256,1,2,128]{3,0,1,2:T(8,128)(2,1)S(1)}, bf16[256,1,2,128]{3,0,1,2:T(8,128)(2,1)S(1)}, u32[]{:S(2)}, u32[]{:S(2)}) collective-permute-start(bf16[256,1,2,128]{3,0,1,2:T(8,128)(2,1)S(1)} %get-tuple-element.55), channel_id=1, source_target_pairs={{0,3},{1,0},{2,1},{3,2},{4,7},{5,4},{6,5},{7,6},{8,11},{9,8},{10,9... | collective-permute-start | bytes 393224 | tf_op jit(solution)/shard_map/ppermute | solution.py:115
  115.5 0.5 fusion.47
  116.1 0.5 slice_multiply_fusion.1
  116.6 0.4 copy-done.30
  117.0 0.3 fusion.51
  117.4 0.4 reduce-precision_convert_fusion.14
  118.0 0.8 copy.120
  118.8 0.8 copy.121
  119.6 0.9 collective-permute-done.5
  120.7 1.1 copy.119
  (105 shorter events, 2.8 us)
Async XLA Ops:
  2.1 5.6 %copy-start.32 = (s32[2,128,32]{1,2,0:T(8,128)S(1)}, s32[2,128,32]{1,2,0:T(8,128)}, u32[]{:S(2)}) copy-start(s32[2,128,32]{1,2,0:T(8,128)} %param.13) | copy-start | bytes 98308
  2.1 5.6 %copy-start.20 = (bf16[256,8,128]{2,1,0:T(8,128)(2,1)S(1)}, bf16[256,8,128]{2,1,0:T(8,128)(2,1)}, u32[]{:S(2)}) copy-start(bf16[256,8,128]{2,1,0:T(8,128)(2,1)} %param.11) | copy-start | bytes 1572868
  2.1 6.0 %copy-start.21 = (bf16[256,8,128]{2,1,0:T(8,128)(2,1)S(1)}, bf16[256,8,128]{2,1,0:T(8,128)(2,1)}, u32[]{:S(2)}) copy-start(bf16[256,8,128]{2,1,0:T(8,128)(2,1)} %param.10) | copy-start | bytes 1572868
  2.3 7.3 %copy-start.28 = (bf16[96,1056,1]{1,0,2:T(8,128)(2,1)S(1)}, bf16[96,1056,1]{1,0,2:T(8,128)(2,1)}, u32[]{:S(2)}) copy-start(bf16[96,1056,1]{1,0,2:T(8,128)(2,1)} %constant.99) | copy-start | bytes 608260
  2.3 19.3 %collective-permute-start.2 = (bf16[2,256,1,2,128]{4,1,3,2,0:T(8,128)(2,1)S(1)}, bf16[2,256,1,2,128]{4,1,3,2,0:T(8,128)(2,1)S(1)}, u32[]{:S(2)}, u32[]{:S(2)}) collective-permute-start(bf16[2,256,1,2,128]{4,1,3,2,0:T(8,128)(2,1)S(1)} %get-tuple-element.46), channel_id=1, source_target_pairs={{0,3},{1,0},{2,1},{3,2},{4,7},{5,4},{6,5},{7,6},{8,11},{9,8},{10,9... | collective-permute-start | bytes 786440 | tf_op jit(solution)/shard_map/ppermute | solution.py:103
  7.0 14.7 %collective-permute-start.1 = (bf16[2,256,1,2,128]{4,1,3,2,0:T(8,128)(2,1)S(1)}, bf16[2,256,1,2,128]{4,1,3,2,0:T(8,128)(2,1)}, u32[]{:S(2)}, u32[]{:S(2)}) collective-permute-start(bf16[2,256,1,2,128]{4,1,3,2,0:T(8,128)(2,1)S(1)} %get-tuple-element.45), channel_id=1, source_target_pairs={{0,2},{1,3},{2,0},{3,1},{4,6},{5,7},{6,4},{7,5},{8,10},{9,11},{10,... | collective-permute-start | bytes 786440 | tf_op jit(solution)/shard_map/ppermute | solution.py:103
  7.0 14.8 %collective-permute-start = (bf16[2,256,1,2,128]{4,1,3,2,0:T(8,128)(2,1)S(1)}, bf16[2,256,1,2,128]{4,1,3,2,0:T(8,128)(2,1)}, u32[]{:S(2)}, u32[]{:S(2)}) collective-permute-start(bf16[2,256,1,2,128]{4,1,3,2,0:T(8,128)(2,1)S(1)} %get-tuple-element.44), channel_id=1, source_target_pairs={{0,1},{1,2},{2,3},{3,0},{4,5},{5,6},{6,7},{7,4},{8,9},{9,10},{10,1... | collective-permute-start | bytes 786440 | tf_op jit(solution)/shard_map/ppermute | solution.py:103
  8.6 3.1 %copy-start.11 = (bf16[256,2,128]{2,0,1:T(8,128)(2,1)}, bf16[256,2,128]{2,0,1:T(8,128)(2,1)S(1)}, u32[]{:S(2)}) copy-start(bf16[256,2,128]{2,0,1:T(8,128)(2,1)S(1)} %get-tuple-element.98) | copy-start | bytes 393220
  8.8 0.8 copy-start.25
  10.1 1.3 %copy-start.3 = (f32[2,256,1056]{1,2,0:T(8,128)}, f32[2,256,1056]{1,2,0:T(8,128)S(1)}, u32[]{:S(2)}) copy-start(f32[2,256,1056]{1,2,0:T(8,128)S(1)} %fusion.109) | copy-start | bytes 6488068
  12.9 21.5 %all-to-all-start = ((f32[32,40,128]{2,1,0:T(8,128)}), f32[32,40,128]{2,1,0:T(8,128)S(1)}, u32[]{:S(2)}, u32[]{:S(2)}) async-start(f32[32,40,128]{2,1,0:T(8,128)} %bitcast.26), calls=%async_computation | async-start | bytes 1310720 | tf_op jit(solution)/shard_map/all_to_all | solution.py:70
  21.6 25.7 %copy-start.14 = (pred[256,256]{0,1:T(8,128)(4,1)}, pred[256,256]{0,1:T(8,128)(4,1)S(1)}, u32[]{:S(2)}) copy-start(pred[256,256]{0,1:T(8,128)(4,1)S(1)} %iota_compare_fusion.1) | copy-start | bytes 196612
  21.8 3.2 %copy-start.29 = (bf16[96,1056,1,1]{1,0,3,2:T(8,128)(2,1)S(1)}, bf16[96,1056,1,1]{1,0,3,2:T(8,128)(2,1)}, u32[]{:S(2)}) copy-start(bf16[96,1056,1,1]{1,0,3,2:T(8,128)(2,1)} %constant.98) | copy-start | bytes 608260
  23.0 1.0 copy-start.5
  29.8 11.1 %copy-start.33 = (bf16[528]{0:T(1024)(128)(2,1)S(1)}, bf16[528]{0:T(1024)(128)(2,1)}, u32[]{:S(2)}) copy-start(bf16[528]{0:T(1024)(128)(2,1)} %constant.81.clone) | copy-start | bytes 3172
  36.2 17.8 %all-to-all-start.1 = ((f32[32,40,128]{2,1,0:T(8,128)}), f32[32,40,128]{2,1,0:T(8,128)}, u32[]{:S(2)}, u32[]{:S(2)}) async-start(f32[32,40,128]{2,1,0:T(8,128)} %copy.94), calls=%async_computation.1 | async-start | bytes 1310720 | tf_op jit(solution)/shard_map/all_to_all | solution.py:84
  45.2 2.1 %copy-start = (bf16[2,4,256,528]{2,3,1,0:T(8,128)(2,1)}, bf16[2,4,256,528]{2,3,1,0:T(8,128)(2,1)S(1)}, u32[]{:S(2)}) copy-start(bf16[2,4,256,528]{2,3,1,0:T(8,128)(2,1)S(1)} %get-tuple-element.28) | copy-start | bytes 6488068
  55.1 3.6 %copy-start.1 = (bf16[2,4,256,528]{2,3,1,0:T(8,128)(2,1)S(1)}, bf16[2,4,256,528]{2,3,1,0:T(8,128)(2,1)}, u32[]{:S(2)}) copy-start(bf16[2,4,256,528]{2,3,1,0:T(8,128)(2,1)} %copy-done) | copy-start | bytes 6488068
  60.9 2.7 %copy-start.2 = (bf16[2,4,256,528]{2,3,1,0:T(8,128)(2,1)S(1)}, bf16[2,4,256,528]{2,3,1,0:T(8,128)(2,1)}, u32[]{:S(2)}) copy-start(bf16[2,4,256,528]{2,3,1,0:T(8,128)(2,1)} %copy-done) | copy-start | bytes 6488068
  61.5 2.6 %copy-start.6 = (bf16[2,256,4,2,128]{4,1,3,2,0:T(8,128)(2,1)S(1)}, bf16[2,256,4,2,128]{4,1,3,2,0:T(8,128)(2,1)}, u32[]{:S(2)}) copy-start(bf16[2,256,4,2,128]{4,1,3,2,0:T(8,128)(2,1)} %copy-done.5) | copy-start | bytes 3145732
  63.6 2.1 %copy-start.12 = (bf16[256,2,128]{2,0,1:T(8,128)(2,1)S(1)}, bf16[256,2,128]{2,0,1:T(8,128)(2,1)}, u32[]{:S(2)}) copy-start(bf16[256,2,128]{2,0,1:T(8,128)(2,1)} %copy-done.11) | copy-start | bytes 393220
  63.6 2.1 %copy-start.16 = (bf16[2,4,256,256]{2,3,1,0:T(8,128)(2,1)S(1)}, bf16[2,4,256,256]{2,3,1,0:T(8,128)(2,1)}, u32[]{:S(2)}) copy-start(bf16[2,4,256,256]{2,3,1,0:T(8,128)(2,1)} %get-tuple-element.94) | copy-start | bytes 3145732
  63.6 2.1 %copy-start.18 = (f32[2,4,256,128]{3,2,0,1:T(8,128)S(1)}, f32[2,4,256,128]{3,2,0,1:T(8,128)}, u32[]{:S(2)}) copy-start(f32[2,4,256,128]{3,2,0,1:T(8,128)} %fusion.23) | copy-start | bytes 3145732
  70.8 17.8 %all-to-all-start.2 = ((f32[32,40,128]{2,1,0:T(8,128)}), f32[32,40,128]{2,1,0:T(8,128)}, u32[]{:S(2)}, u32[]{:S(2)}) async-start(f32[32,40,128]{2,1,0:T(8,128)} %bitcast.188), calls=%async_computation.2 | async-start | bytes 1310720 | tf_op jit(solution)/shard_map/all_to_all | solution.py:70
  77.1 2.8 %copy-start.19 = (bf16[2,4,256,256]{2,3,1,0:T(8,128)(2,1)}, bf16[2,4,256,256]{2,3,1,0:T(8,128)(2,1)S(1)}, u32[]{:S(2)}) copy-start(bf16[2,4,256,256]{2,3,1,0:T(8,128)(2,1)S(1)} %select_convert_fusion) | copy-start | bytes 3145732
  78.1 1.8 %copy-start.8 = (bf16[2,4,256,128]{3,2,0,1:T(8,128)(2,1)S(1)}, bf16[2,4,256,128]{3,2,0,1:T(8,128)(2,1)}, u32[]{:S(2)}) copy-start(bf16[2,4,256,128]{3,2,0,1:T(8,128)(2,1)} %get-tuple-element.43) | copy-start | bytes 1572868
  78.1 1.8 %copy-start.17 = (bf16[2,4,256,256]{2,3,1,0:T(8,128)(2,1)S(1)}, bf16[2,4,256,256]{2,3,1,0:T(8,128)(2,1)}, u32[]{:S(2)}) copy-start(bf16[2,4,256,256]{2,3,1,0:T(8,128)(2,1)} %get-tuple-element.94) | copy-start | bytes 3145732
  79.9 1.2 copy-start.10
  79.9 1.4 %copy-start.9 = (bf16[2,4,256,128]{3,2,0,1:T(8,128)(2,1)S(1)}, bf16[2,4,256,128]{3,2,0,1:T(8,128)(2,1)}, u32[]{:S(2)}) copy-start(bf16[2,4,256,128]{3,2,0,1:T(8,128)(2,1)} %get-tuple-element.41) | copy-start | bytes 1572868
  79.9 1.6 %copy-start.23 = (bf16[2,128,528]{1,2,0:T(8,128)(2,1)S(1)}, bf16[2,128,528]{1,2,0:T(8,128)(2,1)}, u32[]{:S(2)}) copy-start(bf16[2,128,528]{1,2,0:T(8,128)(2,1)} %get-tuple-element.53) | copy-start | bytes 811012
  79.9 1.6 %copy-start.24 = (bf16[2,128,528]{1,2,0:T(8,128)(2,1)S(1)}, bf16[2,128,528]{1,2,0:T(8,128)(2,1)}, u32[]{:S(2)}) copy-start(bf16[2,128,528]{1,2,0:T(8,128)(2,1)} %get-tuple-element.54) | copy-start | bytes 811012
  79.9 1.6 %copy-start.35 = (f32[2,528]{1,0:T(2,128)S(1)}, f32[2,528]{1,0:T(2,128)}, u32[]{:S(2)}) copy-start(f32[2,528]{1,0:T(2,128)} %get-tuple-element.89) | copy-start | bytes 12676
  86.8 10.3 %copy-start.34 = (f32[528]{0:T(1024)S(1)}, f32[528]{0:T(1024)}, u32[]{:S(2)}) copy-start(f32[528]{0:T(1024)} %constant.82.clone) | copy-start | bytes 6340
  91.4 18.6 %all-to-all-start.3 = ((f32[32,40,128]{2,1,0:T(8,128)}), f32[32,40,128]{2,1,0:T(8,128)S(1)}, u32[]{:S(2)}, u32[]{:S(2)}) async-start(f32[32,40,128]{2,1,0:T(8,128)} %copy.116), calls=%async_computation.3 | async-start | bytes 1310720 | tf_op jit(solution)/shard_map/all_to_all | solution.py:84
  103.1 1.4 %copy-start.22 = (bf16[1056,32,1,1]{0,1,2,3:T(8,128)(2,1)S(1)}, bf16[1056,32,1,1]{0,1,2,3:T(8,128)(2,1)}, u32[]{:S(2)}) copy-start(bf16[1056,32,1,1]{0,1,2,3:T(8,128)(2,1)} %constant.100) | copy-start | bytes 202756
  104.5 1.0 copy-start.15
  110.0 5.5 %copy-start.27 = (f32[2,256,128]{2,1,0:T(8,128)S(1)}, f32[2,256,128]{2,1,0:T(8,128)}, u32[]{:S(2)}) copy-start(f32[2,256,128]{2,1,0:T(8,128)} %convolution_bitcast_fusion.1) | copy-start | bytes 786436
  110.2 5.8 %copy-start.4 = (f32[2,256,1056]{1,2,0:T(8,128)S(1)}, f32[2,256,1056]{1,2,0:T(8,128)}, u32[]{:S(2)}) copy-start(f32[2,256,1056]{1,2,0:T(8,128)} %copy-done.3) | copy-start | bytes 6488068
  110.2 5.8 %copy-start.7 = (f32[2,256,528]{1,2,0:T(8,128)S(1)}, f32[2,256,528]{1,2,0:T(8,128)}, u32[]{:S(2)}) copy-start(f32[2,256,528]{1,2,0:T(8,128)} %convolution_bitcast_fusion) | copy-start | bytes 3244036
  110.2 5.8 %copy-start.13 = (bf16[256,2,128]{2,0,1:T(8,128)(2,1)S(1)}, bf16[256,2,128]{2,0,1:T(8,128)(2,1)}, u32[]{:S(2)}) copy-start(bf16[256,2,128]{2,0,1:T(8,128)(2,1)} %copy-done.11) | copy-start | bytes 393220
  110.8 8.8 %collective-permute-start.4 = (bf16[256,1,2,128]{3,0,1,2:T(8,128)(2,1)S(1)}, bf16[256,1,2,128]{3,0,1,2:T(8,128)(2,1)S(1)}, u32[]{:S(2)}, u32[]{:S(2)}) collective-permute-start(bf16[256,1,2,128]{3,0,1,2:T(8,128)(2,1)S(1)} %get-tuple-element.57), channel_id=1, source_target_pairs={{0,2},{1,3},{2,0},{3,1},{4,6},{5,7},{6,4},{7,5},{8,10},{9,11},{10,... | collective-permute-start | bytes 393224 | tf_op jit(solution)/shard_map/ppermute | solution.py:115
  112.8 7.7 %collective-permute-start.5 = (bf16[256,1,2,128]{3,0,1,2:T(8,128)(2,1)S(1)}, bf16[256,1,2,128]{3,0,1,2:T(8,128)(2,1)S(1)}, u32[]{:S(2)}, u32[]{:S(2)}) collective-permute-start(bf16[256,1,2,128]{3,0,1,2:T(8,128)(2,1)S(1)} %get-tuple-element.56), channel_id=1, source_target_pairs={{0,1},{1,2},{2,3},{3,0},{4,5},{5,6},{6,7},{7,4},{8,9},{9,10},{10,1... | collective-permute-start | bytes 393224 | tf_op jit(solution)/shard_map/ppermute | solution.py:115
  113.1 7.4 %collective-permute-start.3 = (bf16[256,1,2,128]{3,0,1,2:T(8,128)(2,1)S(1)}, bf16[256,1,2,128]{3,0,1,2:T(8,128)(2,1)S(1)}, u32[]{:S(2)}, u32[]{:S(2)}) collective-permute-start(bf16[256,1,2,128]{3,0,1,2:T(8,128)(2,1)S(1)} %get-tuple-element.55), channel_id=1, source_target_pairs={{0,3},{1,0},{2,1},{3,2},{4,7},{5,4},{6,5},{7,6},{8,11},{9,8},{10,9... | collective-permute-start | bytes 393224 | tf_op jit(solution)/shard_map/ppermute | solution.py:115
  116.1 0.9 copy-start.30
  116.5 0.8 copy-start.26
  116.6 0.9 copy-start.31

commit v20 on v19

--- a/solution.py
+++ b/solution.py
@@ -181,7 +181,6 @@
 
     query_one, query_two = sketch_parts(query_part, projector, "tmhd,df->hmtf")
     query_feat = tri_features(query_one, query_two, take_a, take_b)
-    query_wfeat = query_feat * weight
     grad_heads = grad_part.transpose(2, 1, 0, 3).astype(f32)
     length = key_feat.shape[1]
     causal = lax.broadcasted_iota(jnp.int32, (length, length), 0) >= lax.broadcasted_iota(
@@ -189,14 +188,14 @@
     )
     scores = jnp.where(
         causal,
-        jnp.einsum("hmif,hjf->hmij", query_wfeat, key_feat, preferred_element_type=f32),
+        jnp.einsum("hmif,hjf->hmij", query_feat, key_wfeat, preferred_element_type=f32),
         0.0,
     )
     weights = scores.astype(bf16)
     numerator = jnp.einsum(
         "hmij,hjd->hmid", weights, value_heads, preferred_element_type=f32
-    ) + dot_split("hmif,hfd->hmid", query_wfeat, state_in)
-    denominator = 1.0 + jnp.sum(scores, -1) + dot_split("hmif,hf->hmi", query_wfeat, total_in)
+    ) + dot_split("hmif,hfd->hmid", query_feat, state_in * weight.astype(f32)[None, :, None])
+    denominator = 1.0 + jnp.sum(scores, -1) + dot_split("hmif,hf->hmi", query_feat, total_in * weight.astype(f32)[None, :])
     output_rows = numerator / denominator[..., None]
     grad_rows = grad_heads / denominator[..., None]
     grad_low = grad_rows.astype(bf16)

time: 123 us -> 119 us (0.967)
  matrix products: 37.6 us -> 34.5 us
    mul x1 -> x0, other arithmetic: 4.22 us -> none  [body(): query_wfeat = query_feat * weight]
    convert_element_type x0 -> x1, other arithmetic: none -> 4.18 us  [tri_features(): return (first * second * (1.0 / width)).astype(bf16)]
    dot_general x12, matrix products: 12.2 us -> 9.06 us  [dot_parts(): term = jnp.einsum(pattern, *args, preferred_element_type=f32)]
    unnamed x75 -> x73, local copies, waits for them, and re-layouts: 5.62 us -> 5.96 us
    convert_element_type x3 -> x4, other arithmetic: 3.08 us -> 3.09 us  [split_parts(): parts.append(hi.astype(bf16))]
  transfers between devices with their start and end apart: 10 -> 10, of which waited for: 6 -> 5; matrix products, arithmetic and copies ran while one was open for 34% -> 36% of each run, Pallas kernels for 0% -> 0%
where the time goes in v20:
time: 119 us; the launch traced here: 118 us
  matrix products  34.5 us (29%)
  starting transfers between devices  33.9 us (28%)
  other arithmetic  18.2 us (15%)
  waiting for transfers between devices  16.7 us (14%)
  local copies, waits for them, and re-layouts  13.5 us (11%)
  between operations  1.45 us (1%)
    all_to_all x2, starting transfers between devices, scan_send(): return lax.all_to_all(flat.reshape(n, per, width), 'ctx', 0, 0, tiled=True)  13.3 us
    all_to_all x2, starting transfers between devices, scan_return(): lax.all_to_all(summed, 'ctx', 0, 0, tiled=True).reshape(n * per, width)  10.5 us
    all_to_all x2, waiting for transfers between devices, scan_return(): lax.all_to_all(summed, 'ctx', 0, 0, tiled=True).reshape(n * per, width)  9.82 us
    dot_general x12, matrix products, dot_parts(): term = jnp.einsum(pattern, *args, preferred_element_type=f32)  9.06 us
    all_to_all x2, waiting for transfers between devices, scan_send(): return lax.all_to_all(flat.reshape(n, per, width), 'ctx', 0, 0, tiled=True)  6 us
    unnamed x73, local copies, waits for them, and re-layouts  5.96 us
    mul x1, other arithmetic, tri_feature_back(): cotangent * second  5.95 us
    ppermute x3, starting transfers between devices, head_exchange(): lax.ppermute(piece, 'head', [(j, (j + k) % count) for j in range(count)])  5.36 us
  transfers between devices with their start and end apart: 10, of which 5 were waited for; matrix products, arithmetic and copies ran while one was open for 36% of the time, Pallas kernels for 0%

profile of v20, /device:TPU:1, one launch (start us, length us, event | category | flops | bytes accessed | tf_op | source)
XLA Modules:
  0.0 118.3 jit_solution(7072676266188192990)
XLA Ops:
  0.7 1.4 %copy_bitcast_fusion = (bf16[1,256,1,8,128]{4,1,3,2,0:T(8,128)(2,1)S(1)}, bf16[1,256,1,8,128]{4,1,3,2,0:T(8,128)(2,1)S(1)}) fusion(bf16[256,1,8,128]{3,2,1,0:T(8,128)(2,1)} %param.12, bf16[256,1,8,128]{3,2,1,0:T(8,128)(2,1)} %param.9), kind=kLoop, calls=%fused_computation.118 | loop fusion | bytes 2097152 | tf_op jit(solution)/shard_map/stack | solution.py:172
  2.3 4.7 %collective-permute-start.2 = (bf16[2,256,1,2,128]{4,1,3,2,0:T(8,128)(2,1)S(1)}, bf16[2,256,1,2,128]{4,1,3,2,0:T(8,128)(2,1)S(1)}, u32[]{:S(2)}, u32[]{:S(2)}) collective-permute-start(bf16[2,256,1,2,128]{4,1,3,2,0:T(8,128)(2,1)S(1)} %get-tuple-element.44), channel_id=1, source_target_pairs={{0,3},{1,0},{2,1},{3,2},{4,7},{5,4},{6,5},{7,6},{8,11},{9,8},{10,9... | collective-permute-start | bytes 786440 | tf_op jit(solution)/shard_map/ppermute | solution.py:103
  7.0 0.7 collective-permute-start
  7.7 0.4 fusion.165
  8.1 0.4 fusion.166
  8.8 0.8 reduce-precision_convert_fusion.16
  9.6 0.5 fusion.113
  10.1 1.3 %copy-done = f32[2,256,1056]{1,2,0:T(8,128)} copy-done((f32[2,256,1056]{1,2,0:T(8,128)}, f32[2,256,1056]{1,2,0:T(8,128)S(1)}, u32[]{:S(2)}) %copy-start) | copy-done | bytes 2162712
  11.8 0.3 fusion.158
  12.1 0.9 fusion.58
  12.9 8.6 %all-to-all-start = ((f32[32,40,128]{2,1,0:T(8,128)}), f32[32,40,128]{2,1,0:T(8,128)S(1)}, u32[]{:S(2)}, u32[]{:S(2)}) async-start(f32[32,40,128]{2,1,0:T(8,128)} %bitcast.26), calls=%async_computation | async-start | bytes 1310720 | tf_op jit(solution)/shard_map/all_to_all | solution.py:70
  21.7 0.6 slice_bitcast_fusion.5
  22.3 1.2 %pad_maximum_fusion.2 = bf16[2,256,4,2,128]{4,1,3,2,0:T(8,128)(2,1)S(1)} fusion(bf16[2,256,1,2,128]{4,1,3,2,0:T(8,128)(2,1)S(1)} %collective-permute-done.2, bf16[2,256,1,2,128]{4,1,3,2,0:T(8,128)(2,1)} %collective-permute-done.1, bf16[2,256,1,2,128]{4,1,3,2,0:T(8,128)(2,1)} %collective-permute-done, bf16[2,256,1,2,128]{4,1,3,2,0:T(8,128)(2,1)S(1)} %get-tuple-element.28), kind=kLoop, calls=%fused_computation.82 | loop fusion | flops 1572864 | bytes 2097152 | tf_op jit(solution)/shard_map/concatenate | solution.py:105
  23.8 0.7 copy-done.2
  24.5 1.0 reduce-precision_convert_fusion.11
  25.5 4.8 %fusion.81 = f32[2,4,256,1056]{2,3,1,0:T(8,128)} fusion(bf16[96,1056,1,1]{1,0,3,2:T(8,128)(2,1)S(1)} %copy-done.26, bf16[2,4,256,32]{2,3,0,1:T(8,128)(2,1)S(1)} %get-tuple-element.70, bf16[2,4,256,32]{2,3,0,1:T(8,128)(2,1)S(1)} %get-tuple-element.69, bf16[2,4,256,32]{2,3,0,1:T(8,128)(2,1)S(1)} %get-tuple-element.68), kind=kOutput, calls=%fused_computation.129 | convolution fusion | flops 416415744 | bytes 9246720 | tf_op jit(solution)/shard_map/...k,kn->...n/dot_general | solution.py:49
  30.3 4.2 %all-to-all-done = f32[32,40,128]{2,1,0:T(8,128)S(1)} async-done(((f32[32,40,128]{2,1,0:T(8,128)}), f32[32,40,128]{2,1,0:T(8,128)S(1)}, u32[]{:S(2)}, u32[]{:S(2)}) %all-to-all-start) | async-done | bytes 655392 | tf_op jit(solution)/shard_map/all_to_all | solution.py:70
  34.5 0.5 fusion.61
  34.9 1.2 %copy.94 = f32[32,40,128]{2,1,0:T(8,128)} copy(f32[32,40,128]{2,0,1:T(8,128)S(1)} %fusion.61) | data formatting | bytes 1310720 | tf_op jit(solution)/shard_map/ij,jrc->irc/dot_general | solution.py:78
  36.2 4.8 %all-to-all-start.1 = ((f32[32,40,128]{2,1,0:T(8,128)}), f32[32,40,128]{2,1,0:T(8,128)}, u32[]{:S(2)}, u32[]{:S(2)}) async-start(f32[32,40,128]{2,1,0:T(8,128)} %copy.94), calls=%async_computation.1 | async-start | bytes 1310720 | tf_op jit(solution)/shard_map/all_to_all | solution.py:84
  41.0 4.2 %multiply_convert_fusion = bf16[2,4,256,528]{2,3,1,0:T(8,128)(2,1)S(1)} fusion(f32[2,4,256,1056]{2,3,1,0:T(8,128)} %fusion.81), kind=kLoop, calls=%fused_computation.10 | loop fusion | flops 3244032 | bytes 10813440 | tf_op jit(solution)/shard_map/convert_element_type | solution.py:132
  45.2 2.1 %select_convert_fusion.1 = (bf16[2,4,256,256]{2,3,1,0:T(8,128)(2,1)}, f32[2,4,256,256]{2,3,1,0:T(8,128)S(1)}) fusion(pred[256,256]{0,1:T(8,128)(4,1)S(1)} %iota_compare_fusion.1, bf16[2,4,256,528]{2,3,1,0:T(8,128)(2,1)S(1)} %multiply_convert_fusion, bf16[2,256,528]{1,2,0:T(8,128)(2,1)S(1)} %get-tuple-element.27, bf16[528]{0:T(1024)(128)(2,1)S(1)} %copy-done.29), kind=kOutput, calls=%fused_computation.25 | convolution fusion | flops 554442752 | bytes 5915680 | tf_op jit(solution)/shard_map/hmif,hjf->hmij/dot_general | solution.py:191
  47.5 6.5 %all-to-all-done.1 = f32[32,40,128]{2,1,0:T(8,128)} async-done(((f32[32,40,128]{2,1,0:T(8,128)}), f32[32,40,128]{2,1,0:T(8,128)}, u32[]{:S(2)}, u32[]{:S(2)}) %all-to-all-start.1) | async-done | bytes 655392 | tf_op jit(solution)/shard_map/all_to_all | solution.py:84
  54.0 1.1 slice.162
  55.1 0.7 slice.160
  55.8 1.2 %fusion.16 = f32[2,4,256,128]{3,2,0,1:T(8,128)S(1)} fusion(bf16[2,4,256,528]{2,3,1,0:T(8,128)(2,1)S(1)} %multiply_convert_fusion, f32[2,528,128]{2,1,0:T(8,128)S(1)} %bitcast.185, f32[528]{0:T(1024)S(1)} %copy-done.32), kind=kOutput, calls=%fused_computation.27 | convolution fusion | flops 277364736 | bytes 3754048 | tf_op jit(solution)/shard_map/hmif,hfd->hmid/dot_general | solution.py:36
  57.1 2.2 %fusion.23 = f32[2,4,256,128]{3,2,0,1:T(8,128)} fusion(f32[2,4,256,128]{3,2,0,1:T(8,128)S(1)} %fusion.16, bf16[2,4,256,528]{2,3,1,0:T(8,128)(2,1)S(1)} %multiply_convert_fusion, f32[2,528,128]{2,1,0:T(8,128)S(1)} %bitcast.186, f32[528]{0:T(1024)S(1)} %copy-done.32), kind=kOutput, calls=%fused_computation.39 | convolution fusion | flops 277491712 | bytes 4802624 | tf_op jit(solution)/shard_map/hmif,hfd->hmid/dot_general | solution.py:36
  59.3 0.4 fusion.143
  59.7 0.4 fusion.145
  60.2 0.4 copy-done.3
  60.6 1.6 %reduce-precision_convert_fusion.2 = (bf16[2,4,256,128]{3,2,0,1:T(8,128)(2,1)}, bf16[2,4,256,128]{3,2,0,1:T(8,128)(2,1)}, bf16[2,4,256,128]{3,2,0,1:T(8,128)(2,1)}) fusion(f32[2,4,256]{2,0,1:T(2,128)S(1)} %copy.95, bf16[2,256,4,2,128]{4,1,3,2,0:T(8,128)(2,1)S(1)} %copy-done.3), kind=kLoop, calls=%fused_computation.32 | loop fusion | flops 1835008 | bytes 2105344 | tf_op jit(solution)/shard_map/convert_element_type | solution.py:26
  62.2 1.1 fusion.33
  63.3 0.7 fusion.134
  64.0 0.7 fusion.136
  64.7 1.8 %fusion.79 = f32[2,528,128,1]{2,1,3,0:T(8,128)S(1)} fusion(bf16[2,4,256,528]{2,3,1,0:T(8,128)(2,1)S(1)} %multiply_convert_fusion, bf16[2,4,256,128]{3,2,0,1:T(8,128)(2,1)} %get-tuple-element.41), kind=kOutput, calls=%fused_computation.126 | convolution fusion | flops 276824064 | bytes 3227648 | tf_op jit(solution)/shard_map/hmif,hmid->hfd/dot_general | solution.py:203
  66.4 0.9 select_maximum_fusion
  67.3 4.7 %all-to-all-start.2 = ((f32[32,40,128]{2,1,0:T(8,128)}), f32[32,40,128]{2,1,0:T(8,128)}, u32[]{:S(2)}, u32[]{:S(2)}) async-start(f32[32,40,128]{2,1,0:T(8,128)} %bitcast.188), calls=%async_computation.2 | async-start | bytes 1310720 | tf_op jit(solution)/shard_map/all_to_all | solution.py:70
  72.1 1.6 %select_convert_fusion = bf16[2,4,256,256]{2,3,1,0:T(8,128)(2,1)S(1)} fusion(f32[2,4,256]{2,1,0:T(4,128)S(1)} %copy.104, pred[256,256]{0,1:T(8,128)(4,1)} %copy-done.13, bf16[2,4,256,128]{3,2,0,1:T(8,128)(2,1)} %get-tuple-element.41, bf16[256,2,128]{2,0,1:T(8,128)(2,1)} %copy-done.8), kind=kOutput, calls=%fused_computation.24 | convolution fusion | flops 135790592 | bytes 1777664 | tf_op jit(solution)/shard_map/hmid,hjd->hmij/dot_general | solution.py:209
  73.7 1.0 fusion.64
  74.7 1.8 %convolution_bitcast_fusion = f32[2,256,528]{1,2,0:T(8,128)} fusion(bf16[2,4,256,256]{2,3,1,0:T(8,128)(2,1)S(1)} %select_convert_fusion, bf16[2,4,256,528]{2,3,1,0:T(8,128)(2,1)S(1)} %multiply_convert_fusion), kind=kOutput, calls=%fused_computation.35 | convolution fusion | flops 553648128 | bytes 4292608 | tf_op jit(solution)/shard_map/hmij,hmif->hjf/dot_general | solution.py:224
  76.5 1.1 convolution_bitcast_fusion.1
  78.1 5.2 %multiply_add_fusion = f32[2,4,256,528]{2,3,1,0:T(8,128)} fusion(f32[2,528]{1,0:T(2,128)S(1)} %get-tuple-element.89, f32[2,4,256]{2,1,0:T(4,128)S(1)} %copy.104, bf16[2,4,256,128]{2,3,1,0:T(8,128)(2,1)S(1)} %copy.107, bf16[2,4,256,128]{2,3,1,0:T(8,128)(2,1)S(1)} %copy.105, bf16[2,4,256,256]{2,3,1,0:T(8,128)(2,1)} %copy-done.16, ...), kind=kOutput, calls=%fused_computation.9 | convolution fusion | flops 1402175488 | bytes 7516288 | tf_op jit(solution)/shard_map/hmik,hkf->hmif/dot_general | solution.py:216
  83.4 1.8 %all-to-all-done.2 = f32[32,40,128]{2,1,0:T(8,128)} async-done(((f32[32,40,128]{2,1,0:T(8,128)}), f32[32,40,128]{2,1,0:T(8,128)}, u32[]{:S(2)}, u32[]{:S(2)}) %all-to-all-start.2) | async-done | bytes 655392 | tf_op jit(solution)/shard_map/all_to_all | solution.py:70
  85.2 1.6 %fusion.59 = f32[32,40,128]{2,0,1:T(8,128)S(1)} fusion(f32[32,40,128]{2,1,0:T(8,128)} %all-to-all-done.2), kind=kOutput, calls=%fused_computation.100 | convolution fusion | flops 62915584 | bytes 1310720 | tf_op jit(solution)/shard_map/ij,jrc->irc/dot_general | solution.py:78
  86.7 1.2 %copy.116 = f32[32,40,128]{2,1,0:T(8,128)} copy(f32[32,40,128]{2,0,1:T(8,128)S(1)} %fusion.59) | data formatting | bytes 1310720 | tf_op jit(solution)/shard_map/optimization_barrier | solution.py:227
  88.0 5.7 %all-to-all-start.3 = ((f32[32,40,128]{2,1,0:T(8,128)}), f32[32,40,128]{2,1,0:T(8,128)S(1)}, u32[]{:S(2)}, u32[]{:S(2)}) async-start(f32[32,40,128]{2,1,0:T(8,128)} %copy.116), calls=%async_computation.3 | async-start | bytes 1310720 | tf_op jit(solution)/shard_map/all_to_all | solution.py:84
  93.7 5.9 %slice_multiply_fusion = (f32[2,4,256,528]{2,3,1,0:T(8,128)S(1)}, f32[2,4,256,528]{2,3,1,0:T(8,128)S(1)}) fusion(f32[2,4,256,528]{2,3,1,0:T(8,128)} %multiply_add_fusion, f32[2,4,256,1056]{2,3,1,0:T(8,128)} %fusion.81, f32[528]{0:T(1024)S(1)} %copy-done.31), kind=kLoop, calls=%fused_computation.11 | loop fusion | flops 3244032 | bytes 21628992 | tf_op jit(solution)/shard_map/mul | solution.py:139
  99.6 1.4 %reduce-precision_convert_fusion = (bf16[2,4,256,1056]{2,3,1,0:T(8,128)(2,1)S(1)}, bf16[2,4,256,1056]{2,3,1,0:T(8,128)(2,1)S(1)}) fusion(f32[2,4,256,528]{2,3,1,0:T(8,128)S(1)} %get-tuple-element.34, f32[2,4,256,528]{2,3,1,0:T(8,128)S(1)} %get-tuple-element.33), kind=kLoop, calls=%fused_computation.1 | loop fusion | flops 10813440 | bytes 17301504 | tf_op jit(solution)/shard_map/convert_element_type | solution.py:26
  101.0 0.9 fusion.1
  102.0 0.9 reduce-precision_convert_fusion.9
  102.9 0.3 fusion.34
  103.3 3.3 %all-to-all-done.3 = f32[32,40,128]{2,1,0:T(8,128)S(1)} async-done(((f32[32,40,128]{2,1,0:T(8,128)}), f32[32,40,128]{2,1,0:T(8,128)S(1)}, u32[]{:S(2)}, u32[]{:S(2)}) %all-to-all-start.3) | async-done | bytes 655392 | tf_op jit(solution)/shard_map/all_to_all | solution.py:84
  106.8 0.5 fusion.74
  107.3 2.1 %collective-permute-start.4 = (bf16[256,1,2,128]{3,0,1,2:T(8,128)(2,1)S(1)}, bf16[256,1,2,128]{3,0,1,2:T(8,128)(2,1)S(1)}, u32[]{:S(2)}, u32[]{:S(2)}) collective-permute-start(bf16[256,1,2,128]{3,0,1,2:T(8,128)(2,1)S(1)} %get-tuple-element.55), channel_id=1, source_target_pairs={{0,2},{1,3},{2,0},{3,1},{4,6},{5,7},{6,4},{7,5},{8,10},{9,11},{10,... | collective-permute-start | bytes 393224 | tf_op jit(solution)/shard_map/ppermute | solution.py:115
  109.7 2.4 %collective-permute-start.3 = (bf16[256,1,2,128]{3,0,1,2:T(8,128)(2,1)S(1)}, bf16[256,1,2,128]{3,0,1,2:T(8,128)(2,1)S(1)}, u32[]{:S(2)}, u32[]{:S(2)}) collective-permute-start(bf16[256,1,2,128]{3,0,1,2:T(8,128)(2,1)S(1)} %get-tuple-element.53), channel_id=1, source_target_pairs={{0,3},{1,0},{2,1},{3,2},{4,7},{5,4},{6,5},{7,6},{8,11},{9,8},{10,9... | collective-permute-start | bytes 393224 | tf_op jit(solution)/shard_map/ppermute | solution.py:115
  112.1 0.5 fusion.47
  112.6 0.5 slice_multiply_fusion.1
  113.1 0.4 copy-done.27
  113.5 0.3 fusion.51
  114.0 0.4 reduce-precision_convert_fusion.14
  114.6 0.8 copy.120
  115.4 0.8 copy.121
  116.1 0.9 collective-permute-done.5
  117.2 1.1 copy.119
  (103 shorter events, 3.0 us)
Async XLA Ops:
  2.1 5.6 %copy-start.30 = (s32[2,128,32]{1,2,0:T(8,128)S(1)}, s32[2,128,32]{1,2,0:T(8,128)}, u32[]{:S(2)}) copy-start(s32[2,128,32]{1,2,0:T(8,128)} %param.13) | copy-start | bytes 98308
  2.1 5.6 %copy-start.17 = (bf16[256,8,128]{2,1,0:T(8,128)(2,1)S(1)}, bf16[256,8,128]{2,1,0:T(8,128)(2,1)}, u32[]{:S(2)}) copy-start(bf16[256,8,128]{2,1,0:T(8,128)(2,1)} %param.11) | copy-start | bytes 1572868
  2.1 6.0 %copy-start.18 = (bf16[256,8,128]{2,1,0:T(8,128)(2,1)S(1)}, bf16[256,8,128]{2,1,0:T(8,128)(2,1)}, u32[]{:S(2)}) copy-start(bf16[256,8,128]{2,1,0:T(8,128)(2,1)} %param.10) | copy-start | bytes 1572868
  2.3 7.3 %copy-start.25 = (bf16[96,1056,1]{1,0,2:T(8,128)(2,1)S(1)}, bf16[96,1056,1]{1,0,2:T(8,128)(2,1)}, u32[]{:S(2)}) copy-start(bf16[96,1056,1]{1,0,2:T(8,128)(2,1)} %constant.100) | copy-start | bytes 608260
  2.3 20.0 %collective-permute-start.2 = (bf16[2,256,1,2,128]{4,1,3,2,0:T(8,128)(2,1)S(1)}, bf16[2,256,1,2,128]{4,1,3,2,0:T(8,128)(2,1)S(1)}, u32[]{:S(2)}, u32[]{:S(2)}) collective-permute-start(bf16[2,256,1,2,128]{4,1,3,2,0:T(8,128)(2,1)S(1)} %get-tuple-element.44), channel_id=1, source_target_pairs={{0,3},{1,0},{2,1},{3,2},{4,7},{5,4},{6,5},{7,6},{8,11},{9,8},{10,9... | collective-permute-start | bytes 786440 | tf_op jit(solution)/shard_map/ppermute | solution.py:103
  7.0 15.3 %collective-permute-start.1 = (bf16[2,256,1,2,128]{4,1,3,2,0:T(8,128)(2,1)S(1)}, bf16[2,256,1,2,128]{4,1,3,2,0:T(8,128)(2,1)}, u32[]{:S(2)}, u32[]{:S(2)}) collective-permute-start(bf16[2,256,1,2,128]{4,1,3,2,0:T(8,128)(2,1)S(1)} %get-tuple-element.43), channel_id=1, source_target_pairs={{0,2},{1,3},{2,0},{3,1},{4,6},{5,7},{6,4},{7,5},{8,10},{9,11},{10,... | collective-permute-start | bytes 786440 | tf_op jit(solution)/shard_map/ppermute | solution.py:103
  7.0 15.3 %collective-permute-start = (bf16[2,256,1,2,128]{4,1,3,2,0:T(8,128)(2,1)S(1)}, bf16[2,256,1,2,128]{4,1,3,2,0:T(8,128)(2,1)}, u32[]{:S(2)}, u32[]{:S(2)}) collective-permute-start(bf16[2,256,1,2,128]{4,1,3,2,0:T(8,128)(2,1)S(1)} %get-tuple-element.42), channel_id=1, source_target_pairs={{0,1},{1,2},{2,3},{3,0},{4,5},{5,6},{6,7},{7,4},{8,9},{9,10},{10,1... | collective-permute-start | bytes 786440 | tf_op jit(solution)/shard_map/ppermute | solution.py:103
  8.6 3.1 %copy-start.8 = (bf16[256,2,128]{2,0,1:T(8,128)(2,1)}, bf16[256,2,128]{2,0,1:T(8,128)(2,1)S(1)}, u32[]{:S(2)}) copy-start(bf16[256,2,128]{2,0,1:T(8,128)(2,1)S(1)} %get-tuple-element.96) | copy-start | bytes 393220
  8.8 0.8 copy-start.22
  10.1 1.4 %copy-start = (f32[2,256,1056]{1,2,0:T(8,128)}, f32[2,256,1056]{1,2,0:T(8,128)S(1)}, u32[]{:S(2)}) copy-start(f32[2,256,1056]{1,2,0:T(8,128)S(1)} %fusion.113) | copy-start | bytes 6488068
  12.9 21.5 %all-to-all-start = ((f32[32,40,128]{2,1,0:T(8,128)}), f32[32,40,128]{2,1,0:T(8,128)S(1)}, u32[]{:S(2)}, u32[]{:S(2)}) async-start(f32[32,40,128]{2,1,0:T(8,128)} %bitcast.26), calls=%async_computation | async-start | bytes 1310720 | tf_op jit(solution)/shard_map/all_to_all | solution.py:70
  21.6 25.7 %copy-start.13 = (pred[256,256]{0,1:T(8,128)(4,1)}, pred[256,256]{0,1:T(8,128)(4,1)S(1)}, u32[]{:S(2)}) copy-start(pred[256,256]{0,1:T(8,128)(4,1)S(1)} %iota_compare_fusion.1) | copy-start | bytes 196612
  22.3 3.2 %copy-start.26 = (bf16[96,1056,1,1]{1,0,3,2:T(8,128)(2,1)S(1)}, bf16[96,1056,1,1]{1,0,3,2:T(8,128)(2,1)}, u32[]{:S(2)}) copy-start(bf16[96,1056,1,1]{1,0,3,2:T(8,128)(2,1)} %constant.99) | copy-start | bytes 608260
  23.5 1.0 copy-start.2
  36.2 17.8 %all-to-all-start.1 = ((f32[32,40,128]{2,1,0:T(8,128)}), f32[32,40,128]{2,1,0:T(8,128)}, u32[]{:S(2)}, u32[]{:S(2)}) async-start(f32[32,40,128]{2,1,0:T(8,128)} %copy.94), calls=%async_computation.1 | async-start | bytes 1310720 | tf_op jit(solution)/shard_map/all_to_all | solution.py:84
  41.0 4.2 %copy-start.29 = (bf16[528]{0:T(1024)(128)(2,1)S(1)}, bf16[528]{0:T(1024)(128)(2,1)}, u32[]{:S(2)}) copy-start(bf16[528]{0:T(1024)(128)(2,1)} %constant.81.clone) | copy-start | bytes 3172
  47.3 8.5 %copy-start.32 = (f32[528]{0:T(1024)S(1)}, f32[528]{0:T(1024)}, u32[]{:S(2)}) copy-start(f32[528]{0:T(1024)} %constant.95) | copy-start | bytes 6340
  59.3 1.2 %copy-start.3 = (bf16[2,256,4,2,128]{4,1,3,2,0:T(8,128)(2,1)S(1)}, bf16[2,256,4,2,128]{4,1,3,2,0:T(8,128)(2,1)}, u32[]{:S(2)}) copy-start(bf16[2,256,4,2,128]{4,1,3,2,0:T(8,128)(2,1)} %copy-done.2) | copy-start | bytes 3145732
  59.7 2.4 %copy-start.9 = (bf16[256,2,128]{2,0,1:T(8,128)(2,1)S(1)}, bf16[256,2,128]{2,0,1:T(8,128)(2,1)}, u32[]{:S(2)}) copy-start(bf16[256,2,128]{2,0,1:T(8,128)(2,1)} %copy-done.8) | copy-start | bytes 393220
  59.7 2.4 %copy-start.11 = (bf16[2,4,256,256]{2,3,1,0:T(8,128)(2,1)S(1)}, bf16[2,4,256,256]{2,3,1,0:T(8,128)(2,1)}, u32[]{:S(2)}) copy-start(bf16[2,4,256,256]{2,3,1,0:T(8,128)(2,1)} %get-tuple-element.92) | copy-start | bytes 3145732
  59.7 2.4 %copy-start.15 = (f32[2,4,256,128]{3,2,0,1:T(8,128)S(1)}, f32[2,4,256,128]{3,2,0,1:T(8,128)}, u32[]{:S(2)}) copy-start(f32[2,4,256,128]{3,2,0,1:T(8,128)} %fusion.23) | copy-start | bytes 3145732
  67.3 17.8 %all-to-all-start.2 = ((f32[32,40,128]{2,1,0:T(8,128)}), f32[32,40,128]{2,1,0:T(8,128)}, u32[]{:S(2)}, u32[]{:S(2)}) async-start(f32[32,40,128]{2,1,0:T(8,128)} %bitcast.188), calls=%async_computation.2 | async-start | bytes 1310720 | tf_op jit(solution)/shard_map/all_to_all | solution.py:70
  73.7 2.8 %copy-start.16 = (bf16[2,4,256,256]{2,3,1,0:T(8,128)(2,1)}, bf16[2,4,256,256]{2,3,1,0:T(8,128)(2,1)S(1)}, u32[]{:S(2)}) copy-start(bf16[2,4,256,256]{2,3,1,0:T(8,128)(2,1)S(1)} %select_convert_fusion) | copy-start | bytes 3145732
  74.7 1.8 %copy-start.5 = (bf16[2,4,256,128]{3,2,0,1:T(8,128)(2,1)S(1)}, bf16[2,4,256,128]{3,2,0,1:T(8,128)(2,1)}, u32[]{:S(2)}) copy-start(bf16[2,4,256,128]{3,2,0,1:T(8,128)(2,1)} %get-tuple-element.41) | copy-start | bytes 1572868
  74.7 1.8 %copy-start.12 = (bf16[2,4,256,256]{2,3,1,0:T(8,128)(2,1)S(1)}, bf16[2,4,256,256]{2,3,1,0:T(8,128)(2,1)}, u32[]{:S(2)}) copy-start(bf16[2,4,256,256]{2,3,1,0:T(8,128)(2,1)} %get-tuple-element.92) | copy-start | bytes 3145732
  74.7 2.9 %copy-start.7 = (bf16[2,4,256,128]{3,2,0,1:T(8,128)(2,1)S(1)}, bf16[2,4,256,128]{3,2,0,1:T(8,128)(2,1)}, u32[]{:S(2)}) copy-start(bf16[2,4,256,128]{3,2,0,1:T(8,128)(2,1)} %get-tuple-element.40) | copy-start | bytes 1572868
  76.5 1.4 %copy-start.6 = (bf16[2,4,256,128]{3,2,0,1:T(8,128)(2,1)S(1)}, bf16[2,4,256,128]{3,2,0,1:T(8,128)(2,1)}, u32[]{:S(2)}) copy-start(bf16[2,4,256,128]{3,2,0,1:T(8,128)(2,1)} %get-tuple-element.39) | copy-start | bytes 1572868
  76.5 1.6 %copy-start.20 = (bf16[2,128,528]{1,2,0:T(8,128)(2,1)S(1)}, bf16[2,128,528]{1,2,0:T(8,128)(2,1)}, u32[]{:S(2)}) copy-start(bf16[2,128,528]{1,2,0:T(8,128)(2,1)} %get-tuple-element.51) | copy-start | bytes 811012
  76.5 1.6 %copy-start.21 = (bf16[2,128,528]{1,2,0:T(8,128)(2,1)S(1)}, bf16[2,128,528]{1,2,0:T(8,128)(2,1)}, u32[]{:S(2)}) copy-start(bf16[2,128,528]{1,2,0:T(8,128)(2,1)} %get-tuple-element.52) | copy-start | bytes 811012
  83.4 10.3 %copy-start.31 = (f32[528]{0:T(1024)S(1)}, f32[528]{0:T(1024)}, u32[]{:S(2)}) copy-start(f32[528]{0:T(1024)} %constant.82.clone) | copy-start | bytes 6340
  88.0 18.6 %all-to-all-start.3 = ((f32[32,40,128]{2,1,0:T(8,128)}), f32[32,40,128]{2,1,0:T(8,128)S(1)}, u32[]{:S(2)}, u32[]{:S(2)}) async-start(f32[32,40,128]{2,1,0:T(8,128)} %copy.116), calls=%async_computation.3 | async-start | bytes 1310720 | tf_op jit(solution)/shard_map/all_to_all | solution.py:84
  99.6 1.4 %copy-start.19 = (bf16[1056,32,1,1]{0,1,2,3:T(8,128)(2,1)S(1)}, bf16[1056,32,1,1]{0,1,2,3:T(8,128)(2,1)}, u32[]{:S(2)}) copy-start(bf16[1056,32,1,1]{0,1,2,3:T(8,128)(2,1)} %constant.101) | copy-start | bytes 202756
  101.0 1.0 copy-start.14
  102.0 0.9 copy-start.33
  102.0 0.9 copy-start.34
  106.6 5.5 %copy-start.24 = (f32[2,256,128]{2,1,0:T(8,128)S(1)}, f32[2,256,128]{2,1,0:T(8,128)}, u32[]{:S(2)}) copy-start(f32[2,256,128]{2,1,0:T(8,128)} %convolution_bitcast_fusion.1) | copy-start | bytes 786436
  106.7 5.9 %copy-start.1 = (f32[2,256,1056]{1,2,0:T(8,128)S(1)}, f32[2,256,1056]{1,2,0:T(8,128)}, u32[]{:S(2)}) copy-start(f32[2,256,1056]{1,2,0:T(8,128)} %copy-done) | copy-start | bytes 6488068
  106.7 5.9 %copy-start.4 = (f32[2,256,528]{1,2,0:T(8,128)S(1)}, f32[2,256,528]{1,2,0:T(8,128)}, u32[]{:S(2)}) copy-start(f32[2,256,528]{1,2,0:T(8,128)} %convolution_bitcast_fusion) | copy-start | bytes 3244036
  106.8 5.9 %copy-start.10 = (bf16[256,2,128]{2,0,1:T(8,128)(2,1)S(1)}, bf16[256,2,128]{2,0,1:T(8,128)(2,1)}, u32[]{:S(2)}) copy-start(bf16[256,2,128]{2,0,1:T(8,128)(2,1)} %copy-done.8) | copy-start | bytes 393220
  107.3 8.8 %collective-permute-start.4 = (bf16[256,1,2,128]{3,0,1,2:T(8,128)(2,1)S(1)}, bf16[256,1,2,128]{3,0,1,2:T(8,128)(2,1)S(1)}, u32[]{:S(2)}, u32[]{:S(2)}) collective-permute-start(bf16[256,1,2,128]{3,0,1,2:T(8,128)(2,1)S(1)} %get-tuple-element.55), channel_id=1, source_target_pairs={{0,2},{1,3},{2,0},{3,1},{4,6},{5,7},{6,4},{7,5},{8,10},{9,11},{10,... | collective-permute-start | bytes 393224 | tf_op jit(solution)/shard_map/ppermute | solution.py:115
  109.4 7.7 %collective-permute-start.5 = (bf16[256,1,2,128]{3,0,1,2:T(8,128)(2,1)S(1)}, bf16[256,1,2,128]{3,0,1,2:T(8,128)(2,1)S(1)}, u32[]{:S(2)}, u32[]{:S(2)}) collective-permute-start(bf16[256,1,2,128]{3,0,1,2:T(8,128)(2,1)S(1)} %get-tuple-element.54), channel_id=1, source_target_pairs={{0,1},{1,2},{2,3},{3,0},{4,5},{5,6},{6,7},{7,4},{8,9},{9,10},{10,1... | collective-permute-start | bytes 393224 | tf_op jit(solution)/shard_map/ppermute | solution.py:115
  109.7 7.4 %collective-permute-start.3 = (bf16[256,1,2,128]{3,0,1,2:T(8,128)(2,1)S(1)}, bf16[256,1,2,128]{3,0,1,2:T(8,128)(2,1)S(1)}, u32[]{:S(2)}, u32[]{:S(2)}) collective-permute-start(bf16[256,1,2,128]{3,0,1,2:T(8,128)(2,1)S(1)} %get-tuple-element.53), channel_id=1, source_target_pairs={{0,3},{1,0},{2,1},{3,2},{4,7},{5,4},{6,5},{7,6},{8,11},{9,8},{10,9... | collective-permute-start | bytes 393224 | tf_op jit(solution)/shard_map/ppermute | solution.py:115
  112.6 0.9 copy-start.27
  113.1 0.8 copy-start.23
  113.1 0.9 copy-start.28
